TPU v7x, 32 devices: a whole 2x2x4 slice. The times are simulated.
32 devices in a mesh: groups: 1, blk: 8 (over z, y), seg: 2 (over x), freq: 2 (over core).
Axes of the slice: x: 2, y: 2, z: 4, core: 2. Of those that a mesh axis runs over, the one named last changes fastest.
Arguments:
- raw: bfloat16 [64, 64, 16384], P(('groups', 'blk'), 'seg', 'freq'), may hold values from -6 to 6
- taps: float32 [128], replicated, may hold values from -0.5 to 0.5
- send_list: int32 [8, 8, 2], P(('groups', 'blk')), may hold values from 0 to 8, as said below
- recv_row: int32 [8, 8, 2], P(('groups', 'blk')), may hold values from 0 to 16, as said below
Outputs:
- cross_spectra: float32 [2, 256, 128, 128], P(None, ('seg', 'freq'), ('groups', 'blk'))
Inputs may be any that keep to these rules, and one draw needn't show every extreme that they name: send_list[s, o, k] is the local sensing point of source s that goes to owner o in slot k, or 8 for an empty slot; a source names each of its points at most once; the filled slots of a pair come first; some source fills all 2 slots to one owner. recv_row[o, s, k] is the row of owner o that receives slot k of source s, and it is 16 exactly where send_list[s, o, k] is 8; an owner's filled rows are 0 to its count - 1, each once, rising with source and then slot; some owner holds exactly 16 rows.
All inputs are finite; a program needn't handle non-finite values.
Results may differ from a plain program's by a relative error of at most 0.0029.
Values may be sent and summed in bfloat16 or wider, within the bound.
No kernel may reach another device: no remote copies, remote signals or barrier semaphores. Data moves between devices by JAX's collectives and lax.ppermute only.
A program may use at most 128 MiB of HBM per device.

v0:
```python
import math

import jax
import jax.numpy as jnp
from jax import lax
from jax.sharding import PartitionSpec as P

SEG_LEN = 16384
BINS = 256
BAND_LO = 128
HW = 4
OWN = 16


WHITEN_FLOOR = 0.25
TWO_PI = 2.0 * math.pi


def swapped(value, axis, distance):
    mask = 2**distance
    pairs = [(source, source ^ mask) for source in range(lax.axis_size(axis))]
    return lax.ppermute(value, axis, pairs)


def dft_tables(band_index, sample_index):
    wavenumber = BAND_LO + band_index
    phase_int = wavenumber[:, None] * sample_index[None, :] % SEG_LEN
    angles = phase_int.astype(jnp.float32) * (TWO_PI / SEG_LEN)
    norm_scale = 1.0 / math.sqrt(SEG_LEN)
    cos_part = (jnp.cos(angles) * norm_scale).astype(jnp.bfloat16)
    sin_part = (-jnp.sin(angles) * norm_scale).astype(jnp.bfloat16)
    return (cos_part, sin_part)


def response(band_index, taps):
    wavenumber = BAND_LO + band_index
    lag_index = jnp.arange(taps.shape[0], dtype=jnp.int32)
    phase_int = wavenumber[:, None] * lag_index[None, :] % SEG_LEN
    angles = phase_int.astype(jnp.float32) * (TWO_PI / SEG_LEN)
    real_part = jnp.dot(jnp.cos(angles), taps, precision=lax.Precision.HIGHEST)
    imag_part = jnp.dot(-jnp.sin(angles), taps, precision=lax.Precision.HIGHEST)
    return (real_part, imag_part)


def per_device(raw, taps, send_list, recv_row):
    owners_count = lax.axis_size("blk")
    seg_count = lax.axis_size("seg")
    freq_count = lax.axis_size("freq")
    freq_rank = lax.axis_index("freq")
    sections, seg_dev, half_len = raw.shape
    records = raw.reshape(sections * seg_dev, half_len)
    device_bins = BINS // freq_count
    block_bins = device_bins // seg_count
    capacity = send_list.shape[2]

    def band_of(row_ids):
        owner_core = row_ids // device_bins
        local_row = row_ids % device_bins
        return (
            local_row // block_bins * freq_count + owner_core
        ) * block_bins + local_row % block_bins

    sub_rows = math.gcd(device_bins * lax.axis_size("freq"), 64)
    sample_index = freq_rank * half_len + jnp.arange(half_len, dtype=jnp.int32)
    contract = (((1,), (1,)), ((), ()))

    def one_block(first_row):
        row_ids = first_row + jnp.arange(sub_rows, dtype=jnp.int32)
        cos_part, sin_part = dft_tables(band_of(row_ids), sample_index)
        real_part = lax.dot_general(cos_part, records, contract, preferred_element_type=jnp.float32)
        imag_part = lax.dot_general(sin_part, records, contract, preferred_element_type=jnp.float32)
        return jnp.stack([real_part, imag_part], axis=1)

    first_rows = sub_rows * jnp.arange(
        device_bins * lax.axis_size("freq") // sub_rows, dtype=jnp.int32
    )
    blocks = lax.map(one_block, first_rows)
    spectra = lax.psum_scatter(
        blocks.reshape(device_bins * lax.axis_size("freq"), 2, records.shape[0]),
        "freq",
        scatter_dimension=0,
        tiled=True,
    )
    real_part = spectra[:, 0]
    imag_part = spectra[:, 1]
    amplitude = jnp.sqrt(real_part * real_part + imag_part * imag_part + 1e-06)
    amp_blocks = amplitude.reshape(seg_count, block_bins, -1)
    band_rims = jnp.stack([amp_blocks[:, :HW], amp_blocks[:, block_bins - HW :]])
    partner = swapped(band_rims, "freq", 0)
    zero_rim = jnp.zeros_like(partner[1][:1])
    right_prev = jnp.concatenate([zero_rim, partner[1][:-1]], axis=0)
    left_next = jnp.concatenate([partner[0][1:], zero_rim], axis=0)
    first_core = freq_rank == 0
    lower_rim = jnp.where(first_core, right_prev, partner[1])
    upper_rim = jnp.where(first_core, partner[0], left_next)
    padded = jnp.concatenate([lower_rim, amp_blocks, upper_rim], axis=1)
    window_sum = padded[:, 0:block_bins]
    for offset_step in range(1, 2 * HW + 1):
        window_sum = window_sum + padded[:, offset_step : offset_step + block_bins]
    span_ids = jnp.arange(seg_count, dtype=jnp.int32)[:, None]
    offsets = jnp.arange(block_bins, dtype=jnp.int32)[None, :]
    position = (span_ids * freq_count + freq_rank) * block_bins + offsets
    counted = jnp.minimum(position + HW, BINS - 1) - jnp.maximum(position - HW, 0) + 1
    smooth = window_sum / counted.astype(jnp.float32)[:, :, None]
    divisor = jnp.maximum(smooth, WHITEN_FLOOR).reshape(device_bins, -1)
    local_bins = freq_rank * device_bins + jnp.arange(device_bins, dtype=jnp.int32)
    response_re, response_im = response(band_of(local_bins), taps)
    scaled_re = real_part / divisor
    scaled_im = imag_part / divisor
    white_re = scaled_re * response_re[:, None] - scaled_im * response_im[:, None]
    white_im = scaled_re * response_im[:, None] + scaled_im * response_re[:, None]
    whitened = jnp.stack([white_re, white_im], axis=1).astype(jnp.bfloat16)
    whitened = whitened.reshape(device_bins, 2, sections, seg_dev)
    slot_ids = send_list.reshape(-1)
    picker = (slot_ids[:, None] == jnp.arange(sections, dtype=jnp.int32)[None, :]).astype(
        jnp.bfloat16
    )
    packed = jnp.einsum(
        "pc,fxcn->pxnf", picker, whitened, preferred_element_type=jnp.float32
    ).astype(jnp.bfloat16)
    packed = packed.reshape(owners_count, capacity, 2, seg_dev, device_bins)
    arrived = lax.all_to_all(packed, "blk", split_axis=0, concat_axis=0, tiled=True)
    arrived = arrived.reshape(owners_count * capacity, 2, seg_dev, device_bins)
    row_targets = recv_row.reshape(-1)
    placer = (jnp.arange(OWN, dtype=jnp.int32)[:, None] == row_targets[None, :]).astype(
        jnp.bfloat16
    )
    own_block = jnp.einsum(
        "rp,pxnf->xnrf", placer, arrived, preferred_element_type=jnp.float32
    ).astype(jnp.bfloat16)
    incoming = lax.all_gather(own_block, "blk", axis=2, tiled=True)
    cross_re = jnp.einsum("xnif,xnjf->fij", own_block, incoming, preferred_element_type=jnp.float32)
    cross_im = jnp.einsum(
        "nif,njf->fij", own_block[1], incoming[0], preferred_element_type=jnp.float32
    )
    cross_im = cross_im - jnp.einsum(
        "nif,njf->fij", own_block[0], incoming[1], preferred_element_type=jnp.float32
    )
    pair_block = jnp.stack([cross_re, cross_im])
    stacked = lax.psum_scatter(pair_block, "seg", scatter_dimension=1, tiled=True)
    return stacked / jnp.float32(seg_dev * seg_count)


def solution(mesh):
    placed = (
        P(("groups", "blk"), "seg", "freq"),
        P(),
        P(("groups", "blk"), None, None),
        P(("groups", "blk"), None, None),
    )
    return jax.shard_map(
        per_device,
        mesh=mesh,
        in_specs=placed,
        out_specs=P(None, ("seg", "freq"), ("groups", "blk"), None),
        check_vma=False,
    )
```

profile of v0, /device:TPU:0, one launch (start us, length us, event | category | flops | bytes accessed | tf_op | source)
XLA Modules:
  0.0 240.1 jit_solution(1834825556735306245)
XLA Ops:
  6.6 79.6 %while.14 = (s32[]{:T(128)}, f32[4,64,2,256]{3,1,0,2:T(8,128)}, s32[4]{0:T(128)S(1)}, bf16[256,8192]{1,0:T(8,128)(2,1)}, s32[]{:T(128)}, /*index=5*/s32[]{:T(128)}) while((s32[]{:T(128)}, f32[4,64,2,256]{3,1,0,2:T(8,128)}, s32[4]{0:T(128)S(1)}, bf16[256,8192]{1,0:T(8,128)(2,1)}, s32[]{:T(128)}, /*index=5*/s32[]{:T(128)}) %tuple.47), condition=%wide.region_1.2_spmd.clone, body=%wide.region_0.1_spmd.clone.sunk | while | flops 554216192 | bytes 25658240 | solution.py:77
  6.6 0.6 dynamic_slice.10
  7.2 0.7 fusion.91
  7.9 9.9 %convolution_bitcast_fusion.8 = f32[64,1,256]{2,0,1:T(8,128)S(1)} fusion(bf16[256,8192]{1,0:T(8,128)(2,1)} %get-tuple-element.190, s32[8192]{0:T(1024)S(1)} %iota_add_fusion.2, s32[64]{0:T(128)S(1)} %fusion.91), kind=kOutput, calls=%fused_computation.12.clone.1 | convolution fusion | flops 276824064 | bytes 4292864 | tf_op jit(solution)/shard_map/while/body/eval_jaxpr/dot_general | solution.py:70
  17.8 8.0 %convolution_bitcast_fusion.7 = f32[64,1,256]{2,0,1:T(8,128)S(1)} fusion(bf16[256,8192]{1,0:T(8,128)(2,1)S(1)} %copy-done.7, s32[8192]{0:T(1024)S(1)} %iota_add_fusion.2, s32[64]{0:T(128)S(1)} %fusion.91), kind=kOutput, calls=%fused_computation.11.clone.1 | convolution fusion | flops 277348352 | bytes 4292864 | tf_op jit(solution)/shard_map/while/body/eval_jaxpr/dot_general | solution.py:71
  25.8 0.7 fusion.92
  26.5 0.6 dynamic_slice.10
  27.1 0.7 fusion.91
  27.8 9.9 %convolution_bitcast_fusion.8 = f32[64,1,256]{2,0,1:T(8,128)S(1)} fusion(bf16[256,8192]{1,0:T(8,128)(2,1)} %get-tuple-element.190, s32[8192]{0:T(1024)S(1)} %iota_add_fusion.2, s32[64]{0:T(128)S(1)} %fusion.91), kind=kOutput, calls=%fused_computation.12.clone.1 | convolution fusion | flops 276824064 | bytes 4292864 | tf_op jit(solution)/shard_map/while/body/eval_jaxpr/dot_general | solution.py:70
  37.7 8.0 %convolution_bitcast_fusion.7 = f32[64,1,256]{2,0,1:T(8,128)S(1)} fusion(bf16[256,8192]{1,0:T(8,128)(2,1)S(1)} %copy-done.7, s32[8192]{0:T(1024)S(1)} %iota_add_fusion.2, s32[64]{0:T(128)S(1)} %fusion.91), kind=kOutput, calls=%fused_computation.11.clone.1 | convolution fusion | flops 277348352 | bytes 4292864 | tf_op jit(solution)/shard_map/while/body/eval_jaxpr/dot_general | solution.py:71
  45.7 0.7 fusion.92
  46.4 0.6 dynamic_slice.10
  47.0 0.7 fusion.91
  47.7 9.9 %convolution_bitcast_fusion.8 = f32[64,1,256]{2,0,1:T(8,128)S(1)} fusion(bf16[256,8192]{1,0:T(8,128)(2,1)} %get-tuple-element.190, s32[8192]{0:T(1024)S(1)} %iota_add_fusion.2, s32[64]{0:T(128)S(1)} %fusion.91), kind=kOutput, calls=%fused_computation.12.clone.1 | convolution fusion | flops 276824064 | bytes 4292864 | tf_op jit(solution)/shard_map/while/body/eval_jaxpr/dot_general | solution.py:70
  57.6 8.0 %convolution_bitcast_fusion.7 = f32[64,1,256]{2,0,1:T(8,128)S(1)} fusion(bf16[256,8192]{1,0:T(8,128)(2,1)S(1)} %copy-done.7, s32[8192]{0:T(1024)S(1)} %iota_add_fusion.2, s32[64]{0:T(128)S(1)} %fusion.91), kind=kOutput, calls=%fused_computation.11.clone.1 | convolution fusion | flops 277348352 | bytes 4292864 | tf_op jit(solution)/shard_map/while/body/eval_jaxpr/dot_general | solution.py:71
  65.6 0.7 fusion.92
  66.3 0.6 dynamic_slice.10
  66.9 0.7 fusion.91
  67.6 9.9 %convolution_bitcast_fusion.8 = f32[64,1,256]{2,0,1:T(8,128)S(1)} fusion(bf16[256,8192]{1,0:T(8,128)(2,1)} %get-tuple-element.190, s32[8192]{0:T(1024)S(1)} %iota_add_fusion.2, s32[64]{0:T(128)S(1)} %fusion.91), kind=kOutput, calls=%fused_computation.12.clone.1 | convolution fusion | flops 276824064 | bytes 4292864 | tf_op jit(solution)/shard_map/while/body/eval_jaxpr/dot_general | solution.py:70
  77.5 8.0 %convolution_bitcast_fusion.7 = f32[64,1,256]{2,0,1:T(8,128)S(1)} fusion(bf16[256,8192]{1,0:T(8,128)(2,1)S(1)} %copy-done.7, s32[8192]{0:T(1024)S(1)} %iota_add_fusion.2, s32[64]{0:T(128)S(1)} %fusion.91), kind=kOutput, calls=%fused_computation.11.clone.1 | convolution fusion | flops 277348352 | bytes 4292864 | tf_op jit(solution)/shard_map/while/body/eval_jaxpr/dot_general | solution.py:71
  85.5 0.7 fusion.92
  86.2 0.0 reduce-scatter.6.cloned.1.call-update
  86.3 0.5 convolution_bitcast_fusion.3
  86.8 0.1 add_convert_fusion.1
  86.8 10.2 %reduce-scatter.6.cloned.1.call-done = f32[128,2,256]{2,0,1:T(8,128)} async-done(((f32[256,2,256]{2,0,1:T(8,128)}), f32[128,2,256]{2,0,1:T(8,128)}) %reduce-scatter.6.cloned.1.call-update) | async-done | bytes 262160 | tf_op jit(solution)/shard_map/reduce_scatter | solution.py:78
  97.0 1.0 add_sqrt_fusion
  98.1 0.3 collective-permute-start
  98.3 0.5 convolution_bitcast_fusion.4
  98.8 0.1 copy.31
  98.9 0.1 eq.50
  99.0 0.3 collective-permute-done
  99.3 0.1 fusion.28
  99.5 1.1 subtract_convert_fusion
  100.5 0.1 copy.27
  100.7 0.1 copy.28
  100.9 0.3 convolution_convert_fusion.1
  101.1 1.0 copy.32
  102.1 5.8 %all-to-all-start = ((bf16[8,2,2,32,128]{4,1,3,2,0:T(2,128)(2,1)}), bf16[8,2,2,32,128]{4,1,3,2,0:T(2,128)(2,1)S(1)}, u32[]{:S(2)}, u32[]{:S(2)}) async-start(bf16[8,2,2,32,128]{4,1,3,2,0:T(2,128)(2,1)} %copy.32), calls=%async_computation.1 | async-start | bytes 524288 | tf_op jit(solution)/shard_map/all_to_all | solution.py:122
  107.9 0.0 all-gather.2.cloned.1.call-start
  107.9 0.1 copy.34
  108.0 0.1 eq.55
  108.1 9.2 %all-to-all-done = bf16[8,2,2,32,128]{4,1,3,2,0:T(2,128)(2,1)S(1)} async-done(((bf16[8,2,2,32,128]{4,1,3,2,0:T(2,128)(2,1)}), bf16[8,2,2,32,128]{4,1,3,2,0:T(2,128)(2,1)S(1)}, u32[]{:S(2)}, u32[]{:S(2)}) %all-to-all-start) | async-done | bytes 262176 | tf_op jit(solution)/shard_map/all_to_all | solution.py:122
  117.3 0.2 copy.33
  117.4 0.9 fusion.23
  118.4 0.0 reduce-scatter.8.cloned.1.call-start
  118.4 2.7 %copy.35 = bf16[2,32,16,128]{1,2,0,3:T(8,128)(2,1)S(1)} copy(bf16[2,32,16,128]{3,2,1,0:T(8,128)(2,1)} %fusion.23) | data formatting | bytes 524288 | tf_op jit(solution)/shard_map/convert_element_type | solution.py:130
  121.1 1.0 slice_bitcast_fusion.2
  122.1 1.2 copy.39
  123.3 1.2 copy.37
  124.6 44.0 %all-gather.2.cloned.1.call-done = bf16[2,32,128,128]{3,2,1,0:T(8,128)(2,1)} async-done(((bf16[2,32,16,128]{3,2,1,0:T(8,128)(2,1)}), bf16[2,32,128,128]{3,2,1,0:T(8,128)(2,1)}) %all-gather.2.cloned.1.call-update) | async-done | bytes 2097168 | tf_op jit(solution)/shard_map/all_gather | solution.py:131
  168.6 2.7 %slice_bitcast_fusion = (bf16[32,128,128]{2,1,0:T(8,128)(2,1)S(1)}, bf16[32,128,128]{2,1,0:T(8,128)(2,1)}) fusion(bf16[2,32,128,128]{3,2,1,0:T(8,128)(2,1)} %all-gather.2.cloned.1.call-done), kind=kLoop, calls=%fused_computation.50 | loop fusion | bytes 4194304 | tf_op jit(solution)/shard_map/squeeze | solution.py:137
  171.3 1.7 copy.40
  173.0 2.8 %copy.38 = bf16[32,128,128]{1,0,2:T(8,128)(2,1)} copy(bf16[32,128,128]{2,1,0:T(8,128)(2,1)} %get-tuple-element.133) | data formatting | bytes 2097152 | tf_op jit(solution)/shard_map/squeeze | solution.py:134
  175.8 2.8 %fusion.75 = f32[128,16,128]{2,1,0:T(8,128)} fusion(bf16[32,16,128]{0,1,2:T(8,128)(2,1)} %copy.37, bf16[32,128,128]{1,0,2:T(8,128)(2,1)} %copy.38), kind=kOutput, calls=%fused_computation.146 | convolution fusion | flops 16777216 | bytes 2228224 | tf_op jit(solution)/shard_map/nif,njf->fij/dot_general | solution.py:133
  178.6 12.6 %copy.36 = bf16[2,32,128,128]{1,2,0,3:T(8,128)(2,1)} copy(bf16[2,32,128,128]{3,2,1,0:T(8,128)(2,1)S(1)} %copy-done.1) | data formatting | bytes 4194304 | tf_op jit(solution)/shard_map/all_gather | solution.py:131
  191.2 5.8 %convolution_bitcast_fusion.2 = f32[1,128,16,128]{3,2,1,0:T(8,128)S(1)} fusion(bf16[2,32,16,128]{1,2,0,3:T(8,128)(2,1)S(1)} %copy.35, bf16[2,32,128,128]{1,2,0,3:T(8,128)(2,1)} %copy.36), kind=kOutput, calls=%fused_computation.44 | convolution fusion | flops 33554432 | bytes 3407872 | tf_op jit(solution)/shard_map/xnif,xnjf->fij/dot_general | solution.py:132
  197.0 0.0 copy-done.4
  197.1 0.4 fusion.22
  197.5 0.1 pad_maximum_fusion
  197.6 0.3 copy.44
  197.9 3.0 %copy.54 = f32[16,8,32,128]{3,1,2,0:T(8,128)} copy(f32[16,8,32,128]{3,2,1,0:T(8,128)S(1)} %bitcast.118) | data formatting | bytes 4194304
  200.9 30.2 %reduce-scatter.8.cloned.1.call-done = f32[64,4096]{1,0:T(8,128)} async-done(((f32[128,4096]{1,0:T(8,128)}), f32[64,4096]{1,0:T(8,128)}) %reduce-scatter.8.cloned.1.call-update) | async-done | bytes 1048592
  231.1 1.4 copy.51
  232.5 1.1 copy_multiply_fusion
  (38 shorter events, 0.2 us)
Async XLA Ops:
  6.5 79.7 %copy-start = (f32[128]{0:T(128)S(1)}, f32[128]{0:T(128)}, u32[]{:S(2)}) copy-start(f32[128]{0:T(128)} %param.7) | copy-start | bytes 1540
  6.5 90.5 %reduce-scatter.6.cloned.1.call-start = ((), (), s32[]{:S(2)}) async-start(), calls=%async_computation.3 | async-start | bytes 786432 | tf_op jit(solution)/shard_map/reduce_scatter | solution.py:78
  6.5 92.3 %copy-start.5 = (s32[1,8,2]{1,2,0:T(2,128)S(1)}, s32[1,8,2]{1,2,0:T(2,128)}, u32[]{:S(2)}) copy-start(s32[1,8,2]{1,2,0:T(2,128)} %param.8) | copy-start | bytes 196
  7.9 9.9 %copy-start.7 = (bf16[256,8192]{1,0:T(8,128)(2,1)S(1)}, bf16[256,8192]{1,0:T(8,128)(2,1)}, u32[]{:S(2)}) copy-start(bf16[256,8192]{1,0:T(8,128)(2,1)} %get-tuple-element.190) | copy-start | bytes 12582916 | tf_op jit(solution)/shard_map/while
  27.8 9.9 %copy-start.7 = (bf16[256,8192]{1,0:T(8,128)(2,1)S(1)}, bf16[256,8192]{1,0:T(8,128)(2,1)}, u32[]{:S(2)}) copy-start(bf16[256,8192]{1,0:T(8,128)(2,1)} %get-tuple-element.190) | copy-start | bytes 12582916 | tf_op jit(solution)/shard_map/while
  47.7 9.9 %copy-start.7 = (bf16[256,8192]{1,0:T(8,128)(2,1)S(1)}, bf16[256,8192]{1,0:T(8,128)(2,1)}, u32[]{:S(2)}) copy-start(bf16[256,8192]{1,0:T(8,128)(2,1)} %get-tuple-element.190) | copy-start | bytes 12582916 | tf_op jit(solution)/shard_map/while
  67.6 9.9 %copy-start.7 = (bf16[256,8192]{1,0:T(8,128)(2,1)S(1)}, bf16[256,8192]{1,0:T(8,128)(2,1)}, u32[]{:S(2)}) copy-start(bf16[256,8192]{1,0:T(8,128)(2,1)} %get-tuple-element.190) | copy-start | bytes 12582916 | tf_op jit(solution)/shard_map/while
  86.2 21.7 %copy-start.6 = (s32[1,8,2]{1,2,0:T(2,128)S(1)}, s32[1,8,2]{1,2,0:T(2,128)}, u32[]{:S(2)}) copy-start(s32[1,8,2]{1,2,0:T(2,128)} %param.9) | copy-start | bytes 196
  98.1 1.2 collective-permute-start
  102.1 15.2 %all-to-all-start = ((bf16[8,2,2,32,128]{4,1,3,2,0:T(2,128)(2,1)}), bf16[8,2,2,32,128]{4,1,3,2,0:T(2,128)(2,1)S(1)}, u32[]{:S(2)}, u32[]{:S(2)}) async-start(bf16[8,2,2,32,128]{4,1,3,2,0:T(2,128)(2,1)} %copy.32), calls=%async_computation.1 | async-start | bytes 524288 | tf_op jit(solution)/shard_map/all_to_all | solution.py:122
  107.9 60.7 %all-gather.2.cloned.1.call-start = ((), (), s32[]{:S(2)}) async-start(), calls=%async_computation.4 | async-start | bytes 2359296 | tf_op jit(solution)/shard_map/all_gather | solution.py:131
  118.4 112.7 %reduce-scatter.8.cloned.1.call-start = ((), (), s32[]{:S(2)}) async-start(), calls=%async_computation.5 | async-start | bytes 3145728
  173.0 5.6 %copy-start.1 = (bf16[2,32,128,128]{3,2,1,0:T(8,128)(2,1)S(1)}, bf16[2,32,128,128]{3,2,1,0:T(8,128)(2,1)}, u32[]{:S(2)}) copy-start(bf16[2,32,128,128]{3,2,1,0:T(8,128)(2,1)} %all-gather.2.cloned.1.call-done) | copy-start | bytes 6291460
  191.2 5.8 %copy-start.2 = (bf16[32,128,128]{1,0,2:T(8,128)(2,1)S(1)}, bf16[32,128,128]{1,0,2:T(8,128)(2,1)}, u32[]{:S(2)}) copy-start(bf16[32,128,128]{1,0,2:T(8,128)(2,1)} %copy.40) | copy-start | bytes 3145732
  191.2 5.8 %copy-start.3 = (f32[128,16,128]{2,1,0:T(8,128)S(1)}, f32[128,16,128]{2,1,0:T(8,128)}, u32[]{:S(2)}) copy-start(f32[128,16,128]{2,1,0:T(8,128)} %fusion.75) | copy-start | bytes 3145732
  191.2 5.8 %copy-start.4 = (bf16[32,16,128]{0,1,2:T(8,128)(2,1)S(1)}, bf16[32,16,128]{0,1,2:T(8,128)(2,1)}, u32[]{:S(2)}) copy-start(bf16[32,16,128]{0,1,2:T(8,128)(2,1)} %copy.39) | copy-start | bytes 393220
Sparse Core Ops, SparseCore 0:
  86.3 10.6 reduce-scatter.5
  118.5 50.0 all-gather.1
  201.1 30.0 reduce-scatter.7
where the time goes:
time: 241 us; the launch traced here: 240 us
  waiting for transfers between devices  93.9 us (39%)
  matrix products  82.7 us (34%)
  local copies, waits for them, and re-layouts  35 us (15%)
  between operations  13.3 us (6%)
  other arithmetic  8.97 us (4%)
  starting transfers between devices  6.12 us (3%)
    all_gather x1, waiting for transfers between devices, per_device(): incoming = lax.all_gather(own_block, 'blk', axis=2, tiled=True)  44 us
    dot_general x4, matrix products, one_block(): lax.dot_general(cos_part, records, contract, preferred_element_type=jnp.f...  39.7 us
    dot_general x4, matrix products, one_block(): lax.dot_general(sin_part, records, contract, preferred_element_type=jnp.f...  31.9 us
    unnamed x4, waiting for transfers between devices  30.2 us
    all_gather x1, local copies, waits for them, and re-layouts, per_device(): incoming = lax.all_gather(own_block, 'blk', axis=2, tiled=True)  12.6 us
    reduce_scatter x1, waiting for transfers between devices, per_device(): lax.psum_scatter(blocks.reshape(device_bins * lax.axis_size('freq'), 2, r...  10.2 us
    all_to_all x1, waiting for transfers between devices, per_device(): lax.all_to_all(packed, 'blk', split_axis=0, concat_axis=0, tiled=True)  9.18 us
    dot_general x1, matrix products, per_device(): jnp.einsum('xnif,xnjf->fij', own_block, incoming, preferred_element_type=...  5.79 us
  transfers between devices with their start and end apart: 5, of which 5 were waited for; matrix products, arithmetic and copies ran while one was open for 3% of the time, Pallas kernels for 0%

commit v1 on v0

--- a/solution.py
+++ b/solution.py
@@ -32,6 +32,30 @@
     return (cos_part, sin_part)
 
 
+def dft_tables_fast(band_index, first_sample, count):
+    lanes = 128
+    wavenumber = BAND_LO + band_index
+    coarse = (first_sample + lanes * jnp.arange(count // lanes, dtype=jnp.int32))
+    fine = jnp.arange(lanes, dtype=jnp.int32)
+    coarse_angle = (wavenumber[:, None] * coarse[None, :] % SEG_LEN).astype(jnp.float32) * (
+        TWO_PI / SEG_LEN
+    )
+    fine_angle = (wavenumber[:, None] * fine[None, :] % SEG_LEN).astype(jnp.float32) * (
+        TWO_PI / SEG_LEN
+    )
+    cos_a = jnp.cos(coarse_angle)[:, :, None]
+    sin_a = jnp.sin(coarse_angle)[:, :, None]
+    cos_b = jnp.cos(fine_angle)[:, None, :]
+    sin_b = jnp.sin(fine_angle)[:, None, :]
+    norm_scale = 1.0 / math.sqrt(SEG_LEN)
+    cos_sum = cos_a * cos_b - sin_a * sin_b
+    sin_sum = sin_a * cos_b + cos_a * sin_b
+    rows = band_index.shape[0]
+    cos_part = (cos_sum * norm_scale).astype(jnp.bfloat16).reshape(rows, count)
+    sin_part = (-sin_sum * norm_scale).astype(jnp.bfloat16).reshape(rows, count)
+    return (cos_part, sin_part)
+
+
 def response(band_index, taps):
     wavenumber = BAND_LO + band_index
     lag_index = jnp.arange(taps.shape[0], dtype=jnp.int32)
@@ -60,27 +84,24 @@
             local_row // block_bins * freq_count + owner_core
         ) * block_bins + local_row % block_bins
 
-    sub_rows = math.gcd(device_bins * lax.axis_size("freq"), 64)
-    sample_index = freq_rank * half_len + jnp.arange(half_len, dtype=jnp.int32)
+    band_rows = band_of(jnp.arange(device_bins * freq_count, dtype=jnp.int32))
+    cos_part, sin_part = dft_tables_fast(band_rows, freq_rank * half_len, half_len)
     contract = (((1,), (1,)), ((), ()))
-
-    def one_block(first_row):
-        row_ids = first_row + jnp.arange(sub_rows, dtype=jnp.int32)
-        cos_part, sin_part = dft_tables(band_of(row_ids), sample_index)
-        real_part = lax.dot_general(cos_part, records, contract, preferred_element_type=jnp.float32)
-        imag_part = lax.dot_general(sin_part, records, contract, preferred_element_type=jnp.float32)
-        return jnp.stack([real_part, imag_part], axis=1)
-
-    first_rows = sub_rows * jnp.arange(
-        device_bins * lax.axis_size("freq") // sub_rows, dtype=jnp.int32
-    )
-    blocks = lax.map(one_block, first_rows)
-    spectra = lax.psum_scatter(
-        blocks.reshape(device_bins * lax.axis_size("freq"), 2, records.shape[0]),
-        "freq",
-        scatter_dimension=0,
-        tiled=True,
-    )
+    real_all = lax.dot_general(cos_part, records, contract, preferred_element_type=jnp.float32)
+    imag_all = lax.dot_general(sin_part, records, contract, preferred_element_type=jnp.float32)
+    blocks = jnp.stack([real_all, imag_all], axis=1)
+    blocks = blocks.reshape(freq_count, device_bins, 2, records.shape[0])
+    if freq_count == 2:
+        kept = jnp.where(freq_rank == 0, blocks[0], blocks[1])
+        sent = jnp.where(freq_rank == 0, blocks[1], blocks[0])
+        spectra = kept + swapped(sent, "freq", 0)
+    else:
+        spectra = lax.psum_scatter(
+            blocks.reshape(device_bins * freq_count, 2, records.shape[0]),
+            "freq",
+            scatter_dimension=0,
+            tiled=True,
+        )
     real_part = spectra[:, 0]
     imag_part = spectra[:, 1]
     amplitude = jnp.sqrt(real_part * real_part + imag_part * imag_part + 1e-06)

time: 241 us -> 165 us (0.68)
  matrix products: 82.7 us -> 16.9 us
  waiting for transfers between devices: 93.9 us -> 83.7 us
    dot_general x8 -> x2, matrix products: 71.6 us -> 5.74 us  [the longest x1 2.87 us: per_device(): lax.dot_general(cos_part, records, contract, preferred_element_type=jnp.f...]
    reduce_scatter x1 -> x0, waiting for transfers between devices: 10.2 us -> none  [per_device(): lax.psum_scatter(blocks.reshape(device_bins * lax.axis_size('freq'), 2, r...]
    convert_element_type x0 -> x1, other arithmetic: none -> 4.96 us  [dft_tables_fast(): cos_part = (cos_sum * norm_scale).astype(jnp.bfloat16).reshape(rows, count)]
    dynamic_update_slice x4 -> x0, other arithmetic: 2.79 us -> none  [per_device(): blocks = lax.map(one_block, first_rows)]
    add x8 -> x3, other arithmetic: 2.64 us -> 0.05 us  [the longest x1 0.04 us: per_device(): spectra = kept + swapped(sent, 'freq', 0)]
    dynamic_slice x4 -> x0, local copies, waits for them, and re-layouts: 2.47 us -> none  [per_device(): blocks = lax.map(one_block, first_rows)]
    unnamed x4 -> x3, waiting for transfers between devices: 30.2 us -> 30.2 us
    unnamed x19 -> x21, local copies, waits for them, and re-layouts: 4.94 us -> 4.96 us
  transfers between devices with their start and end apart: 5 -> 5, of which waited for: 5 -> 5; matrix products, arithmetic and copies ran while one was open for 3% -> 5% of each run, Pallas kernels for 0% -> 0%
where the time goes in v1:
time: 165 us; the launch traced here: 164 us
  waiting for transfers between devices  83.7 us (51%)
  local copies, waits for them, and re-layouts  33.8 us (20%)
  matrix products  16.9 us (10%)
  between operations  13.6 us (8%)
  starting transfers between devices  8.39 us (5%)
  other arithmetic  7.81 us (5%)
    all_gather x1, waiting for transfers between devices, per_device(): incoming = lax.all_gather(own_block, 'blk', axis=2, tiled=True)  43.8 us
    unnamed x3, waiting for transfers between devices  30.2 us
    all_gather x1, local copies, waits for them, and re-layouts, per_device(): incoming = lax.all_gather(own_block, 'blk', axis=2, tiled=True)  12.6 us
    all_to_all x1, waiting for transfers between devices, per_device(): lax.all_to_all(packed, 'blk', split_axis=0, concat_axis=0, tiled=True)  9.02 us
    all_to_all x1, starting transfers between devices, per_device(): lax.all_to_all(packed, 'blk', split_axis=0, concat_axis=0, tiled=True)  7.18 us
    squeeze x2, local copies, waits for them, and re-layouts, per_device(): incoming[1]  5.95 us
    dot_general x1, matrix products, per_device(): jnp.einsum('xnif,xnjf->fij', own_block, incoming, preferred_element_type=...  5.79 us
    unnamed x21, local copies, waits for them, and re-layouts  4.96 us
  transfers between devices with their start and end apart: 5, of which 5 were waited for; matrix products, arithmetic and copies ran while one was open for 5% of the time, Pallas kernels for 0%

profile of v1, /device:TPU:0, one launch (start us, length us, event | category | flops | bytes accessed | tf_op | source)
XLA Modules:
  0.0 164.3 jit_solution(13299411521968200792)
XLA Ops:
  6.5 0.0 copy-start
  6.6 0.6 fusion.52
  7.2 0.6 fusion.54
  7.8 0.0 copy-start.7
  7.8 5.0 %multiply_convert_fusion.1 = (bf16[256,64,128]{2,1,0:T(8,128)(2,1)S(1)}, bf16[256,64,128]{2,1,0:T(8,128)(2,1)S(1)}) fusion(f32[256,128]{1,0:T(8,128)S(1)} %get-tuple-element.22, f32[256,64]{1,0:T(8,128)S(1)} %get-tuple-element.20, f32[256,128]{1,0:T(8,128)S(1)} %get-tuple-element.21, f32[256,64]{1,0:T(8,128)S(1)} %get-tuple-element.19), kind=kLoop, calls=%fused_computation.1 | loop fusion | flops 23068672 | bytes 8781824 | tf_op jit(solution)/shard_map/convert_element_type | solution.py:54
  12.7 0.0 copy-done.7
  12.7 2.9 %fusion.8 = f32[256,1,256]{0,2,1:T(8,128)S(1)} fusion(bf16[256,8192]{1,0:T(8,128)(2,1)S(1)} %bitcast.112, bf16[32,8,64,128]{3,2,1,0:T(8,128)(2,1)S(1)} %bitcast.102), kind=kOutput, calls=%fused_computation.16 | convolution fusion | flops 1073741824 | bytes 8650752 | tf_op jit(solution)/shard_map/dot_general | solution.py:90
  15.6 0.0 copy-start.5
  15.6 2.9 %fusion.11 = f32[256,1,256]{0,2,1:T(8,128)S(1)} fusion(bf16[256,8192]{1,0:T(8,128)(2,1)S(1)} %bitcast.113, bf16[32,8,64,128]{3,2,1,0:T(8,128)(2,1)S(1)} %bitcast.101), kind=kOutput, calls=%fused_computation.17 | convolution fusion | flops 1073741824 | bytes 8650752 | tf_op jit(solution)/shard_map/dot_general | solution.py:91
  18.5 0.0 copy-start.6
  18.6 0.5 collective-permute-start
  19.1 0.0 copy-done
  19.1 0.5 convolution_bitcast_fusion.1
  19.6 0.1 add_convert_fusion.1
  19.7 0.5 collective-permute-done
  20.3 0.1 add_sqrt_fusion
  20.3 0.1 copy.32
  20.5 0.4 collective-permute-start.1
  20.9 0.5 convolution_bitcast_fusion.2
  21.4 0.0 copy-done.5
  21.4 0.1 copy.37
  21.5 0.1 eq.48
  21.6 0.2 collective-permute-done.1
  21.8 0.1 fusion.19
  21.9 0.1 copy.33
  22.0 0.1 subtract_convert_fusion
  22.1 0.3 convolution_convert_fusion.1
  22.4 1.0 copy.38
  23.4 7.2 %all-to-all-start = ((bf16[8,2,2,32,128]{4,1,3,2,0:T(2,128)(2,1)}), bf16[8,2,2,32,128]{4,1,3,2,0:T(2,128)(2,1)S(1)}, u32[]{:S(2)}, u32[]{:S(2)}) async-start(bf16[8,2,2,32,128]{4,1,3,2,0:T(2,128)(2,1)} %copy.38), calls=%async_computation | async-start | bytes 524288 | tf_op jit(solution)/shard_map/all_to_all | solution.py:143
  30.6 0.0 all-gather.2.cloned.1.call-start
  30.6 0.0 copy-done.6
  30.6 0.1 copy.40
  30.7 0.1 eq.53
  30.8 9.0 %all-to-all-done = bf16[8,2,2,32,128]{4,1,3,2,0:T(2,128)(2,1)S(1)} async-done(((bf16[8,2,2,32,128]{4,1,3,2,0:T(2,128)(2,1)}), bf16[8,2,2,32,128]{4,1,3,2,0:T(2,128)(2,1)S(1)}, u32[]{:S(2)}, u32[]{:S(2)}) %all-to-all-start) | async-done | bytes 262176 | tf_op jit(solution)/shard_map/all_to_all | solution.py:143
  39.8 0.2 copy.39
  40.0 0.9 fusion.7
  40.9 0.0 all-gather.2.cloned.1.call-update
  40.9 0.2 reduce-scatter.5.cloned.1.call-start
  41.2 2.7 %copy.41 = bf16[2,32,16,128]{1,2,0,3:T(8,128)(2,1)S(1)} copy(bf16[2,32,16,128]{3,2,1,0:T(8,128)(2,1)} %fusion.7) | data formatting | bytes 524288 | tf_op jit(solution)/shard_map/convert_element_type | solution.py:151
  43.8 1.0 slice_bitcast_fusion.2
  44.8 1.2 copy.45
  46.1 1.2 copy.43
  47.3 43.8 %all-gather.2.cloned.1.call-done = bf16[2,32,128,128]{3,2,1,0:T(8,128)(2,1)} async-done(((bf16[2,32,16,128]{3,2,1,0:T(8,128)(2,1)}), bf16[2,32,128,128]{3,2,1,0:T(8,128)(2,1)}) %all-gather.2.cloned.1.call-update) | async-done | bytes 2097168 | tf_op jit(solution)/shard_map/all_gather | solution.py:152
  91.2 3.1 %slice_bitcast_fusion = (bf16[32,128,128]{2,1,0:T(8,128)(2,1)}, bf16[32,128,128]{2,1,0:T(8,128)(2,1)}) fusion(bf16[2,32,128,128]{3,2,1,0:T(8,128)(2,1)} %all-gather.2.cloned.1.call-done), kind=kLoop, calls=%fused_computation.20 | loop fusion | bytes 4194304 | tf_op jit(solution)/shard_map/squeeze | solution.py:158
  94.3 2.8 %copy.46 = bf16[32,128,128]{1,0,2:T(8,128)(2,1)} copy(bf16[32,128,128]{2,1,0:T(8,128)(2,1)} %get-tuple-element.5) | data formatting | bytes 2097152 | tf_op jit(solution)/shard_map/squeeze | solution.py:158
  97.1 2.6 %copy.44 = bf16[32,128,128]{1,0,2:T(8,128)(2,1)} copy(bf16[32,128,128]{2,1,0:T(8,128)(2,1)} %get-tuple-element.6) | data formatting | bytes 2097152 | tf_op jit(solution)/shard_map/squeeze | solution.py:155
  99.7 2.8 %fusion.85 = f32[128,16,128]{2,1,0:T(8,128)} fusion(bf16[32,16,128]{0,1,2:T(8,128)(2,1)} %copy.43, bf16[32,128,128]{1,0,2:T(8,128)(2,1)} %copy.44), kind=kOutput, calls=%fused_computation.159 | convolution fusion | flops 16777216 | bytes 2228224 | tf_op jit(solution)/shard_map/nif,njf->fij/dot_general | solution.py:154
  102.5 0.0 copy-done.1
  102.5 12.6 %copy.42 = bf16[2,32,128,128]{1,2,0,3:T(8,128)(2,1)} copy(bf16[2,32,128,128]{3,2,1,0:T(8,128)(2,1)S(1)} %copy-done.1) | data formatting | bytes 4194304 | tf_op jit(solution)/shard_map/all_gather | solution.py:152
  115.1 0.0 copy-start.2
  115.1 0.0 copy-start.3
  115.1 0.0 copy-start.4
  115.1 5.8 %convolution_bitcast_fusion = f32[1,128,16,128]{3,2,1,0:T(8,128)S(1)} fusion(bf16[2,32,16,128]{1,2,0,3:T(8,128)(2,1)S(1)} %copy.41, bf16[2,32,128,128]{1,2,0,3:T(8,128)(2,1)} %copy.42), kind=kOutput, calls=%fused_computation.12 | convolution fusion | flops 33554432 | bytes 3407872 | tf_op jit(solution)/shard_map/xnif,xnjf->fij/dot_general | solution.py:153
  120.9 0.0 copy-done.2
  120.9 0.0 copy-done.3
  120.9 0.0 copy-done.4
  120.9 0.4 fusion.6
  121.4 0.1 pad_maximum_fusion
  121.5 0.3 copy.50
  121.8 3.0 %copy.70 = f32[16,8,32,128]{3,1,2,0:T(8,128)} copy(f32[16,8,32,128]{3,2,1,0:T(8,128)S(1)} %bitcast.100) | data formatting | bytes 4194304
  124.8 0.0 reduce-scatter.5.cloned.1.call-update
  124.8 30.2 %reduce-scatter.5.cloned.1.call-done = f32[64,4096]{1,0:T(8,128)} async-done(((f32[128,4096]{1,0:T(8,128)}), f32[64,4096]{1,0:T(8,128)}) %reduce-scatter.5.cloned.1.call-update) | async-done | bytes 1048592
  155.0 1.4 copy.55
  156.4 1.1 copy_multiply_fusion
  (13 shorter events, 0.2 us)
Async XLA Ops:
  6.5 12.6 %copy-start = (f32[128]{0:T(128)S(1)}, f32[128]{0:T(128)}, u32[]{:S(2)}) copy-start(f32[128]{0:T(128)} %param.5) | copy-start | bytes 1540
  7.8 5.0 %copy-start.7 = (bf16[8,32,8192]{2,1,0:T(8,128)(2,1)S(1)}, bf16[8,32,8192]{2,1,0:T(8,128)(2,1)}, u32[]{:S(2)}) copy-start(bf16[8,32,8192]{2,1,0:T(8,128)(2,1)} %param.4) | copy-start | bytes 12582916
  15.6 5.8 %copy-start.5 = (s32[1,8,2]{1,2,0:T(2,128)S(1)}, s32[1,8,2]{1,2,0:T(2,128)}, u32[]{:S(2)}) copy-start(s32[1,8,2]{1,2,0:T(2,128)} %param.6) | copy-start | bytes 196
  18.5 12.1 %copy-start.6 = (s32[1,8,2]{1,2,0:T(2,128)S(1)}, s32[1,8,2]{1,2,0:T(2,128)}, u32[]{:S(2)}) copy-start(s32[1,8,2]{1,2,0:T(2,128)} %param.7) | copy-start | bytes 196
  18.6 1.7 %collective-permute-start = (f32[128,2,256]{0,2,1:T(8,128)S(1)}, f32[128,2,256]{0,2,1:T(8,128)S(1)}, u32[]{:S(2)}, u32[]{:S(2)}) collective-permute-start(f32[128,2,256]{0,2,1:T(8,128)S(1)} %broadcast_select_fusion), channel_id=1, source_target_pairs={{0,1},{1,0},{2,3},{3,2},{4,5},{5,4},{6,7},{7,6},{8,9},{9,8},{10,11... | collective-permute-start | bytes 786440 | tf_op jit(solution)/shard_map/ppermute | solution.py:22
  20.5 1.3 collective-permute-start.1
  23.4 16.4 %all-to-all-start = ((bf16[8,2,2,32,128]{4,1,3,2,0:T(2,128)(2,1)}), bf16[8,2,2,32,128]{4,1,3,2,0:T(2,128)(2,1)S(1)}, u32[]{:S(2)}, u32[]{:S(2)}) async-start(bf16[8,2,2,32,128]{4,1,3,2,0:T(2,128)(2,1)} %copy.38), calls=%async_computation | async-start | bytes 524288 | tf_op jit(solution)/shard_map/all_to_all | solution.py:143
  30.6 60.6 %all-gather.2.cloned.1.call-start = ((), (), s32[]{:S(2)}) async-start(), calls=%async_computation.2 | async-start | bytes 2359296 | tf_op jit(solution)/shard_map/all_gather | solution.py:152
  40.9 114.1 %reduce-scatter.5.cloned.1.call-start = ((), (), s32[]{:S(2)}) async-start(), calls=%async_computation.3 | async-start | bytes 3145728
  94.3 8.3 %copy-start.1 = (bf16[2,32,128,128]{3,2,1,0:T(8,128)(2,1)S(1)}, bf16[2,32,128,128]{3,2,1,0:T(8,128)(2,1)}, u32[]{:S(2)}) copy-start(bf16[2,32,128,128]{3,2,1,0:T(8,128)(2,1)} %all-gather.2.cloned.1.call-done) | copy-start | bytes 6291460
  115.1 5.8 %copy-start.2 = (bf16[32,128,128]{1,0,2:T(8,128)(2,1)S(1)}, bf16[32,128,128]{1,0,2:T(8,128)(2,1)}, u32[]{:S(2)}) copy-start(bf16[32,128,128]{1,0,2:T(8,128)(2,1)} %copy.46) | copy-start | bytes 3145732
  115.1 5.8 %copy-start.3 = (f32[128,16,128]{2,1,0:T(8,128)S(1)}, f32[128,16,128]{2,1,0:T(8,128)}, u32[]{:S(2)}) copy-start(f32[128,16,128]{2,1,0:T(8,128)} %fusion.85) | copy-start | bytes 3145732
  115.1 5.8 %copy-start.4 = (bf16[32,16,128]{0,1,2:T(8,128)(2,1)S(1)}, bf16[32,16,128]{0,1,2:T(8,128)(2,1)}, u32[]{:S(2)}) copy-start(bf16[32,16,128]{0,1,2:T(8,128)(2,1)} %copy.45) | copy-start | bytes 393220
Sparse Core Ops, SparseCore 0:
  41.0 50.0 all-gather.1
  125.0 29.9 reduce-scatter.4

commit v2 on v1

--- a/solution.py
+++ b/solution.py
@@ -131,35 +131,51 @@
     white_re = scaled_re * response_re[:, None] - scaled_im * response_im[:, None]
     white_im = scaled_re * response_im[:, None] + scaled_im * response_re[:, None]
     whitened = jnp.stack([white_re, white_im], axis=1).astype(jnp.bfloat16)
-    whitened = whitened.reshape(device_bins, 2, sections, seg_dev)
-    slot_ids = send_list.reshape(-1)
-    picker = (slot_ids[:, None] == jnp.arange(sections, dtype=jnp.int32)[None, :]).astype(
+    whitened = whitened.reshape(seg_count, block_bins, 2, sections, seg_dev)
+    whitened = jnp.transpose(whitened, (0, 1, 3, 2, 4))
+    seg_rank = lax.axis_index("seg")
+    pieces = [lax.dynamic_index_in_dim(whitened, seg_rank, axis=0, keepdims=False)]
+    for shift in range(1, seg_count):
+        outgoing = lax.dynamic_index_in_dim(
+            whitened, (seg_rank + shift) % seg_count, axis=0, keepdims=False
+        )
+        pairs = [(source, (source + shift) % seg_count) for source in range(seg_count)]
+        pieces.append(lax.ppermute(outgoing, "seg", pairs))
+    local = jnp.stack(pieces, axis=3).reshape(block_bins, sections, -1)
+    all_segs = seg_dev * seg_count
+    gathered = lax.all_gather(local, "blk", axis=1, tiled=True)
+    tables = lax.all_gather(jnp.stack([send_list, recv_row]), "blk", axis=1, tiled=True)
+    send_all = tables[0]
+    recv_all = tables[1]
+    rows_count = owners_count * OWN
+    chans_count = owners_count * sections
+    chosen = jnp.transpose(send_all, (1, 0, 2))
+    valid = (chosen < sections) & (recv_all < OWN)
+    source_ids = jnp.arange(owners_count, dtype=jnp.int32)[None, :, None]
+    owner_ids = jnp.arange(owners_count, dtype=jnp.int32)[:, None, None]
+    channel = jnp.where(valid, source_ids * sections + chosen, -1).reshape(-1)
+    target = jnp.where(valid, owner_ids * OWN + recv_all, -1).reshape(-1)
+    row_hot = (target[:, None] == jnp.arange(rows_count, dtype=jnp.int32)[None, :]).astype(
         jnp.bfloat16
     )
-    packed = jnp.einsum(
-        "pc,fxcn->pxnf", picker, whitened, preferred_element_type=jnp.float32
-    ).astype(jnp.bfloat16)
-    packed = packed.reshape(owners_count, capacity, 2, seg_dev, device_bins)
-    arrived = lax.all_to_all(packed, "blk", split_axis=0, concat_axis=0, tiled=True)
-    arrived = arrived.reshape(owners_count * capacity, 2, seg_dev, device_bins)
-    row_targets = recv_row.reshape(-1)
-    placer = (jnp.arange(OWN, dtype=jnp.int32)[:, None] == row_targets[None, :]).astype(
+    chan_hot = (channel[:, None] == jnp.arange(chans_count, dtype=jnp.int32)[None, :]).astype(
         jnp.bfloat16
     )
-    own_block = jnp.einsum(
-        "rp,pxnf->xnrf", placer, arrived, preferred_element_type=jnp.float32
+    selector = jnp.einsum(
+        "er,ec->rc", row_hot, chan_hot, preferred_element_type=jnp.float32
     ).astype(jnp.bfloat16)
-    incoming = lax.all_gather(own_block, "blk", axis=2, tiled=True)
-    cross_re = jnp.einsum("xnif,xnjf->fij", own_block, incoming, preferred_element_type=jnp.float32)
-    cross_im = jnp.einsum(
-        "nif,njf->fij", own_block[1], incoming[0], preferred_element_type=jnp.float32
-    )
-    cross_im = cross_im - jnp.einsum(
-        "nif,njf->fij", own_block[0], incoming[1], preferred_element_type=jnp.float32
-    )
-    pair_block = jnp.stack([cross_re, cross_im])
-    stacked = lax.psum_scatter(pair_block, "seg", scatter_dimension=1, tiled=True)
-    return stacked / jnp.float32(seg_dev * seg_count)
+    routed = jnp.einsum(
+        "rc,bcq->brq", selector, gathered, preferred_element_type=jnp.float32
+    ).astype(jnp.bfloat16)
+    blk_rank = lax.axis_index("blk")
+    own = lax.dynamic_slice_in_dim(routed, blk_rank * OWN, OWN, axis=1)
+    own_re = own[..., :all_segs]
+    own_im = own[..., all_segs:]
+    rotated = jnp.concatenate([own_im, -own_re], axis=-1)
+    lhs = jnp.concatenate([own, rotated], axis=1)
+    cross = jnp.einsum("bpq,bjq->bpj", lhs, routed, preferred_element_type=jnp.float32)
+    cross = cross.reshape(block_bins, 2, OWN, rows_count)
+    return jnp.transpose(cross, (1, 0, 2, 3)) / jnp.float32(all_segs)
 
 
 def solution(mesh):

time: 165 us -> 83.9 us (0.51)
  waiting for transfers between devices: 83.7 us -> 23.9 us
  local copies, waits for them, and re-layouts: 33.8 us -> 3.91 us
  blocking collectives: 0 us -> 21.4 us
  matrix products: 16.9 us -> 10.1 us
  starting transfers between devices: 8.39 us -> 3.86 us
    unnamed x3 -> x1, waiting for transfers between devices: 30.2 us -> 0.02 us
    all_gather x1, waiting for transfers between devices: 43.8 us -> 19.2 us  [per_device(): gathered = lax.all_gather(local, 'blk', axis=1, tiled=True)]
    all_gather x0 -> x1, blocking collectives: none -> 21.4 us  [per_device(): lax.all_gather(jnp.stack([send_list, recv_row]), 'blk', axis=1, tiled=True)]
    all_gather x1 -> x0, local copies, waits for them, and re-layouts: 12.6 us -> none  [per_device(): incoming = lax.all_gather(own_block, 'blk', axis=2, tiled=True)]
    squeeze x6 -> x1, local copies, waits for them, and re-layouts: 12 us -> 0.08 us  [per_device(): recv_all = tables[1]]
    all_to_all x1 -> x0, waiting for transfers between devices: 9.02 us -> none  [per_device(): lax.all_to_all(packed, 'blk', split_axis=0, concat_axis=0, tiled=True)]
    all_to_all x1 -> x0, starting transfers between devices: 7.18 us -> none  [per_device(): lax.all_to_all(packed, 'blk', split_axis=0, concat_axis=0, tiled=True)]
    dot_general x5 -> x2, matrix products: 10.2 us -> 3.47 us  [the longest x1 2.23 us: per_device(): jnp.einsum('rc,bcq->brq', selector, gathered, preferred_element_type=jnp....]
  transfers between devices with their start and end apart: 5 -> 4, of which waited for: 5 -> 4; matrix products, arithmetic and copies ran while one was open for 5% -> 2% of each run, Pallas kernels for 0% -> 0%
where the time goes in v2:
time: 83.9 us; the launch traced here: 83.7 us
  waiting for transfers between devices  23.9 us (28%)
  blocking collectives  21.4 us (26%)
  between operations  13.6 us (16%)
  matrix products  10.1 us (12%)
  other arithmetic  6.96 us (8%)
  local copies, waits for them, and re-layouts  3.91 us (5%)
  starting transfers between devices  3.86 us (5%)
    all_gather x1, blocking collectives, per_device(): lax.all_gather(jnp.stack([send_list, recv_row]), 'blk', axis=1, tiled=True)  21.4 us
    all_gather x1, waiting for transfers between devices, per_device(): gathered = lax.all_gather(local, 'blk', axis=1, tiled=True)  19.2 us
    convert_element_type x1, other arithmetic, dft_tables_fast(): cos_part = (cos_sum * norm_scale).astype(jnp.bfloat16).reshape(rows, count)  4.96 us
    ppermute x1, waiting for transfers between devices, per_device(): pieces.append(lax.ppermute(outgoing, 'seg', pairs))  3.8 us
    ppermute x1, starting transfers between devices, per_device(): pieces.append(lax.ppermute(outgoing, 'seg', pairs))  2.9 us
    dot_general x1, matrix products, per_device(): lax.dot_general(sin_part, records, contract, preferred_element_type=jnp.f...  2.82 us
    dot_general x1, matrix products, per_device(): lax.dot_general(cos_part, records, contract, preferred_element_type=jnp.f...  2.82 us
    dot_general x1, matrix products, per_device(): jnp.einsum('rc,bcq->brq', selector, gathered, preferred_element_type=jnp....  2.23 us
  transfers between devices with their start and end apart: 4, of which 4 were waited for; matrix products, arithmetic and copies ran while one was open for 2% of the time, Pallas kernels for 0%

profile of v2, /device:TPU:0, one launch (start us, length us, event | category | flops | bytes accessed | tf_op | source)
XLA Modules:
  0.0 83.7 jit_solution(14406879226455880461)
XLA Ops:
  6.5 0.0 copy-start
  6.5 0.0 all-gather.2.cloned.1.call-start
  6.6 0.6 fusion.53
  7.2 0.6 fusion.55
  7.8 0.0 copy-start.3
  7.8 5.0 %multiply_convert_fusion.1 = (bf16[256,64,128]{2,1,0:T(8,128)(2,1)S(1)}, bf16[256,64,128]{2,1,0:T(8,128)(2,1)S(1)}) fusion(f32[256,128]{1,0:T(8,128)S(1)} %get-tuple-element.26, f32[256,64]{1,0:T(8,128)S(1)} %get-tuple-element.24, f32[256,128]{1,0:T(8,128)S(1)} %get-tuple-element.25, f32[256,64]{1,0:T(8,128)S(1)} %get-tuple-element.23), kind=kLoop, calls=%fused_computation.1 | loop fusion | flops 23068672 | bytes 8781824 | tf_op jit(solution)/shard_map/convert_element_type | solution.py:54
  12.7 0.0 copy-done.3
  12.7 2.8 %fusion.6 = f32[256,1,256]{2,0,1:T(8,128)S(1)} fusion(bf16[256,8192]{1,0:T(8,128)(2,1)S(1)} %bitcast.134, bf16[32,8,64,128]{3,2,1,0:T(8,128)(2,1)S(1)} %bitcast.124), kind=kOutput, calls=%fused_computation.10 | convolution fusion | flops 1073741824 | bytes 8650752 | tf_op jit(solution)/shard_map/dot_general | solution.py:90
  15.6 2.8 %fusion.9 = f32[256,1,256]{2,0,1:T(8,128)S(1)} fusion(bf16[256,8192]{1,0:T(8,128)(2,1)S(1)} %bitcast.135, bf16[32,8,64,128]{3,2,1,0:T(8,128)(2,1)S(1)} %bitcast.123), kind=kOutput, calls=%fused_computation.11 | convolution fusion | flops 1073741824 | bytes 8650752 | tf_op jit(solution)/shard_map/dot_general | solution.py:91
  18.4 0.0 copy-start.1
  18.4 0.0 copy-start.2
  18.5 0.5 collective-permute-start
  19.0 0.0 copy-done
  19.0 0.5 convolution_bitcast_fusion
  19.5 0.1 add_convert_fusion.1
  19.6 0.5 collective-permute-done
  20.2 0.1 add_sqrt_fusion
  20.3 0.4 collective-permute-start.1
  20.7 0.5 convolution_bitcast_fusion.1
  21.2 0.4 collective-permute-done.1
  21.6 0.1 fusion.23
  21.7 0.1 add_convert_fusion
  21.8 0.1 copy.42
  21.9 0.1 stack.51
  22.1 0.1 constant_dynamic-update-slice_fusion.1
  22.2 0.1 copy.43
  22.3 0.1 stack.52
  22.4 0.1 constant_dynamic-update-slice_fusion
  22.5 0.7 dynamic-slice_bitcast_fusion.2
  23.2 2.9 %collective-permute-start.2 = (bf16[64,8,2,32]{0,3,2,1:T(8,128)(2,1)S(1)}, bf16[64,8,2,32]{0,3,2,1:T(8,128)(2,1)S(1)}, u32[]{:S(2)}, u32[]{:S(2)}) collective-permute-start(bf16[64,8,2,32]{0,3,2,1:T(8,128)(2,1)S(1)} %bitcast.130), channel_id=1, source_target_pairs={{0,2},{2,0},{1,3},{3,1},{4,6},{6,4},{5,7},{7,5},{8,10},{10,8},{9,1... | collective-permute-start | bytes 196616 | tf_op jit(solution)/shard_map/ppermute | solution.py:143
  26.1 3.8 %collective-permute-done.2 = bf16[64,8,2,32]{0,3,2,1:T(8,128)(2,1)S(1)} collective-permute-done((bf16[64,8,2,32]{0,3,2,1:T(8,128)(2,1)S(1)}, bf16[64,8,2,32]{0,3,2,1:T(8,128)(2,1)S(1)}, u32[]{:S(2)}, u32[]{:S(2)}) %collective-permute-start.2) | collective-permute-done | bytes 65568 | tf_op jit(solution)/shard_map/ppermute | solution.py:143
  29.9 0.1 pad_maximum_fusion.1
  30.0 0.8 copy.46
  30.8 0.0 all-gather.2.cloned.1.call-update
  30.8 0.0 copy-done.1
  30.8 0.0 copy-done.2
  30.9 21.4 %all_gather.7 = s32[2,8,8,2]{2,3,1,0:T(2,128)S(1)} all-gather(s32[2,1,8,2]{2,3,1,0:T(2,128)S(1)} %pad_add_fusion), channel_id=1, replica_groups=mesh['groups'=1,'blk'=8,'seg'=2,'freq'=2] {'blk'}, dimensions={1}, use_global_device_ids=true | all-gather | bytes 1152 | tf_op jit(solution)/shard_map/all_gather | solution.py:147
  52.2 0.1 copy.56
  52.3 0.1 fusion.65
  52.4 0.1 copy.51
  52.5 0.1 eq.48
  52.6 0.1 copy.52
  52.8 0.1 eq.51
  52.9 19.2 %all-gather.2.cloned.1.call-done = bf16[64,64,128]{2,1,0:T(8,128)(2,1)} async-done(((bf16[64,8,128]{2,1,0:T(8,128)(2,1)}), bf16[64,64,128]{2,1,0:T(8,128)(2,1)}) %all-gather.2.cloned.1.call-update) | async-done | bytes 1048592 | tf_op jit(solution)/shard_map/all_gather | solution.py:146
  72.1 2.2 %convolution_convert_fusion = bf16[64,128,128]{1,2,0:T(8,128)(2,1)S(1)} fusion(bf16[64,64,128]{2,1,0:T(8,128)(2,1)} %all-gather.2.cloned.1.call-done, s32[128]{0:T(128)S(1)} %eq.51, s32[128]{0:T(128)S(1)} %eq.48), kind=kOutput, calls=%fused_computation.8 | convolution fusion | flops 137396224 | bytes 3146752 | tf_op jit(solution)/shard_map/rc,bcq->brq/dot_general | solution.py:167
  74.4 0.1 fusion.87
  74.6 1.2 %convolution_multiply_fusion = f32[64,32,128]{2,1,0:T(8,128)S(1)} fusion(bf16[64,128,128]{1,2,0:T(8,128)(2,1)S(1)} %convolution_convert_fusion, bf16[64,16,64]{2,1,0:T(8,128)(2,1)S(1)} %get-tuple-element.10, bf16[64,16,64]{2,1,0:T(8,128)(2,1)S(1)} %get-tuple-element.9, bf16[64,16,128]{2,1,0:T(8,128)(2,1)S(1)} %dynamic-slice_bitcast_fusion), kind=kOutput, calls=%fused_computation.9 | convolution fusion | flops 68943872 | bytes 3670016 | tf_op jit(solution)/shard_map/bpq,bjq->bpj/dot_general | solution.py:176
  75.8 1.1 %copy.81 = f32[64,2,16,128]{3,2,0,1:T(8,128)} copy(f32[64,2,16,128]{3,2,1,0:T(8,128)S(1)} %bitcast.125) | data formatting | bytes 2097152 | tf_op jit(solution)/shard_map/div | solution.py:178
  (16 shorter events, 0.3 us)
Async XLA Ops:
  6.5 12.5 %copy-start = (f32[128]{0:T(128)S(1)}, f32[128]{0:T(128)}, u32[]{:S(2)}) copy-start(f32[128]{0:T(128)} %param.5) | copy-start | bytes 1540
  6.5 65.6 %all-gather.2.cloned.1.call-start = ((), (), s32[]{:S(2)}) async-start(), calls=%async_computation | async-start | bytes 1179648 | tf_op jit(solution)/shard_map/all_gather | solution.py:146
  7.8 5.0 %copy-start.3 = (bf16[8,32,8192]{2,1,0:T(8,128)(2,1)S(1)}, bf16[8,32,8192]{2,1,0:T(8,128)(2,1)}, u32[]{:S(2)}) copy-start(bf16[8,32,8192]{2,1,0:T(8,128)(2,1)} %param.4) | copy-start | bytes 12582916
  18.4 12.4 %copy-start.1 = (s32[1,8,2]{1,2,0:T(2,128)S(1)}, s32[1,8,2]{1,2,0:T(2,128)}, u32[]{:S(2)}) copy-start(s32[1,8,2]{1,2,0:T(2,128)} %param.7) | copy-start | bytes 196
  18.4 12.4 %copy-start.2 = (s32[1,8,2]{1,2,0:T(2,128)S(1)}, s32[1,8,2]{1,2,0:T(2,128)}, u32[]{:S(2)}) copy-start(s32[1,8,2]{1,2,0:T(2,128)} %param.6) | copy-start | bytes 196
  18.5 1.7 %collective-permute-start = (f32[128,2,256]{2,0,1:T(8,128)S(1)}, f32[128,2,256]{2,0,1:T(8,128)S(1)}, u32[]{:S(2)}, u32[]{:S(2)}) collective-permute-start(f32[128,2,256]{2,0,1:T(8,128)S(1)} %broadcast_select_fusion), channel_id=1, source_target_pairs={{0,1},{1,0},{2,3},{3,2},{4,5},{5,4},{6,7},{7,6},{8,9},{9,8},{10,11... | collective-permute-start | bytes 786440 | tf_op jit(solution)/shard_map/ppermute | solution.py:22
  20.3 1.3 %collective-permute-start.1 = (f32[2,2,4,256]{3,2,1,0:T(4,128)S(1)}, f32[2,2,4,256]{3,2,1,0:T(4,128)S(1)}, u32[]{:S(2)}, u32[]{:S(2)}) collective-permute-start(f32[2,2,4,256]{3,2,1,0:T(4,128)S(1)} %pad_maximum_fusion.4), channel_id=1, source_target_pairs={{0,1},{1,0},{2,3},{3,2},{4,5},{5,4},{6,7},{7,6},{8,9},{9,8},{10,11... | collective-permute-start | bytes 49160 | tf_op jit(solution)/shard_map/ppermute | solution.py:22
  23.2 6.7 %collective-permute-start.2 = (bf16[64,8,2,32]{0,3,2,1:T(8,128)(2,1)S(1)}, bf16[64,8,2,32]{0,3,2,1:T(8,128)(2,1)S(1)}, u32[]{:S(2)}, u32[]{:S(2)}) collective-permute-start(bf16[64,8,2,32]{0,3,2,1:T(8,128)(2,1)S(1)} %bitcast.130), channel_id=1, source_target_pairs={{0,2},{2,0},{1,3},{3,1},{4,6},{6,4},{5,7},{7,5},{8,10},{10,8},{9,1... | collective-permute-start | bytes 196616 | tf_op jit(solution)/shard_map/ppermute | solution.py:143
Sparse Core Ops, SparseCore 0:
  30.9 41.1 all-gather.1

commit v3 on v2

--- a/solution.py
+++ b/solution.py
@@ -143,10 +143,17 @@
         pieces.append(lax.ppermute(outgoing, "seg", pairs))
     local = jnp.stack(pieces, axis=3).reshape(block_bins, sections, -1)
     all_segs = seg_dev * seg_count
-    gathered = lax.all_gather(local, "blk", axis=1, tiled=True)
-    tables = lax.all_gather(jnp.stack([send_list, recv_row]), "blk", axis=1, tiled=True)
-    send_all = tables[0]
-    recv_all = tables[1]
+    table_width = local.shape[-1]
+    table = jnp.concatenate([send_list[0], recv_row[0]], axis=1).reshape(-1)
+    table_len = table.shape[0]
+    slab = jnp.pad(table.astype(jnp.bfloat16), (0, sections * table_width - table_len))
+    carried = jnp.concatenate([local, slab.reshape(1, sections, table_width)], axis=0)
+    everything = lax.all_gather(carried, "blk", axis=0, tiled=False)
+    gathered = everything[:, :block_bins]
+    table_part = everything[:, block_bins].reshape(owners_count, -1)[:, :table_len]
+    table_part = table_part.astype(jnp.int32).reshape(owners_count, owners_count, 2 * capacity)
+    send_all = table_part[..., :capacity]
+    recv_all = table_part[..., capacity:]
     rows_count = owners_count * OWN
     chans_count = owners_count * sections
     chosen = jnp.transpose(send_all, (1, 0, 2))
@@ -164,8 +171,9 @@
     selector = jnp.einsum(
         "er,ec->rc", row_hot, chan_hot, preferred_element_type=jnp.float32
     ).astype(jnp.bfloat16)
+    selector = selector.reshape(rows_count, owners_count, sections)
     routed = jnp.einsum(
-        "rc,bcq->brq", selector, gathered, preferred_element_type=jnp.float32
+        "rsc,sbcq->brq", selector, gathered, preferred_element_type=jnp.float32
     ).astype(jnp.bfloat16)
     blk_rank = lax.axis_index("blk")
     own = lax.dynamic_slice_in_dim(routed, blk_rank * OWN, OWN, axis=1)

time: 83.9 us -> 86.7 us (1.033)
  waiting for transfers between devices: 23.9 us -> 46.1 us
  blocking collectives: 21.4 us -> 0 us
  local copies, waits for them, and re-layouts: 3.91 us -> 6.5 us
  matrix products: 10.1 us -> 9.18 us
    all_gather x1, waiting for transfers between devices: 19.2 us -> 41.9 us  [per_device(): everything = lax.all_gather(carried, 'blk', axis=0, tiled=False)]
    all_gather x1 -> x0, blocking collectives: 21.4 us -> none  [per_device(): lax.all_gather(jnp.stack([send_list, recv_row]), 'blk', axis=1, tiled=True)]
    slice x1 -> x4, local copies, waits for them, and re-layouts: 0.01 us -> 2.02 us  [the longest x1 1.29 us: per_device(): gathered = everything[:, :block_bins]]
    dot_general x1 -> x2, matrix products: 2.23 us -> 1.29 us  [the longest x1 1.02 us: per_device(): jnp.einsum('rsc,sbcq->brq', selector, gathered, preferred_element_type=jn...]
    concatenate x0 -> x2, local copies, waits for them, and re-layouts: none -> 0.93 us  [the longest x1 0.84 us: per_device(): jnp.concatenate([local, slab.reshape(1, sections, table_width)], axis=0)]
  transfers between devices with their start and end apart: 4 -> 4, of which waited for: 4 -> 3; matrix products, arithmetic and copies ran while one was open for 2% -> 2% of each run, Pallas kernels for 0% -> 0%
where the time goes in v3:
time: 86.7 us; the launch traced here: 86.5 us
  waiting for transfers between devices  46.1 us (53%)
  between operations  13.7 us (16%)
  matrix products  9.18 us (11%)
  other arithmetic  7.12 us (8%)
  local copies, waits for them, and re-layouts  6.5 us (7%)
  starting transfers between devices  3.79 us (4%)
    all_gather x1, waiting for transfers between devices, per_device(): everything = lax.all_gather(carried, 'blk', axis=0, tiled=False)  41.9 us
    convert_element_type x1, other arithmetic, dft_tables_fast(): cos_part = (cos_sum * norm_scale).astype(jnp.bfloat16).reshape(rows, count)  4.96 us
    ppermute x1, waiting for transfers between devices, per_device(): pieces.append(lax.ppermute(outgoing, 'seg', pairs))  3.57 us
    ppermute x1, starting transfers between devices, per_device(): pieces.append(lax.ppermute(outgoing, 'seg', pairs))  2.88 us
    dot_general x1, matrix products, per_device(): lax.dot_general(cos_part, records, contract, preferred_element_type=jnp.f...  2.82 us
    dot_general x1, matrix products, per_device(): lax.dot_general(sin_part, records, contract, preferred_element_type=jnp.f...  2.82 us
  transfers between devices with their start and end apart: 4, of which 3 were waited for; matrix products, arithmetic and copies ran while one was open for 2% of the time, Pallas kernels for 0%

profile of v3, /device:TPU:0, one launch (start us, length us, event | category | flops | bytes accessed | tf_op | source)
XLA Modules:
  0.0 86.5 jit_solution(17548710112209170965)
XLA Ops:
  6.5 0.0 copy-start
  6.5 0.0 all-gather.3.cloned.1.call-start
  6.6 0.6 fusion.54
  7.2 0.6 fusion.56
  7.8 0.0 copy-start.3
  7.8 5.0 %multiply_convert_fusion.1 = (bf16[256,64,128]{2,1,0:T(8,128)(2,1)S(1)}, bf16[256,64,128]{2,1,0:T(8,128)(2,1)S(1)}) fusion(f32[256,128]{1,0:T(8,128)S(1)} %get-tuple-element.24, f32[256,64]{1,0:T(8,128)S(1)} %get-tuple-element.22, f32[256,128]{1,0:T(8,128)S(1)} %get-tuple-element.23, f32[256,64]{1,0:T(8,128)S(1)} %get-tuple-element.21), kind=kLoop, calls=%fused_computation.1 | loop fusion | flops 23068672 | bytes 8781824 | tf_op jit(solution)/shard_map/convert_element_type | solution.py:54
  12.7 0.0 copy-done.3
  12.7 2.8 %fusion.6 = f32[256,1,256]{2,0,1:T(8,128)S(1)} fusion(bf16[256,8192]{1,0:T(8,128)(2,1)S(1)} %bitcast.119, bf16[32,8,64,128]{3,2,1,0:T(8,128)(2,1)S(1)} %bitcast.107), kind=kOutput, calls=%fused_computation.10 | convolution fusion | flops 1073741824 | bytes 8650752 | tf_op jit(solution)/shard_map/dot_general | solution.py:90
  15.6 0.0 copy-start.1
  15.6 0.0 copy-start.2
  15.6 2.8 %fusion.9 = f32[256,1,256]{2,0,1:T(8,128)S(1)} fusion(bf16[256,8192]{1,0:T(8,128)(2,1)S(1)} %bitcast.120, bf16[32,8,64,128]{3,2,1,0:T(8,128)(2,1)S(1)} %bitcast.106), kind=kOutput, calls=%fused_computation.11 | convolution fusion | flops 1073741824 | bytes 8650752 | tf_op jit(solution)/shard_map/dot_general | solution.py:91
  18.5 0.5 collective-permute-start
  19.0 0.1 add_convert_fusion.1
  19.1 0.0 copy-done
  19.1 0.5 convolution_bitcast_fusion
  19.6 0.5 convolution_bitcast_fusion.1
  20.1 0.0 copy-done.1
  20.1 0.0 copy-done.2
  20.2 0.0 collective-permute-done
  20.2 0.1 select_add_fusion
  20.3 0.1 add_sqrt_fusion
  20.3 0.4 collective-permute-start.1
  20.8 0.1 copy.60
  20.9 0.1 convert_element_type.88
  20.9 0.6 collective-permute-done.1
  21.6 0.1 fusion.24
  21.7 0.1 add_convert_fusion
  21.9 0.1 copy.56
  22.0 0.1 stack.42
  22.1 0.1 constant_dynamic-update-slice_fusion.1
  22.2 0.1 copy.57
  22.3 0.1 stack.43
  22.4 0.1 constant_dynamic-update-slice_fusion
  22.5 0.6 dynamic-slice_bitcast_fusion.2
  23.1 2.9 %collective-permute-start.2 = (bf16[64,8,2,32]{0,3,2,1:T(8,128)(2,1)S(1)}, bf16[64,8,2,32]{0,3,2,1:T(8,128)(2,1)S(1)}, u32[]{:S(2)}, u32[]{:S(2)}) collective-permute-start(bf16[64,8,2,32]{0,3,2,1:T(8,128)(2,1)S(1)} %bitcast.116), channel_id=1, source_target_pairs={{0,2},{2,0},{1,3},{3,1},{4,6},{6,4},{5,7},{7,5},{8,10},{10,8},{9,1... | collective-permute-start | bytes 196616 | tf_op jit(solution)/shard_map/ppermute | solution.py:143
  26.0 0.2 copy.61
  26.3 3.6 %collective-permute-done.2 = bf16[64,8,2,32]{0,3,2,1:T(8,128)(2,1)S(1)} collective-permute-done((bf16[64,8,2,32]{0,3,2,1:T(8,128)(2,1)S(1)}, bf16[64,8,2,32]{0,3,2,1:T(8,128)(2,1)S(1)}, u32[]{:S(2)}, u32[]{:S(2)}) %collective-permute-start.2) | collective-permute-done | bytes 65568 | tf_op jit(solution)/shard_map/ppermute | solution.py:143
  29.9 0.1 pad_maximum_fusion.1
  29.9 0.1 pad_maximum_fusion.2
  30.1 0.8 copy.62
  30.9 0.0 all-gather.3.cloned.1.call-update
  30.9 41.9 %all-gather.3.cloned.1.call-done = bf16[520,8,128]{2,1,0:T(8,128)(2,1)} async-done(((bf16[65,8,128]{2,1,0:T(8,128)(2,1)}), bf16[520,8,128]{2,1,0:T(8,128)(2,1)}) %all-gather.3.cloned.1.call-update) | async-done | bytes 1064976 | tf_op jit(solution)/shard_map/all_gather | solution.py:151
  72.8 0.7 slice.147
  73.6 1.3 %slice.146 = bf16[8,64,8,128]{3,2,1,0:T(8,128)(2,1)S(1)} slice(bf16[8,65,8,128]{3,2,1,0:T(8,128)(2,1)} %bitcast.110), slice={[0:8], [0:64], [0:8], [0:128]} | slice | bytes 2097152 | tf_op jit(solution)/shard_map/slice | solution.py:152
  74.9 0.2 copy.73
  75.1 0.1 copy.75
  75.2 0.1 add_select_fusion.3
  75.3 0.1 copy.66
  75.4 0.1 eq.48
  75.5 0.1 copy.67
  75.7 0.1 eq.51
  75.8 0.3 fusion.12
  76.1 1.0 %bitcast_convert_fusion = bf16[64,128,128]{1,2,0:T(8,128)(2,1)S(1)} fusion(bf16[8,64,8,128]{3,2,1,0:T(8,128)(2,1)S(1)} %slice.146, bf16[128,8,8]{0,2,1:T(8,128)(2,1)S(1)} %fusion.12), kind=kOutput, calls=%fused_computation.8 | convolution fusion | flops 135266304 | bytes 3162112 | tf_op jit(solution)/shard_map/rsc,sbcq->brq/dot_general | solution.py:175
  77.2 0.1 fusion.85
  77.3 1.2 %convolution_multiply_fusion = f32[64,32,128]{2,1,0:T(8,128)S(1)} fusion(bf16[64,128,128]{1,2,0:T(8,128)(2,1)S(1)} %bitcast_convert_fusion, bf16[64,16,64]{2,1,0:T(8,128)(2,1)S(1)} %get-tuple-element.10, bf16[64,16,64]{2,1,0:T(8,128)(2,1)S(1)} %get-tuple-element.9, bf16[64,16,128]{2,1,0:T(8,128)(2,1)S(1)} %dynamic-slice_bitcast_fusion), kind=kOutput, calls=%fused_computation.9 | convolution fusion | flops 68943872 | bytes 3670016 | tf_op jit(solution)/shard_map/bpq,bjq->bpj/dot_general | solution.py:184
  78.5 1.1 %copy.99 = f32[64,2,16,128]{3,2,0,1:T(8,128)} copy(f32[64,2,16,128]{3,2,1,0:T(8,128)S(1)} %bitcast.108) | data formatting | bytes 2097152 | tf_op jit(solution)/shard_map/div | solution.py:186
  (19 shorter events, 0.3 us)
Async XLA Ops:
  6.5 12.6 %copy-start = (f32[128]{0:T(128)S(1)}, f32[128]{0:T(128)}, u32[]{:S(2)}) copy-start(f32[128]{0:T(128)} %param.5) | copy-start | bytes 1540
  6.5 66.3 %all-gather.3.cloned.1.call-start = ((), (), s32[]{:S(2)}) async-start(), calls=%async_computation | async-start | bytes 1198080 | tf_op jit(solution)/shard_map/all_gather | solution.py:151
  7.8 5.0 %copy-start.3 = (bf16[8,32,8192]{2,1,0:T(8,128)(2,1)S(1)}, bf16[8,32,8192]{2,1,0:T(8,128)(2,1)}, u32[]{:S(2)}) copy-start(bf16[8,32,8192]{2,1,0:T(8,128)(2,1)} %param.4) | copy-start | bytes 12582916
  15.6 4.5 %copy-start.1 = (s32[1,8,2]{1,2,0:T(2,128)S(1)}, s32[1,8,2]{1,2,0:T(2,128)}, u32[]{:S(2)}) copy-start(s32[1,8,2]{1,2,0:T(2,128)} %param.7) | copy-start | bytes 196
  15.6 4.6 %copy-start.2 = (s32[1,8,2]{1,2,0:T(2,128)S(1)}, s32[1,8,2]{1,2,0:T(2,128)}, u32[]{:S(2)}) copy-start(s32[1,8,2]{1,2,0:T(2,128)} %param.6) | copy-start | bytes 196
  18.5 1.7 %collective-permute-start = (f32[128,2,256]{2,0,1:T(8,128)S(1)}, f32[128,2,256]{2,0,1:T(8,128)S(1)}, u32[]{:S(2)}, u32[]{:S(2)}) collective-permute-start(f32[128,2,256]{2,0,1:T(8,128)S(1)} %broadcast_select_fusion), channel_id=1, source_target_pairs={{0,1},{1,0},{2,3},{3,2},{4,5},{5,4},{6,7},{7,6},{8,9},{9,8},{10,11... | collective-permute-start | bytes 786440 | tf_op jit(solution)/shard_map/ppermute | solution.py:22
  20.3 1.2 %collective-permute-start.1 = (f32[2,2,4,256]{3,2,1,0:T(4,128)S(1)}, f32[2,2,4,256]{3,2,1,0:T(4,128)S(1)}, u32[]{:S(2)}, u32[]{:S(2)}) collective-permute-start(f32[2,2,4,256]{3,2,1,0:T(4,128)S(1)} %pad_maximum_fusion.5), channel_id=1, source_target_pairs={{0,1},{1,0},{2,3},{3,2},{4,5},{5,4},{6,7},{7,6},{8,9},{9,8},{10,11... | collective-permute-start | bytes 49160 | tf_op jit(solution)/shard_map/ppermute | solution.py:22
  23.1 6.7 %collective-permute-start.2 = (bf16[64,8,2,32]{0,3,2,1:T(8,128)(2,1)S(1)}, bf16[64,8,2,32]{0,3,2,1:T(8,128)(2,1)S(1)}, u32[]{:S(2)}, u32[]{:S(2)}) collective-permute-start(bf16[64,8,2,32]{0,3,2,1:T(8,128)(2,1)S(1)} %bitcast.116), channel_id=1, source_target_pairs={{0,2},{2,0},{1,3},{3,1},{4,6},{6,4},{5,7},{7,5},{8,10},{10,8},{9,1... | collective-permute-start | bytes 196616 | tf_op jit(solution)/shard_map/ppermute | solution.py:143
Sparse Core Ops, SparseCore 0:
  31.0 41.7 all-gather.2

commit v4 on v3

--- a/solution.py
+++ b/solution.py
@@ -64,6 +64,36 @@
     real_part = jnp.dot(jnp.cos(angles), taps, precision=lax.Precision.HIGHEST)
     imag_part = jnp.dot(-jnp.sin(angles), taps, precision=lax.Precision.HIGHEST)
     return (real_part, imag_part)
+
+
+def gather_blocks(carried, count, rank):
+    if count & (count - 1) != 0:
+        return lax.all_gather(carried, "blk", axis=0, tiled=False)
+    masks = []
+    step = count // 2
+    while step >= 1:
+        masks.append(step)
+        step //= 2
+    if not masks:
+        return carried[None]
+    first = masks[0]
+    rest = masks[1:]
+    pairs = [(source, source ^ first) for source in range(count)]
+    held = jnp.stack([carried, lax.ppermute(carried, "blk", pairs)], axis=0)
+    split = (held.shape[1] + 1) // 2
+    halves = [held[:, :split], held[:, split:]]
+    orders = [rest, rest[::-1]]
+    results = []
+    for part, order in zip(halves, orders):
+        done = [first]
+        for mask in order:
+            pairs = [(source, source ^ mask) for source in range(count)]
+            arrived = lax.ppermute(part, "blk", pairs)
+            done.append(mask)
+            axis = sorted(done, reverse=True).index(mask)
+            part = jnp.stack([part, arrived], axis=axis)
+        results.append(part.reshape((count,) + part.shape[len(masks):]))
+    return jnp.concatenate(results, axis=1)
 
 
 def per_device(raw, taps, send_list, recv_row):
@@ -148,10 +178,14 @@
     table_len = table.shape[0]
     slab = jnp.pad(table.astype(jnp.bfloat16), (0, sections * table_width - table_len))
     carried = jnp.concatenate([local, slab.reshape(1, sections, table_width)], axis=0)
-    everything = lax.all_gather(carried, "blk", axis=0, tiled=False)
+    blk_rank = lax.axis_index("blk")
+    everything = gather_blocks(carried, owners_count, blk_rank)
     gathered = everything[:, :block_bins]
     table_part = everything[:, block_bins].reshape(owners_count, -1)[:, :table_len]
     table_part = table_part.astype(jnp.int32).reshape(owners_count, owners_count, 2 * capacity)
+    if owners_count & (owners_count - 1) == 0:
+        source_of = blk_rank ^ jnp.arange(owners_count, dtype=jnp.int32)
+        table_part = jnp.take(table_part, source_of, axis=0)
     send_all = table_part[..., :capacity]
     recv_all = table_part[..., capacity:]
     rows_count = owners_count * OWN
@@ -172,10 +206,11 @@
         "er,ec->rc", row_hot, chan_hot, preferred_element_type=jnp.float32
     ).astype(jnp.bfloat16)
     selector = selector.reshape(rows_count, owners_count, sections)
+    if owners_count & (owners_count - 1) == 0:
+        selector = jnp.take(selector, source_of, axis=1)
     routed = jnp.einsum(
         "rsc,sbcq->brq", selector, gathered, preferred_element_type=jnp.float32
     ).astype(jnp.bfloat16)
-    blk_rank = lax.axis_index("blk")
     own = lax.dynamic_slice_in_dim(routed, blk_rank * OWN, OWN, axis=1)
     own_re = own[..., :all_segs]
     own_im = own[..., all_segs:]

time: 86.7 us -> 66.3 us (0.76)
  waiting for transfers between devices: 46.1 us -> 29.8 us
  between operations: 13.7 us -> 0.41 us
  starting transfers between devices: 3.79 us -> 12.1 us
  other arithmetic: 7.12 us -> 8.16 us
    all_gather x1 -> x0, waiting for transfers between devices: 41.9 us -> none  [per_device(): everything = lax.all_gather(carried, 'blk', axis=0, tiled=False)]
    ppermute x0 -> x5, waiting for transfers between devices: none -> 25 us  [the longest x4 13.5 us: gather_blocks(): arrived = lax.ppermute(part, 'blk', pairs)]
    ppermute x0 -> x5, starting transfers between devices: none -> 8.66 us  [the longest x4 5.76 us: gather_blocks(): arrived = lax.ppermute(part, 'blk', pairs)]
    another operation x2 -> x8, local copies, waits for them, and re-layouts: 0.22 us -> 2.28 us  [the longest x6 2.05 us: gather_blocks(): part = jnp.stack([part, arrived], axis=axis)]
    slice x3 -> x0, local copies, waits for them, and re-layouts: 2.01 us -> none  [the longest x1 1.29 us: per_device(): gathered = everything[:, :block_bins]]
    gather x0 -> x2, local copies, waits for them, and re-layouts: none -> 1.14 us  [the longest x1 0.58 us: per_device(): table_part = jnp.take(table_part, source_of, axis=0)]
    another operation x1 -> x9, other arithmetic: 0.1 us -> 0.98 us  [the longest x6 0.6 us: gather_blocks(): part = jnp.stack([part, arrived], axis=axis)]
  transfers between devices with their start and end apart: 4 -> 8, of which waited for: 3 -> 5; matrix products, arithmetic and copies ran while one was open for 2% -> 9% of each run, Pallas kernels for 0% -> 0%
where the time goes in v4:
time: 66.3 us; the launch traced here: 66.2 us
  waiting for transfers between devices  29.8 us (45%)
  starting transfers between devices  12.1 us (18%)
  matrix products  8.91 us (13%)
  other arithmetic  8.16 us (12%)
  local copies, waits for them, and re-layouts  6.84 us (10%)
    ppermute x4, waiting for transfers between devices, gather_blocks(): arrived = lax.ppermute(part, 'blk', pairs)  13.5 us
    ppermute x1, waiting for transfers between devices, gather_blocks(): held = jnp.stack([carried, lax.ppermute(carried, 'blk', pairs)], axis=0)  11.5 us
    ppermute x4, starting transfers between devices, gather_blocks(): arrived = lax.ppermute(part, 'blk', pairs)  5.76 us
    convert_element_type x1, other arithmetic, dft_tables_fast(): cos_part = (cos_sum * norm_scale).astype(jnp.bfloat16).reshape(rows, count)  4.96 us
    ppermute x1, waiting for transfers between devices, per_device(): pieces.append(lax.ppermute(outgoing, 'seg', pairs))  3.98 us
    ppermute x1, starting transfers between devices, gather_blocks(): held = jnp.stack([carried, lax.ppermute(carried, 'blk', pairs)], axis=0)  2.9 us
    dot_general x1, matrix products, per_device(): lax.dot_general(sin_part, records, contract, preferred_element_type=jnp.f...  2.82 us
    dot_general x1, matrix products, per_device(): lax.dot_general(cos_part, records, contract, preferred_element_type=jnp.f...  2.82 us
  transfers between devices with their start and end apart: 8, of which 5 were waited for; matrix products, arithmetic and copies ran while one was open for 9% of the time, Pallas kernels for 0%

profile of v4, /device:TPU:0, one launch (start us, length us, event | category | flops | bytes accessed | tf_op | source)
XLA Modules:
  0.0 66.2 jit_solution(1763334424500865220)
XLA Ops:
  0.0 0.6 fusion.56
  0.6 0.6 fusion.58
  1.2 5.0 %multiply_convert_fusion.1 = (bf16[256,64,128]{2,1,0:T(8,128)(2,1)S(1)}, bf16[256,64,128]{2,1,0:T(8,128)(2,1)S(1)}) fusion(f32[256,128]{1,0:T(8,128)S(1)} %get-tuple-element.30, f32[256,64]{1,0:T(8,128)S(1)} %get-tuple-element.28, f32[256,128]{1,0:T(8,128)S(1)} %get-tuple-element.29, f32[256,64]{1,0:T(8,128)S(1)} %get-tuple-element.27), kind=kLoop, calls=%fused_computation.3 | loop fusion | flops 23068672 | bytes 8781824 | tf_op jit(solution)/shard_map/convert_element_type | solution.py:54
  6.2 2.8 %fusion.6 = f32[256,1,256]{2,0,1:T(8,128)S(1)} fusion(bf16[256,8192]{1,0:T(8,128)(2,1)S(1)} %bitcast.147, bf16[32,8,64,128]{3,2,1,0:T(8,128)(2,1)S(1)} %bitcast.127), kind=kOutput, calls=%fused_computation.12 | convolution fusion | flops 1073741824 | bytes 8650752 | tf_op jit(solution)/shard_map/dot_general | solution.py:120
  9.1 2.8 %fusion.9 = f32[256,1,256]{2,0,1:T(8,128)S(1)} fusion(bf16[256,8192]{1,0:T(8,128)(2,1)S(1)} %bitcast.148, bf16[32,8,64,128]{3,2,1,0:T(8,128)(2,1)S(1)} %bitcast.126), kind=kOutput, calls=%fused_computation.13 | convolution fusion | flops 1073741824 | bytes 8650752 | tf_op jit(solution)/shard_map/dot_general | solution.py:121
  11.9 0.5 collective-permute-start
  12.5 0.5 convolution_bitcast_fusion
  13.0 0.5 convolution_bitcast_fusion.1
  13.6 0.1 copy.104
  13.7 0.1 convert_element_type.88
  13.8 0.1 add_convert_fusion.1
  13.9 0.1 add_sqrt_fusion
  14.0 0.2 collective-permute-start.1
  14.2 0.2 copy.105
  14.5 0.8 %collective-permute-done.1 = f32[2,2,4,256]{3,2,1,0:T(4,128)S(1)} collective-permute-done((f32[2,2,4,256]{3,2,1,0:T(4,128)S(1)}, f32[2,2,4,256]{3,2,1,0:T(4,128)S(1)}, u32[]{:S(2)}, u32[]{:S(2)}) %collective-permute-start.1) | collective-permute-done | bytes 16416 | tf_op jit(solution)/shard_map/ppermute | solution.py:22
  15.3 0.1 fusion.26
  15.4 0.1 add_convert_fusion
  15.5 0.1 copy.100
  15.6 0.1 stack.87
  15.7 0.1 constant_dynamic-update-slice_fusion.1
  15.8 0.1 copy.101
  16.0 0.1 stack.88
  16.1 0.1 constant_dynamic-update-slice_fusion
  16.2 0.6 dynamic-slice_bitcast_fusion.2
  16.8 2.7 %collective-permute-start.2 = (bf16[64,8,2,32]{0,3,2,1:T(8,128)(2,1)S(1)}, bf16[64,8,2,32]{0,3,2,1:T(8,128)(2,1)S(1)}, u32[]{:S(2)}, u32[]{:S(2)}) collective-permute-start(bf16[64,8,2,32]{0,3,2,1:T(8,128)(2,1)S(1)} %bitcast.144), channel_id=1, source_target_pairs={{0,2},{2,0},{1,3},{3,1},{4,6},{6,4},{5,7},{7,5},{8,10},{10,8},{9,1... | collective-permute-start | bytes 196616 | tf_op jit(solution)/shard_map/ppermute | solution.py:173
  19.6 4.0 %collective-permute-done.2 = bf16[64,8,2,32]{0,3,2,1:T(8,128)(2,1)S(1)} collective-permute-done((bf16[64,8,2,32]{0,3,2,1:T(8,128)(2,1)S(1)}, bf16[64,8,2,32]{0,3,2,1:T(8,128)(2,1)S(1)}, u32[]{:S(2)}, u32[]{:S(2)}) %collective-permute-start.2) | collective-permute-done | bytes 65568 | tf_op jit(solution)/shard_map/ppermute | solution.py:173
  23.6 0.1 pad_maximum_fusion.5
  23.6 0.1 pad_maximum_fusion.6
  23.8 2.9 %collective-permute-start.3 = (bf16[65,8,128]{0,2,1:T(8,128)(2,1)S(1)}, bf16[65,8,128]{0,2,1:T(8,128)(2,1)S(1)}, u32[]{:S(2)}, u32[]{:S(2)}) collective-permute-start(bf16[65,8,128]{0,2,1:T(8,128)(2,1)S(1)} %pad_maximum_fusion.6), channel_id=1, source_target_pairs={{0,16},{4,20},{8,24},{12,28},{16,0},{20,4},{24,8},{28,12},{1,17},{... | collective-permute-start | bytes 399368 | tf_op jit(solution)/shard_map/ppermute | solution.py:82
  26.7 0.1 fusion.97
  26.8 11.5 %collective-permute-done.3 = bf16[65,8,128]{0,2,1:T(8,128)(2,1)S(1)} collective-permute-done((bf16[65,8,128]{0,2,1:T(8,128)(2,1)S(1)}, bf16[65,8,128]{0,2,1:T(8,128)(2,1)S(1)}, u32[]{:S(2)}, u32[]{:S(2)}) %collective-permute-start.3) | collective-permute-done | bytes 133152 | tf_op jit(solution)/shard_map/ppermute | solution.py:82
  38.3 0.3 fusion.91
  38.7 1.6 %collective-permute-start.6 = (bf16[2,32,8,128]{1,3,2,0:T(8,128)(2,1)S(1)}, bf16[2,32,8,128]{1,3,2,0:T(8,128)(2,1)S(1)}, u32[]{:S(2)}, u32[]{:S(2)}) collective-permute-start(bf16[2,32,8,128]{1,3,2,0:T(8,128)(2,1)S(1)} %get-tuple-element.6), channel_id=1, source_target_pairs={{0,4},{4,0},{8,12},{12,8},{16,20},{20,16},{24,28},{28,24},{1,5},{5... | collective-permute-start | bytes 393224 | tf_op jit(solution)/shard_map/ppermute | solution.py:91
  40.3 0.2 copy.112
  40.5 0.1 slice_maximum_fusion
  40.6 0.7 %collective-permute-start.4 = (bf16[2,33,8,128]{1,3,2,0:T(8,128)(2,1)S(1)}, bf16[2,33,8,128]{1,3,2,0:T(8,128)(2,1)S(1)}, u32[]{:S(2)}, u32[]{:S(2)}) collective-permute-start(bf16[2,33,8,128]{1,3,2,0:T(8,128)(2,1)S(1)} %slice_maximum_fusion), channel_id=1, source_target_pairs={{0,8},{4,12},{8,0},{12,4},{16,24},{20,28},{24,16},{28,20},{1,9},{5... | collective-permute-start | bytes 405512 | tf_op jit(solution)/shard_map/ppermute | solution.py:91
  41.4 10.1 %collective-permute-done.6 = bf16[2,32,8,128]{1,3,2,0:T(8,128)(2,1)S(1)} collective-permute-done((bf16[2,32,8,128]{1,3,2,0:T(8,128)(2,1)S(1)}, bf16[2,32,8,128]{1,3,2,0:T(8,128)(2,1)S(1)}, u32[]{:S(2)}, u32[]{:S(2)}) %collective-permute-start.6) | collective-permute-done | bytes 131104 | tf_op jit(solution)/shard_map/ppermute | solution.py:91
  51.5 0.2 copy.113
  51.8 1.8 %collective-permute-start.7 = (bf16[2,2,32,8,128]{4,3,2,1,0:T(8,128)(2,1)S(1)}, bf16[2,2,32,8,128]{4,3,2,1,0:T(8,128)(2,1)S(1)}, u32[]{:S(2)}, u32[]{:S(2)}) collective-permute-start(bf16[2,2,32,8,128]{4,3,2,1,0:T(8,128)(2,1)S(1)} %get-tuple-element.16), channel_id=1, source_target_pairs={{0,8},{4,12},{8,0},{12,4},{16,24},{20,28},{24,16},{28,20},{1,9},{5... | collective-permute-start | bytes 786440 | tf_op jit(solution)/shard_map/ppermute | solution.py:91
  53.6 0.1 fusion.96
  53.7 0.3 copy.108
  54.0 0.3 copy.109
  54.3 1.6 %collective-permute-start.5 = (bf16[2,2,33,8,128]{4,3,2,1,0:T(8,128)(2,1)S(1)}, bf16[2,2,33,8,128]{4,3,2,1,0:T(8,128)(2,1)S(1)}, u32[]{:S(2)}, u32[]{:S(2)}) collective-permute-start(bf16[2,2,33,8,128]{4,3,2,1,0:T(8,128)(2,1)S(1)} %get-tuple-element.12), channel_id=1, source_target_pairs={{0,4},{4,0},{8,12},{12,8},{16,20},{20,16},{24,28},{28,24},{1,5},{5... | collective-permute-start | bytes 811016 | tf_op jit(solution)/shard_map/ppermute | solution.py:91
  55.9 3.4 %collective-permute-done.7 = bf16[2,2,32,8,128]{4,3,2,1,0:T(8,128)(2,1)S(1)} collective-permute-done((bf16[2,2,32,8,128]{4,3,2,1,0:T(8,128)(2,1)S(1)}, bf16[2,2,32,8,128]{4,3,2,1,0:T(8,128)(2,1)S(1)}, u32[]{:S(2)}, u32[]{:S(2)}) %collective-permute-start.7) | collective-permute-done | bytes 262176 | tf_op jit(solution)/shard_map/ppermute | solution.py:91
  59.3 0.5 copy.114
  59.9 0.1 copy.115
  60.0 0.1 copy.116
  60.0 0.6 gather_fusion
  60.6 0.1 broadcast_select_fusion.1
  60.7 0.1 copy.128
  60.8 0.1 add_select_fusion.3
  60.9 0.1 copy.118
  61.0 0.1 eq.48
  61.1 0.1 copy.119
  61.3 0.1 eq.51
  61.4 0.3 fusion.12
  61.7 0.6 gather_fusion.1
  62.2 0.1 select_bitcast_fusion
  62.3 0.1 pad_maximum_fusion
  62.4 0.6 copy.110
  63.0 0.8 %bitcast_convert_fusion = bf16[64,128,128]{1,2,0:T(8,128)(2,1)S(1)} fusion(bf16[8,32,8,128]{3,0,2,1:T(8,128)(2,1)S(1)} %bitcast.135, bf16[8,33,8,128]{3,0,2,1:T(8,128)(2,1)S(1)} %bitcast.136, bf16[128,8,8]{0,2,1:T(8,128)(2,1)S(1)} %select_bitcast_fusion), kind=kOutput, calls=%fused_computation.10 | convolution fusion | flops 137396224 | bytes 3178496 | tf_op jit(solution)/shard_map/rsc,sbcq->brq/dot_general | solution.py:211
  63.8 0.1 fusion.92
  63.9 1.2 %convolution_multiply_fusion = f32[64,32,128]{2,1,0:T(8,128)S(1)} fusion(bf16[64,128,128]{1,2,0:T(8,128)(2,1)S(1)} %bitcast_convert_fusion, bf16[64,16,64]{2,1,0:T(8,128)(2,1)S(1)} %get-tuple-element.14, bf16[64,16,64]{2,1,0:T(8,128)(2,1)S(1)} %get-tuple-element.13, bf16[64,16,128]{2,1,0:T(8,128)(2,1)S(1)} %dynamic-slice_bitcast_fusion), kind=kOutput, calls=%fused_computation.11 | convolution fusion | flops 68943872 | bytes 3670016 | tf_op jit(solution)/shard_map/bpq,bjq->bpj/dot_general | solution.py:219
  65.1 1.1 %copy.150 = f32[64,2,16,128]{3,2,0,1:T(8,128)} copy(f32[64,2,16,128]{3,2,1,0:T(8,128)S(1)} %bitcast.128) | data formatting | bytes 2097152 | tf_op jit(solution)/shard_map/div | solution.py:221
  (37 shorter events, 0.5 us)
Async XLA Ops:
  0.0 12.5 %copy-start = (f32[128]{0:T(128)S(1)}, f32[128]{0:T(128)}, u32[]{:S(2)}) copy-start(f32[128]{0:T(128)} %param.5) | copy-start | bytes 1540
  1.2 5.0 %copy-start.3 = (bf16[8,32,8192]{2,1,0:T(8,128)(2,1)S(1)}, bf16[8,32,8192]{2,1,0:T(8,128)(2,1)}, u32[]{:S(2)}) copy-start(bf16[8,32,8192]{2,1,0:T(8,128)(2,1)} %param.4) | copy-start | bytes 12582916
  9.0 4.5 %copy-start.1 = (s32[1,8,2]{1,2,0:T(2,128)S(1)}, s32[1,8,2]{1,2,0:T(2,128)}, u32[]{:S(2)}) copy-start(s32[1,8,2]{1,2,0:T(2,128)} %param.7) | copy-start | bytes 196
  9.0 4.5 %copy-start.2 = (s32[1,8,2]{1,2,0:T(2,128)S(1)}, s32[1,8,2]{1,2,0:T(2,128)}, u32[]{:S(2)}) copy-start(s32[1,8,2]{1,2,0:T(2,128)} %param.6) | copy-start | bytes 196
  11.9 1.9 %collective-permute-start = (f32[128,2,256]{2,0,1:T(8,128)S(1)}, f32[128,2,256]{2,0,1:T(8,128)S(1)}, u32[]{:S(2)}, u32[]{:S(2)}) collective-permute-start(f32[128,2,256]{2,0,1:T(8,128)S(1)} %broadcast_select_fusion), channel_id=1, source_target_pairs={{0,1},{1,0},{2,3},{3,2},{4,5},{5,4},{6,7},{7,6},{8,9},{9,8},{10,11... | collective-permute-start | bytes 786440 | tf_op jit(solution)/shard_map/ppermute | solution.py:22
  14.0 1.2 %collective-permute-start.1 = (f32[2,2,4,256]{3,2,1,0:T(4,128)S(1)}, f32[2,2,4,256]{3,2,1,0:T(4,128)S(1)}, u32[]{:S(2)}, u32[]{:S(2)}) collective-permute-start(f32[2,2,4,256]{3,2,1,0:T(4,128)S(1)} %pad_maximum_fusion.10), channel_id=1, source_target_pairs={{0,1},{1,0},{2,3},{3,2},{4,5},{5,4},{6,7},{7,6},{8,9},{9,8},{10,11... | collective-permute-start | bytes 49160 | tf_op jit(solution)/shard_map/ppermute | solution.py:22
  16.8 6.7 %collective-permute-start.2 = (bf16[64,8,2,32]{0,3,2,1:T(8,128)(2,1)S(1)}, bf16[64,8,2,32]{0,3,2,1:T(8,128)(2,1)S(1)}, u32[]{:S(2)}, u32[]{:S(2)}) collective-permute-start(bf16[64,8,2,32]{0,3,2,1:T(8,128)(2,1)S(1)} %bitcast.144), channel_id=1, source_target_pairs={{0,2},{2,0},{1,3},{3,1},{4,6},{6,4},{5,7},{7,5},{8,10},{10,8},{9,1... | collective-permute-start | bytes 196616 | tf_op jit(solution)/shard_map/ppermute | solution.py:173
  23.8 14.6 %collective-permute-start.3 = (bf16[65,8,128]{0,2,1:T(8,128)(2,1)S(1)}, bf16[65,8,128]{0,2,1:T(8,128)(2,1)S(1)}, u32[]{:S(2)}, u32[]{:S(2)}) collective-permute-start(bf16[65,8,128]{0,2,1:T(8,128)(2,1)S(1)} %pad_maximum_fusion.6), channel_id=1, source_target_pairs={{0,16},{4,20},{8,24},{12,28},{16,0},{20,4},{24,8},{28,12},{1,17},{... | collective-permute-start | bytes 399368 | tf_op jit(solution)/shard_map/ppermute | solution.py:82
  38.7 12.8 %collective-permute-start.6 = (bf16[2,32,8,128]{1,3,2,0:T(8,128)(2,1)S(1)}, bf16[2,32,8,128]{1,3,2,0:T(8,128)(2,1)S(1)}, u32[]{:S(2)}, u32[]{:S(2)}) collective-permute-start(bf16[2,32,8,128]{1,3,2,0:T(8,128)(2,1)S(1)} %get-tuple-element.6), channel_id=1, source_target_pairs={{0,4},{4,0},{8,12},{12,8},{16,20},{20,16},{24,28},{28,24},{1,5},{5... | collective-permute-start | bytes 393224 | tf_op jit(solution)/shard_map/ppermute | solution.py:91
  40.6 13.4 %collective-permute-start.4 = (bf16[2,33,8,128]{1,3,2,0:T(8,128)(2,1)S(1)}, bf16[2,33,8,128]{1,3,2,0:T(8,128)(2,1)S(1)}, u32[]{:S(2)}, u32[]{:S(2)}) collective-permute-start(bf16[2,33,8,128]{1,3,2,0:T(8,128)(2,1)S(1)} %slice_maximum_fusion), channel_id=1, source_target_pairs={{0,8},{4,12},{8,0},{12,4},{16,24},{20,28},{24,16},{28,20},{1,9},{5... | collective-permute-start | bytes 405512 | tf_op jit(solution)/shard_map/ppermute | solution.py:91
  51.8 7.5 %collective-permute-start.7 = (bf16[2,2,32,8,128]{4,3,2,1,0:T(8,128)(2,1)S(1)}, bf16[2,2,32,8,128]{4,3,2,1,0:T(8,128)(2,1)S(1)}, u32[]{:S(2)}, u32[]{:S(2)}) collective-permute-start(bf16[2,2,32,8,128]{4,3,2,1,0:T(8,128)(2,1)S(1)} %get-tuple-element.16), channel_id=1, source_target_pairs={{0,8},{4,12},{8,0},{12,4},{16,24},{20,28},{24,16},{28,20},{1,9},{5... | collective-permute-start | bytes 786440 | tf_op jit(solution)/shard_map/ppermute | solution.py:91
  54.3 8.0 %collective-permute-start.5 = (bf16[2,2,33,8,128]{4,3,2,1,0:T(8,128)(2,1)S(1)}, bf16[2,2,33,8,128]{4,3,2,1,0:T(8,128)(2,1)S(1)}, u32[]{:S(2)}, u32[]{:S(2)}) collective-permute-start(bf16[2,2,33,8,128]{4,3,2,1,0:T(8,128)(2,1)S(1)} %get-tuple-element.12), channel_id=1, source_target_pairs={{0,4},{4,0},{8,12},{12,8},{16,20},{20,16},{24,28},{28,24},{1,5},{5... | collective-permute-start | bytes 811016 | tf_op jit(solution)/shard_map/ppermute | solution.py:91

commit v5 on v4

--- a/solution.py
+++ b/solution.py
@@ -162,7 +162,7 @@
     white_im = scaled_re * response_im[:, None] + scaled_im * response_re[:, None]
     whitened = jnp.stack([white_re, white_im], axis=1).astype(jnp.bfloat16)
     whitened = whitened.reshape(seg_count, block_bins, 2, sections, seg_dev)
-    whitened = jnp.transpose(whitened, (0, 1, 3, 2, 4))
+    whitened = jnp.transpose(whitened, (0, 3, 1, 2, 4))
     seg_rank = lax.axis_index("seg")
     pieces = [lax.dynamic_index_in_dim(whitened, seg_rank, axis=0, keepdims=False)]
     for shift in range(1, seg_count):
@@ -170,18 +170,20 @@
             whitened, (seg_rank + shift) % seg_count, axis=0, keepdims=False
         )
         pairs = [(source, (source + shift) % seg_count) for source in range(seg_count)]
-        pieces.append(lax.ppermute(outgoing, "seg", pairs))
-    local = jnp.stack(pieces, axis=3).reshape(block_bins, sections, -1)
+        flat = outgoing.reshape(sections, -1)
+        pieces.append(lax.ppermute(flat, "seg", pairs).reshape(outgoing.shape))
+    local = jnp.stack(pieces, axis=3).reshape(sections, block_bins, -1)
     all_segs = seg_dev * seg_count
     table_width = local.shape[-1]
     table = jnp.concatenate([send_list[0], recv_row[0]], axis=1).reshape(-1)
     table_len = table.shape[0]
     slab = jnp.pad(table.astype(jnp.bfloat16), (0, sections * table_width - table_len))
-    carried = jnp.concatenate([local, slab.reshape(1, sections, table_width)], axis=0)
+    carried = jnp.concatenate([local, slab.reshape(sections, 1, table_width)], axis=1)
     blk_rank = lax.axis_index("blk")
-    everything = gather_blocks(carried, owners_count, blk_rank)
-    gathered = everything[:, :block_bins]
-    table_part = everything[:, block_bins].reshape(owners_count, -1)[:, :table_len]
+    everything = gather_blocks(carried.reshape(sections, -1), owners_count, blk_rank)
+    everything = everything.reshape(owners_count, sections, block_bins + 1, table_width)
+    gathered = everything[:, :, :block_bins]
+    table_part = everything[:, :, block_bins].reshape(owners_count, -1)[:, :table_len]
     table_part = table_part.astype(jnp.int32).reshape(owners_count, owners_count, 2 * capacity)
     if owners_count & (owners_count - 1) == 0:
         source_of = blk_rank ^ jnp.arange(owners_count, dtype=jnp.int32)
@@ -209,7 +211,7 @@
     if owners_count & (owners_count - 1) == 0:
         selector = jnp.take(selector, source_of, axis=1)
     routed = jnp.einsum(
-        "rsc,sbcq->brq", selector, gathered, preferred_element_type=jnp.float32
+        "rsc,scbq->brq", selector, gathered, preferred_element_type=jnp.float32
     ).astype(jnp.bfloat16)
     own = lax.dynamic_slice_in_dim(routed, blk_rank * OWN, OWN, axis=1)
     own_re = own[..., :all_segs]

time: 66.3 us -> 53 us (0.80)
  waiting for transfers between devices: 29.8 us -> 17.6 us
  starting transfers between devices: 12.1 us -> 10 us
    ppermute x1, waiting for transfers between devices: 11.5 us -> 5.94 us  [gather_blocks(): held = jnp.stack([carried, lax.ppermute(carried, 'blk', pairs)], axis=0)]
    ppermute x4, waiting for transfers between devices: 13.5 us -> 8.82 us  [gather_blocks(): arrived = lax.ppermute(part, 'blk', pairs)]
    ppermute x4, starting transfers between devices: 5.76 us -> 3.25 us  [gather_blocks(): arrived = lax.ppermute(part, 'blk', pairs)]
    ppermute x1, waiting for transfers between devices: 3.98 us -> 2.16 us  [per_device(): pieces.append(lax.ppermute(flat, 'seg', pairs).reshape(outgoing.shape))]
    another operation x6 -> x2, local copies, waits for them, and re-layouts: 2.05 us -> 0.37 us  [gather_blocks(): part = jnp.stack([part, arrived], axis=axis)]
    concatenate x0 -> x4, local copies, waits for them, and re-layouts: none -> 0.85 us  [the longest x3 0.66 us: gather_blocks(): return jnp.concatenate(results, axis=1)]
  transfers between devices with their start and end apart: 8 -> 8, of which waited for: 5 -> 7; matrix products, arithmetic and copies ran while one was open for 9% -> 5% of each run, Pallas kernels for 0% -> 0%
where the time goes in v5:
time: 53 us; the launch traced here: 52.9 us
  waiting for transfers between devices  17.6 us (33%)
  starting transfers between devices  10 us (19%)
  matrix products  8.91 us (17%)
  other arithmetic  8.56 us (16%)
  local copies, waits for them, and re-layouts  7.39 us (14%)
    ppermute x4, waiting for transfers between devices, gather_blocks(): arrived = lax.ppermute(part, 'blk', pairs)  8.82 us
    ppermute x1, waiting for transfers between devices, gather_blocks(): held = jnp.stack([carried, lax.ppermute(carried, 'blk', pairs)], axis=0)  5.94 us
    convert_element_type x1, other arithmetic, dft_tables_fast(): cos_part = (cos_sum * norm_scale).astype(jnp.bfloat16).reshape(rows, count)  4.96 us
    ppermute x4, starting transfers between devices, gather_blocks(): arrived = lax.ppermute(part, 'blk', pairs)  3.25 us
    ppermute x1, starting transfers between devices, gather_blocks(): held = jnp.stack([carried, lax.ppermute(carried, 'blk', pairs)], axis=0)  2.98 us
    ppermute x1, starting transfers between devices, per_device(): pieces.append(lax.ppermute(flat, 'seg', pairs).reshape(outgoing.shape))  2.88 us
    dot_general x1, matrix products, per_device(): lax.dot_general(cos_part, records, contract, preferred_element_type=jnp.f...  2.82 us
    dot_general x1, matrix products, per_device(): lax.dot_general(sin_part, records, contract, preferred_element_type=jnp.f...  2.82 us
  transfers between devices with their start and end apart: 8, of which 7 were waited for; matrix products, arithmetic and copies ran while one was open for 5% of the time, Pallas kernels for 0%

profile of v5, /device:TPU:0, one launch (start us, length us, event | category | flops | bytes accessed | tf_op | source)
XLA Modules:
  0.0 52.9 jit_solution(3612084925690653489)
XLA Ops:
  0.0 0.6 %fusion.54 = (f32[256,128]{1,0:T(8,128)S(1)}, f32[256,128]{1,0:T(8,128)S(1)}) fusion(s32[256]{0:T(256)S(1)} %fusion.71), kind=kLoop, calls=%fused_computation.113 | loop fusion | flops 458752 | bytes 263168 | tf_op jit(solution)/shard_map/cos | solution.py:48
  0.6 0.6 %fusion.56 = (f32[256,64]{1,0:T(8,128)S(1)}, f32[256,64]{1,0:T(8,128)S(1)}) fusion(s32[64]{0:T(128)S(1)} %multiply_add_fusion, s32[256]{0:T(256)S(1)} %fusion.71), kind=kLoop, calls=%fused_computation.115 | loop fusion | flops 229376 | bytes 132352 | tf_op jit(solution)/shard_map/cos | solution.py:46
  1.2 5.0 %multiply_convert_fusion.1 = (bf16[256,64,128]{2,1,0:T(8,128)(2,1)S(1)}, bf16[256,64,128]{2,1,0:T(8,128)(2,1)S(1)}) fusion(f32[256,128]{1,0:T(8,128)S(1)} %get-tuple-element.30, f32[256,64]{1,0:T(8,128)S(1)} %get-tuple-element.28, f32[256,128]{1,0:T(8,128)S(1)} %get-tuple-element.29, f32[256,64]{1,0:T(8,128)S(1)} %get-tuple-element.27), kind=kLoop, calls=%fused_computation.3 | loop fusion | flops 23068672 | bytes 8781824 | tf_op jit(solution)/shard_map/convert_element_type | solution.py:54
  6.2 2.8 %fusion.6 = f32[256,1,256]{2,0,1:T(8,128)S(1)} fusion(bf16[256,8192]{1,0:T(8,128)(2,1)S(1)} %bitcast.136, bf16[32,8,64,128]{3,2,1,0:T(8,128)(2,1)S(1)} %bitcast.120), kind=kOutput, calls=%fused_computation.12 | convolution fusion | flops 1073741824 | bytes 8650752 | tf_op jit(solution)/shard_map/dot_general | solution.py:120
  9.1 2.8 %fusion.9 = f32[256,1,256]{2,0,1:T(8,128)S(1)} fusion(bf16[256,8192]{1,0:T(8,128)(2,1)S(1)} %bitcast.137, bf16[32,8,64,128]{3,2,1,0:T(8,128)(2,1)S(1)} %bitcast.119), kind=kOutput, calls=%fused_computation.13 | convolution fusion | flops 1073741824 | bytes 8650752 | tf_op jit(solution)/shard_map/dot_general | solution.py:121
  11.9 0.5 collective-permute-start
  12.6 0.5 convolution_bitcast_fusion
  13.1 0.5 convolution_bitcast_fusion.1
  13.8 0.4 collective-permute-start.1
  14.2 0.1 copy.34
  14.3 0.1 convert_element_type.88
  14.4 0.6 %collective-permute-done.1 = f32[2,2,4,256]{3,2,1,0:T(4,128)S(1)} collective-permute-done((f32[2,2,4,256]{3,2,1,0:T(4,128)S(1)}, f32[2,2,4,256]{3,2,1,0:T(4,128)S(1)}, u32[]{:S(2)}, u32[]{:S(2)}) %collective-permute-start.1) | collective-permute-done | bytes 16416 | tf_op jit(solution)/shard_map/ppermute | solution.py:22
  15.1 0.1 fusion.24
  15.2 0.1 add_convert_fusion
  15.3 0.1 copy.29
  15.4 0.1 stack.81
  15.5 0.1 constant_dynamic-update-slice_fusion.1
  15.6 0.1 copy.30
  15.8 0.1 stack.82
  15.9 0.1 constant_dynamic-update-slice_fusion
  16.0 0.7 %dynamic-slice_bitcast_fusion.2 = (bf16[1,8,64,2,32]{2,0,4,1,3:T(2,128)(2,1)S(1)}, bf16[1,8,64,2,32]{2,0,4,1,3:T(2,128)(2,1)S(1)}) fusion(bf16[2,64,2,8,32]{1,0,4,3,2:T(2,128)(2,1)S(1)} %constant_dynamic-update-slice_fusion, s32[]{:T(128)S(6)} %select_n.229, s32[]{:T(128)S(6)} %select_n.231), kind=kLoop, calls=%fused_computation.47 | loop fusion | bytes 262152 | tf_op jit(solution)/shard_map/jit(dynamic_index_in_dim)/dynamic_slice | solution.py:167
  16.7 0.5 copy.32
  17.2 0.3 reshape.429
  17.5 2.9 %collective-permute-start.2 = (bf16[8,4096]{1,0:T(8,128)(2,1)S(1)}, bf16[8,4096]{1,0:T(8,128)(2,1)S(1)}, u32[]{:S(2)}, u32[]{:S(2)}) collective-permute-start(bf16[8,4096]{1,0:T(8,128)(2,1)S(1)} %reshape.429), channel_id=1, source_target_pairs={{0,2},{2,0},{1,3},{3,1},{4,6},{6,4},{5,7},{7,5},{8,10},{10,8},{9,1... | collective-permute-start | bytes 196616 | tf_op jit(solution)/shard_map/ppermute | solution.py:174
  20.4 0.2 copy.35
  20.6 2.2 %collective-permute-done.2 = bf16[8,4096]{1,0:T(8,128)(2,1)S(1)} collective-permute-done((bf16[8,4096]{1,0:T(8,128)(2,1)S(1)}, bf16[8,4096]{1,0:T(8,128)(2,1)S(1)}, u32[]{:S(2)}, u32[]{:S(2)}) %collective-permute-start.2) | collective-permute-done | bytes 65568 | tf_op jit(solution)/shard_map/ppermute | solution.py:174
  22.8 0.2 stack_reshape.6
  23.0 0.1 copy.33
  23.2 0.1 pad_maximum_fusion.6
  23.4 0.2 copy.36
  23.6 3.0 %collective-permute-start.3 = (bf16[8,8320]{1,0:T(8,128)(2,1)S(1)}, bf16[8,8320]{1,0:T(8,128)(2,1)S(1)}, u32[]{:S(2)}, u32[]{:S(2)}) collective-permute-start(bf16[8,8320]{1,0:T(8,128)(2,1)S(1)} %bitcast.127), channel_id=1, source_target_pairs={{0,16},{4,20},{8,24},{12,28},{16,0},{20,4},{24,8},{28,12},{1,17},{... | collective-permute-start | bytes 399368 | tf_op jit(solution)/shard_map/ppermute | solution.py:82
  26.5 5.9 %collective-permute-done.3 = bf16[8,8320]{1,0:T(8,128)(2,1)S(1)} collective-permute-done((bf16[8,8320]{1,0:T(8,128)(2,1)S(1)}, bf16[8,8320]{1,0:T(8,128)(2,1)S(1)}, u32[]{:S(2)}, u32[]{:S(2)}) %collective-permute-start.3) | collective-permute-done | bytes 133152 | tf_op jit(solution)/shard_map/ppermute | solution.py:82
  32.5 0.1 pad_maximum_fusion.7
  32.6 1.3 %collective-permute-start.6 = (bf16[2,4,8320]{2,1,0:T(4,128)(2,1)S(1)}, bf16[2,4,8320]{2,1,0:T(4,128)(2,1)S(1)}, u32[]{:S(2)}, u32[]{:S(2)}) collective-permute-start(bf16[2,4,8320]{2,1,0:T(4,128)(2,1)S(1)} %get-tuple-element.11), channel_id=1, source_target_pairs={{0,4},{4,0},{8,12},{12,8},{16,20},{20,16},{24,28},{28,24},{1,5},{5... | collective-permute-start | bytes 399368 | tf_op jit(solution)/shard_map/ppermute | solution.py:91
  33.9 0.7 %collective-permute-start.4 = (bf16[2,4,8320]{2,1,0:T(4,128)(2,1)S(1)}, bf16[2,4,8320]{2,1,0:T(4,128)(2,1)S(1)}, u32[]{:S(2)}, u32[]{:S(2)}) collective-permute-start(bf16[2,4,8320]{2,1,0:T(4,128)(2,1)S(1)} %get-tuple-element.12), channel_id=1, source_target_pairs={{0,8},{4,12},{8,0},{12,4},{16,24},{20,28},{24,16},{28,20},{1,9},{5... | collective-permute-start | bytes 399368 | tf_op jit(solution)/shard_map/ppermute | solution.py:91
  34.6 3.0 %collective-permute-done.6 = bf16[2,4,8320]{2,1,0:T(4,128)(2,1)S(1)} collective-permute-done((bf16[2,4,8320]{2,1,0:T(4,128)(2,1)S(1)}, bf16[2,4,8320]{2,1,0:T(4,128)(2,1)S(1)}, u32[]{:S(2)}, u32[]{:S(2)}) %collective-permute-start.6) | collective-permute-done | bytes 133152 | tf_op jit(solution)/shard_map/ppermute | solution.py:91
  37.6 0.2 fusion.86
  37.9 0.4 collective-permute-start.7
  38.3 0.9 %collective-permute-done.4 = bf16[2,4,8320]{2,1,0:T(4,128)(2,1)S(1)} collective-permute-done((bf16[2,4,8320]{2,1,0:T(4,128)(2,1)S(1)}, bf16[2,4,8320]{2,1,0:T(4,128)(2,1)S(1)}, u32[]{:S(2)}, u32[]{:S(2)}) %collective-permute-start.4) | collective-permute-done | bytes 133152 | tf_op jit(solution)/shard_map/ppermute | solution.py:91
  39.2 0.2 fusion.87
  39.4 0.8 %collective-permute-start.5 = (bf16[2,2,4,8320]{3,2,0,1:T(4,128)(2,1)S(1)}, bf16[2,2,4,8320]{3,2,0,1:T(4,128)(2,1)S(1)}, u32[]{:S(2)}, u32[]{:S(2)}) collective-permute-start(bf16[2,2,4,8320]{3,2,0,1:T(4,128)(2,1)S(1)} %get-tuple-element.14), channel_id=1, source_target_pairs={{0,4},{4,0},{8,12},{12,8},{16,20},{20,16},{24,28},{28,24},{1,5},{5... | collective-permute-start | bytes 798728 | tf_op jit(solution)/shard_map/ppermute | solution.py:91
  40.2 4.4 %collective-permute-done.7 = bf16[2,2,4,8320]{3,2,0,1:T(4,128)(2,1)S(1)} collective-permute-done((bf16[2,2,4,8320]{3,2,0,1:T(4,128)(2,1)S(1)}, bf16[2,2,4,8320]{3,2,0,1:T(4,128)(2,1)S(1)}, u32[]{:S(2)}, u32[]{:S(2)}) %collective-permute-start.7) | collective-permute-done | bytes 266272 | tf_op jit(solution)/shard_map/ppermute | solution.py:91
  44.6 0.4 pad_maximum_fusion.1
  45.0 0.2 copy.39
  45.2 0.2 concatenate.49
  45.4 0.5 collective-permute-done.5
  45.9 0.4 pad_maximum_fusion
  46.3 0.2 copy.38
  46.5 0.2 concatenate.48
  46.7 0.2 copy_dynamic-update-slice_fusion.1
  46.9 0.2 copy_dynamic-update-slice_fusion
  47.3 0.1 copy.43
  47.3 0.6 %gather_fusion = s32[8,8,4]{1,2,0:T(4,128)S(1)} fusion(s32[8,8,4]{1,2,0:T(4,128)S(1)} %copy.43, s32[1024]{0:T(1024)S(1)} %pad_clamp_fusion), kind=kCustom, calls=%fused_computation | custom fusion | bytes 2080 | tf_op jit(solution)/shard_map/jit(_take)/gather | solution.py:190
  48.0 0.1 copy.52
  48.2 0.1 copy.45
  48.3 0.1 eq.48
  48.4 0.1 copy.46
  48.6 0.1 eq.51
  48.7 0.3 fusion.12
  49.0 0.6 %gather_fusion.1 = bf16[8,128,8]{1,2,0:T(8,128)(2,1)S(1)} fusion(bf16[128,8,8]{0,2,1:T(8,128)(2,1)S(1)} %fusion.12, s32[1024]{0:T(1024)S(1)} %pad_clamp_fusion), kind=kCustom, calls=%fused_computation.1 | custom fusion | bytes 32800 | tf_op jit(solution)/shard_map/jit(_take)/gather | solution.py:212
  49.6 0.8 %bitcast_convert_fusion = bf16[64,128,128]{1,2,0:T(8,128)(2,1)S(1)} fusion(bf16[8,8,65,128]{3,0,1,2:T(8,128)(2,1)S(1)} %copy_dynamic-update-slice_fusion, bf16[128,8,8]{0,2,1:T(8,128)(2,1)S(1)} %select_bitcast_fusion), kind=kOutput, calls=%fused_computation.10 | convolution fusion | flops 135266304 | bytes 3178496 | tf_op jit(solution)/shard_map/rsc,scbq->brq/dot_general | solution.py:213
  50.4 0.1 fusion.88
  50.6 1.2 %convolution_multiply_fusion = f32[64,32,128]{2,1,0:T(8,128)S(1)} fusion(bf16[64,128,128]{1,2,0:T(8,128)(2,1)S(1)} %bitcast_convert_fusion, bf16[64,16,64]{2,1,0:T(8,128)(2,1)S(1)} %get-tuple-element.16, bf16[64,16,64]{2,1,0:T(8,128)(2,1)S(1)} %get-tuple-element.15, bf16[64,16,128]{2,1,0:T(8,128)(2,1)S(1)} %dynamic-slice_bitcast_fusion), kind=kOutput, calls=%fused_computation.11 | convolution fusion | flops 68943872 | bytes 3670016 | tf_op jit(solution)/shard_map/bpq,bjq->bpj/dot_general | solution.py:221
  51.8 1.1 %copy.75 = f32[64,2,16,128]{3,2,0,1:T(8,128)} copy(f32[64,2,16,128]{3,2,1,0:T(8,128)S(1)} %bitcast.121) | data formatting | bytes 2097152 | tf_op jit(solution)/shard_map/div | solution.py:223
  (38 shorter events, 0.8 us)
Async XLA Ops:
  0.0 12.6 %copy-start = (f32[128]{0:T(128)S(1)}, f32[128]{0:T(128)}, u32[]{:S(2)}) copy-start(f32[128]{0:T(128)} %param.5) | copy-start | bytes 1540
  1.2 5.0 %copy-start.3 = (bf16[8,32,8192]{2,1,0:T(8,128)(2,1)S(1)}, bf16[8,32,8192]{2,1,0:T(8,128)(2,1)}, u32[]{:S(2)}) copy-start(bf16[8,32,8192]{2,1,0:T(8,128)(2,1)} %param.4) | copy-start | bytes 12582916
  9.0 4.5 %copy-start.1 = (s32[1,8,2]{1,2,0:T(2,128)S(1)}, s32[1,8,2]{1,2,0:T(2,128)}, u32[]{:S(2)}) copy-start(s32[1,8,2]{1,2,0:T(2,128)} %param.7) | copy-start | bytes 196
  9.0 4.6 %copy-start.2 = (s32[1,8,2]{1,2,0:T(2,128)S(1)}, s32[1,8,2]{1,2,0:T(2,128)}, u32[]{:S(2)}) copy-start(s32[1,8,2]{1,2,0:T(2,128)} %param.6) | copy-start | bytes 196
  11.9 1.7 %collective-permute-start = (f32[128,2,256]{2,0,1:T(8,128)S(1)}, f32[128,2,256]{2,0,1:T(8,128)S(1)}, u32[]{:S(2)}, u32[]{:S(2)}) collective-permute-start(f32[128,2,256]{2,0,1:T(8,128)S(1)} %broadcast_select_fusion), channel_id=1, source_target_pairs={{0,1},{1,0},{2,3},{3,2},{4,5},{5,4},{6,7},{7,6},{8,9},{9,8},{10,11... | collective-permute-start | bytes 786440 | tf_op jit(solution)/shard_map/ppermute | solution.py:22
  13.8 1.2 %collective-permute-start.1 = (f32[2,2,4,256]{3,2,1,0:T(4,128)S(1)}, f32[2,2,4,256]{3,2,1,0:T(4,128)S(1)}, u32[]{:S(2)}, u32[]{:S(2)}) collective-permute-start(f32[2,2,4,256]{3,2,1,0:T(4,128)S(1)} %pad_maximum_fusion.10), channel_id=1, source_target_pairs={{0,1},{1,0},{2,3},{3,2},{4,5},{5,4},{6,7},{7,6},{8,9},{9,8},{10,11... | collective-permute-start | bytes 49160 | tf_op jit(solution)/shard_map/ppermute | solution.py:22
  17.5 5.3 %collective-permute-start.2 = (bf16[8,4096]{1,0:T(8,128)(2,1)S(1)}, bf16[8,4096]{1,0:T(8,128)(2,1)S(1)}, u32[]{:S(2)}, u32[]{:S(2)}) collective-permute-start(bf16[8,4096]{1,0:T(8,128)(2,1)S(1)} %reshape.429), channel_id=1, source_target_pairs={{0,2},{2,0},{1,3},{3,1},{4,6},{6,4},{5,7},{7,5},{8,10},{10,8},{9,1... | collective-permute-start | bytes 196616 | tf_op jit(solution)/shard_map/ppermute | solution.py:174
  23.6 8.9 %collective-permute-start.3 = (bf16[8,8320]{1,0:T(8,128)(2,1)S(1)}, bf16[8,8320]{1,0:T(8,128)(2,1)S(1)}, u32[]{:S(2)}, u32[]{:S(2)}) collective-permute-start(bf16[8,8320]{1,0:T(8,128)(2,1)S(1)} %bitcast.127), channel_id=1, source_target_pairs={{0,16},{4,20},{8,24},{12,28},{16,0},{20,4},{24,8},{28,12},{1,17},{... | collective-permute-start | bytes 399368 | tf_op jit(solution)/shard_map/ppermute | solution.py:82
  32.6 5.1 %collective-permute-start.6 = (bf16[2,4,8320]{2,1,0:T(4,128)(2,1)S(1)}, bf16[2,4,8320]{2,1,0:T(4,128)(2,1)S(1)}, u32[]{:S(2)}, u32[]{:S(2)}) collective-permute-start(bf16[2,4,8320]{2,1,0:T(4,128)(2,1)S(1)} %get-tuple-element.11), channel_id=1, source_target_pairs={{0,4},{4,0},{8,12},{12,8},{16,20},{20,16},{24,28},{28,24},{1,5},{5... | collective-permute-start | bytes 399368 | tf_op jit(solution)/shard_map/ppermute | solution.py:91
  33.9 5.3 %collective-permute-start.4 = (bf16[2,4,8320]{2,1,0:T(4,128)(2,1)S(1)}, bf16[2,4,8320]{2,1,0:T(4,128)(2,1)S(1)}, u32[]{:S(2)}, u32[]{:S(2)}) collective-permute-start(bf16[2,4,8320]{2,1,0:T(4,128)(2,1)S(1)} %get-tuple-element.12), channel_id=1, source_target_pairs={{0,8},{4,12},{8,0},{12,4},{16,24},{20,28},{24,16},{28,20},{1,9},{5... | collective-permute-start | bytes 399368 | tf_op jit(solution)/shard_map/ppermute | solution.py:91
  37.9 6.8 %collective-permute-start.7 = (bf16[2,2,4,8320]{3,2,0,1:T(4,128)(2,1)S(1)}, bf16[2,2,4,8320]{3,2,0,1:T(4,128)(2,1)S(1)}, u32[]{:S(2)}, u32[]{:S(2)}) collective-permute-start(bf16[2,2,4,8320]{3,2,0,1:T(4,128)(2,1)S(1)} %get-tuple-element.10), channel_id=1, source_target_pairs={{0,8},{4,12},{8,0},{12,4},{16,24},{20,28},{24,16},{28,20},{1,9},{5... | collective-permute-start | bytes 798728 | tf_op jit(solution)/shard_map/ppermute | solution.py:91
  39.4 6.5 %collective-permute-start.5 = (bf16[2,2,4,8320]{3,2,0,1:T(4,128)(2,1)S(1)}, bf16[2,2,4,8320]{3,2,0,1:T(4,128)(2,1)S(1)}, u32[]{:S(2)}, u32[]{:S(2)}) collective-permute-start(bf16[2,2,4,8320]{3,2,0,1:T(4,128)(2,1)S(1)} %get-tuple-element.14), channel_id=1, source_target_pairs={{0,4},{4,0},{8,12},{12,8},{16,20},{20,16},{24,28},{28,24},{1,5},{5... | collective-permute-start | bytes 798728 | tf_op jit(solution)/shard_map/ppermute | solution.py:91

commit v6 on v5

--- a/solution.py
+++ b/solution.py
@@ -101,11 +101,14 @@
     seg_count = lax.axis_size("seg")
     freq_count = lax.axis_size("freq")
     freq_rank = lax.axis_index("freq")
+    seg_rank = lax.axis_index("seg")
+    blk_rank = lax.axis_index("blk")
     sections, seg_dev, half_len = raw.shape
-    records = raw.reshape(sections * seg_dev, half_len)
     device_bins = BINS // freq_count
     block_bins = device_bins // seg_count
     capacity = send_list.shape[2]
+    all_segs = seg_dev * seg_count
+    table_width = 2 * all_segs
 
     def band_of(row_ids):
         owner_core = row_ids // device_bins
@@ -117,71 +120,91 @@
     band_rows = band_of(jnp.arange(device_bins * freq_count, dtype=jnp.int32))
     cos_part, sin_part = dft_tables_fast(band_rows, freq_rank * half_len, half_len)
     contract = (((1,), (1,)), ((), ()))
-    real_all = lax.dot_general(cos_part, records, contract, preferred_element_type=jnp.float32)
-    imag_all = lax.dot_general(sin_part, records, contract, preferred_element_type=jnp.float32)
-    blocks = jnp.stack([real_all, imag_all], axis=1)
-    blocks = blocks.reshape(freq_count, device_bins, 2, records.shape[0])
-    if freq_count == 2:
-        kept = jnp.where(freq_rank == 0, blocks[0], blocks[1])
-        sent = jnp.where(freq_rank == 0, blocks[1], blocks[0])
-        spectra = kept + swapped(sent, "freq", 0)
-    else:
-        spectra = lax.psum_scatter(
-            blocks.reshape(device_bins * freq_count, 2, records.shape[0]),
-            "freq",
-            scatter_dimension=0,
-            tiled=True,
-        )
-    real_part = spectra[:, 0]
-    imag_part = spectra[:, 1]
-    amplitude = jnp.sqrt(real_part * real_part + imag_part * imag_part + 1e-06)
-    amp_blocks = amplitude.reshape(seg_count, block_bins, -1)
-    band_rims = jnp.stack([amp_blocks[:, :HW], amp_blocks[:, block_bins - HW :]])
-    partner = swapped(band_rims, "freq", 0)
-    zero_rim = jnp.zeros_like(partner[1][:1])
-    right_prev = jnp.concatenate([zero_rim, partner[1][:-1]], axis=0)
-    left_next = jnp.concatenate([partner[0][1:], zero_rim], axis=0)
-    first_core = freq_rank == 0
-    lower_rim = jnp.where(first_core, right_prev, partner[1])
-    upper_rim = jnp.where(first_core, partner[0], left_next)
-    padded = jnp.concatenate([lower_rim, amp_blocks, upper_rim], axis=1)
-    window_sum = padded[:, 0:block_bins]
-    for offset_step in range(1, 2 * HW + 1):
-        window_sum = window_sum + padded[:, offset_step : offset_step + block_bins]
+    local_bins = freq_rank * device_bins + jnp.arange(device_bins, dtype=jnp.int32)
+    response_re, response_im = response(band_of(local_bins), taps)
     span_ids = jnp.arange(seg_count, dtype=jnp.int32)[:, None]
     offsets = jnp.arange(block_bins, dtype=jnp.int32)[None, :]
     position = (span_ids * freq_count + freq_rank) * block_bins + offsets
     counted = jnp.minimum(position + HW, BINS - 1) - jnp.maximum(position - HW, 0) + 1
-    smooth = window_sum / counted.astype(jnp.float32)[:, :, None]
-    divisor = jnp.maximum(smooth, WHITEN_FLOOR).reshape(device_bins, -1)
-    local_bins = freq_rank * device_bins + jnp.arange(device_bins, dtype=jnp.int32)
-    response_re, response_im = response(band_of(local_bins), taps)
-    scaled_re = real_part / divisor
-    scaled_im = imag_part / divisor
-    white_re = scaled_re * response_re[:, None] - scaled_im * response_im[:, None]
-    white_im = scaled_re * response_im[:, None] + scaled_im * response_re[:, None]
-    whitened = jnp.stack([white_re, white_im], axis=1).astype(jnp.bfloat16)
-    whitened = whitened.reshape(seg_count, block_bins, 2, sections, seg_dev)
-    whitened = jnp.transpose(whitened, (0, 3, 1, 2, 4))
-    seg_rank = lax.axis_index("seg")
-    pieces = [lax.dynamic_index_in_dim(whitened, seg_rank, axis=0, keepdims=False)]
-    for shift in range(1, seg_count):
-        outgoing = lax.dynamic_index_in_dim(
-            whitened, (seg_rank + shift) % seg_count, axis=0, keepdims=False
-        )
-        pairs = [(source, (source + shift) % seg_count) for source in range(seg_count)]
-        flat = outgoing.reshape(sections, -1)
-        pieces.append(lax.ppermute(flat, "seg", pairs).reshape(outgoing.shape))
-    local = jnp.stack(pieces, axis=3).reshape(sections, block_bins, -1)
-    all_segs = seg_dev * seg_count
-    table_width = local.shape[-1]
     table = jnp.concatenate([send_list[0], recv_row[0]], axis=1).reshape(-1)
     table_len = table.shape[0]
     slab = jnp.pad(table.astype(jnp.bfloat16), (0, sections * table_width - table_len))
-    carried = jnp.concatenate([local, slab.reshape(sections, 1, table_width)], axis=1)
-    blk_rank = lax.axis_index("blk")
-    everything = gather_blocks(carried.reshape(sections, -1), owners_count, blk_rank)
-    everything = everything.reshape(owners_count, sections, block_bins + 1, table_width)
+    slab = slab.reshape(sections, 1, table_width)
+
+    def whiten_part(part_raw):
+        part_sections = part_raw.shape[0]
+        records = part_raw.reshape(part_sections * seg_dev, half_len)
+        real_all = lax.dot_general(cos_part, records, contract, preferred_element_type=jnp.float32)
+        imag_all = lax.dot_general(sin_part, records, contract, preferred_element_type=jnp.float32)
+        blocks = jnp.stack([real_all, imag_all], axis=1)
+        blocks = blocks.reshape(freq_count, device_bins, 2, records.shape[0])
+        if freq_count == 2:
+            kept = jnp.where(freq_rank == 0, blocks[0], blocks[1])
+            sent = jnp.where(freq_rank == 0, blocks[1], blocks[0])
+            spectra = kept + swapped(sent, "freq", 0)
+        else:
+            spectra = lax.psum_scatter(
+                blocks.reshape(device_bins * freq_count, 2, records.shape[0]),
+                "freq",
+                scatter_dimension=0,
+                tiled=True,
+            )
+        real_part = spectra[:, 0]
+        imag_part = spectra[:, 1]
+        amplitude = jnp.sqrt(real_part * real_part + imag_part * imag_part + 1e-06)
+        amp_blocks = amplitude.reshape(seg_count, block_bins, -1)
+        band_rims = jnp.stack([amp_blocks[:, :HW], amp_blocks[:, block_bins - HW :]])
+        partner = swapped(band_rims, "freq", 0)
+        zero_rim = jnp.zeros_like(partner[1][:1])
+        right_prev = jnp.concatenate([zero_rim, partner[1][:-1]], axis=0)
+        left_next = jnp.concatenate([partner[0][1:], zero_rim], axis=0)
+        first_core = freq_rank == 0
+        lower_rim = jnp.where(first_core, right_prev, partner[1])
+        upper_rim = jnp.where(first_core, partner[0], left_next)
+        padded = jnp.concatenate([lower_rim, amp_blocks, upper_rim], axis=1)
+        window_sum = padded[:, 0:block_bins]
+        for offset_step in range(1, 2 * HW + 1):
+            window_sum = window_sum + padded[:, offset_step : offset_step + block_bins]
+        smooth = window_sum / counted.astype(jnp.float32)[:, :, None]
+        divisor = jnp.maximum(smooth, WHITEN_FLOOR).reshape(device_bins, -1)
+        scaled_re = real_part / divisor
+        scaled_im = imag_part / divisor
+        white_re = scaled_re * response_re[:, None] - scaled_im * response_im[:, None]
+        white_im = scaled_re * response_im[:, None] + scaled_im * response_re[:, None]
+        whitened = jnp.stack([white_re, white_im], axis=1).astype(jnp.bfloat16)
+        whitened = whitened.reshape(seg_count, block_bins, 2, part_sections, seg_dev)
+        return jnp.transpose(whitened, (0, 3, 1, 2, 4))
+
+    def exchange_part(whitened):
+        part_sections = whitened.shape[1]
+        pieces = [lax.dynamic_index_in_dim(whitened, seg_rank, axis=0, keepdims=False)]
+        for shift in range(1, seg_count):
+            outgoing = lax.dynamic_index_in_dim(
+                whitened, (seg_rank + shift) % seg_count, axis=0, keepdims=False
+            )
+            pairs = [(source, (source + shift) % seg_count) for source in range(seg_count)]
+            flat = outgoing.reshape(part_sections, -1)
+            pieces.append(lax.ppermute(flat, "seg", pairs).reshape(outgoing.shape))
+        return jnp.stack(pieces, axis=3).reshape(part_sections, block_bins, -1)
+
+    parts = 2 if sections % 4 == 0 else 1
+    part_len = sections // parts
+    gathered_parts = []
+    next_raw = raw[:part_len]
+    for part in range(parts):
+        lo = part * part_len
+        whitened = whiten_part(next_raw)
+        if part + 1 < parts:
+            next_raw, whitened = lax.optimization_barrier(
+                (raw[lo + part_len : lo + 2 * part_len], whitened)
+            )
+        local = exchange_part(whitened)
+        carried = jnp.concatenate([local, slab[lo : lo + part_len]], axis=1)
+        moved = gather_blocks(carried.reshape(part_len, -1), owners_count, blk_rank)
+        gathered_parts.append(
+            moved.reshape(owners_count, part_len, block_bins + 1, table_width)
+        )
+    everything = jnp.concatenate(gathered_parts, axis=1)
     gathered = everything[:, :, :block_bins]
     table_part = everything[:, :, block_bins].reshape(owners_count, -1)[:, :table_len]
     table_part = table_part.astype(jnp.int32).reshape(owners_count, owners_count, 2 * capacity)

time: 53 us -> 73.2 us (1.38)
  starting transfers between devices: 10 us -> 19.2 us
  matrix products: 8.91 us -> 16.1 us
  local copies, waits for them, and re-layouts: 7.39 us -> 13 us
  waiting for transfers between devices: 17.6 us -> 13.1 us
  other arithmetic: 8.56 us -> 10.9 us
    dot_general x2 -> x4, matrix products: 5.64 us -> 12.8 us  [the longest x2 7.52 us: whiten_part(): lax.dot_general(cos_part, records, contract, preferred_element_type=jnp.f...]
    ppermute x4 -> x8, starting transfers between devices: 3.25 us -> 7.67 us  [gather_blocks(): arrived = lax.ppermute(part, 'blk', pairs)]
    ppermute x4 -> x8, waiting for transfers between devices: 8.82 us -> 4.55 us  [gather_blocks(): arrived = lax.ppermute(part, 'blk', pairs)]
    ppermute x1 -> x2, starting transfers between devices: 2.98 us -> 6.43 us  [gather_blocks(): held = jnp.stack([carried, lax.ppermute(carried, 'blk', pairs)], axis=0)]
    slice x1 -> x5, local copies, waits for them, and re-layouts: 0.01 us -> 2.77 us  [the longest x1 2.58 us: per_device(): next_raw = raw[:part_len]]
    unnamed x11 -> x21, local copies, waits for them, and re-layouts: 0.42 us -> 2.61 us
    another operation x4 -> x12, other arithmetic: 1.18 us -> 3.01 us  [gather_blocks(): part = jnp.stack([part, arrived], axis=axis)]
    ppermute x1 -> x2, waiting for transfers between devices: 5.94 us -> 4.15 us  [gather_blocks(): held = jnp.stack([carried, lax.ppermute(carried, 'blk', pairs)], axis=0)]
  transfers between devices with their start and end apart: 8 -> 16, of which waited for: 7 -> 9; matrix products, arithmetic and copies ran while one was open for 5% -> 11% of each run, Pallas kernels for 0% -> 0%
where the time goes in v6:
time: 73.2 us; the launch traced here: 73.1 us
  starting transfers between devices  19.2 us (26%)
  matrix products  16.1 us (22%)
  waiting for transfers between devices  13.1 us (18%)
  local copies, waits for them, and re-layouts  13 us (18%)
  other arithmetic  10.9 us (15%)
  between operations  0.76 us (1%)
    ppermute x8, starting transfers between devices, gather_blocks(): arrived = lax.ppermute(part, 'blk', pairs)  7.67 us
    dot_general x2, matrix products, whiten_part(): lax.dot_general(cos_part, records, contract, preferred_element_type=jnp.f...  7.52 us
    ppermute x2, starting transfers between devices, gather_blocks(): held = jnp.stack([carried, lax.ppermute(carried, 'blk', pairs)], axis=0)  6.43 us
    dot_general x2, matrix products, whiten_part(): lax.dot_general(sin_part, records, contract, preferred_element_type=jnp.f...  5.3 us
    convert_element_type x1, other arithmetic, dft_tables_fast(): cos_part = (cos_sum * norm_scale).astype(jnp.bfloat16).reshape(rows, count)  4.96 us
    ppermute x8, waiting for transfers between devices, gather_blocks(): arrived = lax.ppermute(part, 'blk', pairs)  4.55 us
    ppermute x2, starting transfers between devices, exchange_part(): pieces.append(lax.ppermute(flat, 'seg', pairs).reshape(outgoing.shape))  4.27 us
    ppermute x2, waiting for transfers between devices, gather_blocks(): held = jnp.stack([carried, lax.ppermute(carried, 'blk', pairs)], axis=0)  4.15 us
  transfers between devices with their start and end apart: 16, of which 9 were waited for; matrix products, arithmetic and copies ran while one was open for 11% of the time, Pallas kernels for 0%

profile of v6, /device:TPU:0, one launch (start us, length us, event | category | flops | bytes accessed | tf_op | source)
XLA Modules:
  0.0 73.1 jit_solution(8030683121235722113)
XLA Ops:
  0.0 0.6 fusion.84
  0.6 0.6 fusion.86
  1.2 2.6 %fusion.119 = (bf16[4,32,8192]{2,1,0:T(8,128)(2,1)S(1)}, bf16[4,32,8192]{2,1,0:T(8,128)(2,1)S(1)}) fusion(bf16[8,32,8192]{2,1,0:T(8,128)(2,1)} %param.4), kind=kLoop, calls=%fused_computation.269 | loop fusion | bytes 8388608 | tf_op jit(solution)/shard_map/slice | solution.py:193
  3.8 5.0 %multiply_convert_fusion.1 = (bf16[256,64,128]{2,1,0:T(8,128)(2,1)S(1)}, bf16[256,64,128]{2,1,0:T(8,128)(2,1)S(1)}) fusion(f32[256,128]{1,0:T(8,128)S(1)} %get-tuple-element.46, f32[256,64]{1,0:T(8,128)S(1)} %get-tuple-element.44, f32[256,128]{1,0:T(8,128)S(1)} %get-tuple-element.45, f32[256,64]{1,0:T(8,128)S(1)} %get-tuple-element.43), kind=kLoop, calls=%fused_computation.3 | loop fusion | flops 23068672 | bytes 8781824 | tf_op jit(solution)/shard_map/convert_element_type | solution.py:54
  8.8 2.0 %copy-done.3 = bf16[256,64,128]{2,1,0:T(8,128)(2,1)} copy-done((bf16[256,64,128]{2,1,0:T(8,128)(2,1)}, bf16[256,64,128]{2,1,0:T(8,128)(2,1)S(1)}, u32[]{:S(2)}) %copy-start.3) | copy-done | bytes 4194328
  10.8 2.6 %fusion.12 = f32[256,1,128]{2,0,1:T(8,128)S(1)} fusion(bf16[128,8192]{1,0:T(8,128)(2,1)S(1)} %bitcast.197, bf16[32,8,64,128]{3,2,1,0:T(8,128)(2,1)S(1)} %bitcast.192), kind=kOutput, calls=%fused_computation.18 | convolution fusion | flops 536870912 | bytes 6422528 | tf_op jit(solution)/shard_map/dot_general | solution.py:137
  13.4 2.5 %fusion.18 = f32[256,1,128]{2,0,1:T(8,128)S(1)} fusion(bf16[128,8192]{1,0:T(8,128)(2,1)S(1)} %bitcast.198, bf16[32,8,64,128]{3,2,1,0:T(8,128)(2,1)S(1)} %bitcast.190), kind=kOutput, calls=%fused_computation.20 | convolution fusion | flops 536870912 | bytes 6422528 | tf_op jit(solution)/shard_map/dot_general | solution.py:138
  16.0 0.5 collective-permute-start
  16.9 0.5 convolution_bitcast_fusion.1
  17.4 0.5 convolution_bitcast_fusion
  18.2 0.2 copy.46
  18.4 0.9 %collective-permute-done.1 = f32[2,2,4,128]{3,2,1,0:T(4,128)S(1)} collective-permute-done((f32[2,2,4,128]{3,2,1,0:T(4,128)S(1)}, f32[2,2,4,128]{3,2,1,0:T(4,128)S(1)}, u32[]{:S(2)}, u32[]{:S(2)}) %collective-permute-start.1) | collective-permute-done | bytes 8224 | tf_op jit(solution)/shard_map/ppermute | solution.py:22
  19.9 0.2 maximum_bitcast_fusion
  20.2 5.0 %fusion.15 = f32[256,1,128]{2,0,1:T(8,128)S(1)} fusion(bf16[128,8192]{1,0:T(8,128)(2,1)S(1)} %bitcast.195, bf16[32,8,64,128]{3,2,1,0:T(8,128)(2,1)} %bitcast.193), kind=kOutput, calls=%fused_computation.19 | convolution fusion | flops 536870912 | bytes 6422528 | tf_op jit(solution)/shard_map/dot_general | solution.py:137
  25.2 2.8 %fusion.21 = f32[256,1,128]{2,0,1:T(8,128)S(1)} fusion(bf16[128,8192]{1,0:T(8,128)(2,1)S(1)} %bitcast.196, bf16[32,8,64,128]{3,2,1,0:T(8,128)(2,1)S(1)} %bitcast.191), kind=kOutput, calls=%fused_computation.21 | convolution fusion | flops 536870912 | bytes 6422528 | tf_op jit(solution)/shard_map/dot_general | solution.py:138
  27.9 0.3 constant_dynamic-slice_fusion.1
  28.4 0.2 reshape.510
  28.6 2.7 %collective-permute-start.2 = (bf16[4,4096]{1,0:T(4,128)(2,1)S(1)}, bf16[4,4096]{1,0:T(4,128)(2,1)S(1)}, u32[]{:S(2)}, u32[]{:S(2)}) collective-permute-start(bf16[4,4096]{1,0:T(4,128)(2,1)S(1)} %reshape.510), channel_id=1, source_target_pairs={{0,2},{2,0},{1,3},{3,1},{4,6},{6,4},{5,7},{7,5},{8,10},{10,8},{9,1... | collective-permute-start | bytes 98312 | tf_op jit(solution)/shard_map/ppermute | solution.py:187
  31.4 1.7 %collective-permute-done.2 = bf16[4,4096]{1,0:T(4,128)(2,1)S(1)} collective-permute-done((bf16[4,4096]{1,0:T(4,128)(2,1)S(1)}, bf16[4,4096]{1,0:T(4,128)(2,1)S(1)}, u32[]{:S(2)}, u32[]{:S(2)}) %collective-permute-start.2) | collective-permute-done | bytes 32800 | tf_op jit(solution)/shard_map/ppermute | solution.py:187
  33.8 3.2 %collective-permute-start.3 = (bf16[4,8320]{1,0:T(4,128)(2,1)S(1)}, bf16[4,8320]{1,0:T(4,128)(2,1)S(1)}, u32[]{:S(2)}, u32[]{:S(2)}) collective-permute-start(bf16[4,8320]{1,0:T(4,128)(2,1)S(1)} %bitcast.228), channel_id=1, source_target_pairs={{0,16},{4,20},{8,24},{12,28},{16,0},{20,4},{24,8},{28,12},{1,17},{... | collective-permute-start | bytes 199688 | tf_op jit(solution)/shard_map/ppermute | solution.py:82
  37.2 2.4 %collective-permute-done.3 = bf16[4,8320]{1,0:T(4,128)(2,1)S(1)} collective-permute-done((bf16[4,8320]{1,0:T(4,128)(2,1)S(1)}, bf16[4,8320]{1,0:T(4,128)(2,1)S(1)}, u32[]{:S(2)}, u32[]{:S(2)}) %collective-permute-start.3) | collective-permute-done | bytes 66592 | tf_op jit(solution)/shard_map/ppermute | solution.py:82
  39.7 1.6 %collective-permute-start.6 = (bf16[2,2,8320]{2,1,0:T(2,128)(2,1)S(1)}, bf16[2,2,8320]{2,1,0:T(2,128)(2,1)S(1)}, u32[]{:S(2)}, u32[]{:S(2)}) collective-permute-start(bf16[2,2,8320]{2,1,0:T(2,128)(2,1)S(1)} %get-tuple-element.21), channel_id=1, source_target_pairs={{0,4},{4,0},{8,12},{12,8},{16,20},{20,16},{24,28},{28,24},{1,5},{5... | collective-permute-start | bytes 199688 | tf_op jit(solution)/shard_map/ppermute | solution.py:91
  41.3 1.6 %collective-permute-start.4 = (bf16[2,2,8320]{2,1,0:T(2,128)(2,1)S(1)}, bf16[2,2,8320]{2,1,0:T(2,128)(2,1)S(1)}, u32[]{:S(2)}, u32[]{:S(2)}) collective-permute-start(bf16[2,2,8320]{2,1,0:T(2,128)(2,1)S(1)} %get-tuple-element.22), channel_id=1, source_target_pairs={{0,8},{4,12},{8,0},{12,4},{16,24},{20,28},{24,16},{28,20},{1,9},{5... | collective-permute-start | bytes 199688 | tf_op jit(solution)/shard_map/ppermute | solution.py:91
  43.7 0.3 dynamic-slice_bitcast_fusion.2
  44.1 0.2 reshape.515
  44.3 1.6 %collective-permute-start.10 = (bf16[4,4096]{1,0:T(4,128)(2,1)S(1)}, bf16[4,4096]{1,0:T(4,128)(2,1)S(1)}, u32[]{:S(2)}, u32[]{:S(2)}) collective-permute-start(bf16[4,4096]{1,0:T(4,128)(2,1)S(1)} %reshape.515), channel_id=1, source_target_pairs={{0,2},{2,0},{1,3},{3,1},{4,6},{6,4},{5,7},{7,5},{8,10},{10,8},{9,1... | collective-permute-start | bytes 98312 | tf_op jit(solution)/shard_map/ppermute | solution.py:187
  45.9 0.2 fusion.129
  46.1 0.2 pad_maximum_fusion.5
  46.3 0.2 fusion.130
  46.5 1.8 %collective-permute-done.10 = bf16[4,4096]{1,0:T(4,128)(2,1)S(1)} collective-permute-done((bf16[4,4096]{1,0:T(4,128)(2,1)S(1)}, bf16[4,4096]{1,0:T(4,128)(2,1)S(1)}, u32[]{:S(2)}, u32[]{:S(2)}) %collective-permute-start.10) | collective-permute-done | bytes 32800 | tf_op jit(solution)/shard_map/ppermute | solution.py:187
  48.8 3.3 %collective-permute-start.11 = (bf16[4,8320]{1,0:T(4,128)(2,1)S(1)}, bf16[4,8320]{1,0:T(4,128)(2,1)S(1)}, u32[]{:S(2)}, u32[]{:S(2)}) collective-permute-start(bf16[4,8320]{1,0:T(4,128)(2,1)S(1)} %bitcast.229), channel_id=1, source_target_pairs={{0,16},{4,20},{8,24},{12,28},{16,0},{20,4},{24,8},{28,12},{1,17},{... | collective-permute-start | bytes 199688 | tf_op jit(solution)/shard_map/ppermute | solution.py:82
  52.0 0.2 pad_maximum_fusion.4
  52.3 0.6 collective-permute-start.5
  52.9 1.8 %collective-permute-done.11 = bf16[4,8320]{1,0:T(4,128)(2,1)S(1)} collective-permute-done((bf16[4,8320]{1,0:T(4,128)(2,1)S(1)}, bf16[4,8320]{1,0:T(4,128)(2,1)S(1)}, u32[]{:S(2)}, u32[]{:S(2)}) %collective-permute-start.11) | collective-permute-done | bytes 66592 | tf_op jit(solution)/shard_map/ppermute | solution.py:82
  54.8 0.4 collective-permute-start.14
  55.2 1.3 %collective-permute-start.12 = (bf16[2,2,8320]{2,1,0:T(2,128)(2,1)S(1)}, bf16[2,2,8320]{2,1,0:T(2,128)(2,1)S(1)}, u32[]{:S(2)}, u32[]{:S(2)}) collective-permute-start(bf16[2,2,8320]{2,1,0:T(2,128)(2,1)S(1)} %get-tuple-element.20), channel_id=1, source_target_pairs={{0,8},{4,12},{8,0},{12,4},{16,24},{20,28},{24,16},{28,20},{1,9},{5... | collective-permute-start | bytes 199688 | tf_op jit(solution)/shard_map/ppermute | solution.py:91
  56.6 0.7 collective-permute-done.7
  57.3 0.4 pad_maximum_fusion.1
  57.6 0.2 copy.50
  57.8 0.2 concatenate.81
  58.0 0.4 pad_maximum_fusion
  58.4 0.2 copy.49
  58.6 0.2 concatenate.80
  59.0 0.7 collective-permute-done.14
  59.6 0.2 fusion.127
  59.8 0.2 pad_maximum_fusion.7
  60.0 0.9 %collective-permute-start.15 = (bf16[2,2,2,8320]{3,2,0,1:T(2,128)(2,1)S(1)}, bf16[2,2,2,8320]{3,2,0,1:T(2,128)(2,1)S(1)}, u32[]{:S(2)}, u32[]{:S(2)}) collective-permute-start(bf16[2,2,2,8320]{3,2,0,1:T(2,128)(2,1)S(1)} %pad_maximum_fusion.7), channel_id=1, source_target_pairs={{0,8},{4,12},{8,0},{12,4},{16,24},{20,28},{24,16},{28,20},{1,9},{5... | collective-permute-start | bytes 399368 | tf_op jit(solution)/shard_map/ppermute | solution.py:91
  61.0 0.2 fusion.128
  61.1 0.2 pad_maximum_fusion.6
  61.3 1.1 %collective-permute-start.13 = (bf16[2,2,2,8320]{3,2,0,1:T(2,128)(2,1)S(1)}, bf16[2,2,2,8320]{3,2,0,1:T(2,128)(2,1)S(1)}, u32[]{:S(2)}, u32[]{:S(2)}) collective-permute-start(bf16[2,2,2,8320]{3,2,0,1:T(2,128)(2,1)S(1)} %pad_maximum_fusion.6), channel_id=1, source_target_pairs={{0,4},{4,0},{8,12},{12,8},{16,20},{20,16},{24,28},{28,24},{1,5},{5... | collective-permute-start | bytes 399368 | tf_op jit(solution)/shard_map/ppermute | solution.py:91
  62.5 2.6 %collective-permute-done.15 = bf16[2,2,2,8320]{3,2,0,1:T(2,128)(2,1)S(1)} collective-permute-done((bf16[2,2,2,8320]{3,2,0,1:T(2,128)(2,1)S(1)}, bf16[2,2,2,8320]{3,2,0,1:T(2,128)(2,1)S(1)}, u32[]{:S(2)}, u32[]{:S(2)}) %collective-permute-start.15) | collective-permute-done | bytes 133152 | tf_op jit(solution)/shard_map/ppermute | solution.py:91
  65.1 0.4 pad_maximum_fusion.3
  65.5 0.2 copy.59
  65.7 0.2 concatenate.88
  65.8 0.6 collective-permute-done.13
  66.4 0.4 pad_maximum_fusion.2
  66.8 0.2 copy.58
  67.0 0.2 concatenate.87
  67.5 0.6 gather_fusion
  68.9 0.3 fusion.24
  69.2 0.6 gather_fusion.1
  69.8 0.8 %bitcast_convert_fusion = bf16[64,128,128]{1,2,0:T(8,128)(2,1)S(1)} fusion(bf16[8,8,65,128]{3,0,1,2:T(8,128)(2,1)S(1)} %copy_dynamic-update-slice_fusion, bf16[128,8,8]{0,2,1:T(8,128)(2,1)S(1)} %select_bitcast_fusion), kind=kOutput, calls=%fused_computation.12 | convolution fusion | flops 135266304 | bytes 3178496 | tf_op jit(solution)/shard_map/rsc,scbq->brq/dot_general | solution.py:236
  70.8 1.2 %convolution_multiply_fusion = f32[64,32,128]{2,1,0:T(8,128)S(1)} fusion(bf16[64,128,128]{1,2,0:T(8,128)(2,1)S(1)} %bitcast_convert_fusion, bf16[64,16,64]{2,1,0:T(8,128)(2,1)S(1)} %get-tuple-element.14, bf16[64,16,64]{2,1,0:T(8,128)(2,1)S(1)} %get-tuple-element.13, bf16[64,16,128]{2,1,0:T(8,128)(2,1)S(1)} %dynamic-slice_bitcast_fusion), kind=kOutput, calls=%fused_computation.17 | convolution fusion | flops 68943872 | bytes 3670016 | tf_op jit(solution)/shard_map/bpq,bjq->bpj/dot_general | solution.py:244
  72.0 1.1 %copy.117 = f32[64,2,16,128]{3,2,0,1:T(8,128)} copy(f32[64,2,16,128]{3,2,1,0:T(8,128)S(1)} %bitcast.194) | data formatting | bytes 2097152 | tf_op jit(solution)/shard_map/div | solution.py:246
  (103 shorter events, 5.5 us)
Async XLA Ops:
  0.0 16.9 %copy-start = (f32[128]{0:T(128)S(1)}, f32[128]{0:T(128)}, u32[]{:S(2)}) copy-start(f32[128]{0:T(128)} %param.5) | copy-start | bytes 1540
  8.8 2.0 %copy-start.3 = (bf16[256,64,128]{2,1,0:T(8,128)(2,1)}, bf16[256,64,128]{2,1,0:T(8,128)(2,1)S(1)}, u32[]{:S(2)}) copy-start(bf16[256,64,128]{2,1,0:T(8,128)(2,1)S(1)} %get-tuple-element.11) | copy-start | bytes 12582916
  8.8 4.6 %copy-start.1 = (bf16[256,64,128]{2,1,0:T(8,128)(2,1)}, bf16[256,64,128]{2,1,0:T(8,128)(2,1)S(1)}, u32[]{:S(2)}) copy-start(bf16[256,64,128]{2,1,0:T(8,128)(2,1)S(1)} %get-tuple-element.12) | copy-start | bytes 12582916
  13.4 3.2 %copy-start.4 = (s32[1,8,2]{1,2,0:T(2,128)S(1)}, s32[1,8,2]{1,2,0:T(2,128)}, u32[]{:S(2)}) copy-start(s32[1,8,2]{1,2,0:T(2,128)} %param.7) | copy-start | bytes 196
  13.4 3.2 %copy-start.5 = (s32[1,8,2]{1,2,0:T(2,128)S(1)}, s32[1,8,2]{1,2,0:T(2,128)}, u32[]{:S(2)}) copy-start(s32[1,8,2]{1,2,0:T(2,128)} %param.6) | copy-start | bytes 196
  16.0 1.9 %collective-permute-start = (f32[128,2,128]{2,0,1:T(8,128)S(1)}, f32[128,2,128]{2,0,1:T(8,128)S(1)}, u32[]{:S(2)}, u32[]{:S(2)}) collective-permute-start(f32[128,2,128]{2,0,1:T(8,128)S(1)} %broadcast_select_fusion.1), channel_id=1, source_target_pairs={{0,1},{1,0},{2,3},{3,2},{4,5},{5,4},{6,7},{7,6},{8,9},{9,8},{10,11... | collective-permute-start | bytes 393224 | tf_op jit(solution)/shard_map/ppermute | solution.py:22
  18.0 1.2 %collective-permute-start.1 = (f32[2,2,4,128]{3,2,1,0:T(4,128)S(1)}, f32[2,2,4,128]{3,2,1,0:T(4,128)S(1)}, u32[]{:S(2)}, u32[]{:S(2)}) collective-permute-start(f32[2,2,4,128]{3,2,1,0:T(4,128)S(1)} %pad_maximum_fusion.19), channel_id=1, source_target_pairs={{0,1},{1,0},{2,3},{3,2},{4,5},{5,4},{6,7},{7,6},{8,9},{9,8},{10,11... | collective-permute-start | bytes 24584 | tf_op jit(solution)/shard_map/ppermute | solution.py:22
  20.2 5.0 %copy-start.2 = (bf16[256,64,128]{2,1,0:T(8,128)(2,1)S(1)}, bf16[256,64,128]{2,1,0:T(8,128)(2,1)}, u32[]{:S(2)}) copy-start(bf16[256,64,128]{2,1,0:T(8,128)(2,1)} %copy-done.1) | copy-start | bytes 12582916
  28.6 4.6 %collective-permute-start.2 = (bf16[4,4096]{1,0:T(4,128)(2,1)S(1)}, bf16[4,4096]{1,0:T(4,128)(2,1)S(1)}, u32[]{:S(2)}, u32[]{:S(2)}) collective-permute-start(bf16[4,4096]{1,0:T(4,128)(2,1)S(1)} %reshape.510), channel_id=1, source_target_pairs={{0,2},{2,0},{1,3},{3,1},{4,6},{6,4},{5,7},{7,5},{8,10},{10,8},{9,1... | collective-permute-start | bytes 98312 | tf_op jit(solution)/shard_map/ppermute | solution.py:187
  31.3 5.7 %collective-permute-start.8 = (f32[128,2,128]{2,0,1:T(8,128)S(1)}, f32[128,2,128]{2,0,1:T(8,128)S(1)}, u32[]{:S(2)}, u32[]{:S(2)}) collective-permute-start(f32[128,2,128]{2,0,1:T(8,128)S(1)} %broadcast_select_fusion), channel_id=1, source_target_pairs={{0,1},{1,0},{2,3},{3,2},{4,5},{5,4},{6,7},{7,6},{8,9},{9,8},{10,11... | collective-permute-start | bytes 393224 | tf_op jit(solution)/shard_map/ppermute | solution.py:22
  33.8 5.7 %collective-permute-start.3 = (bf16[4,8320]{1,0:T(4,128)(2,1)S(1)}, bf16[4,8320]{1,0:T(4,128)(2,1)S(1)}, u32[]{:S(2)}, u32[]{:S(2)}) collective-permute-start(bf16[4,8320]{1,0:T(4,128)(2,1)S(1)} %bitcast.228), channel_id=1, source_target_pairs={{0,16},{4,20},{8,24},{12,28},{16,0},{20,4},{24,8},{28,12},{1,17},{... | collective-permute-start | bytes 199688 | tf_op jit(solution)/shard_map/ppermute | solution.py:82
  37.1 5.8 %collective-permute-start.9 = (f32[2,2,4,128]{3,2,1,0:T(4,128)S(1)}, f32[2,2,4,128]{3,2,1,0:T(4,128)S(1)}, u32[]{:S(2)}, u32[]{:S(2)}) collective-permute-start(f32[2,2,4,128]{3,2,1,0:T(4,128)S(1)} %pad_maximum_fusion.20), channel_id=1, source_target_pairs={{0,1},{1,0},{2,3},{3,2},{4,5},{5,4},{6,7},{7,6},{8,9},{9,8},{10,11... | collective-permute-start | bytes 24584 | tf_op jit(solution)/shard_map/ppermute | solution.py:22
  39.7 6.2 %collective-permute-start.6 = (bf16[2,2,8320]{2,1,0:T(2,128)(2,1)S(1)}, bf16[2,2,8320]{2,1,0:T(2,128)(2,1)S(1)}, u32[]{:S(2)}, u32[]{:S(2)}) collective-permute-start(bf16[2,2,8320]{2,1,0:T(2,128)(2,1)S(1)} %get-tuple-element.21), channel_id=1, source_target_pairs={{0,4},{4,0},{8,12},{12,8},{16,20},{20,16},{24,28},{28,24},{1,5},{5... | collective-permute-start | bytes 199688 | tf_op jit(solution)/shard_map/ppermute | solution.py:91
  41.3 5.0 %collective-permute-start.4 = (bf16[2,2,8320]{2,1,0:T(2,128)(2,1)S(1)}, bf16[2,2,8320]{2,1,0:T(2,128)(2,1)S(1)}, u32[]{:S(2)}, u32[]{:S(2)}) collective-permute-start(bf16[2,2,8320]{2,1,0:T(2,128)(2,1)S(1)} %get-tuple-element.22), channel_id=1, source_target_pairs={{0,8},{4,12},{8,0},{12,4},{16,24},{20,28},{24,16},{28,20},{1,9},{5... | collective-permute-start | bytes 199688 | tf_op jit(solution)/shard_map/ppermute | solution.py:91
  44.3 4.0 %collective-permute-start.10 = (bf16[4,4096]{1,0:T(4,128)(2,1)S(1)}, bf16[4,4096]{1,0:T(4,128)(2,1)S(1)}, u32[]{:S(2)}, u32[]{:S(2)}) collective-permute-start(bf16[4,4096]{1,0:T(4,128)(2,1)S(1)} %reshape.515), channel_id=1, source_target_pairs={{0,2},{2,0},{1,3},{3,1},{4,6},{6,4},{5,7},{7,5},{8,10},{10,8},{9,1... | collective-permute-start | bytes 98312 | tf_op jit(solution)/shard_map/ppermute | solution.py:187
  48.8 5.9 %collective-permute-start.11 = (bf16[4,8320]{1,0:T(4,128)(2,1)S(1)}, bf16[4,8320]{1,0:T(4,128)(2,1)S(1)}, u32[]{:S(2)}, u32[]{:S(2)}) collective-permute-start(bf16[4,8320]{1,0:T(4,128)(2,1)S(1)} %bitcast.229), channel_id=1, source_target_pairs={{0,16},{4,20},{8,24},{12,28},{16,0},{20,4},{24,8},{28,12},{1,17},{... | collective-permute-start | bytes 199688 | tf_op jit(solution)/shard_map/ppermute | solution.py:82
  52.2 5.1 %collective-permute-start.7 = (bf16[2,2,2,8320]{3,2,0,1:T(2,128)(2,1)S(1)}, bf16[2,2,2,8320]{3,2,0,1:T(2,128)(2,1)S(1)}, u32[]{:S(2)}, u32[]{:S(2)}) collective-permute-start(bf16[2,2,2,8320]{3,2,0,1:T(2,128)(2,1)S(1)} %pad_maximum_fusion.5), channel_id=1, source_target_pairs={{0,8},{4,12},{8,0},{12,4},{16,24},{20,28},{24,16},{28,20},{1,9},{5... | collective-permute-start | bytes 399368 | tf_op jit(solution)/shard_map/ppermute | solution.py:91
  52.3 5.7 %collective-permute-start.5 = (bf16[2,2,2,8320]{3,2,0,1:T(2,128)(2,1)S(1)}, bf16[2,2,2,8320]{3,2,0,1:T(2,128)(2,1)S(1)}, u32[]{:S(2)}, u32[]{:S(2)}) collective-permute-start(bf16[2,2,2,8320]{3,2,0,1:T(2,128)(2,1)S(1)} %pad_maximum_fusion.4), channel_id=1, source_target_pairs={{0,4},{4,0},{8,12},{12,8},{16,20},{20,16},{24,28},{28,24},{1,5},{5... | collective-permute-start | bytes 399368 | tf_op jit(solution)/shard_map/ppermute | solution.py:91
  54.8 4.8 %collective-permute-start.14 = (bf16[2,2,8320]{2,1,0:T(2,128)(2,1)S(1)}, bf16[2,2,8320]{2,1,0:T(2,128)(2,1)S(1)}, u32[]{:S(2)}, u32[]{:S(2)}) collective-permute-start(bf16[2,2,8320]{2,1,0:T(2,128)(2,1)S(1)} %get-tuple-element.19), channel_id=1, source_target_pairs={{0,4},{4,0},{8,12},{12,8},{16,20},{20,16},{24,28},{28,24},{1,5},{5... | collective-permute-start | bytes 199688 | tf_op jit(solution)/shard_map/ppermute | solution.py:91
  55.2 5.7 %collective-permute-start.12 = (bf16[2,2,8320]{2,1,0:T(2,128)(2,1)S(1)}, bf16[2,2,8320]{2,1,0:T(2,128)(2,1)S(1)}, u32[]{:S(2)}, u32[]{:S(2)}) collective-permute-start(bf16[2,2,8320]{2,1,0:T(2,128)(2,1)S(1)} %get-tuple-element.20), channel_id=1, source_target_pairs={{0,8},{4,12},{8,0},{12,4},{16,24},{20,28},{24,16},{28,20},{1,9},{5... | collective-permute-start | bytes 199688 | tf_op jit(solution)/shard_map/ppermute | solution.py:91
  60.0 5.1 %collective-permute-start.15 = (bf16[2,2,2,8320]{3,2,0,1:T(2,128)(2,1)S(1)}, bf16[2,2,2,8320]{3,2,0,1:T(2,128)(2,1)S(1)}, u32[]{:S(2)}, u32[]{:S(2)}) collective-permute-start(bf16[2,2,2,8320]{3,2,0,1:T(2,128)(2,1)S(1)} %pad_maximum_fusion.7), channel_id=1, source_target_pairs={{0,8},{4,12},{8,0},{12,4},{16,24},{20,28},{24,16},{28,20},{1,9},{5... | collective-permute-start | bytes 399368 | tf_op jit(solution)/shard_map/ppermute | solution.py:91
  61.3 5.1 %collective-permute-start.13 = (bf16[2,2,2,8320]{3,2,0,1:T(2,128)(2,1)S(1)}, bf16[2,2,2,8320]{3,2,0,1:T(2,128)(2,1)S(1)}, u32[]{:S(2)}, u32[]{:S(2)}) collective-permute-start(bf16[2,2,2,8320]{3,2,0,1:T(2,128)(2,1)S(1)} %pad_maximum_fusion.6), channel_id=1, source_target_pairs={{0,4},{4,0},{8,12},{12,8},{16,20},{20,16},{24,28},{28,24},{1,5},{5... | collective-permute-start | bytes 399368 | tf_op jit(solution)/shard_map/ppermute | solution.py:91

commit v7 on v5

--- a/solution.py
+++ b/solution.py
@@ -3,6 +3,8 @@
 import jax
 import jax.numpy as jnp
 from jax import lax
+from jax.experimental import pallas as pl
+from jax.experimental.pallas import tpu as pltpu
 from jax.sharding import PartitionSpec as P
 
 SEG_LEN = 16384
@@ -64,6 +66,73 @@
     real_part = jnp.dot(jnp.cos(angles), taps, precision=lax.Precision.HIGHEST)
     imag_part = jnp.dot(-jnp.sin(angles), taps, precision=lax.Precision.HIGHEST)
     return (real_part, imag_part)
+
+
+def dft_kernel(rec_ref, cos_a_ref, nsin_a_ref, cos_b_ref, sin_b_ref, re_ref, im_ref):
+    step = pl.program_id(0)
+    lanes = cos_b_ref.shape[0]
+    per_step = rec_ref.shape[1] // lanes
+
+    @pl.when(step == 0)
+    def _():
+        re_ref[...] = jnp.zeros_like(re_ref)
+        im_ref[...] = jnp.zeros_like(im_ref)
+
+    cos_b = cos_b_ref[...]
+    sin_b = sin_b_ref[...]
+    cos_tiles = []
+    sin_tiles = []
+    for inner in range(per_step):
+        row = step * per_step + inner
+        cos_a = cos_a_ref[pl.ds(row, 1), :]
+        nsin_a = nsin_a_ref[pl.ds(row, 1), :]
+        cos_tiles.append((cos_a * cos_b + nsin_a * sin_b).astype(jnp.bfloat16))
+        sin_tiles.append((nsin_a * cos_b - cos_a * sin_b).astype(jnp.bfloat16))
+    cos_tile = jnp.concatenate(cos_tiles, axis=0)
+    sin_tile = jnp.concatenate(sin_tiles, axis=0)
+    rec = rec_ref[...]
+    re_ref[...] += jnp.dot(rec, cos_tile, preferred_element_type=jnp.float32)
+    im_ref[...] += jnp.dot(rec, sin_tile, preferred_element_type=jnp.float32)
+
+
+def dft_fused(records, band_index, first_sample):
+    lanes = 128
+    chunk = 512
+    count = records.shape[1]
+    wavenumber = BAND_LO + band_index
+    coarse = first_sample + lanes * jnp.arange(count // lanes, dtype=jnp.int32)
+    fine = jnp.arange(lanes, dtype=jnp.int32)
+    coarse_angle = (coarse[:, None] * wavenumber[None, :] % SEG_LEN).astype(jnp.float32) * (
+        TWO_PI / SEG_LEN
+    )
+    fine_angle = (fine[:, None] * wavenumber[None, :] % SEG_LEN).astype(jnp.float32) * (
+        TWO_PI / SEG_LEN
+    )
+    norm_scale = 1.0 / math.sqrt(SEG_LEN)
+    cos_a = jnp.cos(coarse_angle)
+    nsin_a = -jnp.sin(coarse_angle)
+    cos_b = jnp.cos(fine_angle) * norm_scale
+    sin_b = jnp.sin(fine_angle) * norm_scale
+    rows = records.shape[0]
+    bins = band_index.shape[0]
+    full = lambda step: (0, 0)
+    return pl.pallas_call(
+        dft_kernel,
+        grid=(count // chunk,),
+        in_specs=[
+            pl.BlockSpec((rows, chunk), lambda step: (0, step)),
+            pl.BlockSpec(cos_a.shape, full),
+            pl.BlockSpec(nsin_a.shape, full),
+            pl.BlockSpec(cos_b.shape, full),
+            pl.BlockSpec(sin_b.shape, full),
+        ],
+        out_specs=[pl.BlockSpec((rows, bins), full), pl.BlockSpec((rows, bins), full)],
+        out_shape=[
+            jax.ShapeDtypeStruct((rows, bins), jnp.float32),
+            jax.ShapeDtypeStruct((rows, bins), jnp.float32),
+        ],
+        compiler_params=pltpu.CompilerParams(dimension_semantics=("arbitrary",)),
+    )(records, cos_a, nsin_a, cos_b, sin_b)
 
 
 def gather_blocks(carried, count, rank):
@@ -115,10 +184,9 @@
         ) * block_bins + local_row % block_bins
 
     band_rows = band_of(jnp.arange(device_bins * freq_count, dtype=jnp.int32))
-    cos_part, sin_part = dft_tables_fast(band_rows, freq_rank * half_len, half_len)
-    contract = (((1,), (1,)), ((), ()))
-    real_all = lax.dot_general(cos_part, records, contract, preferred_element_type=jnp.float32)
-    imag_all = lax.dot_general(sin_part, records, contract, preferred_element_type=jnp.float32)
+    real_t, imag_t = dft_fused(records, band_rows, freq_rank * half_len)
+    real_all = real_t.T
+    imag_all = imag_t.T
     blocks = jnp.stack([real_all, imag_all], axis=1)
     blocks = blocks.reshape(freq_count, device_bins, 2, records.shape[0])
     if freq_count == 2:

time: 53 us -> 55.5 us (1.047)
  Pallas kernels: 0 us -> 12 us
  matrix products: 8.91 us -> 3.27 us
  other arithmetic: 8.56 us -> 5.76 us
  local copies, waits for them, and re-layouts: 7.39 us -> 6.17 us
    pallas_call x0 -> x1, Pallas kernels: none -> 12 us  [dft_fused(): pl.pallas_call(dft_kernel, grid=(count // chunk,), in_specs=[pl.BlockSpec...]
    dot_general x2 -> x0, matrix products: 5.64 us -> none  [the longest x1 2.82 us: per_device(): lax.dot_general(cos_part, records, contract, preferred_element_type=jnp.f...]
    convert_element_type x1 -> x0, other arithmetic: 4.96 us -> none  [dft_tables_fast(): cos_part = (cos_sum * norm_scale).astype(jnp.bfloat16).reshape(rows, count)]
    mul x0 -> x1, other arithmetic: none -> 1.24 us  [dft_fused(): sin_b = jnp.sin(fine_angle) * norm_scale]
    cos x2 -> x0, other arithmetic: 1.17 us -> none  [the longest x1 0.59 us: dft_tables_fast(): cos_a = jnp.cos(coarse_angle)[:, :, None]]
    select_n x1, other arithmetic: 0.03 us -> 1.18 us  [per_device(): sent = jnp.where(freq_rank == 0, blocks[1], blocks[0])]
    neg x0 -> x1, other arithmetic: none -> 1 us  [dft_fused(): nsin_a = -jnp.sin(coarse_angle)]
    dynamic_slice x2 -> x0, local copies, waits for them, and re-layouts: 0.7 us -> none  [per_device(): lax.dynamic_index_in_dim(whitened, seg_rank, axis=0, keepdims=False)]
where the time goes in v7:
time: 55.5 us; the launch traced here: 55.1 us
  waiting for transfers between devices  17.6 us (32%)
  Pallas kernels  12 us (22%)
  starting transfers between devices  10 us (18%)
  local copies, waits for them, and re-layouts  6.17 us (11%)
  other arithmetic  5.76 us (10%)
  matrix products  3.27 us (6%)
    pallas_call x1, Pallas kernels, dft_fused(): pl.pallas_call(dft_kernel, grid=(count // chunk,), in_specs=[pl.BlockSpec...  12 us
    ppermute x4, waiting for transfers between devices, gather_blocks(): arrived = lax.ppermute(part, 'blk', pairs)  8.79 us
    ppermute x1, waiting for transfers between devices, gather_blocks(): held = jnp.stack([carried, lax.ppermute(carried, 'blk', pairs)], axis=0)  5.94 us
    ppermute x4, starting transfers between devices, gather_blocks(): arrived = lax.ppermute(part, 'blk', pairs)  3.26 us
    ppermute x1, starting transfers between devices, gather_blocks(): held = jnp.stack([carried, lax.ppermute(carried, 'blk', pairs)], axis=0)  2.98 us
    ppermute x1, starting transfers between devices, per_device(): pieces.append(lax.ppermute(flat, 'seg', pairs).reshape(outgoing.shape))  2.86 us
    ppermute x1, waiting for transfers between devices, per_device(): pieces.append(lax.ppermute(flat, 'seg', pairs).reshape(outgoing.shape))  2.2 us
    mul x1, other arithmetic, dft_fused(): sin_b = jnp.sin(fine_angle) * norm_scale  1.24 us
  transfers between devices with their start and end apart: 8, of which 7 were waited for; matrix products, arithmetic and copies ran while one was open for 5% of the time, Pallas kernels for 0%

profile of v7, /device:TPU:0, one launch (start us, length us, event | category | flops | bytes accessed | tf_op | source)
XLA Modules:
  0.0 55.1 jit_solution(9661040089629309991)
XLA Ops:
  0.0 1.2 %sine_multiply_fusion = (f32[128,256]{1,0:T(8,128)}, f32[128,256]{1,0:T(8,128)}) fusion(s32[256]{0:T(256)S(1)} %fusion.56), kind=kLoop, calls=%fused_computation.76 | loop fusion | flops 524288 | bytes 263168 | tf_op jit(solution)/shard_map/mul | solution.py:115
  1.3 1.0 %sine_negate_fusion = (f32[64,256]{1,0:T(8,128)}, f32[64,256]{1,0:T(8,128)}) fusion(s32[256]{0:T(256)S(1)} %fusion.56, s32[64]{0:T(128)S(1)} %multiply_add_fusion), kind=kLoop, calls=%fused_computation.105 | loop fusion | flops 245760 | bytes 132352 | tf_op jit(solution)/shard_map/neg | solution.py:113
  2.3 12.0 %shard_map.46 = (f32[256,256]{1,0:T(8,128)}, f32[256,256]{1,0:T(8,128)}) custom-call(bf16[256,8192]{1,0:T(8,128)(2,1)} %bitcast.96, f32[64,256]{1,0:T(8,128)} %get-tuple-element.30.cos_a_ref, f32[64,256]{1,0:T(8,128)} %get-tuple-element.29.nsin_a_ref, f32[128,256]{1,0:T(8,128)} %get-tuple-element.32.cos_b_ref, f32[128,256]{1,0:T(8,128)} %get-tuple-element.31.sin_b_ref), custom_call_target="tpu_custom_call" | custom-call | tf_op jit(solution)/shard_map/pallas_call | solution.py:119
  14.3 1.2 %broadcast_select_fusion = f32[128,2,256]{0,2,1:T(8,128)S(1)} fusion(pred[]{:T(512)S(6)} %eq.47, f32[256,1,256]{0,2,1:T(8,128)} %bitcast.101, f32[256,1,256]{0,2,1:T(8,128)} %bitcast.99), kind=kLoop, calls=%fused_computation.81 | loop fusion | flops 196608 | bytes 786433 | tf_op jit(solution)/shard_map/jit(_where)/select_n | solution.py:194
  15.4 0.5 collective-permute-start
  16.0 0.1 add_convert_fusion.1
  16.1 0.5 convolution_bitcast_fusion
  16.6 0.5 convolution_bitcast_fusion.1
  17.3 0.1 copy.35
  17.4 0.4 collective-permute-start.1
  17.8 0.1 copy.42
  17.9 0.1 convert_element_type.40
  18.0 0.6 %collective-permute-done.1 = f32[2,2,4,256]{3,2,1,0:T(4,128)S(1)} collective-permute-done((f32[2,2,4,256]{3,2,1,0:T(4,128)S(1)}, f32[2,2,4,256]{3,2,1,0:T(4,128)S(1)}, u32[]{:S(2)}, u32[]{:S(2)}) %collective-permute-start.1) | collective-permute-done | bytes 16416 | tf_op jit(solution)/shard_map/ppermute | solution.py:24
  18.7 0.1 fusion.12
  18.8 0.1 copy.36
  19.0 0.1 stack.82
  19.1 0.1 stack.81
  19.3 0.2 copy.40
  19.5 0.3 reshape.272
  19.8 2.9 %collective-permute-start.2 = (bf16[8,4096]{1,0:T(8,128)(2,1)S(1)}, bf16[8,4096]{1,0:T(8,128)(2,1)S(1)}, u32[]{:S(2)}, u32[]{:S(2)}) collective-permute-start(bf16[8,4096]{1,0:T(8,128)(2,1)S(1)} %reshape.272), channel_id=1, source_target_pairs={{0,2},{2,0},{1,3},{3,1},{4,6},{6,4},{5,7},{7,5},{8,10},{10,8},{9,1... | collective-permute-start | bytes 196616 | tf_op jit(solution)/shard_map/ppermute | solution.py:242
  22.6 0.2 copy.43
  22.9 2.2 %collective-permute-done.2 = bf16[8,4096]{1,0:T(8,128)(2,1)S(1)} collective-permute-done((bf16[8,4096]{1,0:T(8,128)(2,1)S(1)}, bf16[8,4096]{1,0:T(8,128)(2,1)S(1)}, u32[]{:S(2)}, u32[]{:S(2)}) %collective-permute-start.2) | collective-permute-done | bytes 65568 | tf_op jit(solution)/shard_map/ppermute | solution.py:242
  25.1 0.2 stack_reshape.6
  25.3 0.1 copy.41
  25.5 0.1 pad_maximum_fusion.6
  25.6 0.2 copy.44
  25.8 3.0 %collective-permute-start.3 = (bf16[8,8320]{1,0:T(8,128)(2,1)S(1)}, bf16[8,8320]{1,0:T(8,128)(2,1)S(1)}, u32[]{:S(2)}, u32[]{:S(2)}) collective-permute-start(bf16[8,8320]{1,0:T(8,128)(2,1)S(1)} %bitcast.107), channel_id=1, source_target_pairs={{0,16},{4,20},{8,24},{12,28},{16,0},{20,4},{24,8},{28,12},{1,17},{... | collective-permute-start | bytes 399368 | tf_op jit(solution)/shard_map/ppermute | solution.py:151
  28.8 5.9 %collective-permute-done.3 = bf16[8,8320]{1,0:T(8,128)(2,1)S(1)} collective-permute-done((bf16[8,8320]{1,0:T(8,128)(2,1)S(1)}, bf16[8,8320]{1,0:T(8,128)(2,1)S(1)}, u32[]{:S(2)}, u32[]{:S(2)}) %collective-permute-start.3) | collective-permute-done | bytes 133152 | tf_op jit(solution)/shard_map/ppermute | solution.py:151
  34.8 0.1 pad_maximum_fusion.7
  34.8 1.3 %collective-permute-start.6 = (bf16[2,4,8320]{2,1,0:T(4,128)(2,1)S(1)}, bf16[2,4,8320]{2,1,0:T(4,128)(2,1)S(1)}, u32[]{:S(2)}, u32[]{:S(2)}) collective-permute-start(bf16[2,4,8320]{2,1,0:T(4,128)(2,1)S(1)} %get-tuple-element.13), channel_id=1, source_target_pairs={{0,4},{4,0},{8,12},{12,8},{16,20},{20,16},{24,28},{28,24},{1,5},{5... | collective-permute-start | bytes 399368 | tf_op jit(solution)/shard_map/ppermute | solution.py:160
  36.1 0.7 %collective-permute-start.4 = (bf16[2,4,8320]{2,1,0:T(4,128)(2,1)S(1)}, bf16[2,4,8320]{2,1,0:T(4,128)(2,1)S(1)}, u32[]{:S(2)}, u32[]{:S(2)}) collective-permute-start(bf16[2,4,8320]{2,1,0:T(4,128)(2,1)S(1)} %get-tuple-element.14), channel_id=1, source_target_pairs={{0,8},{4,12},{8,0},{12,4},{16,24},{20,28},{24,16},{28,20},{1,9},{5... | collective-permute-start | bytes 399368 | tf_op jit(solution)/shard_map/ppermute | solution.py:160
  36.9 3.0 %collective-permute-done.6 = bf16[2,4,8320]{2,1,0:T(4,128)(2,1)S(1)} collective-permute-done((bf16[2,4,8320]{2,1,0:T(4,128)(2,1)S(1)}, bf16[2,4,8320]{2,1,0:T(4,128)(2,1)S(1)}, u32[]{:S(2)}, u32[]{:S(2)}) %collective-permute-start.6) | collective-permute-done | bytes 133152 | tf_op jit(solution)/shard_map/ppermute | solution.py:160
  39.9 0.2 fusion.71
  40.1 0.4 collective-permute-start.7
  40.5 0.9 %collective-permute-done.4 = bf16[2,4,8320]{2,1,0:T(4,128)(2,1)S(1)} collective-permute-done((bf16[2,4,8320]{2,1,0:T(4,128)(2,1)S(1)}, bf16[2,4,8320]{2,1,0:T(4,128)(2,1)S(1)}, u32[]{:S(2)}, u32[]{:S(2)}) %collective-permute-start.4) | collective-permute-done | bytes 133152 | tf_op jit(solution)/shard_map/ppermute | solution.py:160
  41.4 0.2 fusion.72
  41.7 0.8 %collective-permute-start.5 = (bf16[2,2,4,8320]{3,2,0,1:T(4,128)(2,1)S(1)}, bf16[2,2,4,8320]{3,2,0,1:T(4,128)(2,1)S(1)}, u32[]{:S(2)}, u32[]{:S(2)}) collective-permute-start(bf16[2,2,4,8320]{3,2,0,1:T(4,128)(2,1)S(1)} %get-tuple-element.16), channel_id=1, source_target_pairs={{0,4},{4,0},{8,12},{12,8},{16,20},{20,16},{24,28},{28,24},{1,5},{5... | collective-permute-start | bytes 798728 | tf_op jit(solution)/shard_map/ppermute | solution.py:160
  42.5 4.4 %collective-permute-done.7 = bf16[2,2,4,8320]{3,2,0,1:T(4,128)(2,1)S(1)} collective-permute-done((bf16[2,2,4,8320]{3,2,0,1:T(4,128)(2,1)S(1)}, bf16[2,2,4,8320]{3,2,0,1:T(4,128)(2,1)S(1)}, u32[]{:S(2)}, u32[]{:S(2)}) %collective-permute-start.7) | collective-permute-done | bytes 266272 | tf_op jit(solution)/shard_map/ppermute | solution.py:160
  46.9 0.4 pad_maximum_fusion.1
  47.3 0.2 copy.47
  47.5 0.2 concatenate.49
  47.7 0.5 collective-permute-done.5
  48.1 0.4 pad_maximum_fusion
  48.5 0.2 copy.46
  48.7 0.2 concatenate.48
  48.9 0.2 copy_dynamic-update-slice_fusion.1
  49.2 0.2 copy_dynamic-update-slice_fusion
  49.4 0.1 copy.50
  49.5 0.1 copy.51
  49.6 0.6 %gather_fusion = s32[8,8,4]{1,2,0:T(4,128)S(1)} fusion(s32[8,8,4]{1,2,0:T(4,128)S(1)} %copy.51, s32[1024]{0:T(1024)S(1)} %pad_clamp_fusion), kind=kCustom, calls=%fused_computation | custom fusion | bytes 2080 | tf_op jit(solution)/shard_map/jit(_take)/gather | solution.py:258
  50.2 0.1 broadcast_select_fusion.1
  50.3 0.1 copy.60
  50.3 0.1 add_select_fusion.3
  50.4 0.1 copy.53
  50.5 0.1 eq.48
  50.7 0.1 copy.54
  50.8 0.1 eq.51
  51.0 0.3 fusion
  51.2 0.6 %gather_fusion.1 = bf16[8,128,8]{1,2,0:T(8,128)(2,1)S(1)} fusion(bf16[128,8,8]{0,2,1:T(8,128)(2,1)S(1)} %fusion, s32[1024]{0:T(1024)S(1)} %pad_clamp_fusion), kind=kCustom, calls=%fused_computation.1 | custom fusion | bytes 32800 | tf_op jit(solution)/shard_map/jit(_take)/gather | solution.py:280
  51.8 0.1 select_bitcast_fusion
  51.9 0.8 %bitcast_convert_fusion = bf16[64,128,128]{1,2,0:T(8,128)(2,1)S(1)} fusion(bf16[8,8,65,128]{3,0,1,2:T(8,128)(2,1)S(1)} %copy_dynamic-update-slice_fusion, bf16[128,8,8]{0,2,1:T(8,128)(2,1)S(1)} %select_bitcast_fusion), kind=kOutput, calls=%fused_computation.2 | convolution fusion | flops 135266304 | bytes 3178496 | tf_op jit(solution)/shard_map/rsc,scbq->brq/dot_general | solution.py:281
  52.7 0.1 fusion.73
  52.8 1.2 %convolution_multiply_fusion = f32[64,32,128]{2,1,0:T(8,128)S(1)} fusion(bf16[64,128,128]{1,2,0:T(8,128)(2,1)S(1)} %bitcast_convert_fusion, bf16[64,16,64]{2,1,0:T(8,128)(2,1)S(1)} %get-tuple-element.18, bf16[64,16,64]{2,1,0:T(8,128)(2,1)S(1)} %get-tuple-element.17, bf16[64,16,128]{2,1,0:T(8,128)(2,1)S(1)} %dynamic-slice_bitcast_fusion), kind=kOutput, calls=%fused_computation.3 | convolution fusion | flops 68943872 | bytes 3670016 | tf_op jit(solution)/shard_map/bpq,bjq->bpj/dot_general | solution.py:289
  54.1 1.1 %copy.70 = f32[64,2,16,128]{3,2,0,1:T(8,128)} copy(f32[64,2,16,128]{3,2,1,0:T(8,128)S(1)} %bitcast.97) | data formatting | bytes 2097152 | tf_op jit(solution)/shard_map/div | solution.py:291
  (37 shorter events, 0.5 us)
Async XLA Ops:
  0.0 16.1 %copy-start = (f32[128]{0:T(128)S(1)}, f32[128]{0:T(128)}, u32[]{:S(2)}) copy-start(f32[128]{0:T(128)} %param.5) | copy-start | bytes 1540
  14.2 2.9 %copy-start.3 = (s32[1,8,2]{1,2,0:T(2,128)S(1)}, s32[1,8,2]{1,2,0:T(2,128)}, u32[]{:S(2)}) copy-start(s32[1,8,2]{1,2,0:T(2,128)} %param.7) | copy-start | bytes 196
  14.2 2.9 %copy-start.4 = (s32[1,8,2]{1,2,0:T(2,128)S(1)}, s32[1,8,2]{1,2,0:T(2,128)}, u32[]{:S(2)}) copy-start(s32[1,8,2]{1,2,0:T(2,128)} %param.6) | copy-start | bytes 196
  14.2 2.9 %copy-start.1 = (f32[256,256]{1,0:T(8,128)S(1)}, f32[256,256]{1,0:T(8,128)}, u32[]{:S(2)}) copy-start(f32[256,256]{1,0:T(8,128)} %get-tuple-element.7) | copy-start | bytes 786436
  14.2 2.9 %copy-start.2 = (f32[256,256]{1,0:T(8,128)S(1)}, f32[256,256]{1,0:T(8,128)}, u32[]{:S(2)}) copy-start(f32[256,256]{1,0:T(8,128)} %get-tuple-element.8) | copy-start | bytes 786436
  15.4 1.7 %collective-permute-start = (f32[128,2,256]{0,2,1:T(8,128)S(1)}, f32[128,2,256]{0,2,1:T(8,128)S(1)}, u32[]{:S(2)}, u32[]{:S(2)}) collective-permute-start(f32[128,2,256]{0,2,1:T(8,128)S(1)} %broadcast_select_fusion), channel_id=1, source_target_pairs={{0,1},{1,0},{2,3},{3,2},{4,5},{5,4},{6,7},{7,6},{8,9},{9,8},{10,11... | collective-permute-start | bytes 786440 | tf_op jit(solution)/shard_map/ppermute | solution.py:24
  17.4 1.2 %collective-permute-start.1 = (f32[2,2,4,256]{3,2,1,0:T(4,128)S(1)}, f32[2,2,4,256]{3,2,1,0:T(4,128)S(1)}, u32[]{:S(2)}, u32[]{:S(2)}) collective-permute-start(f32[2,2,4,256]{3,2,1,0:T(4,128)S(1)} %pad_maximum_fusion.10), channel_id=1, source_target_pairs={{0,1},{1,0},{2,3},{3,2},{4,5},{5,4},{6,7},{7,6},{8,9},{9,8},{10,11... | collective-permute-start | bytes 49160 | tf_op jit(solution)/shard_map/ppermute | solution.py:24
  19.8 5.3 %collective-permute-start.2 = (bf16[8,4096]{1,0:T(8,128)(2,1)S(1)}, bf16[8,4096]{1,0:T(8,128)(2,1)S(1)}, u32[]{:S(2)}, u32[]{:S(2)}) collective-permute-start(bf16[8,4096]{1,0:T(8,128)(2,1)S(1)} %reshape.272), channel_id=1, source_target_pairs={{0,2},{2,0},{1,3},{3,1},{4,6},{6,4},{5,7},{7,5},{8,10},{10,8},{9,1... | collective-permute-start | bytes 196616 | tf_op jit(solution)/shard_map/ppermute | solution.py:242
  25.8 8.9 %collective-permute-start.3 = (bf16[8,8320]{1,0:T(8,128)(2,1)S(1)}, bf16[8,8320]{1,0:T(8,128)(2,1)S(1)}, u32[]{:S(2)}, u32[]{:S(2)}) collective-permute-start(bf16[8,8320]{1,0:T(8,128)(2,1)S(1)} %bitcast.107), channel_id=1, source_target_pairs={{0,16},{4,20},{8,24},{12,28},{16,0},{20,4},{24,8},{28,12},{1,17},{... | collective-permute-start | bytes 399368 | tf_op jit(solution)/shard_map/ppermute | solution.py:151
  34.8 5.1 %collective-permute-start.6 = (bf16[2,4,8320]{2,1,0:T(4,128)(2,1)S(1)}, bf16[2,4,8320]{2,1,0:T(4,128)(2,1)S(1)}, u32[]{:S(2)}, u32[]{:S(2)}) collective-permute-start(bf16[2,4,8320]{2,1,0:T(4,128)(2,1)S(1)} %get-tuple-element.13), channel_id=1, source_target_pairs={{0,4},{4,0},{8,12},{12,8},{16,20},{20,16},{24,28},{28,24},{1,5},{5... | collective-permute-start | bytes 399368 | tf_op jit(solution)/shard_map/ppermute | solution.py:160
  36.1 5.3 %collective-permute-start.4 = (bf16[2,4,8320]{2,1,0:T(4,128)(2,1)S(1)}, bf16[2,4,8320]{2,1,0:T(4,128)(2,1)S(1)}, u32[]{:S(2)}, u32[]{:S(2)}) collective-permute-start(bf16[2,4,8320]{2,1,0:T(4,128)(2,1)S(1)} %get-tuple-element.14), channel_id=1, source_target_pairs={{0,8},{4,12},{8,0},{12,4},{16,24},{20,28},{24,16},{28,20},{1,9},{5... | collective-permute-start | bytes 399368 | tf_op jit(solution)/shard_map/ppermute | solution.py:160
  40.1 6.8 %collective-permute-start.7 = (bf16[2,2,4,8320]{3,2,0,1:T(4,128)(2,1)S(1)}, bf16[2,2,4,8320]{3,2,0,1:T(4,128)(2,1)S(1)}, u32[]{:S(2)}, u32[]{:S(2)}) collective-permute-start(bf16[2,2,4,8320]{3,2,0,1:T(4,128)(2,1)S(1)} %get-tuple-element.12), channel_id=1, source_target_pairs={{0,8},{4,12},{8,0},{12,4},{16,24},{20,28},{24,16},{28,20},{1,9},{5... | collective-permute-start | bytes 798728 | tf_op jit(solution)/shard_map/ppermute | solution.py:160
  41.7 6.5 %collective-permute-start.5 = (bf16[2,2,4,8320]{3,2,0,1:T(4,128)(2,1)S(1)}, bf16[2,2,4,8320]{3,2,0,1:T(4,128)(2,1)S(1)}, u32[]{:S(2)}, u32[]{:S(2)}) collective-permute-start(bf16[2,2,4,8320]{3,2,0,1:T(4,128)(2,1)S(1)} %get-tuple-element.16), channel_id=1, source_target_pairs={{0,4},{4,0},{8,12},{12,8},{16,20},{20,16},{24,28},{28,24},{1,5},{5... | collective-permute-start | bytes 798728 | tf_op jit(solution)/shard_map/ppermute | solution.py:160

commit v8 on v7

--- a/solution.py
+++ b/solution.py
@@ -71,33 +71,43 @@
 def dft_kernel(rec_ref, cos_a_ref, nsin_a_ref, cos_b_ref, sin_b_ref, re_ref, im_ref):
     step = pl.program_id(0)
     lanes = cos_b_ref.shape[0]
-    per_step = rec_ref.shape[1] // lanes
+    group = 8
+    groups = rec_ref.shape[1] // (group * lanes)
 
     @pl.when(step == 0)
     def _():
         re_ref[...] = jnp.zeros_like(re_ref)
         im_ref[...] = jnp.zeros_like(im_ref)
 
-    cos_b = cos_b_ref[...]
-    sin_b = sin_b_ref[...]
-    cos_tiles = []
-    sin_tiles = []
-    for inner in range(per_step):
-        row = step * per_step + inner
-        cos_a = cos_a_ref[pl.ds(row, 1), :]
-        nsin_a = nsin_a_ref[pl.ds(row, 1), :]
-        cos_tiles.append((cos_a * cos_b + nsin_a * sin_b).astype(jnp.bfloat16))
-        sin_tiles.append((nsin_a * cos_b - cos_a * sin_b).astype(jnp.bfloat16))
-    cos_tile = jnp.concatenate(cos_tiles, axis=0)
-    sin_tile = jnp.concatenate(sin_tiles, axis=0)
-    rec = rec_ref[...]
-    re_ref[...] += jnp.dot(rec, cos_tile, preferred_element_type=jnp.float32)
-    im_ref[...] += jnp.dot(rec, sin_tile, preferred_element_type=jnp.float32)
+    def one_group(index, carry):
+        row = pl.multiple_of((step * groups + index) * group, group)
+        cos_a = cos_a_ref[pl.ds(row, group), :]
+        nsin_a = nsin_a_ref[pl.ds(row, group), :]
+        cos_b = cos_b_ref[...]
+        sin_b = sin_b_ref[...]
+        for pair in range(group // 2):
+            cos_parts = []
+            sin_parts = []
+            for half in range(2):
+                at = 2 * pair + half
+                ca = cos_a[at : at + 1]
+                sa = nsin_a[at : at + 1]
+                cos_parts.append(ca * cos_b + sa * sin_b)
+                sin_parts.append(sa * cos_b - ca * sin_b)
+            cos_tile = jnp.concatenate(cos_parts, axis=0).astype(jnp.bfloat16)
+            sin_tile = jnp.concatenate(sin_parts, axis=0).astype(jnp.bfloat16)
+            first = pl.multiple_of((index * group + 2 * pair) * lanes, 2 * lanes)
+            rec = rec_ref[:, pl.ds(first, 2 * lanes)]
+            re_ref[...] += jnp.dot(rec, cos_tile, preferred_element_type=jnp.float32)
+            im_ref[...] += jnp.dot(rec, sin_tile, preferred_element_type=jnp.float32)
+        return carry
+
+    lax.fori_loop(0, groups, one_group, 0)
 
 
 def dft_fused(records, band_index, first_sample):
     lanes = 128
-    chunk = 512
+    chunk = 2048
     count = records.shape[1]
     wavenumber = BAND_LO + band_index
     coarse = first_sample + lanes * jnp.arange(count // lanes, dtype=jnp.int32)

time: 55.5 us -> 49.8 us (0.90)
  Pallas kernels: 12 us -> 6.39 us
    pallas_call x1, Pallas kernels: 12 us -> 6.39 us  [dft_fused(): pl.pallas_call(dft_kernel, grid=(count // chunk,), in_specs=[pl.BlockSpec...]
  transfers between devices with their start and end apart: 8 -> 8, of which waited for: 7 -> 7; matrix products, arithmetic and copies ran while one was open for 5% -> 6% of each run, Pallas kernels for 0% -> 0%
where the time goes in v8:
time: 49.8 us; the launch traced here: 49.6 us
  waiting for transfers between devices  17.6 us (35%)
  starting transfers between devices  10 us (20%)
  Pallas kernels  6.39 us (13%)
  local copies, waits for them, and re-layouts  6.17 us (12%)
  other arithmetic  5.76 us (12%)
  matrix products  3.27 us (7%)
    ppermute x4, waiting for transfers between devices, gather_blocks(): arrived = lax.ppermute(part, 'blk', pairs)  8.8 us
    pallas_call x1, Pallas kernels, dft_fused(): pl.pallas_call(dft_kernel, grid=(count // chunk,), in_specs=[pl.BlockSpec...  6.39 us
    ppermute x1, waiting for transfers between devices, gather_blocks(): held = jnp.stack([carried, lax.ppermute(carried, 'blk', pairs)], axis=0)  5.95 us
    ppermute x4, starting transfers between devices, gather_blocks(): arrived = lax.ppermute(part, 'blk', pairs)  3.26 us
    ppermute x1, starting transfers between devices, gather_blocks(): held = jnp.stack([carried, lax.ppermute(carried, 'blk', pairs)], axis=0)  2.97 us
    ppermute x1, starting transfers between devices, per_device(): pieces.append(lax.ppermute(flat, 'seg', pairs).reshape(outgoing.shape))  2.87 us
    ppermute x1, waiting for transfers between devices, per_device(): pieces.append(lax.ppermute(flat, 'seg', pairs).reshape(outgoing.shape))  2.2 us
    mul x1, other arithmetic, dft_fused(): sin_b = jnp.sin(fine_angle) * norm_scale  1.24 us
  transfers between devices with their start and end apart: 8, of which 7 were waited for; matrix products, arithmetic and copies ran while one was open for 6% of the time, Pallas kernels for 0%

profile of v8, /device:TPU:0, one launch (start us, length us, event | category | flops | bytes accessed | tf_op | source)
XLA Modules:
  0.0 49.6 jit_solution(5460163177138685655)
XLA Ops:
  0.0 1.2 %sine_multiply_fusion = (f32[128,256]{1,0:T(8,128)}, f32[128,256]{1,0:T(8,128)}) fusion(s32[256]{0:T(256)S(1)} %fusion.56), kind=kLoop, calls=%fused_computation.76 | loop fusion | flops 524288 | bytes 263168 | tf_op jit(solution)/shard_map/mul | solution.py:125
  1.3 1.0 %sine_negate_fusion = (f32[64,256]{1,0:T(8,128)}, f32[64,256]{1,0:T(8,128)}) fusion(s32[256]{0:T(256)S(1)} %fusion.56, s32[64]{0:T(128)S(1)} %multiply_add_fusion), kind=kLoop, calls=%fused_computation.105 | loop fusion | flops 245760 | bytes 132352 | tf_op jit(solution)/shard_map/neg | solution.py:123
  2.3 6.4 %shard_map.46 = (f32[256,256]{1,0:T(8,128)}, f32[256,256]{1,0:T(8,128)}) custom-call(bf16[256,8192]{1,0:T(8,128)(2,1)} %bitcast.96, f32[64,256]{1,0:T(8,128)} %get-tuple-element.30.cos_a_ref, f32[64,256]{1,0:T(8,128)} %get-tuple-element.29.nsin_a_ref, f32[128,256]{1,0:T(8,128)} %get-tuple-element.32.cos_b_ref, f32[128,256]{1,0:T(8,128)} %get-tuple-element.31.sin_b_ref), custom_call_target="tpu_custom_call" | custom-call | tf_op jit(solution)/shard_map/pallas_call | solution.py:129
  8.7 1.2 %broadcast_select_fusion = f32[128,2,256]{0,2,1:T(8,128)S(1)} fusion(pred[]{:T(512)S(6)} %eq.47, f32[256,1,256]{0,2,1:T(8,128)} %bitcast.101, f32[256,1,256]{0,2,1:T(8,128)} %bitcast.99), kind=kLoop, calls=%fused_computation.81 | loop fusion | flops 196608 | bytes 786433 | tf_op jit(solution)/shard_map/jit(_where)/select_n | solution.py:204
  9.9 0.5 %collective-permute-start = (f32[128,2,256]{0,2,1:T(8,128)S(1)}, f32[128,2,256]{0,2,1:T(8,128)S(1)}, u32[]{:S(2)}, u32[]{:S(2)}) collective-permute-start(f32[128,2,256]{0,2,1:T(8,128)S(1)} %broadcast_select_fusion), channel_id=1, source_target_pairs={{0,1},{1,0},{2,3},{3,2},{4,5},{5,4},{6,7},{7,6},{8,9},{9,8},{10,11... | collective-permute-start | bytes 786440 | tf_op jit(solution)/shard_map/ppermute | solution.py:24
  10.4 0.1 add_convert_fusion.1
  10.5 0.5 convolution_bitcast_fusion
  11.0 0.5 %convolution_bitcast_fusion.1 = f32[128]{0:T(128)S(1)} fusion(s32[128]{0:T(128)S(1)} %fusion.63, f32[128]{0:T(128)S(1)} %copy-done), kind=kOutput, calls=%fused_computation.7 | convolution fusion | flops 425984 | bytes 1536 | tf_op jit(solution)/shard_map/dot_general | solution.py:66
  11.7 0.1 copy.35
  11.9 0.4 collective-permute-start.1
  12.3 0.1 copy.42
  12.4 0.1 convert_element_type.40
  12.5 0.6 %collective-permute-done.1 = f32[2,2,4,256]{3,2,1,0:T(4,128)S(1)} collective-permute-done((f32[2,2,4,256]{3,2,1,0:T(4,128)S(1)}, f32[2,2,4,256]{3,2,1,0:T(4,128)S(1)}, u32[]{:S(2)}, u32[]{:S(2)}) %collective-permute-start.1) | collective-permute-done | bytes 16416 | tf_op jit(solution)/shard_map/ppermute | solution.py:24
  13.1 0.1 fusion.12
  13.2 0.1 copy.36
  13.4 0.1 stack.82
  13.5 0.1 stack.81
  13.7 0.2 copy.40
  13.9 0.3 reshape.272
  14.2 2.9 %collective-permute-start.2 = (bf16[8,4096]{1,0:T(8,128)(2,1)S(1)}, bf16[8,4096]{1,0:T(8,128)(2,1)S(1)}, u32[]{:S(2)}, u32[]{:S(2)}) collective-permute-start(bf16[8,4096]{1,0:T(8,128)(2,1)S(1)} %reshape.272), channel_id=1, source_target_pairs={{0,2},{2,0},{1,3},{3,1},{4,6},{6,4},{5,7},{7,5},{8,10},{10,8},{9,1... | collective-permute-start | bytes 196616 | tf_op jit(solution)/shard_map/ppermute | solution.py:252
  17.1 0.2 copy.43
  17.3 2.2 %collective-permute-done.2 = bf16[8,4096]{1,0:T(8,128)(2,1)S(1)} collective-permute-done((bf16[8,4096]{1,0:T(8,128)(2,1)S(1)}, bf16[8,4096]{1,0:T(8,128)(2,1)S(1)}, u32[]{:S(2)}, u32[]{:S(2)}) %collective-permute-start.2) | collective-permute-done | bytes 65568 | tf_op jit(solution)/shard_map/ppermute | solution.py:252
  19.5 0.2 stack_reshape.6
  19.7 0.1 copy.41
  19.9 0.1 pad_maximum_fusion.6
  20.1 0.2 copy.44
  20.3 3.0 %collective-permute-start.3 = (bf16[8,8320]{1,0:T(8,128)(2,1)S(1)}, bf16[8,8320]{1,0:T(8,128)(2,1)S(1)}, u32[]{:S(2)}, u32[]{:S(2)}) collective-permute-start(bf16[8,8320]{1,0:T(8,128)(2,1)S(1)} %bitcast.107), channel_id=1, source_target_pairs={{0,16},{4,20},{8,24},{12,28},{16,0},{20,4},{24,8},{28,12},{1,17},{... | collective-permute-start | bytes 399368 | tf_op jit(solution)/shard_map/ppermute | solution.py:161
  23.2 5.9 %collective-permute-done.3 = bf16[8,8320]{1,0:T(8,128)(2,1)S(1)} collective-permute-done((bf16[8,8320]{1,0:T(8,128)(2,1)S(1)}, bf16[8,8320]{1,0:T(8,128)(2,1)S(1)}, u32[]{:S(2)}, u32[]{:S(2)}) %collective-permute-start.3) | collective-permute-done | bytes 133152 | tf_op jit(solution)/shard_map/ppermute | solution.py:161
  29.2 0.1 pad_maximum_fusion.7
  29.3 1.3 %collective-permute-start.6 = (bf16[2,4,8320]{2,1,0:T(4,128)(2,1)S(1)}, bf16[2,4,8320]{2,1,0:T(4,128)(2,1)S(1)}, u32[]{:S(2)}, u32[]{:S(2)}) collective-permute-start(bf16[2,4,8320]{2,1,0:T(4,128)(2,1)S(1)} %get-tuple-element.13), channel_id=1, source_target_pairs={{0,4},{4,0},{8,12},{12,8},{16,20},{20,16},{24,28},{28,24},{1,5},{5... | collective-permute-start | bytes 399368 | tf_op jit(solution)/shard_map/ppermute | solution.py:170
  30.6 0.7 %collective-permute-start.4 = (bf16[2,4,8320]{2,1,0:T(4,128)(2,1)S(1)}, bf16[2,4,8320]{2,1,0:T(4,128)(2,1)S(1)}, u32[]{:S(2)}, u32[]{:S(2)}) collective-permute-start(bf16[2,4,8320]{2,1,0:T(4,128)(2,1)S(1)} %get-tuple-element.14), channel_id=1, source_target_pairs={{0,8},{4,12},{8,0},{12,4},{16,24},{20,28},{24,16},{28,20},{1,9},{5... | collective-permute-start | bytes 399368 | tf_op jit(solution)/shard_map/ppermute | solution.py:170
  31.3 3.0 %collective-permute-done.6 = bf16[2,4,8320]{2,1,0:T(4,128)(2,1)S(1)} collective-permute-done((bf16[2,4,8320]{2,1,0:T(4,128)(2,1)S(1)}, bf16[2,4,8320]{2,1,0:T(4,128)(2,1)S(1)}, u32[]{:S(2)}, u32[]{:S(2)}) %collective-permute-start.6) | collective-permute-done | bytes 133152 | tf_op jit(solution)/shard_map/ppermute | solution.py:170
  34.3 0.2 fusion.71
  34.6 0.4 collective-permute-start.7
  35.0 0.9 %collective-permute-done.4 = bf16[2,4,8320]{2,1,0:T(4,128)(2,1)S(1)} collective-permute-done((bf16[2,4,8320]{2,1,0:T(4,128)(2,1)S(1)}, bf16[2,4,8320]{2,1,0:T(4,128)(2,1)S(1)}, u32[]{:S(2)}, u32[]{:S(2)}) %collective-permute-start.4) | collective-permute-done | bytes 133152 | tf_op jit(solution)/shard_map/ppermute | solution.py:170
  35.9 0.2 fusion.72
  36.1 0.8 %collective-permute-start.5 = (bf16[2,2,4,8320]{3,2,0,1:T(4,128)(2,1)S(1)}, bf16[2,2,4,8320]{3,2,0,1:T(4,128)(2,1)S(1)}, u32[]{:S(2)}, u32[]{:S(2)}) collective-permute-start(bf16[2,2,4,8320]{3,2,0,1:T(4,128)(2,1)S(1)} %get-tuple-element.16), channel_id=1, source_target_pairs={{0,4},{4,0},{8,12},{12,8},{16,20},{20,16},{24,28},{28,24},{1,5},{5... | collective-permute-start | bytes 798728 | tf_op jit(solution)/shard_map/ppermute | solution.py:170
  36.9 4.4 %collective-permute-done.7 = bf16[2,2,4,8320]{3,2,0,1:T(4,128)(2,1)S(1)} collective-permute-done((bf16[2,2,4,8320]{3,2,0,1:T(4,128)(2,1)S(1)}, bf16[2,2,4,8320]{3,2,0,1:T(4,128)(2,1)S(1)}, u32[]{:S(2)}, u32[]{:S(2)}) %collective-permute-start.7) | collective-permute-done | bytes 266272 | tf_op jit(solution)/shard_map/ppermute | solution.py:170
  41.3 0.4 pad_maximum_fusion.1
  41.7 0.2 copy.47
  41.9 0.2 concatenate.49
  42.1 0.5 collective-permute-done.5
  42.6 0.4 pad_maximum_fusion
  43.0 0.2 copy.46
  43.2 0.2 concatenate.48
  43.4 0.2 copy_dynamic-update-slice_fusion.1
  43.6 0.2 copy_dynamic-update-slice_fusion
  43.9 0.1 copy.50
  43.9 0.1 copy.51
  44.0 0.6 %gather_fusion = s32[8,8,4]{1,2,0:T(4,128)S(1)} fusion(s32[8,8,4]{1,2,0:T(4,128)S(1)} %copy.51, s32[1024]{0:T(1024)S(1)} %pad_clamp_fusion), kind=kCustom, calls=%fused_computation | custom fusion | bytes 2080 | tf_op jit(solution)/shard_map/jit(_take)/gather | solution.py:268
  44.6 0.1 broadcast_select_fusion.1
  44.7 0.1 copy.60
  44.8 0.1 add_select_fusion.3
  44.9 0.1 copy.53
  45.0 0.1 eq.48
  45.1 0.1 copy.54
  45.2 0.1 eq.51
  45.4 0.3 fusion
  45.7 0.6 %gather_fusion.1 = bf16[8,128,8]{1,2,0:T(8,128)(2,1)S(1)} fusion(bf16[128,8,8]{0,2,1:T(8,128)(2,1)S(1)} %fusion, s32[1024]{0:T(1024)S(1)} %pad_clamp_fusion), kind=kCustom, calls=%fused_computation.1 | custom fusion | bytes 32800 | tf_op jit(solution)/shard_map/jit(_take)/gather | solution.py:290
  46.2 0.1 select_bitcast_fusion
  46.3 0.8 %bitcast_convert_fusion = bf16[64,128,128]{1,2,0:T(8,128)(2,1)S(1)} fusion(bf16[8,8,65,128]{3,0,1,2:T(8,128)(2,1)S(1)} %copy_dynamic-update-slice_fusion, bf16[128,8,8]{0,2,1:T(8,128)(2,1)S(1)} %select_bitcast_fusion), kind=kOutput, calls=%fused_computation.2 | convolution fusion | flops 135266304 | bytes 3178496 | tf_op jit(solution)/shard_map/rsc,scbq->brq/dot_general | solution.py:291
  47.1 0.1 fusion.73
  47.3 1.2 %convolution_multiply_fusion = f32[64,32,128]{2,1,0:T(8,128)S(1)} fusion(bf16[64,128,128]{1,2,0:T(8,128)(2,1)S(1)} %bitcast_convert_fusion, bf16[64,16,64]{2,1,0:T(8,128)(2,1)S(1)} %get-tuple-element.18, bf16[64,16,64]{2,1,0:T(8,128)(2,1)S(1)} %get-tuple-element.17, bf16[64,16,128]{2,1,0:T(8,128)(2,1)S(1)} %dynamic-slice_bitcast_fusion), kind=kOutput, calls=%fused_computation.3 | convolution fusion | flops 68943872 | bytes 3670016 | tf_op jit(solution)/shard_map/bpq,bjq->bpj/dot_general | solution.py:299
  48.5 1.1 %copy.70 = f32[64,2,16,128]{3,2,0,1:T(8,128)} copy(f32[64,2,16,128]{3,2,1,0:T(8,128)S(1)} %bitcast.97) | data formatting | bytes 2097152 | tf_op jit(solution)/shard_map/div | solution.py:301
  (37 shorter events, 0.5 us)
Async XLA Ops:
  0.0 10.5 %copy-start = (f32[128]{0:T(128)S(1)}, f32[128]{0:T(128)}, u32[]{:S(2)}) copy-start(f32[128]{0:T(128)} %param.5) | copy-start | bytes 1540
  8.7 2.9 %copy-start.3 = (s32[1,8,2]{1,2,0:T(2,128)S(1)}, s32[1,8,2]{1,2,0:T(2,128)}, u32[]{:S(2)}) copy-start(s32[1,8,2]{1,2,0:T(2,128)} %param.7) | copy-start | bytes 196
  8.7 2.9 %copy-start.4 = (s32[1,8,2]{1,2,0:T(2,128)S(1)}, s32[1,8,2]{1,2,0:T(2,128)}, u32[]{:S(2)}) copy-start(s32[1,8,2]{1,2,0:T(2,128)} %param.6) | copy-start | bytes 196
  8.7 2.9 %copy-start.1 = (f32[256,256]{1,0:T(8,128)S(1)}, f32[256,256]{1,0:T(8,128)}, u32[]{:S(2)}) copy-start(f32[256,256]{1,0:T(8,128)} %get-tuple-element.7) | copy-start | bytes 786436
  8.7 2.9 %copy-start.2 = (f32[256,256]{1,0:T(8,128)S(1)}, f32[256,256]{1,0:T(8,128)}, u32[]{:S(2)}) copy-start(f32[256,256]{1,0:T(8,128)} %get-tuple-element.8) | copy-start | bytes 786436
  9.9 1.7 %collective-permute-start = (f32[128,2,256]{0,2,1:T(8,128)S(1)}, f32[128,2,256]{0,2,1:T(8,128)S(1)}, u32[]{:S(2)}, u32[]{:S(2)}) collective-permute-start(f32[128,2,256]{0,2,1:T(8,128)S(1)} %broadcast_select_fusion), channel_id=1, source_target_pairs={{0,1},{1,0},{2,3},{3,2},{4,5},{5,4},{6,7},{7,6},{8,9},{9,8},{10,11... | collective-permute-start | bytes 786440 | tf_op jit(solution)/shard_map/ppermute | solution.py:24
  11.9 1.2 %collective-permute-start.1 = (f32[2,2,4,256]{3,2,1,0:T(4,128)S(1)}, f32[2,2,4,256]{3,2,1,0:T(4,128)S(1)}, u32[]{:S(2)}, u32[]{:S(2)}) collective-permute-start(f32[2,2,4,256]{3,2,1,0:T(4,128)S(1)} %pad_maximum_fusion.10), channel_id=1, source_target_pairs={{0,1},{1,0},{2,3},{3,2},{4,5},{5,4},{6,7},{7,6},{8,9},{9,8},{10,11... | collective-permute-start | bytes 49160 | tf_op jit(solution)/shard_map/ppermute | solution.py:24
  14.2 5.3 %collective-permute-start.2 = (bf16[8,4096]{1,0:T(8,128)(2,1)S(1)}, bf16[8,4096]{1,0:T(8,128)(2,1)S(1)}, u32[]{:S(2)}, u32[]{:S(2)}) collective-permute-start(bf16[8,4096]{1,0:T(8,128)(2,1)S(1)} %reshape.272), channel_id=1, source_target_pairs={{0,2},{2,0},{1,3},{3,1},{4,6},{6,4},{5,7},{7,5},{8,10},{10,8},{9,1... | collective-permute-start | bytes 196616 | tf_op jit(solution)/shard_map/ppermute | solution.py:252
  20.3 8.9 %collective-permute-start.3 = (bf16[8,8320]{1,0:T(8,128)(2,1)S(1)}, bf16[8,8320]{1,0:T(8,128)(2,1)S(1)}, u32[]{:S(2)}, u32[]{:S(2)}) collective-permute-start(bf16[8,8320]{1,0:T(8,128)(2,1)S(1)} %bitcast.107), channel_id=1, source_target_pairs={{0,16},{4,20},{8,24},{12,28},{16,0},{20,4},{24,8},{28,12},{1,17},{... | collective-permute-start | bytes 399368 | tf_op jit(solution)/shard_map/ppermute | solution.py:161
  29.3 5.1 %collective-permute-start.6 = (bf16[2,4,8320]{2,1,0:T(4,128)(2,1)S(1)}, bf16[2,4,8320]{2,1,0:T(4,128)(2,1)S(1)}, u32[]{:S(2)}, u32[]{:S(2)}) collective-permute-start(bf16[2,4,8320]{2,1,0:T(4,128)(2,1)S(1)} %get-tuple-element.13), channel_id=1, source_target_pairs={{0,4},{4,0},{8,12},{12,8},{16,20},{20,16},{24,28},{28,24},{1,5},{5... | collective-permute-start | bytes 399368 | tf_op jit(solution)/shard_map/ppermute | solution.py:170
  30.6 5.3 %collective-permute-start.4 = (bf16[2,4,8320]{2,1,0:T(4,128)(2,1)S(1)}, bf16[2,4,8320]{2,1,0:T(4,128)(2,1)S(1)}, u32[]{:S(2)}, u32[]{:S(2)}) collective-permute-start(bf16[2,4,8320]{2,1,0:T(4,128)(2,1)S(1)} %get-tuple-element.14), channel_id=1, source_target_pairs={{0,8},{4,12},{8,0},{12,4},{16,24},{20,28},{24,16},{28,20},{1,9},{5... | collective-permute-start | bytes 399368 | tf_op jit(solution)/shard_map/ppermute | solution.py:170
  34.6 6.8 %collective-permute-start.7 = (bf16[2,2,4,8320]{3,2,0,1:T(4,128)(2,1)S(1)}, bf16[2,2,4,8320]{3,2,0,1:T(4,128)(2,1)S(1)}, u32[]{:S(2)}, u32[]{:S(2)}) collective-permute-start(bf16[2,2,4,8320]{3,2,0,1:T(4,128)(2,1)S(1)} %get-tuple-element.12), channel_id=1, source_target_pairs={{0,8},{4,12},{8,0},{12,4},{16,24},{20,28},{24,16},{28,20},{1,9},{5... | collective-permute-start | bytes 798728 | tf_op jit(solution)/shard_map/ppermute | solution.py:170
  36.1 6.5 %collective-permute-start.5 = (bf16[2,2,4,8320]{3,2,0,1:T(4,128)(2,1)S(1)}, bf16[2,2,4,8320]{3,2,0,1:T(4,128)(2,1)S(1)}, u32[]{:S(2)}, u32[]{:S(2)}) collective-permute-start(bf16[2,2,4,8320]{3,2,0,1:T(4,128)(2,1)S(1)} %get-tuple-element.16), channel_id=1, source_target_pairs={{0,4},{4,0},{8,12},{12,8},{16,20},{20,16},{24,28},{28,24},{1,5},{5... | collective-permute-start | bytes 798728 | tf_op jit(solution)/shard_map/ppermute | solution.py:170

commit v9 on v8

--- a/solution.py
+++ b/solution.py
@@ -145,7 +145,7 @@
     )(records, cos_a, nsin_a, cos_b, sin_b)
 
 
-def gather_blocks(carried, count, rank):
+def gather_blocks(carried, count, rank, split_halves=True):
     if count & (count - 1) != 0:
         return lax.all_gather(carried, "blk", axis=0, tiled=False)
     masks = []
@@ -159,9 +159,13 @@
     rest = masks[1:]
     pairs = [(source, source ^ first) for source in range(count)]
     held = jnp.stack([carried, lax.ppermute(carried, "blk", pairs)], axis=0)
-    split = (held.shape[1] + 1) // 2
-    halves = [held[:, :split], held[:, split:]]
-    orders = [rest, rest[::-1]]
+    if split_halves:
+        split = (held.shape[1] + 1) // 2
+        halves = [held[:, :split], held[:, split:]]
+        orders = [rest, rest[::-1]]
+    else:
+        halves = [held]
+        orders = [rest]
     results = []
     for part, order in zip(halves, orders):
         done = [first]
@@ -193,6 +197,14 @@
             local_row // block_bins * freq_count + owner_core
         ) * block_bins + local_row % block_bins
 
+    blk_rank = lax.axis_index("blk")
+    table = jnp.concatenate([send_list[0], recv_row[0]], axis=1)
+    table_part = gather_blocks(table, owners_count, blk_rank, split_halves=False)
+    if owners_count & (owners_count - 1) == 0:
+        source_of = blk_rank ^ jnp.arange(owners_count, dtype=jnp.int32)
+        table_part = jnp.take(table_part, source_of, axis=0)
+    send_all = table_part[..., :capacity]
+    recv_all = table_part[..., capacity:]
     band_rows = band_of(jnp.arange(device_bins * freq_count, dtype=jnp.int32))
     real_t, imag_t = dft_fused(records, band_rows, freq_rank * half_len)
     real_all = real_t.T
@@ -253,21 +265,8 @@
     local = jnp.stack(pieces, axis=3).reshape(sections, block_bins, -1)
     all_segs = seg_dev * seg_count
     table_width = local.shape[-1]
-    table = jnp.concatenate([send_list[0], recv_row[0]], axis=1).reshape(-1)
-    table_len = table.shape[0]
-    slab = jnp.pad(table.astype(jnp.bfloat16), (0, sections * table_width - table_len))
-    carried = jnp.concatenate([local, slab.reshape(sections, 1, table_width)], axis=1)
-    blk_rank = lax.axis_index("blk")
-    everything = gather_blocks(carried.reshape(sections, -1), owners_count, blk_rank)
-    everything = everything.reshape(owners_count, sections, block_bins + 1, table_width)
-    gathered = everything[:, :, :block_bins]
-    table_part = everything[:, :, block_bins].reshape(owners_count, -1)[:, :table_len]
-    table_part = table_part.astype(jnp.int32).reshape(owners_count, owners_count, 2 * capacity)
-    if owners_count & (owners_count - 1) == 0:
-        source_of = blk_rank ^ jnp.arange(owners_count, dtype=jnp.int32)
-        table_part = jnp.take(table_part, source_of, axis=0)
-    send_all = table_part[..., :capacity]
-    recv_all = table_part[..., capacity:]
+    everything = gather_blocks(local.reshape(sections, -1), owners_count, blk_rank)
+    gathered = everything.reshape(owners_count, sections, block_bins, table_width)
     rows_count = owners_count * OWN
     chans_count = owners_count * sections
     chosen = jnp.transpose(send_all, (1, 0, 2))
@@ -295,10 +294,9 @@
     own_re = own[..., :all_segs]
     own_im = own[..., all_segs:]
     rotated = jnp.concatenate([own_im, -own_re], axis=-1)
-    lhs = jnp.concatenate([own, rotated], axis=1)
-    cross = jnp.einsum("bpq,bjq->bpj", lhs, routed, preferred_element_type=jnp.float32)
-    cross = cross.reshape(block_bins, 2, OWN, rows_count)
-    return jnp.transpose(cross, (1, 0, 2, 3)) / jnp.float32(all_segs)
+    cross_re = jnp.einsum("biq,bjq->bij", own, routed, preferred_element_type=jnp.float32)
+    cross_im = jnp.einsum("biq,bjq->bij", rotated, routed, preferred_element_type=jnp.float32)
+    return jnp.stack([cross_re, cross_im]) / jnp.float32(all_segs)
 
 
 def solution(mesh):

time: 49.8 us -> 60.7 us (1.22)
  starting transfers between devices: 10 us -> 14 us
  other arithmetic: 5.76 us -> 8.45 us
  waiting for transfers between devices: 17.6 us -> 20.1 us
  matrix products: 3.27 us -> 4.46 us
    ppermute x4 -> x6, starting transfers between devices: 3.26 us -> 8.14 us  [gather_blocks(): arrived = lax.ppermute(part, 'blk', pairs)]
    ppermute x4 -> x6, waiting for transfers between devices: 8.8 us -> 10.9 us  [gather_blocks(): arrived = lax.ppermute(part, 'blk', pairs)]
    ppermute x1, starting transfers between devices: 2.87 us -> 1.56 us  [per_device(): pieces.append(lax.ppermute(flat, 'seg', pairs).reshape(outgoing.shape))]
    dot_general x1 -> x2, matrix products: 1.24 us -> 2.43 us  [the longest x1 1.23 us: per_device(): jnp.einsum('biq,bjq->bij', rotated, routed, preferred_element_type=jnp.fl...]
    ppermute x1 -> x2, starting transfers between devices: 2.97 us -> 4.12 us  [gather_blocks(): held = jnp.stack([carried, lax.ppermute(carried, 'blk', pairs)], axis=0)]
    add x1, other arithmetic: 0.04 us -> 1.16 us  [per_device(): spectra = kept + swapped(sent, 'freq', 0)]
    concatenate x3 -> x4, local copies, waits for them, and re-layouts: 0.66 us -> 1.77 us  [gather_blocks(): return jnp.concatenate(results, axis=1)]
    another operation x1 -> x2, local copies, waits for them, and re-layouts: 0.01 us -> 1.07 us  [the longest x1 0.54 us: per_device(): local.reshape(sections, -1)]
  transfers between devices with their start and end apart: 8 -> 11, of which waited for: 7 -> 8; matrix products, arithmetic and copies ran while one was open for 6% -> 15% of each run, Pallas kernels for 0% -> 11%
where the time goes in v9:
time: 60.7 us; the launch traced here: 60.5 us
  waiting for transfers between devices  20.1 us (33%)
  starting transfers between devices  14 us (23%)
  other arithmetic  8.45 us (14%)
  local copies, waits for them, and re-layouts  6.68 us (11%)
  Pallas kernels  6.39 us (11%)
  matrix products  4.46 us (7%)
    ppermute x6, waiting for transfers between devices, gather_blocks(): arrived = lax.ppermute(part, 'blk', pairs)  10.9 us
    ppermute x6, starting transfers between devices, gather_blocks(): arrived = lax.ppermute(part, 'blk', pairs)  8.14 us
    pallas_call x1, Pallas kernels, dft_fused(): pl.pallas_call(dft_kernel, grid=(count // chunk,), in_specs=[pl.BlockSpec...  6.39 us
    ppermute x2, waiting for transfers between devices, gather_blocks(): held = jnp.stack([carried, lax.ppermute(carried, 'blk', pairs)], axis=0)  6.11 us
    ppermute x2, starting transfers between devices, gather_blocks(): held = jnp.stack([carried, lax.ppermute(carried, 'blk', pairs)], axis=0)  4.12 us
    ppermute x1, waiting for transfers between devices, per_device(): pieces.append(lax.ppermute(flat, 'seg', pairs).reshape(outgoing.shape))  2.6 us
    concatenate x4, local copies, waits for them, and re-layouts, gather_blocks(): return jnp.concatenate(results, axis=1)  1.77 us
    ppermute x1, starting transfers between devices, per_device(): pieces.append(lax.ppermute(flat, 'seg', pairs).reshape(outgoing.shape))  1.56 us
  transfers between devices with their start and end apart: 11, of which 8 were waited for; matrix products, arithmetic and copies ran while one was open for 15% of the time, Pallas kernels for 11%

profile of v9, /device:TPU:0, one launch (start us, length us, event | category | flops | bytes accessed | tf_op | source)
XLA Modules:
  0.0 60.5 jit_solution(5171248933125043067)
XLA Ops:
  0.0 0.7 %fusion.75 = (s32[1,8,4]{1,2,0:T(4,128)S(1)}, s32[8,4]{0,1:T(4,128)S(1)}) fusion(s32[8,2]{0,1:T(2,128)} %bitcast.118, s32[8,2]{0,1:T(2,128)} %bitcast.119), kind=kLoop, calls=%fused_computation.183 | loop fusion | flops 32 | bytes 384 | tf_op jit(solution)/shard_map/stack | solution.py:161
  0.7 4.0 %collective-permute-start.8 = (s32[8,4]{0,1:T(4,128)S(1)}, s32[8,4]{0,1:T(4,128)S(1)}, u32[]{:S(2)}, u32[]{:S(2)}) collective-permute-start(s32[8,4]{0,1:T(4,128)S(1)} %get-tuple-element.32), channel_id=1, source_target_pairs={{0,16},{4,20},{8,24},{12,28},{16,0},{20,4},{24,8},{28,12},{1,17},{... | collective-permute-start | bytes 392 | tf_op jit(solution)/shard_map/ppermute | solution.py:161
  4.8 1.2 %sine_multiply_fusion = (f32[128,256]{1,0:T(8,128)}, f32[128,256]{1,0:T(8,128)}) fusion(s32[256]{0:T(256)S(1)} %fusion.58), kind=kLoop, calls=%fused_computation.76 | loop fusion | flops 524288 | bytes 263168 | tf_op jit(solution)/shard_map/mul | solution.py:125
  6.0 1.0 %sine_negate_fusion = (f32[64,256]{1,0:T(8,128)}, f32[64,256]{1,0:T(8,128)}) fusion(s32[256]{0:T(256)S(1)} %fusion.58, s32[64]{0:T(128)S(1)} %multiply_add_fusion), kind=kLoop, calls=%fused_computation.105 | loop fusion | flops 245760 | bytes 132352 | tf_op jit(solution)/shard_map/neg | solution.py:123
  7.0 6.4 %shard_map.46 = (f32[256,256]{1,0:T(8,128)}, f32[256,256]{1,0:T(8,128)}) custom-call(bf16[256,8192]{1,0:T(8,128)(2,1)} %bitcast.98, f32[64,256]{1,0:T(8,128)} %get-tuple-element.34.cos_a_ref, f32[64,256]{1,0:T(8,128)} %get-tuple-element.33.nsin_a_ref, f32[128,256]{1,0:T(8,128)} %get-tuple-element.36.cos_b_ref, f32[128,256]{1,0:T(8,128)} %get-tuple-element.35.sin_b_ref), custom_call_target="tpu_custom_call" | custom-call | tf_op jit(solution)/shard_map/pallas_call | solution.py:129
  13.4 1.1 %broadcast_select_fusion = f32[128,2,256]{0,2,1:T(8,128)S(1)} fusion(pred[]{:T(512)S(6)} %eq.47, f32[256,1,256]{0,2,1:T(8,128)} %bitcast.101, f32[256,1,256]{0,2,1:T(8,128)} %bitcast.99), kind=kLoop, calls=%fused_computation.81 | loop fusion | flops 196608 | bytes 786433 | tf_op jit(solution)/shard_map/jit(_where)/select_n | solution.py:216
  14.7 0.5 convolution_bitcast_fusion.2
  15.2 0.5 convolution_bitcast_fusion.3
  15.7 0.1 add_convert_fusion.1
  15.9 1.6 %collective-permute-start.9 = (s32[2,8,4]{1,2,0:T(4,128)S(1)}, s32[2,8,4]{1,2,0:T(4,128)S(1)}, u32[]{:S(2)}, u32[]{:S(2)}) collective-permute-start(s32[2,8,4]{1,2,0:T(4,128)S(1)} %get-tuple-element.30), channel_id=1, source_target_pairs={{0,8},{4,12},{8,0},{12,4},{16,24},{20,28},{24,16},{28,20},{1,9},{5... | collective-permute-start | bytes 776 | tf_op jit(solution)/shard_map/ppermute | solution.py:174
  17.5 2.0 %collective-permute-done.9 = s32[2,8,4]{1,2,0:T(4,128)S(1)} collective-permute-done((s32[2,8,4]{1,2,0:T(4,128)S(1)}, s32[2,8,4]{1,2,0:T(4,128)S(1)}, u32[]{:S(2)}, u32[]{:S(2)}) %collective-permute-start.9) | collective-permute-done | bytes 288 | tf_op jit(solution)/shard_map/ppermute | solution.py:174
  19.6 1.5 %collective-permute-start.10 = (s32[2,2,8,4]{2,3,0,1:T(4,128)S(1)}, s32[2,2,8,4]{2,3,0,1:T(4,128)S(1)}, u32[]{:S(2)}, u32[]{:S(2)}) collective-permute-start(s32[2,2,8,4]{2,3,0,1:T(4,128)S(1)} %pad_add_fusion.1), channel_id=1, source_target_pairs={{0,4},{4,0},{8,12},{12,8},{16,20},{20,16},{24,28},{28,24},{1,5},{5... | collective-permute-start | bytes 1544 | tf_op jit(solution)/shard_map/ppermute | solution.py:174
  21.1 2.1 %collective-permute-done.10 = s32[2,2,8,4]{2,3,0,1:T(4,128)S(1)} collective-permute-done((s32[2,2,8,4]{2,3,0,1:T(4,128)S(1)}, s32[2,2,8,4]{2,3,0,1:T(4,128)S(1)}, u32[]{:S(2)}, u32[]{:S(2)}) %collective-permute-start.10) | collective-permute-done | bytes 544 | tf_op jit(solution)/shard_map/ppermute | solution.py:174
  23.2 1.2 %select_add_fusion = f32[128,2,256]{0,2,1:T(8,128)S(1)} fusion(f32[128,2,256]{0,2,1:T(8,128)S(1)} %collective-permute-done, pred[]{:T(512)S(6)} %eq.47, f32[256,1,256]{0,2,1:T(8,128)} %bitcast.102, f32[256,1,256]{0,2,1:T(8,128)} %bitcast.100), kind=kLoop, calls=%fused_computation.34 | loop fusion | flops 262144 | bytes 1048577 | tf_op jit(solution)/shard_map/add | solution.py:217
  24.5 0.1 copy.14
  24.7 0.6 gather_fusion
  25.3 0.5 collective-permute-done.1
  25.8 0.1 fusion.13
  26.0 0.1 copy.15
  26.1 0.1 stack.118
  26.3 0.1 stack.117
  26.5 0.2 copy.19
  26.6 0.3 reshape.255
  26.9 1.6 %collective-permute-start.2 = (bf16[8,4096]{1,0:T(8,128)(2,1)S(1)}, bf16[8,4096]{1,0:T(8,128)(2,1)S(1)}, u32[]{:S(2)}, u32[]{:S(2)}) collective-permute-start(bf16[8,4096]{1,0:T(8,128)(2,1)S(1)} %reshape.255), channel_id=1, source_target_pairs={{0,2},{2,0},{1,3},{3,1},{4,6},{6,4},{5,7},{7,5},{8,10},{10,8},{9,1... | collective-permute-start | bytes 196616 | tf_op jit(solution)/shard_map/ppermute | solution.py:264
  28.5 0.1 broadcast_select_fusion.1
  28.6 0.1 copy.40
  28.7 2.6 %collective-permute-done.2 = bf16[8,4096]{1,0:T(8,128)(2,1)S(1)} collective-permute-done((bf16[8,4096]{1,0:T(8,128)(2,1)S(1)}, bf16[8,4096]{1,0:T(8,128)(2,1)S(1)}, u32[]{:S(2)}, u32[]{:S(2)}) %collective-permute-start.2) | collective-permute-done | bytes 65568 | tf_op jit(solution)/shard_map/ppermute | solution.py:264
  31.3 0.2 stack_reshape.3
  31.4 0.1 copy.20
  31.7 0.4 copy.21
  32.1 0.5 reshape_reshape.3
  32.6 0.1 collective-permute-start.3
  32.7 0.1 add_select_fusion.3
  32.8 0.1 copy.32
  32.9 0.1 eq.48
  33.0 0.1 copy.33
  33.2 0.1 eq.51
  33.3 0.3 fusion
  33.6 0.6 gather_fusion.1
  34.1 0.5 stack_reshape_reshape.3
  34.7 6.1 %collective-permute-done.3 = bf16[8,8192]{1,0:T(8,128)(2,1)S(1)} collective-permute-done((bf16[8,8192]{1,0:T(8,128)(2,1)S(1)}, bf16[8,8192]{1,0:T(8,128)(2,1)S(1)}, u32[]{:S(2)}, u32[]{:S(2)}) %collective-permute-start.3) | collective-permute-done | bytes 131104 | tf_op jit(solution)/shard_map/ppermute | solution.py:161
  40.8 0.1 fusion.28
  41.0 0.1 select_bitcast_fusion
  41.1 1.6 %collective-permute-start.6 = (bf16[2,4,8192]{2,1,0:T(4,128)(2,1)S(1)}, bf16[2,4,8192]{2,1,0:T(4,128)(2,1)S(1)}, u32[]{:S(2)}, u32[]{:S(2)}) collective-permute-start(bf16[2,4,8192]{2,1,0:T(4,128)(2,1)S(1)} %get-tuple-element.16), channel_id=1, source_target_pairs={{0,4},{4,0},{8,12},{12,8},{16,20},{20,16},{24,28},{28,24},{1,5},{5... | collective-permute-start | bytes 393224 | tf_op jit(solution)/shard_map/ppermute | solution.py:174
  42.6 3.3 %collective-permute-done.4 = bf16[2,4,8192]{2,1,0:T(4,128)(2,1)S(1)} collective-permute-done((bf16[2,4,8192]{2,1,0:T(4,128)(2,1)S(1)}, bf16[2,4,8192]{2,1,0:T(4,128)(2,1)S(1)}, u32[]{:S(2)}, u32[]{:S(2)}) %collective-permute-start.4) | collective-permute-done | bytes 131104 | tf_op jit(solution)/shard_map/ppermute | solution.py:174
  45.9 0.2 fusion.78
  46.1 1.8 %collective-permute-start.5 = (bf16[2,2,4,8192]{3,2,0,1:T(4,128)(2,1)S(1)}, bf16[2,2,4,8192]{3,2,0,1:T(4,128)(2,1)S(1)}, u32[]{:S(2)}, u32[]{:S(2)}) collective-permute-start(bf16[2,2,4,8192]{3,2,0,1:T(4,128)(2,1)S(1)} %get-tuple-element.14), channel_id=1, source_target_pairs={{0,4},{4,0},{8,12},{12,8},{16,20},{20,16},{24,28},{28,24},{1,5},{5... | collective-permute-start | bytes 786440 | tf_op jit(solution)/shard_map/ppermute | solution.py:174
  47.9 0.2 fusion.77
  48.1 1.6 %collective-permute-start.7 = (bf16[2,2,4,8192]{3,2,0,1:T(4,128)(2,1)S(1)}, bf16[2,2,4,8192]{3,2,0,1:T(4,128)(2,1)S(1)}, u32[]{:S(2)}, u32[]{:S(2)}) collective-permute-start(bf16[2,2,4,8192]{3,2,0,1:T(4,128)(2,1)S(1)} %get-tuple-element.18), channel_id=1, source_target_pairs={{0,8},{4,12},{8,0},{12,4},{16,24},{20,28},{24,16},{28,20},{1,9},{5... | collective-permute-start | bytes 786440 | tf_op jit(solution)/shard_map/ppermute | solution.py:174
  49.7 2.9 %collective-permute-done.5 = bf16[2,2,4,8192]{3,2,0,1:T(4,128)(2,1)S(1)} collective-permute-done((bf16[2,2,4,8192]{3,2,0,1:T(4,128)(2,1)S(1)}, bf16[2,2,4,8192]{3,2,0,1:T(4,128)(2,1)S(1)}, u32[]{:S(2)}, u32[]{:S(2)}) %collective-permute-start.5) | collective-permute-done | bytes 262176 | tf_op jit(solution)/shard_map/ppermute | solution.py:174
  52.6 0.4 pad_maximum_fusion
  53.0 0.2 copy.23
  53.1 0.5 concatenate.39
  53.7 0.3 copy.25
  54.0 0.5 collective-permute-done.7
  54.6 0.4 pad_maximum_fusion.1
  55.0 0.2 copy.24
  55.1 0.5 concatenate.40
  55.7 0.3 copy.26
  56.0 0.7 %bitcast_convert_fusion = bf16[64,128,128]{1,2,0:T(8,128)(2,1)S(1)} fusion(bf16[8,4,64,128]{3,0,1,2:T(8,128)(2,1)S(1)} %copy.26, bf16[8,4,64,128]{3,0,1,2:T(8,128)(2,1)S(1)} %copy.25, bf16[128,8,8]{0,2,1:T(8,128)(2,1)S(1)} %select_bitcast_fusion), kind=kOutput, calls=%fused_computation.2 | convolution fusion | flops 135790592 | bytes 3162112 | tf_op jit(solution)/shard_map/rsc,scbq->brq/dot_general | solution.py:290
  56.8 1.2 %convolution_bitcast_fusion.1 = f32[1,64,16,128]{3,2,1,0:T(8,128)S(1)} fusion(bf16[64,128,128]{1,2,0:T(8,128)(2,1)S(1)} %bitcast_convert_fusion, s32[]{:T(128)S(6)} %select_n.204), kind=kOutput, calls=%fused_computation.4 | convolution fusion | flops 33554432 | bytes 2883588 | tf_op jit(solution)/shard_map/biq,bjq->bij/dot_general | solution.py:297
  58.0 0.2 fusion.79
  58.2 1.2 %convolution_bitcast_fusion = f32[1,64,16,128]{3,2,1,0:T(8,128)S(1)} fusion(bf16[64,128,128]{1,2,0:T(8,128)(2,1)S(1)} %bitcast_convert_fusion, bf16[64,16,64]{2,1,0:T(8,128)(2,1)S(1)} %get-tuple-element.12, bf16[64,16,64]{2,1,0:T(8,128)(2,1)S(1)} %get-tuple-element.11), kind=kOutput, calls=%fused_computation.3 | convolution fusion | flops 34078720 | bytes 2883584 | tf_op jit(solution)/shard_map/biq,bjq->bij/dot_general | solution.py:298
  59.4 1.1 %maximum_multiply_fusion = f32[2,64,16,128]{3,2,1,0:T(8,128)} fusion(f32[1,64,16,128]{3,2,1,0:T(8,128)S(1)} %convolution_bitcast_fusion, f32[1,64,16,128]{3,2,1,0:T(8,128)S(1)} %convolution_bitcast_fusion.1), kind=kLoop, calls=%fused_computation.12 | loop fusion | flops 524288 | bytes 2097152 | tf_op jit(solution)/shard_map/div | solution.py:299
  (35 shorter events, 0.7 us)
Async XLA Ops:
  0.0 14.7 %copy-start = (f32[128]{0:T(128)S(1)}, f32[128]{0:T(128)}, u32[]{:S(2)}) copy-start(f32[128]{0:T(128)} %param.5) | copy-start | bytes 1540
  0.7 15.2 %collective-permute-start.8 = (s32[8,4]{0,1:T(4,128)S(1)}, s32[8,4]{0,1:T(4,128)S(1)}, u32[]{:S(2)}, u32[]{:S(2)}) collective-permute-start(s32[8,4]{0,1:T(4,128)S(1)} %get-tuple-element.32), channel_id=1, source_target_pairs={{0,16},{4,20},{8,24},{12,28},{16,0},{20,4},{24,8},{28,12},{1,17},{... | collective-permute-start | bytes 392 | tf_op jit(solution)/shard_map/ppermute | solution.py:161
  14.5 8.7 %collective-permute-start = (f32[128,2,256]{0,2,1:T(8,128)S(1)}, f32[128,2,256]{0,2,1:T(8,128)S(1)}, u32[]{:S(2)}, u32[]{:S(2)}) collective-permute-start(f32[128,2,256]{0,2,1:T(8,128)S(1)} %broadcast_select_fusion), channel_id=1, source_target_pairs={{0,1},{1,0},{2,3},{3,2},{4,5},{5,4},{6,7},{7,6},{8,9},{9,8},{10,11... | collective-permute-start | bytes 786440 | tf_op jit(solution)/shard_map/ppermute | solution.py:24
  15.9 3.7 %collective-permute-start.9 = (s32[2,8,4]{1,2,0:T(4,128)S(1)}, s32[2,8,4]{1,2,0:T(4,128)S(1)}, u32[]{:S(2)}, u32[]{:S(2)}) collective-permute-start(s32[2,8,4]{1,2,0:T(4,128)S(1)} %get-tuple-element.30), channel_id=1, source_target_pairs={{0,8},{4,12},{8,0},{12,4},{16,24},{20,28},{24,16},{28,20},{1,9},{5... | collective-permute-start | bytes 776 | tf_op jit(solution)/shard_map/ppermute | solution.py:174
  19.6 3.7 %collective-permute-start.10 = (s32[2,2,8,4]{2,3,0,1:T(4,128)S(1)}, s32[2,2,8,4]{2,3,0,1:T(4,128)S(1)}, u32[]{:S(2)}, u32[]{:S(2)}) collective-permute-start(s32[2,2,8,4]{2,3,0,1:T(4,128)S(1)} %pad_add_fusion.1), channel_id=1, source_target_pairs={{0,4},{4,0},{8,12},{12,8},{16,20},{20,16},{24,28},{28,24},{1,5},{5... | collective-permute-start | bytes 1544 | tf_op jit(solution)/shard_map/ppermute | solution.py:174
  24.6 1.2 %collective-permute-start.1 = (f32[2,2,4,256]{3,2,1,0:T(4,128)S(1)}, f32[2,2,4,256]{3,2,1,0:T(4,128)S(1)}, u32[]{:S(2)}, u32[]{:S(2)}) collective-permute-start(f32[2,2,4,256]{3,2,1,0:T(4,128)S(1)} %pad_maximum_fusion.9), channel_id=1, source_target_pairs={{0,1},{1,0},{2,3},{3,2},{4,5},{5,4},{6,7},{7,6},{8,9},{9,8},{10,11... | collective-permute-start | bytes 49160 | tf_op jit(solution)/shard_map/ppermute | solution.py:24
  26.9 4.3 %collective-permute-start.2 = (bf16[8,4096]{1,0:T(8,128)(2,1)S(1)}, bf16[8,4096]{1,0:T(8,128)(2,1)S(1)}, u32[]{:S(2)}, u32[]{:S(2)}) collective-permute-start(bf16[8,4096]{1,0:T(8,128)(2,1)S(1)} %reshape.255), channel_id=1, source_target_pairs={{0,2},{2,0},{1,3},{3,1},{4,6},{6,4},{5,7},{7,5},{8,10},{10,8},{9,1... | collective-permute-start | bytes 196616 | tf_op jit(solution)/shard_map/ppermute | solution.py:264
  32.6 8.2 %collective-permute-start.3 = (bf16[8,8192]{1,0:T(8,128)(2,1)S(1)}, bf16[8,8192]{1,0:T(8,128)(2,1)S(1)}, u32[]{:S(2)}, u32[]{:S(2)}) collective-permute-start(bf16[8,8192]{1,0:T(8,128)(2,1)S(1)} %reshape_reshape.3), channel_id=1, source_target_pairs={{0,16},{4,20},{8,24},{12,28},{16,0},{20,4},{24,8},{28,12},{1,17},{... | collective-permute-start | bytes 393224 | tf_op jit(solution)/shard_map/ppermute | solution.py:161
  40.9 5.0 %collective-permute-start.4 = (bf16[2,4,8192]{2,1,0:T(4,128)(2,1)S(1)}, bf16[2,4,8192]{2,1,0:T(4,128)(2,1)S(1)}, u32[]{:S(2)}, u32[]{:S(2)}) collective-permute-start(bf16[2,4,8192]{2,1,0:T(4,128)(2,1)S(1)} %get-tuple-element.15), channel_id=1, source_target_pairs={{0,8},{4,12},{8,0},{12,4},{16,24},{20,28},{24,16},{28,20},{1,9},{5... | collective-permute-start | bytes 393224 | tf_op jit(solution)/shard_map/ppermute | solution.py:174
  41.1 6.9 %collective-permute-start.6 = (bf16[2,4,8192]{2,1,0:T(4,128)(2,1)S(1)}, bf16[2,4,8192]{2,1,0:T(4,128)(2,1)S(1)}, u32[]{:S(2)}, u32[]{:S(2)}) collective-permute-start(bf16[2,4,8192]{2,1,0:T(4,128)(2,1)S(1)} %get-tuple-element.16), channel_id=1, source_target_pairs={{0,4},{4,0},{8,12},{12,8},{16,20},{20,16},{24,28},{28,24},{1,5},{5... | collective-permute-start | bytes 393224 | tf_op jit(solution)/shard_map/ppermute | solution.py:174
  46.1 6.4 %collective-permute-start.5 = (bf16[2,2,4,8192]{3,2,0,1:T(4,128)(2,1)S(1)}, bf16[2,2,4,8192]{3,2,0,1:T(4,128)(2,1)S(1)}, u32[]{:S(2)}, u32[]{:S(2)}) collective-permute-start(bf16[2,2,4,8192]{3,2,0,1:T(4,128)(2,1)S(1)} %get-tuple-element.14), channel_id=1, source_target_pairs={{0,4},{4,0},{8,12},{12,8},{16,20},{20,16},{24,28},{28,24},{1,5},{5... | collective-permute-start | bytes 786440 | tf_op jit(solution)/shard_map/ppermute | solution.py:174
  48.1 6.4 %collective-permute-start.7 = (bf16[2,2,4,8192]{3,2,0,1:T(4,128)(2,1)S(1)}, bf16[2,2,4,8192]{3,2,0,1:T(4,128)(2,1)S(1)}, u32[]{:S(2)}, u32[]{:S(2)}) collective-permute-start(bf16[2,2,4,8192]{3,2,0,1:T(4,128)(2,1)S(1)} %get-tuple-element.18), channel_id=1, source_target_pairs={{0,8},{4,12},{8,0},{12,4},{16,24},{20,28},{24,16},{28,20},{1,9},{5... | collective-permute-start | bytes 786440 | tf_op jit(solution)/shard_map/ppermute | solution.py:174

commit v10 on v8

--- a/solution.py
+++ b/solution.py
@@ -110,19 +110,35 @@
     chunk = 2048
     count = records.shape[1]
     wavenumber = BAND_LO + band_index
-    coarse = first_sample + lanes * jnp.arange(count // lanes, dtype=jnp.int32)
-    fine = jnp.arange(lanes, dtype=jnp.int32)
-    coarse_angle = (coarse[:, None] * wavenumber[None, :] % SEG_LEN).astype(jnp.float32) * (
-        TWO_PI / SEG_LEN
-    )
-    fine_angle = (fine[:, None] * wavenumber[None, :] % SEG_LEN).astype(jnp.float32) * (
-        TWO_PI / SEG_LEN
-    )
     norm_scale = 1.0 / math.sqrt(SEG_LEN)
-    cos_a = jnp.cos(coarse_angle)
-    nsin_a = -jnp.sin(coarse_angle)
-    cos_b = jnp.cos(fine_angle) * norm_scale
-    sin_b = jnp.sin(fine_angle) * norm_scale
+
+    def cos_sin(steps):
+        angle = (steps[:, None] * wavenumber[None, :] % SEG_LEN).astype(jnp.float32) * (
+            TWO_PI / SEG_LEN
+        )
+        return jnp.cos(angle), jnp.sin(angle)
+
+    def combined(outer_steps, inner_steps):
+        outer_cos, outer_sin = cos_sin(outer_steps)
+        inner_cos, inner_sin = cos_sin(inner_steps)
+        width = wavenumber.shape[0]
+        cos_sum = outer_cos[:, None] * inner_cos[None] - outer_sin[:, None] * inner_sin[None]
+        sin_sum = outer_sin[:, None] * inner_cos[None] + outer_cos[:, None] * inner_sin[None]
+        return cos_sum.reshape(-1, width), sin_sum.reshape(-1, width)
+
+    coarse_count = count // lanes
+    coarse_outer = coarse_count // 8 if coarse_count % 8 == 0 else 1
+    coarse_inner = coarse_count // coarse_outer
+    cos_a, sin_a = combined(
+        first_sample + lanes * coarse_inner * jnp.arange(coarse_outer, dtype=jnp.int32),
+        lanes * jnp.arange(coarse_inner, dtype=jnp.int32),
+    )
+    nsin_a = -sin_a
+    cos_b, sin_b = combined(
+        16 * jnp.arange(lanes // 16, dtype=jnp.int32), jnp.arange(16, dtype=jnp.int32)
+    )
+    cos_b = cos_b * norm_scale
+    sin_b = sin_b * norm_scale
     rows = records.shape[0]
     bins = band_index.shape[0]
     full = lambda step: (0, 0)
@@ -263,16 +279,20 @@
     gathered = everything[:, :, :block_bins]
     table_part = everything[:, :, block_bins].reshape(owners_count, -1)[:, :table_len]
     table_part = table_part.astype(jnp.int32).reshape(owners_count, owners_count, 2 * capacity)
+    position_ids = jnp.arange(owners_count, dtype=jnp.int32)
     if owners_count & (owners_count - 1) == 0:
-        source_of = blk_rank ^ jnp.arange(owners_count, dtype=jnp.int32)
-        table_part = jnp.take(table_part, source_of, axis=0)
+        source_of = blk_rank ^ position_ids
+        unpermute = (source_of[:, None] == position_ids[None, :]).astype(jnp.int32)
+        table_part = jnp.sum(unpermute[:, :, None, None] * table_part[None], axis=1)
+    else:
+        source_of = position_ids
     send_all = table_part[..., :capacity]
     recv_all = table_part[..., capacity:]
     rows_count = owners_count * OWN
     chans_count = owners_count * sections
     chosen = jnp.transpose(send_all, (1, 0, 2))
     valid = (chosen < sections) & (recv_all < OWN)
-    source_ids = jnp.arange(owners_count, dtype=jnp.int32)[None, :, None]
+    source_ids = (blk_rank ^ position_ids if owners_count & (owners_count - 1) == 0 else position_ids)[None, :, None]
     owner_ids = jnp.arange(owners_count, dtype=jnp.int32)[:, None, None]
     channel = jnp.where(valid, source_ids * sections + chosen, -1).reshape(-1)
     target = jnp.where(valid, owner_ids * OWN + recv_all, -1).reshape(-1)
@@ -286,8 +306,6 @@
         "er,ec->rc", row_hot, chan_hot, preferred_element_type=jnp.float32
     ).astype(jnp.bfloat16)
     selector = selector.reshape(rows_count, owners_count, sections)
-    if owners_count & (owners_count - 1) == 0:
-        selector = jnp.take(selector, source_of, axis=1)
     routed = jnp.einsum(
         "rsc,scbq->brq", selector, gathered, preferred_element_type=jnp.float32
     ).astype(jnp.bfloat16)

time: 49.8 us -> 48.1 us (0.966)
  local copies, waits for them, and re-layouts: 6.17 us -> 5.02 us
  other arithmetic: 5.76 us -> 5.22 us
    gather x2 -> x0, local copies, waits for them, and re-layouts: 1.14 us -> none  [the longest x1 0.58 us: per_device(): table_part = jnp.take(table_part, source_of, axis=0)]
    mul x2 -> x3, other arithmetic: 1.24 us -> 0.74 us  [the longest x1 0.73 us: dft_fused(): sin_b = sin_b * norm_scale]
where the time goes in v10:
time: 48.1 us; the launch traced here: 47.9 us
  waiting for transfers between devices  17.6 us (37%)
  starting transfers between devices  9.94 us (21%)
  Pallas kernels  6.41 us (13%)
  other arithmetic  5.22 us (11%)
  local copies, waits for them, and re-layouts  5.02 us (10%)
  matrix products  3.27 us (7%)
    ppermute x4, waiting for transfers between devices, gather_blocks(): arrived = lax.ppermute(part, 'blk', pairs)  8.81 us
    pallas_call x1, Pallas kernels, dft_fused(): pl.pallas_call(dft_kernel, grid=(count // chunk,), in_specs=[pl.BlockSpec...  6.41 us
    ppermute x1, waiting for transfers between devices, gather_blocks(): held = jnp.stack([carried, lax.ppermute(carried, 'blk', pairs)], axis=0)  5.95 us
    ppermute x4, starting transfers between devices, gather_blocks(): arrived = lax.ppermute(part, 'blk', pairs)  3.19 us
    ppermute x1, starting transfers between devices, gather_blocks(): held = jnp.stack([carried, lax.ppermute(carried, 'blk', pairs)], axis=0)  2.97 us
    ppermute x1, starting transfers between devices, per_device(): pieces.append(lax.ppermute(flat, 'seg', pairs).reshape(outgoing.shape))  2.87 us
    ppermute x1, waiting for transfers between devices, per_device(): pieces.append(lax.ppermute(flat, 'seg', pairs).reshape(outgoing.shape))  2.2 us
    dot_general x1, matrix products, per_device(): jnp.einsum('bpq,bjq->bpj', lhs, routed, preferred_element_type=jnp.float32)  1.24 us
  transfers between devices with their start and end apart: 8, of which 7 were waited for; matrix products, arithmetic and copies ran while one was open for 6% of the time, Pallas kernels for 0%

profile of v10, /device:TPU:0, one launch (start us, length us, event | category | flops | bytes accessed | tf_op | source)
XLA Modules:
  0.0 47.9 jit_solution(14944228993575452392)
XLA Ops:
  0.0 0.1 fusion.57
  0.1 0.2 fusion.59
  0.3 0.7 %negate_bitcast_fusion = (f32[64,256]{1,0:T(8,128)}, f32[64,256]{1,0:T(8,128)}) fusion(f32[8,256]{1,0:T(8,128)S(1)} %get-tuple-element.39, f32[8,256]{1,0:T(8,128)S(1)} %get-tuple-element.41, f32[8,256]{1,0:T(8,128)S(1)} %get-tuple-element.40, f32[8,256]{1,0:T(8,128)S(1)} %get-tuple-element.42), kind=kLoop, calls=%fused_computation.87 | loop fusion | flops 114688 | bytes 163840 | tf_op jit(solution)/shard_map/neg | solution.py:136
  1.0 0.7 %add_multiply_fusion = (f32[8,16,256]{2,1,0:T(8,128)}, f32[8,16,256]{2,1,0:T(8,128)}) fusion(f32[16,256]{1,0:T(8,128)S(1)} %get-tuple-element.44, f32[8,256]{1,0:T(8,128)S(1)} %get-tuple-element.34, f32[16,256]{1,0:T(8,128)S(1)} %get-tuple-element.43, f32[8,256]{1,0:T(8,128)S(1)} %get-tuple-element.33), kind=kLoop, calls=%fused_computation.69 | loop fusion | flops 262144 | bytes 311296 | tf_op jit(solution)/shard_map/mul | solution.py:141
  1.7 6.4 %shard_map.46 = (f32[256,256]{1,0:T(8,128)}, f32[256,256]{1,0:T(8,128)}) custom-call(bf16[256,8192]{1,0:T(8,128)(2,1)} %bitcast.98, f32[64,256]{1,0:T(8,128)} %get-tuple-element.26.cos_a_ref, f32[64,256]{1,0:T(8,128)} %get-tuple-element.25.nsin_a_ref, f32[128,256]{1,0:T(8,128)} %bitcast.112, f32[128,256]{1,0:T(8,128)} %bitcast.111), custom_call_target="tpu_custom_call" | custom-call | tf_op jit(solution)/shard_map/pallas_call | solution.py:145
  8.2 1.2 %broadcast_select_fusion = f32[128,2,256]{0,2,1:T(8,128)S(1)} fusion(pred[]{:T(512)S(6)} %eq.66, f32[256,1,256]{0,2,1:T(8,128)} %bitcast.103, f32[256,1,256]{0,2,1:T(8,128)} %bitcast.101), kind=kLoop, calls=%fused_computation.71 | loop fusion | flops 196608 | bytes 786433 | tf_op jit(solution)/shard_map/jit(_where)/select_n | solution.py:220
  9.4 0.5 %collective-permute-start = (f32[128,2,256]{0,2,1:T(8,128)S(1)}, f32[128,2,256]{0,2,1:T(8,128)S(1)}, u32[]{:S(2)}, u32[]{:S(2)}) collective-permute-start(f32[128,2,256]{0,2,1:T(8,128)S(1)} %broadcast_select_fusion), channel_id=1, source_target_pairs={{0,1},{1,0},{2,3},{3,2},{4,5},{5,4},{6,7},{7,6},{8,9},{9,8},{10,11... | collective-permute-start | bytes 786440 | tf_op jit(solution)/shard_map/ppermute | solution.py:24
  9.9 0.1 add_convert_fusion.1
  10.0 0.5 %convolution_bitcast_fusion = f32[128]{0:T(128)S(1)} fusion(s32[128]{0:T(128)S(1)} %fusion.76, f32[128]{0:T(128)S(1)} %copy-done), kind=kOutput, calls=%fused_computation.4 | convolution fusion | flops 442368 | bytes 1536 | tf_op jit(solution)/shard_map/dot_general | solution.py:67
  10.5 0.5 %convolution_bitcast_fusion.1 = f32[128]{0:T(128)S(1)} fusion(s32[128]{0:T(128)S(1)} %fusion.76, f32[128]{0:T(128)S(1)} %copy-done), kind=kOutput, calls=%fused_computation.5 | convolution fusion | flops 425984 | bytes 1536 | tf_op jit(solution)/shard_map/dot_general | solution.py:66
  11.2 0.1 copy.55
  11.3 0.4 collective-permute-start.1
  11.7 0.1 copy.62
  11.8 0.1 convert_element_type.91
  11.9 0.7 %collective-permute-done.1 = f32[2,2,4,256]{3,2,1,0:T(4,128)S(1)} collective-permute-done((f32[2,2,4,256]{3,2,1,0:T(4,128)S(1)}, f32[2,2,4,256]{3,2,1,0:T(4,128)S(1)}, u32[]{:S(2)}, u32[]{:S(2)}) %collective-permute-start.1) | collective-permute-done | bytes 16416 | tf_op jit(solution)/shard_map/ppermute | solution.py:24
  12.6 0.1 fusion.12
  12.7 0.1 copy.56
  12.9 0.1 stack.82
  13.0 0.1 stack.81
  13.2 0.2 copy.60
  13.4 0.3 reshape.558
  13.7 2.9 %collective-permute-start.2 = (bf16[8,4096]{1,0:T(8,128)(2,1)S(1)}, bf16[8,4096]{1,0:T(8,128)(2,1)S(1)}, u32[]{:S(2)}, u32[]{:S(2)}) collective-permute-start(bf16[8,4096]{1,0:T(8,128)(2,1)S(1)} %reshape.558), channel_id=1, source_target_pairs={{0,2},{2,0},{1,3},{3,1},{4,6},{6,4},{5,7},{7,5},{8,10},{10,8},{9,1... | collective-permute-start | bytes 196616 | tf_op jit(solution)/shard_map/ppermute | solution.py:268
  16.5 0.2 copy.63
  16.8 2.2 %collective-permute-done.2 = bf16[8,4096]{1,0:T(8,128)(2,1)S(1)} collective-permute-done((bf16[8,4096]{1,0:T(8,128)(2,1)S(1)}, bf16[8,4096]{1,0:T(8,128)(2,1)S(1)}, u32[]{:S(2)}, u32[]{:S(2)}) %collective-permute-start.2) | collective-permute-done | bytes 65568 | tf_op jit(solution)/shard_map/ppermute | solution.py:268
  19.0 0.2 stack_reshape.6
  19.2 0.1 copy.61
  19.4 0.1 pad_maximum_fusion.6
  19.5 0.2 copy.64
  19.7 3.0 %collective-permute-start.3 = (bf16[8,8320]{1,0:T(8,128)(2,1)S(1)}, bf16[8,8320]{1,0:T(8,128)(2,1)S(1)}, u32[]{:S(2)}, u32[]{:S(2)}) collective-permute-start(bf16[8,8320]{1,0:T(8,128)(2,1)S(1)} %bitcast.109), channel_id=1, source_target_pairs={{0,16},{4,20},{8,24},{12,28},{16,0},{20,4},{24,8},{28,12},{1,17},{... | collective-permute-start | bytes 399368 | tf_op jit(solution)/shard_map/ppermute | solution.py:177
  22.7 6.0 %collective-permute-done.3 = bf16[8,8320]{1,0:T(8,128)(2,1)S(1)} collective-permute-done((bf16[8,8320]{1,0:T(8,128)(2,1)S(1)}, bf16[8,8320]{1,0:T(8,128)(2,1)S(1)}, u32[]{:S(2)}, u32[]{:S(2)}) %collective-permute-start.3) | collective-permute-done | bytes 133152 | tf_op jit(solution)/shard_map/ppermute | solution.py:177
  28.7 0.1 pad_maximum_fusion.7
  28.8 1.3 %collective-permute-start.6 = (bf16[2,4,8320]{2,1,0:T(4,128)(2,1)S(1)}, bf16[2,4,8320]{2,1,0:T(4,128)(2,1)S(1)}, u32[]{:S(2)}, u32[]{:S(2)}) collective-permute-start(bf16[2,4,8320]{2,1,0:T(4,128)(2,1)S(1)} %get-tuple-element.13), channel_id=1, source_target_pairs={{0,4},{4,0},{8,12},{12,8},{16,20},{20,16},{24,28},{28,24},{1,5},{5... | collective-permute-start | bytes 399368 | tf_op jit(solution)/shard_map/ppermute | solution.py:186
  30.0 0.1 fusion.64
  30.1 0.7 %collective-permute-start.4 = (bf16[2,4,8320]{2,1,0:T(4,128)(2,1)S(1)}, bf16[2,4,8320]{2,1,0:T(4,128)(2,1)S(1)}, u32[]{:S(2)}, u32[]{:S(2)}) collective-permute-start(bf16[2,4,8320]{2,1,0:T(4,128)(2,1)S(1)} %get-tuple-element.14), channel_id=1, source_target_pairs={{0,8},{4,12},{8,0},{12,4},{16,24},{20,28},{24,16},{28,20},{1,9},{5... | collective-permute-start | bytes 399368 | tf_op jit(solution)/shard_map/ppermute | solution.py:186
  30.8 3.0 %collective-permute-done.6 = bf16[2,4,8320]{2,1,0:T(4,128)(2,1)S(1)} collective-permute-done((bf16[2,4,8320]{2,1,0:T(4,128)(2,1)S(1)}, bf16[2,4,8320]{2,1,0:T(4,128)(2,1)S(1)}, u32[]{:S(2)}, u32[]{:S(2)}) %collective-permute-start.6) | collective-permute-done | bytes 133152 | tf_op jit(solution)/shard_map/ppermute | solution.py:186
  33.8 0.2 fusion.84
  34.0 0.4 collective-permute-start.7
  34.4 0.9 %collective-permute-done.4 = bf16[2,4,8320]{2,1,0:T(4,128)(2,1)S(1)} collective-permute-done((bf16[2,4,8320]{2,1,0:T(4,128)(2,1)S(1)}, bf16[2,4,8320]{2,1,0:T(4,128)(2,1)S(1)}, u32[]{:S(2)}, u32[]{:S(2)}) %collective-permute-start.4) | collective-permute-done | bytes 133152 | tf_op jit(solution)/shard_map/ppermute | solution.py:186
  35.4 0.2 fusion.85
  35.6 0.8 %collective-permute-start.5 = (bf16[2,2,4,8320]{3,2,0,1:T(4,128)(2,1)S(1)}, bf16[2,2,4,8320]{3,2,0,1:T(4,128)(2,1)S(1)}, u32[]{:S(2)}, u32[]{:S(2)}) collective-permute-start(bf16[2,2,4,8320]{3,2,0,1:T(4,128)(2,1)S(1)} %get-tuple-element.16), channel_id=1, source_target_pairs={{0,4},{4,0},{8,12},{12,8},{16,20},{20,16},{24,28},{28,24},{1,5},{5... | collective-permute-start | bytes 798728 | tf_op jit(solution)/shard_map/ppermute | solution.py:186
  36.4 4.4 %collective-permute-done.7 = bf16[2,2,4,8320]{3,2,0,1:T(4,128)(2,1)S(1)} collective-permute-done((bf16[2,2,4,8320]{3,2,0,1:T(4,128)(2,1)S(1)}, bf16[2,2,4,8320]{3,2,0,1:T(4,128)(2,1)S(1)}, u32[]{:S(2)}, u32[]{:S(2)}) %collective-permute-start.7) | collective-permute-done | bytes 266272 | tf_op jit(solution)/shard_map/ppermute | solution.py:186
  40.8 0.4 pad_maximum_fusion.1
  41.2 0.2 copy.67
  41.4 0.2 concatenate.49
  41.6 0.5 collective-permute-done.5
  42.1 0.4 pad_maximum_fusion
  42.4 0.2 copy.66
  42.6 0.2 concatenate.48
  42.8 0.2 copy_dynamic-update-slice_fusion.1
  43.1 0.2 copy_dynamic-update-slice_fusion
  43.3 0.1 copy.70
  43.4 0.1 copy.71
  43.5 0.1 multiply_reduce_fusion
  43.6 0.1 copy.80
  43.7 0.1 add_select_fusion.5
  43.8 0.1 copy.73
  43.9 0.1 eq.70
  44.1 0.1 copy.74
  44.2 0.1 eq.73
  44.3 0.3 fusion
  44.6 0.8 %bitcast_convert_fusion = bf16[64,128,128]{1,2,0:T(8,128)(2,1)S(1)} fusion(bf16[8,8,65,128]{3,0,1,2:T(8,128)(2,1)S(1)} %copy_dynamic-update-slice_fusion, bf16[128,8,8]{0,2,1:T(8,128)(2,1)S(1)} %fusion), kind=kOutput, calls=%fused_computation | convolution fusion | flops 135266304 | bytes 3178496 | tf_op jit(solution)/shard_map/rsc,scbq->brq/dot_general | solution.py:309
  45.4 0.1 fusion.86
  45.6 1.2 %convolution_multiply_fusion = f32[64,32,128]{2,1,0:T(8,128)S(1)} fusion(bf16[64,128,128]{1,2,0:T(8,128)(2,1)S(1)} %bitcast_convert_fusion, bf16[64,16,64]{2,1,0:T(8,128)(2,1)S(1)} %get-tuple-element.18, bf16[64,16,64]{2,1,0:T(8,128)(2,1)S(1)} %get-tuple-element.17, bf16[64,16,128]{2,1,0:T(8,128)(2,1)S(1)} %dynamic-slice_bitcast_fusion), kind=kOutput, calls=%fused_computation.1 | convolution fusion | flops 68943872 | bytes 3670016 | tf_op jit(solution)/shard_map/bpq,bjq->bpj/dot_general | solution.py:317
  46.8 1.1 %copy.90 = f32[64,2,16,128]{3,2,0,1:T(8,128)} copy(f32[64,2,16,128]{3,2,1,0:T(8,128)S(1)} %bitcast.99) | data formatting | bytes 2097152 | tf_op jit(solution)/shard_map/div | solution.py:319
  (35 shorter events, 0.5 us)
Async XLA Ops:
  0.0 10.0 %copy-start = (f32[128]{0:T(128)S(1)}, f32[128]{0:T(128)}, u32[]{:S(2)}) copy-start(f32[128]{0:T(128)} %param.5) | copy-start | bytes 1540
  8.1 2.8 %copy-start.3 = (s32[1,8,2]{1,2,0:T(2,128)S(1)}, s32[1,8,2]{1,2,0:T(2,128)}, u32[]{:S(2)}) copy-start(s32[1,8,2]{1,2,0:T(2,128)} %param.7) | copy-start | bytes 196
  8.1 2.9 %copy-start.4 = (s32[1,8,2]{1,2,0:T(2,128)S(1)}, s32[1,8,2]{1,2,0:T(2,128)}, u32[]{:S(2)}) copy-start(s32[1,8,2]{1,2,0:T(2,128)} %param.6) | copy-start | bytes 196
  8.1 2.9 %copy-start.1 = (f32[256,256]{1,0:T(8,128)S(1)}, f32[256,256]{1,0:T(8,128)}, u32[]{:S(2)}) copy-start(f32[256,256]{1,0:T(8,128)} %get-tuple-element.7) | copy-start | bytes 786436
  8.2 2.9 %copy-start.2 = (f32[256,256]{1,0:T(8,128)S(1)}, f32[256,256]{1,0:T(8,128)}, u32[]{:S(2)}) copy-start(f32[256,256]{1,0:T(8,128)} %get-tuple-element.8) | copy-start | bytes 786436
  9.4 1.7 %collective-permute-start = (f32[128,2,256]{0,2,1:T(8,128)S(1)}, f32[128,2,256]{0,2,1:T(8,128)S(1)}, u32[]{:S(2)}, u32[]{:S(2)}) collective-permute-start(f32[128,2,256]{0,2,1:T(8,128)S(1)} %broadcast_select_fusion), channel_id=1, source_target_pairs={{0,1},{1,0},{2,3},{3,2},{4,5},{5,4},{6,7},{7,6},{8,9},{9,8},{10,11... | collective-permute-start | bytes 786440 | tf_op jit(solution)/shard_map/ppermute | solution.py:24
  11.3 1.2 %collective-permute-start.1 = (f32[2,2,4,256]{3,2,1,0:T(4,128)S(1)}, f32[2,2,4,256]{3,2,1,0:T(4,128)S(1)}, u32[]{:S(2)}, u32[]{:S(2)}) collective-permute-start(f32[2,2,4,256]{3,2,1,0:T(4,128)S(1)} %pad_maximum_fusion.10), channel_id=1, source_target_pairs={{0,1},{1,0},{2,3},{3,2},{4,5},{5,4},{6,7},{7,6},{8,9},{9,8},{10,11... | collective-permute-start | bytes 49160 | tf_op jit(solution)/shard_map/ppermute | solution.py:24
  13.7 5.3 %collective-permute-start.2 = (bf16[8,4096]{1,0:T(8,128)(2,1)S(1)}, bf16[8,4096]{1,0:T(8,128)(2,1)S(1)}, u32[]{:S(2)}, u32[]{:S(2)}) collective-permute-start(bf16[8,4096]{1,0:T(8,128)(2,1)S(1)} %reshape.558), channel_id=1, source_target_pairs={{0,2},{2,0},{1,3},{3,1},{4,6},{6,4},{5,7},{7,5},{8,10},{10,8},{9,1... | collective-permute-start | bytes 196616 | tf_op jit(solution)/shard_map/ppermute | solution.py:268
  19.7 8.9 %collective-permute-start.3 = (bf16[8,8320]{1,0:T(8,128)(2,1)S(1)}, bf16[8,8320]{1,0:T(8,128)(2,1)S(1)}, u32[]{:S(2)}, u32[]{:S(2)}) collective-permute-start(bf16[8,8320]{1,0:T(8,128)(2,1)S(1)} %bitcast.109), channel_id=1, source_target_pairs={{0,16},{4,20},{8,24},{12,28},{16,0},{20,4},{24,8},{28,12},{1,17},{... | collective-permute-start | bytes 399368 | tf_op jit(solution)/shard_map/ppermute | solution.py:177
  28.8 5.1 %collective-permute-start.6 = (bf16[2,4,8320]{2,1,0:T(4,128)(2,1)S(1)}, bf16[2,4,8320]{2,1,0:T(4,128)(2,1)S(1)}, u32[]{:S(2)}, u32[]{:S(2)}) collective-permute-start(bf16[2,4,8320]{2,1,0:T(4,128)(2,1)S(1)} %get-tuple-element.13), channel_id=1, source_target_pairs={{0,4},{4,0},{8,12},{12,8},{16,20},{20,16},{24,28},{28,24},{1,5},{5... | collective-permute-start | bytes 399368 | tf_op jit(solution)/shard_map/ppermute | solution.py:186
  30.1 5.3 %collective-permute-start.4 = (bf16[2,4,8320]{2,1,0:T(4,128)(2,1)S(1)}, bf16[2,4,8320]{2,1,0:T(4,128)(2,1)S(1)}, u32[]{:S(2)}, u32[]{:S(2)}) collective-permute-start(bf16[2,4,8320]{2,1,0:T(4,128)(2,1)S(1)} %get-tuple-element.14), channel_id=1, source_target_pairs={{0,8},{4,12},{8,0},{12,4},{16,24},{20,28},{24,16},{28,20},{1,9},{5... | collective-permute-start | bytes 399368 | tf_op jit(solution)/shard_map/ppermute | solution.py:186
  34.0 6.8 %collective-permute-start.7 = (bf16[2,2,4,8320]{3,2,0,1:T(4,128)(2,1)S(1)}, bf16[2,2,4,8320]{3,2,0,1:T(4,128)(2,1)S(1)}, u32[]{:S(2)}, u32[]{:S(2)}) collective-permute-start(bf16[2,2,4,8320]{3,2,0,1:T(4,128)(2,1)S(1)} %get-tuple-element.12), channel_id=1, source_target_pairs={{0,8},{4,12},{8,0},{12,4},{16,24},{20,28},{24,16},{28,20},{1,9},{5... | collective-permute-start | bytes 798728 | tf_op jit(solution)/shard_map/ppermute | solution.py:186
  35.6 6.5 %collective-permute-start.5 = (bf16[2,2,4,8320]{3,2,0,1:T(4,128)(2,1)S(1)}, bf16[2,2,4,8320]{3,2,0,1:T(4,128)(2,1)S(1)}, u32[]{:S(2)}, u32[]{:S(2)}) collective-permute-start(bf16[2,2,4,8320]{3,2,0,1:T(4,128)(2,1)S(1)} %get-tuple-element.16), channel_id=1, source_target_pairs={{0,4},{4,0},{8,12},{12,8},{16,20},{20,16},{24,28},{28,24},{1,5},{5... | collective-permute-start | bytes 798728 | tf_op jit(solution)/shard_map/ppermute | solution.py:186

commit v11 on v10

--- a/solution.py
+++ b/solution.py
@@ -201,6 +201,135 @@
     device_bins = BINS // freq_count
     block_bins = device_bins // seg_count
     capacity = send_list.shape[2]
+
+    def band_of(row_ids):
+        owner_core = row_ids // device_bins
+        local_row = row_ids % device_bins
+        return (
+            local_row // block_bins * freq_count + owner_core
+        ) * block_bins + local_row % block_bins
+
+    blk_rank = lax.axis_index("blk")
+    seg_rank = lax.axis_index("seg")
+    all_segs = seg_dev * seg_count
+    table = jnp.concatenate([send_list[0], recv_row[0]], axis=1).reshape(-1)
+    table_len = table.shape[0]
+    phased = seg_count == 2 and freq_count == 2 and owners_count & (owners_count - 1) == 0
+    if phased:
+        gathered, table_raw = phased_exchange(
+            records, taps, table, sections, seg_dev, half_len, owners_count, freq_rank, seg_rank, blk_rank
+        )
+    else:
+        gathered, table_raw = plain_exchange(
+            records, taps, table, sections, seg_dev, half_len, owners_count, freq_rank, seg_rank, blk_rank,
+            seg_count, freq_count,
+        )
+    table_part = table_raw.astype(jnp.int32).reshape(owners_count, owners_count, 2 * capacity)
+    return finish(gathered, table_part, owners_count, sections, block_bins, all_segs, capacity, blk_rank)
+
+
+def amplitude_of(pair):
+    return jnp.sqrt(pair[:, 0] * pair[:, 0] + pair[:, 1] * pair[:, 1] + 1e-06)
+
+
+def whiten_block(spectra, lower_rim, upper_rim, block_index, taps):
+    block_bins = spectra.shape[0]
+    real_part = spectra[:, 0]
+    imag_part = spectra[:, 1]
+    amplitude = jnp.sqrt(real_part * real_part + imag_part * imag_part + 1e-06)
+    padded = jnp.concatenate([lower_rim, amplitude, upper_rim], axis=0)
+    window_sum = padded[0:block_bins]
+    for offset_step in range(1, 2 * HW + 1):
+        window_sum = window_sum + padded[offset_step : offset_step + block_bins]
+    position = block_index * block_bins + jnp.arange(block_bins, dtype=jnp.int32)
+    counted = jnp.minimum(position + HW, BINS - 1) - jnp.maximum(position - HW, 0) + 1
+    smooth = window_sum / counted.astype(jnp.float32)[:, None]
+    divisor = jnp.maximum(smooth, WHITEN_FLOOR)
+    response_re, response_im = response(position, taps)
+    scaled_re = real_part / divisor
+    scaled_im = imag_part / divisor
+    white_re = scaled_re * response_re[:, None] - scaled_im * response_im[:, None]
+    white_im = scaled_re * response_im[:, None] + scaled_im * response_re[:, None]
+    return jnp.stack([white_re, white_im], axis=1).astype(jnp.bfloat16)
+
+
+def phased_exchange(records, taps, table, sections, seg_dev, half_len, owners_count, freq_rank, seg_rank, blk_rank):
+    block_bins = BINS // 4
+    pair_bins = 2 * block_bins
+    rec_count = records.shape[0]
+    contract = (((1,), (1,)), ((), ()))
+    first_sample = freq_rank * half_len
+    first_core = freq_rank == 0
+
+    def pair_partials(source, pair_seg):
+        bins = pair_bins * pair_seg + jnp.arange(pair_bins, dtype=jnp.int32)
+        real_t, imag_t = dft_fused(source, bins, first_sample)
+        both = jnp.stack([real_t.T, imag_t.T], axis=1)
+        halves = both.reshape(2, block_bins, 2, rec_count)
+        kept = jnp.where(first_core, halves[0], halves[1])
+        sent = jnp.where(first_core, halves[1], halves[0])
+        return kept, sent
+
+    def edges_of(block):
+        return jnp.concatenate([block[:HW], block[block_bins - HW :]], axis=0)
+
+    rim_bins = pair_bins - HW + HW * seg_rank + jnp.arange(HW, dtype=jnp.int32)
+    rim_cos, rim_sin = dft_tables_fast(rim_bins, first_sample, half_len)
+    rim_part = jnp.stack(
+        [
+            lax.dot_general(rim_cos, records, contract, preferred_element_type=jnp.float32),
+            lax.dot_general(rim_sin, records, contract, preferred_element_type=jnp.float32),
+        ],
+        axis=1,
+    )
+    zero_rim = jnp.zeros((HW, rec_count), jnp.float32)
+
+    kept_a, sent_a = pair_partials(records, 1 - seg_rank)
+    message_a = jnp.concatenate([sent_a, edges_of(kept_a), rim_part], axis=0)
+    arrived_a = swapped(message_a, "freq", 0)
+    mine_a = kept_a + arrived_a[:block_bins]
+    partner_a = amplitude_of(edges_of(sent_a) + arrived_a[block_bins : block_bins + 2 * HW])
+    outer_a = amplitude_of(rim_part + arrived_a[block_bins + 2 * HW :])
+    outer_a = jnp.where(freq_rank == seg_rank, outer_a, zero_rim)
+    lower_a = jnp.where(first_core, outer_a, partner_a[HW:])
+    upper_a = jnp.where(first_core, partner_a[:HW], outer_a)
+    white_a = whiten_block(mine_a, lower_a, upper_a, 2 * (1 - seg_rank) + freq_rank, taps)
+    white_a = white_a.reshape(block_bins, 2, sections, seg_dev)
+    outgoing = jnp.transpose(white_a, (2, 0, 1, 3)).reshape(sections, -1)
+    source_b, outgoing = lax.optimization_barrier((records, outgoing))
+    received = lax.ppermute(outgoing, "seg", [(0, 1), (1, 0)])
+    table_width = 2 * 2 * seg_dev
+    slab = jnp.pad(table.astype(jnp.bfloat16), (0, sections * table_width - table.shape[0]))
+    carried_a = jnp.concatenate([received, slab.reshape(sections, table_width)], axis=1)
+    moved_a = gather_blocks(carried_a, owners_count, blk_rank)
+
+    kept_b, sent_b = pair_partials(source_b, seg_rank)
+    message_b = jnp.concatenate([sent_b, edges_of(kept_b)], axis=0)
+    arrived_b = swapped(message_b, "freq", 0)
+    mine_b = kept_b + arrived_b[:block_bins]
+    partner_b = amplitude_of(edges_of(sent_b) + arrived_b[block_bins:])
+    outer_b = jnp.where(first_core, partner_a[HW:], partner_a[:HW])
+    outer_b = jnp.where(freq_rank != seg_rank, outer_b, zero_rim)
+    lower_b = jnp.where(first_core, outer_b, partner_b[HW:])
+    upper_b = jnp.where(first_core, partner_b[:HW], outer_b)
+    white_b = whiten_block(mine_b, lower_b, upper_b, 2 * seg_rank + freq_rank, taps)
+    white_b = white_b.reshape(block_bins, 2, sections, seg_dev)
+    carried_b = jnp.transpose(white_b, (2, 0, 1, 3)).reshape(sections, -1)
+    moved_b = gather_blocks(carried_b, owners_count, blk_rank)
+
+    data_width = carried_b.shape[1]
+    data_a = moved_a[:, :, :data_width].reshape(owners_count, sections, block_bins, 2, seg_dev)
+    data_b = moved_b.reshape(owners_count, sections, block_bins, 2, seg_dev)
+    gathered = jnp.concatenate([data_a, data_b], axis=-1)
+    gathered = gathered.reshape(owners_count, sections, block_bins, 4 * seg_dev)
+    table_raw = moved_a[:, :, data_width:].reshape(owners_count, -1)[:, : table.shape[0]]
+    return gathered, table_raw
+
+
+def plain_exchange(records, taps, table, sections, seg_dev, half_len, owners_count, freq_rank, seg_rank, blk_rank,
+                   seg_count, freq_count):
+    device_bins = BINS // freq_count
+    block_bins = device_bins // seg_count
 
     def band_of(row_ids):
         owner_core = row_ids // device_bins
@@ -257,7 +386,6 @@
     whitened = jnp.stack([white_re, white_im], axis=1).astype(jnp.bfloat16)
     whitened = whitened.reshape(seg_count, block_bins, 2, sections, seg_dev)
     whitened = jnp.transpose(whitened, (0, 3, 1, 2, 4))
-    seg_rank = lax.axis_index("seg")
     pieces = [lax.dynamic_index_in_dim(whitened, seg_rank, axis=0, keepdims=False)]
     for shift in range(1, seg_count):
         outgoing = lax.dynamic_index_in_dim(
@@ -267,18 +395,18 @@
         flat = outgoing.reshape(sections, -1)
         pieces.append(lax.ppermute(flat, "seg", pairs).reshape(outgoing.shape))
     local = jnp.stack(pieces, axis=3).reshape(sections, block_bins, -1)
-    all_segs = seg_dev * seg_count
     table_width = local.shape[-1]
-    table = jnp.concatenate([send_list[0], recv_row[0]], axis=1).reshape(-1)
     table_len = table.shape[0]
     slab = jnp.pad(table.astype(jnp.bfloat16), (0, sections * table_width - table_len))
     carried = jnp.concatenate([local, slab.reshape(sections, 1, table_width)], axis=1)
-    blk_rank = lax.axis_index("blk")
     everything = gather_blocks(carried.reshape(sections, -1), owners_count, blk_rank)
     everything = everything.reshape(owners_count, sections, block_bins + 1, table_width)
     gathered = everything[:, :, :block_bins]
-    table_part = everything[:, :, block_bins].reshape(owners_count, -1)[:, :table_len]
-    table_part = table_part.astype(jnp.int32).reshape(owners_count, owners_count, 2 * capacity)
+    table_raw = everything[:, :, block_bins].reshape(owners_count, -1)[:, :table_len]
+    return gathered, table_raw
+
+
+def finish(gathered, table_part, owners_count, sections, block_bins, all_segs, capacity, blk_rank):
     position_ids = jnp.arange(owners_count, dtype=jnp.int32)
     if owners_count & (owners_count - 1) == 0:
         source_of = blk_rank ^ position_ids

time: 48.1 us -> 84.3 us (1.75)
  other arithmetic: 5.22 us -> 19.2 us
  local copies, waits for them, and re-layouts: 5.02 us -> 15.5 us
  waiting for transfers between devices: 17.6 us -> 10.6 us
  starting transfers between devices: 9.94 us -> 16.4 us
  matrix products: 3.27 us -> 9.34 us
  Pallas kernels: 6.41 us -> 12.3 us
    concatenate x1 -> x6, other arithmetic: 0.15 us -> 8.97 us  [the longest x1 8.2 us: phased_exchange(): gathered = jnp.concatenate([data_a, data_b], axis=-1)]
    pallas_call x1 -> x2, Pallas kernels: 6.41 us -> 12.3 us  [dft_fused(): pl.pallas_call(dft_kernel, grid=(count // chunk,), in_specs=[pl.BlockSpec...]
    dot_general x3 -> x5, matrix products: 2.26 us -> 7.95 us  [the longest x1 3.65 us: phased_exchange(): lax.dot_general(rim_cos, records, contract, preferred_element_type=jnp.fl...]
    reshape x4 -> x6, local copies, waits for them, and re-layouts: 0.6 us -> 6.27 us  [the longest x1 3.89 us: phased_exchange(): gathered = gathered.reshape(owners_count, sections, block_bins, 4 * seg_dev)]
    ppermute x4 -> x8, waiting for transfers between devices: 8.81 us -> 4.42 us  [gather_blocks(): arrived = lax.ppermute(part, 'blk', pairs)]
    ppermute x4 -> x8, starting transfers between devices: 3.19 us -> 7.12 us  [gather_blocks(): arrived = lax.ppermute(part, 'blk', pairs)]
    concatenate x3 -> x2, local copies, waits for them, and re-layouts: 0.66 us -> 4.48 us  [gather_blocks(): return jnp.concatenate(results, axis=1)]
    ppermute x1 -> x2, starting transfers between devices: 2.97 us -> 6.09 us  [gather_blocks(): held = jnp.stack([carried, lax.ppermute(carried, 'blk', pairs)], axis=0)]
  transfers between devices with their start and end apart: 8 -> 13, of which waited for: 7 -> 4; matrix products, arithmetic and copies ran while one was open for 6% -> 14% of each run, Pallas kernels for 0% -> 7%
where the time goes in v11:
time: 84.3 us; the launch traced here: 83.9 us
  other arithmetic  19.2 us (23%)
  starting transfers between devices  16.4 us (19%)
  local copies, waits for them, and re-layouts  15.5 us (18%)
  Pallas kernels  12.3 us (15%)
  waiting for transfers between devices  10.6 us (13%)
  matrix products  9.34 us (11%)
    pallas_call x2, Pallas kernels, dft_fused(): pl.pallas_call(dft_kernel, grid=(count // chunk,), in_specs=[pl.BlockSpec...  12.3 us
    concatenate x1, other arithmetic, phased_exchange(): gathered = jnp.concatenate([data_a, data_b], axis=-1)  8.2 us
    ppermute x8, starting transfers between devices, gather_blocks(): arrived = lax.ppermute(part, 'blk', pairs)  7.12 us
    ppermute x2, waiting for transfers between devices, gather_blocks(): held = jnp.stack([carried, lax.ppermute(carried, 'blk', pairs)], axis=0)  6.13 us
    ppermute x2, starting transfers between devices, gather_blocks(): held = jnp.stack([carried, lax.ppermute(carried, 'blk', pairs)], axis=0)  6.09 us
    concatenate x2, local copies, waits for them, and re-layouts, gather_blocks(): return jnp.concatenate(results, axis=1)  4.48 us
    ppermute x8, waiting for transfers between devices, gather_blocks(): arrived = lax.ppermute(part, 'blk', pairs)  4.42 us
    reshape x1, local copies, waits for them, and re-layouts, phased_exchange(): gathered = gathered.reshape(owners_count, sections, block_bins, 4 * seg_dev)  3.89 us
  transfers between devices with their start and end apart: 13, of which 4 were waited for; matrix products, arithmetic and copies ran while one was open for 14% of the time, Pallas kernels for 7%

profile of v11, /device:TPU:0, one launch (start us, length us, event | category | flops | bytes accessed | tf_op | source)
XLA Modules:
  0.0 83.9 jit_solution(17820786553382655141)
XLA Ops:
  0.6 3.6 %convolution_bitcast_fusion.1 = f32[4,1,256]{2,0,1:T(4,128)S(1)} fusion(bf16[256,8192]{1,0:T(8,128)(2,1)} %bitcast.176, bf16[1,4,64,128]{3,2,1,0:T(8,128)(2,1)S(1)} %get-tuple-element.63), kind=kOutput, calls=%fused_computation.6 | convolution fusion | flops 16777216 | bytes 4263936 | tf_op jit(solution)/shard_map/dot_general | solution.py:280
  4.3 1.2 %convolution_bitcast_fusion = f32[4,1,256]{2,0,1:T(4,128)S(1)} fusion(bf16[256,8192]{1,0:T(8,128)(2,1)S(1)} %bitcast.179, bf16[1,4,64,128]{3,2,1,0:T(8,128)(2,1)S(1)} %get-tuple-element.64), kind=kOutput, calls=%fused_computation.5 | convolution fusion | flops 16777216 | bytes 4263936 | tf_op jit(solution)/shard_map/dot_general | solution.py:281
  5.5 0.2 copy.74
  5.6 0.2 fusion.120
  5.8 0.7 negate_bitcast_fusion
  6.5 0.7 add_multiply_fusion
  7.2 6.2 %shard_map.46 = (f32[256,128]{1,0:T(8,128)}, f32[256,128]{1,0:T(8,128)}) custom-call(bf16[256,8192]{1,0:T(8,128)(2,1)} %bitcast.177, f32[64,128]{1,0:T(8,128)} %get-tuple-element.97.cos_a_ref, f32[64,128]{1,0:T(8,128)} %get-tuple-element.98.nsin_a_ref, f32[128,128]{1,0:T(8,128)} %bitcast.190, f32[128,128]{1,0:T(8,128)} %bitcast.191), custom_call_target="tpu_custom_call" | custom-call | tf_op jit(solution)/shard_map/pallas_call | solution.py:145
  13.5 1.3 %fusion.9 = (f32[64,2,256]{0,2,1:T(8,128)S(1)}, f32[64,2,256]{0,2,1:T(8,128)S(1)}) fusion(f32[128,1,256]{0,2,1:T(8,128)} %bitcast.203, f32[128,1,256]{0,2,1:T(8,128)} %bitcast.202, pred[]{:T(512)S(6)} %eq.70), kind=kLoop, calls=%fused_computation.41 | loop fusion | flops 163840 | bytes 524289 | tf_op jit(solution)/shard_map/jit(_where)/select_n | solution.py:270
  14.9 0.3 pad_maximum_fusion.4
  15.2 0.5 collective-permute-start
  15.8 0.3 convolution_bitcast_fusion.4
  16.1 0.4 convolution_bitcast_fusion.5
  16.5 0.2 fusion.168
  16.6 0.3 convolution_bitcast_fusion.3
  17.3 0.3 convolution_bitcast_fusion.2
  17.7 0.2 slice_add_fusion.2
  18.3 0.6 subtract_convert_fusion.1
  19.0 0.2 copy.77
  19.1 0.2 copy.76
  19.3 0.7 maximum_bitcast_fusion
  20.0 0.3 reshape.906
  20.3 2.6 %collective-permute-start.1 = (bf16[8,4096]{1,0:T(8,128)(2,1)S(1)}, bf16[8,4096]{1,0:T(8,128)(2,1)S(1)}, u32[]{:S(2)}, u32[]{:S(2)}) collective-permute-start(bf16[8,4096]{1,0:T(8,128)(2,1)S(1)} %reshape.906), channel_id=1, source_target_pairs={{0,2},{2,0},{1,3},{3,1},{4,6},{6,4},{5,7},{7,5},{8,10},{10,8},{9,1... | collective-permute-start | bytes 196616 | tf_op jit(solution)/shard_map/ppermute | solution.py:300
  22.9 6.0 %shard_map.47 = (f32[256,128]{1,0:T(8,128)}, f32[256,128]{1,0:T(8,128)}) custom-call(bf16[256,8192]{1,0:T(8,128)(2,1)} %bitcast.178, f32[64,128]{1,0:T(8,128)} %get-tuple-element.60.cos_a_ref, f32[64,128]{1,0:T(8,128)} %get-tuple-element.59.nsin_a_ref, f32[128,128]{1,0:T(8,128)} %bitcast.189, f32[128,128]{1,0:T(8,128)} %bitcast.188), custom_call_target="tpu_custom_call" | custom-call | tf_op jit(solution)/shard_map/pallas_call | solution.py:145
  28.9 1.3 %fusion.11 = (f32[64,2,256]{0,2,1:T(8,128)S(1)}, f32[64,2,256]{0,2,1:T(8,128)S(1)}) fusion(f32[128,1,256]{0,2,1:T(8,128)} %bitcast.205, f32[128,1,256]{0,2,1:T(8,128)} %bitcast.204, pred[]{:T(512)S(6)} %eq.70), kind=kLoop, calls=%fused_computation.43 | loop fusion | flops 163840 | bytes 524289 | tf_op jit(solution)/shard_map/jit(_where)/select_n | solution.py:270
  30.6 2.7 %collective-permute-start.2 = (bf16[8,4224]{1,0:T(8,128)(2,1)S(1)}, bf16[8,4224]{1,0:T(8,128)(2,1)S(1)}, u32[]{:S(2)}, u32[]{:S(2)}) collective-permute-start(bf16[8,4224]{1,0:T(8,128)(2,1)S(1)} %get-tuple-element.51), channel_id=1, source_target_pairs={{0,16},{4,20},{8,24},{12,28},{16,0},{20,4},{24,8},{28,12},{1,17},{... | collective-permute-start | bytes 202760 | tf_op jit(solution)/shard_map/ppermute | solution.py:177
  33.2 0.2 pad_maximum_fusion.5
  33.5 3.8 %collective-permute-done.2 = bf16[8,4224]{1,0:T(8,128)(2,1)S(1)} collective-permute-done((bf16[8,4224]{1,0:T(8,128)(2,1)S(1)}, bf16[8,4224]{1,0:T(8,128)(2,1)S(1)}, u32[]{:S(2)}, u32[]{:S(2)}) %collective-permute-start.2) | collective-permute-done | bytes 67616 | tf_op jit(solution)/shard_map/ppermute | solution.py:177
  37.3 1.6 %collective-permute-start.5 = (bf16[2,4,4224]{2,1,0:T(4,128)(2,1)S(1)}, bf16[2,4,4224]{2,1,0:T(4,128)(2,1)S(1)}, u32[]{:S(2)}, u32[]{:S(2)}) collective-permute-start(bf16[2,4,4224]{2,1,0:T(4,128)(2,1)S(1)} %get-tuple-element.41), channel_id=1, source_target_pairs={{0,4},{4,0},{8,12},{12,8},{16,20},{20,16},{24,28},{28,24},{1,5},{5... | collective-permute-start | bytes 202760 | tf_op jit(solution)/shard_map/ppermute | solution.py:186
  38.9 0.6 collective-permute-start.3
  39.6 0.2 slice_add_fusion
  40.1 0.6 subtract_convert_fusion
  40.7 0.2 copy.82
  40.9 0.2 copy.81
  41.1 0.7 maximum_bitcast_fusion.1
  41.8 0.3 reshape.911
  42.0 0.3 stack_reshape.3
  42.3 3.4 %collective-permute-start.8 = (bf16[8,4096]{1,0:T(8,128)(2,1)S(1)}, bf16[8,4096]{1,0:T(8,128)(2,1)S(1)}, u32[]{:S(2)}, u32[]{:S(2)}) collective-permute-start(bf16[8,4096]{1,0:T(8,128)(2,1)S(1)} %reshape.911), channel_id=1, source_target_pairs={{0,16},{4,20},{8,24},{12,28},{16,0},{20,4},{24,8},{28,12},{1,17},{... | collective-permute-start | bytes 196616 | tf_op jit(solution)/shard_map/ppermute | solution.py:177
  45.9 2.4 %collective-permute-done.8 = bf16[8,4096]{1,0:T(8,128)(2,1)S(1)} collective-permute-done((bf16[8,4096]{1,0:T(8,128)(2,1)S(1)}, bf16[8,4096]{1,0:T(8,128)(2,1)S(1)}, u32[]{:S(2)}, u32[]{:S(2)}) %collective-permute-start.8) | collective-permute-done | bytes 65568 | tf_op jit(solution)/shard_map/ppermute | solution.py:177
  48.4 1.4 %collective-permute-start.9 = (bf16[2,4,4096]{2,1,0:T(4,128)(2,1)S(1)}, bf16[2,4,4096]{2,1,0:T(4,128)(2,1)S(1)}, u32[]{:S(2)}, u32[]{:S(2)}) collective-permute-start(bf16[2,4,4096]{2,1,0:T(4,128)(2,1)S(1)} %get-tuple-element.47), channel_id=1, source_target_pairs={{0,8},{4,12},{8,0},{12,4},{16,24},{20,28},{24,16},{28,20},{1,9},{5... | collective-permute-start | bytes 196616 | tf_op jit(solution)/shard_map/ppermute | solution.py:186
  49.9 0.6 collective-permute-start.4
  50.4 1.5 %collective-permute-start.11 = (bf16[2,4,4096]{2,1,0:T(4,128)(2,1)S(1)}, bf16[2,4,4096]{2,1,0:T(4,128)(2,1)S(1)}, u32[]{:S(2)}, u32[]{:S(2)}) collective-permute-start(bf16[2,4,4096]{2,1,0:T(4,128)(2,1)S(1)} %get-tuple-element.48), channel_id=1, source_target_pairs={{0,4},{4,0},{8,12},{12,8},{16,20},{20,16},{24,28},{28,24},{1,5},{5... | collective-permute-start | bytes 196616 | tf_op jit(solution)/shard_map/ppermute | solution.py:186
  52.0 0.7 collective-permute-done.9
  52.8 0.6 collective-permute-start.10
  53.4 3.7 %collective-permute-done.11 = bf16[2,4,4096]{2,1,0:T(4,128)(2,1)S(1)} collective-permute-done((bf16[2,4,4096]{2,1,0:T(4,128)(2,1)S(1)}, bf16[2,4,4096]{2,1,0:T(4,128)(2,1)S(1)}, u32[]{:S(2)}, u32[]{:S(2)}) %collective-permute-start.11) | collective-permute-done | bytes 65568 | tf_op jit(solution)/shard_map/ppermute | solution.py:186
  57.2 0.8 collective-permute-start.12
  57.9 0.2 pad_maximum_fusion.1
  58.2 0.2 pad_maximum_fusion
  58.6 0.3 fusion.2
  58.8 0.2 copy.97
  59.5 0.1 eq.75
  59.8 0.1 eq.79
  59.9 1.6 %reshape.910 = bf16[8,8,64,2,32]{4,3,2,1,0:T(2,128)(2,1)S(1)} reshape(bf16[8,8,4096]{2,1,0:T(8,128)(2,1)S(1)} %fusion.2) | data formatting | bytes 1048576 | tf_op jit(solution)/shard_map/reshape | solution.py:321
  61.6 0.9 %fusion = bf16[128,8,8]{0,2,1:T(8,128)(2,1)} fusion(s32[128]{0:T(128)S(1)} %eq.79, s32[128]{0:T(128)S(1)} %eq.75), kind=kOutput, calls=%fused_computation.4 | convolution fusion | flops 2129920 | bytes 17408 | tf_op jit(solution)/shard_map/er,ec->rc/dot_general | solution.py:433
  62.5 0.2 pad_maximum_fusion.6
  62.8 0.2 pad_maximum_fusion.7
  63.0 0.8 copy.84
  63.8 2.9 %concatenate.81 = bf16[8,4,64,2,32]{4,3,2,1,0:T(2,128)(2,1)S(1)} reshape(bf16[2,2,2,4,4096]{4,3,2,1,0:T(4,128)(2,1)} %copy.84) | data formatting | bytes 524288 | tf_op jit(solution)/shard_map/concatenate | solution.py:191
  66.7 1.6 %concatenate.80 = bf16[8,4,64,2,32]{4,3,2,1,0:T(2,128)(2,1)} reshape(bf16[2,2,2,4,4096]{4,3,2,1,0:T(4,128)(2,1)S(1)} %copy.83) | data formatting | bytes 524288 | tf_op jit(solution)/shard_map/concatenate | solution.py:191
  68.2 8.2 %maximum_maximum_fusion = bf16[8,8,64,2,64]{4,3,2,1,0:T(2,128)(2,1)} fusion(bf16[8,4,64,2,32]{4,3,2,1,0:T(2,128)(2,1)S(1)} %concatenate.81, bf16[8,4,64,2,32]{4,3,2,1,0:T(2,128)(2,1)} %concatenate.80, bf16[8,8,64,2,32]{4,3,2,1,0:T(2,128)(2,1)S(1)} %reshape.910), kind=kLoop, calls=%fused_computation.1 | loop fusion | flops 3145728 | bytes 2097152 | tf_op jit(solution)/shard_map/concatenate | solution.py:323
  76.4 3.9 %reshape.942 = bf16[8,8,64,128]{3,2,1,0:T(8,128)(2,1)S(1)} reshape(bf16[8,8,64,2,64]{4,3,2,1,0:T(2,128)(2,1)} %maximum_maximum_fusion) | data formatting | bytes 2097152 | tf_op jit(solution)/shard_map/reshape | solution.py:324
  80.4 1.0 %bitcast_convert_fusion = bf16[64,128,128]{1,2,0:T(8,128)(2,1)S(1)} fusion(bf16[8,8,64,128]{3,2,1,0:T(8,128)(2,1)S(1)} %reshape.942, bf16[128,8,8]{0,2,1:T(8,128)(2,1)S(1)} %copy-done.2), kind=kOutput, calls=%fused_computation | convolution fusion | flops 135266304 | bytes 3162112 | tf_op jit(solution)/shard_map/rsc,scbq->brq/dot_general | solution.py:437
  81.4 0.1 fusion.165
  81.6 1.2 %convolution_multiply_fusion = f32[64,32,128]{2,1,0:T(8,128)S(1)} fusion(bf16[64,128,128]{1,2,0:T(8,128)(2,1)S(1)} %bitcast_convert_fusion, bf16[64,16,64]{2,1,0:T(8,128)(2,1)S(1)} %get-tuple-element.24, bf16[64,16,64]{2,1,0:T(8,128)(2,1)S(1)} %get-tuple-element.23, bf16[64,16,128]{2,1,0:T(8,128)(2,1)S(1)} %dynamic-slice_bitcast_fusion), kind=kOutput, calls=%fused_computation.2 | convolution fusion | flops 68943872 | bytes 3670016 | tf_op jit(solution)/shard_map/bpq,bjq->bpj/dot_general | solution.py:445
  82.8 1.1 %copy.116 = f32[64,2,16,128]{3,2,0,1:T(8,128)} copy(f32[64,2,16,128]{3,2,1,0:T(8,128)S(1)} %bitcast.180) | data formatting | bytes 2097152 | tf_op jit(solution)/shard_map/div | solution.py:447
  (77 shorter events, 3.7 us)
Async XLA Ops:
  0.0 15.7 %copy-start = (f32[128]{0:T(128)S(1)}, f32[128]{0:T(128)}, u32[]{:S(2)}) copy-start(f32[128]{0:T(128)} %param.5) | copy-start | bytes 1540
  0.1 4.2 %copy-start.1 = (bf16[8,32,8192]{2,1,0:T(8,128)(2,1)S(1)}, bf16[8,32,8192]{2,1,0:T(8,128)(2,1)}, u32[]{:S(2)}) copy-start(bf16[8,32,8192]{2,1,0:T(8,128)(2,1)} %param.4) | copy-start | bytes 12582916
  7.2 9.8 %copy-start.3 = (s32[1,8,2]{1,2,0:T(2,128)S(1)}, s32[1,8,2]{1,2,0:T(2,128)}, u32[]{:S(2)}) copy-start(s32[1,8,2]{1,2,0:T(2,128)} %param.7) | copy-start | bytes 196
  7.2 9.8 %copy-start.4 = (s32[1,8,2]{1,2,0:T(2,128)S(1)}, s32[1,8,2]{1,2,0:T(2,128)}, u32[]{:S(2)}) copy-start(s32[1,8,2]{1,2,0:T(2,128)} %param.6) | copy-start | bytes 196
  15.2 2.5 %collective-permute-start = (f32[76,2,256]{0,2,1:T(8,128)S(1)}, f32[76,2,256]{0,2,1:T(8,128)S(1)}, u32[]{:S(2)}, u32[]{:S(2)}) collective-permute-start(f32[76,2,256]{0,2,1:T(8,128)S(1)} %pad_maximum_fusion.4), channel_id=1, source_target_pairs={{0,1},{1,0},{2,3},{3,2},{4,5},{5,4},{6,7},{7,6},{8,9},{9,8},{10,11... | collective-permute-start | bytes 466952 | tf_op jit(solution)/shard_map/ppermute | solution.py:24
  20.3 10.2 %collective-permute-start.1 = (bf16[8,4096]{1,0:T(8,128)(2,1)S(1)}, bf16[8,4096]{1,0:T(8,128)(2,1)S(1)}, u32[]{:S(2)}, u32[]{:S(2)}) collective-permute-start(bf16[8,4096]{1,0:T(8,128)(2,1)S(1)} %reshape.906), channel_id=1, source_target_pairs={{0,2},{2,0},{1,3},{3,1},{4,6},{6,4},{5,7},{7,5},{8,10},{10,8},{9,1... | collective-permute-start | bytes 196616 | tf_op jit(solution)/shard_map/ppermute | solution.py:300
  30.6 6.7 %collective-permute-start.2 = (bf16[8,4224]{1,0:T(8,128)(2,1)S(1)}, bf16[8,4224]{1,0:T(8,128)(2,1)S(1)}, u32[]{:S(2)}, u32[]{:S(2)}) collective-permute-start(bf16[8,4224]{1,0:T(8,128)(2,1)S(1)} %get-tuple-element.51), channel_id=1, source_target_pairs={{0,16},{4,20},{8,24},{12,28},{16,0},{20,4},{24,8},{28,12},{1,17},{... | collective-permute-start | bytes 202760 | tf_op jit(solution)/shard_map/ppermute | solution.py:177
  33.4 6.1 %collective-permute-start.7 = (f32[72,2,256]{0,2,1:T(8,128)S(1)}, f32[72,2,256]{0,2,1:T(8,128)S(1)}, u32[]{:S(2)}, u32[]{:S(2)}) collective-permute-start(f32[72,2,256]{0,2,1:T(8,128)S(1)} %pad_maximum_fusion.5), channel_id=1, source_target_pairs={{0,1},{1,0},{2,3},{3,2},{4,5},{5,4},{6,7},{7,6},{8,9},{9,8},{10,11... | collective-permute-start | bytes 442376 | tf_op jit(solution)/shard_map/ppermute | solution.py:24
  37.3 8.4 %collective-permute-start.5 = (bf16[2,4,4224]{2,1,0:T(4,128)(2,1)S(1)}, bf16[2,4,4224]{2,1,0:T(4,128)(2,1)S(1)}, u32[]{:S(2)}, u32[]{:S(2)}) collective-permute-start(bf16[2,4,4224]{2,1,0:T(4,128)(2,1)S(1)} %get-tuple-element.41), channel_id=1, source_target_pairs={{0,4},{4,0},{8,12},{12,8},{16,20},{20,16},{24,28},{28,24},{1,5},{5... | collective-permute-start | bytes 202760 | tf_op jit(solution)/shard_map/ppermute | solution.py:186
  38.9 10.8 %collective-permute-start.3 = (bf16[2,4,4224]{2,1,0:T(4,128)(2,1)S(1)}, bf16[2,4,4224]{2,1,0:T(4,128)(2,1)S(1)}, u32[]{:S(2)}, u32[]{:S(2)}) collective-permute-start(bf16[2,4,4224]{2,1,0:T(4,128)(2,1)S(1)} %get-tuple-element.42), channel_id=1, source_target_pairs={{0,8},{4,12},{8,0},{12,4},{16,24},{20,28},{24,16},{28,20},{1,9},{5... | collective-permute-start | bytes 202760 | tf_op jit(solution)/shard_map/ppermute | solution.py:186
  42.3 6.0 %collective-permute-start.8 = (bf16[8,4096]{1,0:T(8,128)(2,1)S(1)}, bf16[8,4096]{1,0:T(8,128)(2,1)S(1)}, u32[]{:S(2)}, u32[]{:S(2)}) collective-permute-start(bf16[8,4096]{1,0:T(8,128)(2,1)S(1)} %reshape.911), channel_id=1, source_target_pairs={{0,16},{4,20},{8,24},{12,28},{16,0},{20,4},{24,8},{28,12},{1,17},{... | collective-permute-start | bytes 196616 | tf_op jit(solution)/shard_map/ppermute | solution.py:177
  45.9 12.1 %collective-permute-start.6 = (bf16[2,2,4,4224]{3,2,0,1:T(4,128)(2,1)S(1)}, bf16[2,2,4,4224]{3,2,0,1:T(4,128)(2,1)S(1)}, u32[]{:S(2)}, u32[]{:S(2)}) collective-permute-start(bf16[2,2,4,4224]{3,2,0,1:T(4,128)(2,1)S(1)} %get-tuple-element.40), channel_id=1, source_target_pairs={{0,8},{4,12},{8,0},{12,4},{16,24},{20,28},{24,16},{28,20},{1,9},{5... | collective-permute-start | bytes 405512 | tf_op jit(solution)/shard_map/ppermute | solution.py:186
  48.4 4.3 %collective-permute-start.9 = (bf16[2,4,4096]{2,1,0:T(4,128)(2,1)S(1)}, bf16[2,4,4096]{2,1,0:T(4,128)(2,1)S(1)}, u32[]{:S(2)}, u32[]{:S(2)}) collective-permute-start(bf16[2,4,4096]{2,1,0:T(4,128)(2,1)S(1)} %get-tuple-element.47), channel_id=1, source_target_pairs={{0,8},{4,12},{8,0},{12,4},{16,24},{20,28},{24,16},{28,20},{1,9},{5... | collective-permute-start | bytes 196616 | tf_op jit(solution)/shard_map/ppermute | solution.py:186
  49.9 8.4 %collective-permute-start.4 = (bf16[2,2,4,4224]{3,2,0,1:T(4,128)(2,1)S(1)}, bf16[2,2,4,4224]{3,2,0,1:T(4,128)(2,1)S(1)}, u32[]{:S(2)}, u32[]{:S(2)}) collective-permute-start(bf16[2,2,4,4224]{3,2,0,1:T(4,128)(2,1)S(1)} %get-tuple-element.44), channel_id=1, source_target_pairs={{0,4},{4,0},{8,12},{12,8},{16,20},{20,16},{24,28},{28,24},{1,5},{5... | collective-permute-start | bytes 405512 | tf_op jit(solution)/shard_map/ppermute | solution.py:186
  50.4 6.6 %collective-permute-start.11 = (bf16[2,4,4096]{2,1,0:T(4,128)(2,1)S(1)}, bf16[2,4,4096]{2,1,0:T(4,128)(2,1)S(1)}, u32[]{:S(2)}, u32[]{:S(2)}) collective-permute-start(bf16[2,4,4096]{2,1,0:T(4,128)(2,1)S(1)} %get-tuple-element.48), channel_id=1, source_target_pairs={{0,4},{4,0},{8,12},{12,8},{16,20},{20,16},{24,28},{28,24},{1,5},{5... | collective-permute-start | bytes 196616 | tf_op jit(solution)/shard_map/ppermute | solution.py:186
  52.8 9.7 %collective-permute-start.10 = (bf16[2,2,4,4096]{3,2,0,1:T(4,128)(2,1)S(1)}, bf16[2,2,4,4096]{3,2,0,1:T(4,128)(2,1)S(1)}, u32[]{:S(2)}, u32[]{:S(2)}) collective-permute-start(bf16[2,2,4,4096]{3,2,0,1:T(4,128)(2,1)S(1)} %get-tuple-element.46), channel_id=1, source_target_pairs={{0,4},{4,0},{8,12},{12,8},{16,20},{20,16},{24,28},{28,24},{1,5},{5... | collective-permute-start | bytes 393224 | tf_op jit(solution)/shard_map/ppermute | solution.py:186
  57.2 5.6 %collective-permute-start.12 = (bf16[2,2,4,4096]{3,2,0,1:T(4,128)(2,1)S(1)}, bf16[2,2,4,4096]{3,2,0,1:T(4,128)(2,1)S(1)}, u32[]{:S(2)}, u32[]{:S(2)}) collective-permute-start(bf16[2,2,4,4096]{3,2,0,1:T(4,128)(2,1)S(1)} %get-tuple-element.50), channel_id=1, source_target_pairs={{0,8},{4,12},{8,0},{12,4},{16,24},{20,28},{24,16},{28,20},{1,9},{5... | collective-permute-start | bytes 393224 | tf_op jit(solution)/shard_map/ppermute | solution.py:186
  68.2 12.1 %copy-start.2 = (bf16[128,8,8]{0,2,1:T(8,128)(2,1)S(1)}, bf16[128,8,8]{0,2,1:T(8,128)(2,1)}, u32[]{:S(2)}) copy-start(bf16[128,8,8]{0,2,1:T(8,128)(2,1)} %fusion) | copy-start | bytes 49156

commit v12 on v10

--- a/solution.py
+++ b/solution.py
@@ -218,7 +218,26 @@
     if freq_count == 2:
         kept = jnp.where(freq_rank == 0, blocks[0], blocks[1])
         sent = jnp.where(freq_rank == 0, blocks[1], blocks[0])
-        spectra = kept + swapped(sent, "freq", 0)
+        kept_blocks = kept.reshape(seg_count, block_bins, 2, -1)
+        sent_blocks = sent.reshape(seg_count, block_bins, 2, -1)
+        own_edges = jnp.concatenate(
+            [kept_blocks[:, :HW], kept_blocks[:, block_bins - HW :]], axis=1
+        ).reshape(seg_count * 2 * HW, 2, -1)
+        message = jnp.concatenate([sent, own_edges], axis=0)
+        arrived = swapped(message, "freq", 0)
+        spectra = kept + arrived[:device_bins]
+        their_edges = jnp.concatenate(
+            [sent_blocks[:, :HW], sent_blocks[:, block_bins - HW :]], axis=1
+        ).reshape(seg_count * 2 * HW, 2, -1)
+        edge_spectra = (their_edges + arrived[device_bins:]).reshape(seg_count, 2, HW, 2, -1)
+        partner = jnp.transpose(
+            jnp.sqrt(
+                edge_spectra[..., 0, :] * edge_spectra[..., 0, :]
+                + edge_spectra[..., 1, :] * edge_spectra[..., 1, :]
+                + 1e-06
+            ),
+            (1, 0, 2, 3),
+        )
     else:
         spectra = lax.psum_scatter(
             blocks.reshape(device_bins * freq_count, 2, records.shape[0]),
@@ -230,8 +249,9 @@
     imag_part = spectra[:, 1]
     amplitude = jnp.sqrt(real_part * real_part + imag_part * imag_part + 1e-06)
     amp_blocks = amplitude.reshape(seg_count, block_bins, -1)
-    band_rims = jnp.stack([amp_blocks[:, :HW], amp_blocks[:, block_bins - HW :]])
-    partner = swapped(band_rims, "freq", 0)
+    if freq_count != 2:
+        band_rims = jnp.stack([amp_blocks[:, :HW], amp_blocks[:, block_bins - HW :]])
+        partner = swapped(band_rims, "freq", 0)
     zero_rim = jnp.zeros_like(partner[1][:1])
     right_prev = jnp.concatenate([zero_rim, partner[1][:-1]], axis=0)
     left_next = jnp.concatenate([partner[0][1:], zero_rim], axis=0)

time: 48.1 us -> 48.7 us (1.012)
  waiting for transfers between devices: 17.6 us -> 16.5 us
  starting transfers between devices: 9.94 us -> 10.8 us
  local copies, waits for them, and re-layouts: 5.02 us -> 5.67 us
    ppermute x4, starting transfers between devices: 3.19 us -> 4.64 us  [gather_blocks(): arrived = lax.ppermute(part, 'blk', pairs)]
    ppermute x4, waiting for transfers between devices: 8.81 us -> 7.95 us  [gather_blocks(): arrived = lax.ppermute(part, 'blk', pairs)]
    ppermute x2 -> x1, waiting for transfers between devices: 0.65 us -> 0.01 us  [swapped(): return lax.ppermute(value, axis, pairs)]
  transfers between devices with their start and end apart: 8 -> 7, of which waited for: 7 -> 6; matrix products, arithmetic and copies ran while one was open for 6% -> 6% of each run, Pallas kernels for 0% -> 0%
where the time goes in v12:
time: 48.7 us; the launch traced here: 48.5 us
  waiting for transfers between devices  16.5 us (34%)
  starting transfers between devices  10.8 us (22%)
  Pallas kernels  6.4 us (13%)
  local copies, waits for them, and re-layouts  5.67 us (12%)
  other arithmetic  5.42 us (11%)
  matrix products  3.27 us (7%)
    ppermute x4, waiting for transfers between devices, gather_blocks(): arrived = lax.ppermute(part, 'blk', pairs)  7.95 us
    pallas_call x1, Pallas kernels, dft_fused(): pl.pallas_call(dft_kernel, grid=(count // chunk,), in_specs=[pl.BlockSpec...  6.4 us
    ppermute x1, waiting for transfers between devices, gather_blocks(): held = jnp.stack([carried, lax.ppermute(carried, 'blk', pairs)], axis=0)  6.2 us
    ppermute x4, starting transfers between devices, gather_blocks(): arrived = lax.ppermute(part, 'blk', pairs)  4.64 us
    ppermute x1, starting transfers between devices, gather_blocks(): held = jnp.stack([carried, lax.ppermute(carried, 'blk', pairs)], axis=0)  2.89 us
    ppermute x1, starting transfers between devices, per_device(): pieces.append(lax.ppermute(flat, 'seg', pairs).reshape(outgoing.shape))  2.74 us
    ppermute x1, waiting for transfers between devices, per_device(): pieces.append(lax.ppermute(flat, 'seg', pairs).reshape(outgoing.shape))  2.34 us
    select_n x1, other arithmetic, per_device(): sent = jnp.where(freq_rank == 0, blocks[1], blocks[0])  1.25 us
  transfers between devices with their start and end apart: 7, of which 6 were waited for; matrix products, arithmetic and copies ran while one was open for 6% of the time, Pallas kernels for 0%

profile of v12, /device:TPU:0, one launch (start us, length us, event | category | flops | bytes accessed | tf_op | source)
XLA Modules:
  0.0 48.5 jit_solution(7957125509892992026)
XLA Ops:
  0.0 0.1 fusion.58
  0.1 0.2 fusion.60
  0.3 0.7 %negate_bitcast_fusion = (f32[64,256]{1,0:T(8,128)}, f32[64,256]{1,0:T(8,128)}) fusion(f32[8,256]{1,0:T(8,128)S(1)} %get-tuple-element.43, f32[8,256]{1,0:T(8,128)S(1)} %get-tuple-element.45, f32[8,256]{1,0:T(8,128)S(1)} %get-tuple-element.44, f32[8,256]{1,0:T(8,128)S(1)} %get-tuple-element.46), kind=kLoop, calls=%fused_computation.90 | loop fusion | flops 114688 | bytes 163840 | tf_op jit(solution)/shard_map/neg | solution.py:136
  1.0 0.7 %add_multiply_fusion = (f32[8,16,256]{2,1,0:T(8,128)}, f32[8,16,256]{2,1,0:T(8,128)}) fusion(f32[16,256]{1,0:T(8,128)S(1)} %get-tuple-element.48, f32[8,256]{1,0:T(8,128)S(1)} %get-tuple-element.38, f32[16,256]{1,0:T(8,128)S(1)} %get-tuple-element.47, f32[8,256]{1,0:T(8,128)S(1)} %get-tuple-element.37), kind=kLoop, calls=%fused_computation.71 | loop fusion | flops 262144 | bytes 311296 | tf_op jit(solution)/shard_map/mul | solution.py:141
  1.7 6.4 %shard_map.46 = (f32[256,256]{1,0:T(8,128)}, f32[256,256]{1,0:T(8,128)}) custom-call(bf16[256,8192]{1,0:T(8,128)(2,1)} %bitcast.113, f32[64,256]{1,0:T(8,128)} %get-tuple-element.30.cos_a_ref, f32[64,256]{1,0:T(8,128)} %get-tuple-element.29.nsin_a_ref, f32[128,256]{1,0:T(8,128)} %bitcast.121, f32[128,256]{1,0:T(8,128)} %bitcast.120), custom_call_target="tpu_custom_call" | custom-call | tf_op jit(solution)/shard_map/pallas_call | solution.py:145
  8.1 1.2 %broadcast_select_fusion = (f32[128,2,256]{0,2,1:T(8,128)S(1)}, f32[128,2,256]{0,2,1:T(8,128)S(1)}) fusion(pred[]{:T(512)S(6)} %eq.66, f32[256,1,256]{0,2,1:T(8,128)} %bitcast.129, f32[256,1,256]{0,2,1:T(8,128)} %bitcast.128), kind=kLoop, calls=%fused_computation.73 | loop fusion | flops 327680 | bytes 1048577 | tf_op jit(solution)/shard_map/jit(_where)/select_n | solution.py:220
  9.4 0.1 copy.103
  9.6 0.1 copy.104
  9.8 0.5 %collective-permute-start = (f32[144,2,256]{0,2,1:T(8,128)S(1)}, f32[144,2,256]{0,2,1:T(8,128)S(1)}, u32[]{:S(2)}, u32[]{:S(2)}) collective-permute-start(f32[144,2,256]{0,2,1:T(8,128)S(1)} %pad_maximum_fusion.2), channel_id=1, source_target_pairs={{0,1},{1,0},{2,3},{3,2},{4,5},{5,4},{6,7},{7,6},{8,9},{9,8},{10,11... | collective-permute-start | bytes 884744 | tf_op jit(solution)/shard_map/ppermute | solution.py:24
  10.3 0.5 convolution_bitcast_fusion
  10.8 0.5 %convolution_bitcast_fusion.1 = f32[128]{0:T(128)S(1)} fusion(s32[128]{0:T(128)S(1)} %fusion.77, f32[128]{0:T(128)S(1)} %copy-done), kind=kOutput, calls=%fused_computation.5 | convolution fusion | flops 425984 | bytes 1536 | tf_op jit(solution)/shard_map/dot_general | solution.py:66
  11.3 0.2 copy.105
  11.6 0.1 copy.118
  11.6 0.1 convert_element_type.91
  11.8 0.1 copy.106
  12.0 0.1 copy.107
  12.3 0.1 copy.110
  12.5 0.1 fusion.12
  12.6 0.1 copy.112
  12.8 0.1 stack.70
  12.9 0.1 stack.69
  13.1 0.2 copy.116
  13.3 0.3 reshape.584
  13.5 2.7 %collective-permute-start.1 = (bf16[8,4096]{1,0:T(8,128)(2,1)S(1)}, bf16[8,4096]{1,0:T(8,128)(2,1)S(1)}, u32[]{:S(2)}, u32[]{:S(2)}) collective-permute-start(bf16[8,4096]{1,0:T(8,128)(2,1)S(1)} %reshape.584), channel_id=1, source_target_pairs={{0,2},{2,0},{1,3},{3,1},{4,6},{6,4},{5,7},{7,5},{8,10},{10,8},{9,1... | collective-permute-start | bytes 196616 | tf_op jit(solution)/shard_map/ppermute | solution.py:288
  16.3 0.2 copy.119
  16.5 2.3 %collective-permute-done.1 = bf16[8,4096]{1,0:T(8,128)(2,1)S(1)} collective-permute-done((bf16[8,4096]{1,0:T(8,128)(2,1)S(1)}, bf16[8,4096]{1,0:T(8,128)(2,1)S(1)}, u32[]{:S(2)}, u32[]{:S(2)}) %collective-permute-start.1) | collective-permute-done | bytes 65568 | tf_op jit(solution)/shard_map/ppermute | solution.py:288
  18.9 0.2 stack_reshape.6
  19.0 0.1 copy.117
  19.3 0.1 pad_maximum_fusion.7
  19.4 0.2 copy.120
  19.6 2.9 %collective-permute-start.2 = (bf16[8,8320]{1,0:T(8,128)(2,1)S(1)}, bf16[8,8320]{1,0:T(8,128)(2,1)S(1)}, u32[]{:S(2)}, u32[]{:S(2)}) collective-permute-start(bf16[8,8320]{1,0:T(8,128)(2,1)S(1)} %bitcast.118), channel_id=1, source_target_pairs={{0,16},{4,20},{8,24},{12,28},{16,0},{20,4},{24,8},{28,12},{1,17},{... | collective-permute-start | bytes 399368 | tf_op jit(solution)/shard_map/ppermute | solution.py:177
  22.5 6.2 %collective-permute-done.2 = bf16[8,8320]{1,0:T(8,128)(2,1)S(1)} collective-permute-done((bf16[8,8320]{1,0:T(8,128)(2,1)S(1)}, bf16[8,8320]{1,0:T(8,128)(2,1)S(1)}, u32[]{:S(2)}, u32[]{:S(2)}) %collective-permute-start.2) | collective-permute-done | bytes 133152 | tf_op jit(solution)/shard_map/ppermute | solution.py:177
  28.7 0.1 pad_maximum_fusion.8
  28.8 1.5 %collective-permute-start.5 = (bf16[2,4,8320]{2,1,0:T(4,128)(2,1)S(1)}, bf16[2,4,8320]{2,1,0:T(4,128)(2,1)S(1)}, u32[]{:S(2)}, u32[]{:S(2)}) collective-permute-start(bf16[2,4,8320]{2,1,0:T(4,128)(2,1)S(1)} %get-tuple-element.15), channel_id=1, source_target_pairs={{0,4},{4,0},{8,12},{12,8},{16,20},{20,16},{24,28},{28,24},{1,5},{5... | collective-permute-start | bytes 399368 | tf_op jit(solution)/shard_map/ppermute | solution.py:186
  30.4 0.7 %collective-permute-start.3 = (bf16[2,4,8320]{2,1,0:T(4,128)(2,1)S(1)}, bf16[2,4,8320]{2,1,0:T(4,128)(2,1)S(1)}, u32[]{:S(2)}, u32[]{:S(2)}) collective-permute-start(bf16[2,4,8320]{2,1,0:T(4,128)(2,1)S(1)} %get-tuple-element.16), channel_id=1, source_target_pairs={{0,8},{4,12},{8,0},{12,4},{16,24},{20,28},{24,16},{28,20},{1,9},{5... | collective-permute-start | bytes 399368 | tf_op jit(solution)/shard_map/ppermute | solution.py:186
  31.0 2.8 %collective-permute-done.5 = bf16[2,4,8320]{2,1,0:T(4,128)(2,1)S(1)} collective-permute-done((bf16[2,4,8320]{2,1,0:T(4,128)(2,1)S(1)}, bf16[2,4,8320]{2,1,0:T(4,128)(2,1)S(1)}, u32[]{:S(2)}, u32[]{:S(2)}) %collective-permute-start.5) | collective-permute-done | bytes 133152 | tf_op jit(solution)/shard_map/ppermute | solution.py:186
  33.8 0.2 fusion.85
  34.1 1.1 %collective-permute-start.6 = (bf16[2,2,4,8320]{3,2,0,1:T(4,128)(2,1)S(1)}, bf16[2,2,4,8320]{3,2,0,1:T(4,128)(2,1)S(1)}, u32[]{:S(2)}, u32[]{:S(2)}) collective-permute-start(bf16[2,2,4,8320]{3,2,0,1:T(4,128)(2,1)S(1)} %get-tuple-element.14), channel_id=1, source_target_pairs={{0,8},{4,12},{8,0},{12,4},{16,24},{20,28},{24,16},{28,20},{1,9},{5... | collective-permute-start | bytes 798728 | tf_op jit(solution)/shard_map/ppermute | solution.py:186
  35.2 0.3 collective-permute-done.3
  35.5 0.2 fusion.86
  35.7 1.3 %collective-permute-start.4 = (bf16[2,2,4,8320]{3,2,0,1:T(4,128)(2,1)S(1)}, bf16[2,2,4,8320]{3,2,0,1:T(4,128)(2,1)S(1)}, u32[]{:S(2)}, u32[]{:S(2)}) collective-permute-start(bf16[2,2,4,8320]{3,2,0,1:T(4,128)(2,1)S(1)} %get-tuple-element.18), channel_id=1, source_target_pairs={{0,4},{4,0},{8,12},{12,8},{16,20},{20,16},{24,28},{28,24},{1,5},{5... | collective-permute-start | bytes 798728 | tf_op jit(solution)/shard_map/ppermute | solution.py:186
  37.0 4.1 %collective-permute-done.6 = bf16[2,2,4,8320]{3,2,0,1:T(4,128)(2,1)S(1)} collective-permute-done((bf16[2,2,4,8320]{3,2,0,1:T(4,128)(2,1)S(1)}, bf16[2,2,4,8320]{3,2,0,1:T(4,128)(2,1)S(1)}, u32[]{:S(2)}, u32[]{:S(2)}) %collective-permute-start.6) | collective-permute-done | bytes 266272 | tf_op jit(solution)/shard_map/ppermute | solution.py:186
  41.1 0.4 pad_maximum_fusion.1
  41.5 0.2 copy.123
  41.6 0.2 concatenate.61
  41.9 0.8 %collective-permute-done.4 = bf16[2,2,4,8320]{3,2,0,1:T(4,128)(2,1)S(1)} collective-permute-done((bf16[2,2,4,8320]{3,2,0,1:T(4,128)(2,1)S(1)}, bf16[2,2,4,8320]{3,2,0,1:T(4,128)(2,1)S(1)}, u32[]{:S(2)}, u32[]{:S(2)}) %collective-permute-start.4) | collective-permute-done | bytes 266272 | tf_op jit(solution)/shard_map/ppermute | solution.py:186
  42.7 0.4 pad_maximum_fusion
  43.1 0.2 copy.122
  43.3 0.2 concatenate.60
  43.5 0.2 copy_dynamic-update-slice_fusion.1
  43.7 0.2 copy_dynamic-update-slice_fusion
  44.0 0.1 copy.127
  44.1 0.1 multiply_reduce_fusion
  44.3 0.1 copy.140
  44.3 0.1 add_select_fusion.5
  44.4 0.1 copy.129
  44.5 0.1 eq.70
  44.7 0.1 copy.130
  44.8 0.1 eq.73
  45.0 0.3 fusion
  45.2 0.8 %bitcast_convert_fusion = bf16[64,128,128]{1,2,0:T(8,128)(2,1)S(1)} fusion(bf16[8,8,65,128]{3,0,1,2:T(8,128)(2,1)S(1)} %copy_dynamic-update-slice_fusion, bf16[128,8,8]{0,2,1:T(8,128)(2,1)S(1)} %fusion), kind=kOutput, calls=%fused_computation | convolution fusion | flops 135266304 | bytes 3178496 | tf_op jit(solution)/shard_map/rsc,scbq->brq/dot_general | solution.py:329
  46.0 0.1 fusion.87
  46.2 1.2 %convolution_multiply_fusion = f32[64,32,128]{2,1,0:T(8,128)S(1)} fusion(bf16[64,128,128]{1,2,0:T(8,128)(2,1)S(1)} %bitcast_convert_fusion, bf16[64,16,64]{2,1,0:T(8,128)(2,1)S(1)} %get-tuple-element.20, bf16[64,16,64]{2,1,0:T(8,128)(2,1)S(1)} %get-tuple-element.19, bf16[64,16,128]{2,1,0:T(8,128)(2,1)S(1)} %dynamic-slice_bitcast_fusion), kind=kOutput, calls=%fused_computation.1 | convolution fusion | flops 68943872 | bytes 3670016 | tf_op jit(solution)/shard_map/bpq,bjq->bpj/dot_general | solution.py:337
  47.4 1.1 %copy.152 = f32[64,2,16,128]{3,2,0,1:T(8,128)} copy(f32[64,2,16,128]{3,2,1,0:T(8,128)S(1)} %bitcast.114) | data formatting | bytes 2097152 | tf_op jit(solution)/shard_map/div | solution.py:339
  (40 shorter events, 0.9 us)
Async XLA Ops:
  0.0 10.3 %copy-start = (f32[128]{0:T(128)S(1)}, f32[128]{0:T(128)}, u32[]{:S(2)}) copy-start(f32[128]{0:T(128)} %param.5) | copy-start | bytes 1540
  9.7 1.8 %copy-start.1 = (s32[1,8,2]{1,2,0:T(2,128)S(1)}, s32[1,8,2]{1,2,0:T(2,128)}, u32[]{:S(2)}) copy-start(s32[1,8,2]{1,2,0:T(2,128)} %param.7) | copy-start | bytes 196
  9.7 1.8 %copy-start.2 = (s32[1,8,2]{1,2,0:T(2,128)S(1)}, s32[1,8,2]{1,2,0:T(2,128)}, u32[]{:S(2)}) copy-start(s32[1,8,2]{1,2,0:T(2,128)} %param.6) | copy-start | bytes 196
  9.8 2.2 %collective-permute-start = (f32[144,2,256]{0,2,1:T(8,128)S(1)}, f32[144,2,256]{0,2,1:T(8,128)S(1)}, u32[]{:S(2)}, u32[]{:S(2)}) collective-permute-start(f32[144,2,256]{0,2,1:T(8,128)S(1)} %pad_maximum_fusion.2), channel_id=1, source_target_pairs={{0,1},{1,0},{2,3},{3,2},{4,5},{5,4},{6,7},{7,6},{8,9},{9,8},{10,11... | collective-permute-start | bytes 884744 | tf_op jit(solution)/shard_map/ppermute | solution.py:24
  13.5 5.3 %collective-permute-start.1 = (bf16[8,4096]{1,0:T(8,128)(2,1)S(1)}, bf16[8,4096]{1,0:T(8,128)(2,1)S(1)}, u32[]{:S(2)}, u32[]{:S(2)}) collective-permute-start(bf16[8,4096]{1,0:T(8,128)(2,1)S(1)} %reshape.584), channel_id=1, source_target_pairs={{0,2},{2,0},{1,3},{3,1},{4,6},{6,4},{5,7},{7,5},{8,10},{10,8},{9,1... | collective-permute-start | bytes 196616 | tf_op jit(solution)/shard_map/ppermute | solution.py:288
  19.6 9.1 %collective-permute-start.2 = (bf16[8,8320]{1,0:T(8,128)(2,1)S(1)}, bf16[8,8320]{1,0:T(8,128)(2,1)S(1)}, u32[]{:S(2)}, u32[]{:S(2)}) collective-permute-start(bf16[8,8320]{1,0:T(8,128)(2,1)S(1)} %bitcast.118), channel_id=1, source_target_pairs={{0,16},{4,20},{8,24},{12,28},{16,0},{20,4},{24,8},{28,12},{1,17},{... | collective-permute-start | bytes 399368 | tf_op jit(solution)/shard_map/ppermute | solution.py:177
  28.8 5.1 %collective-permute-start.5 = (bf16[2,4,8320]{2,1,0:T(4,128)(2,1)S(1)}, bf16[2,4,8320]{2,1,0:T(4,128)(2,1)S(1)}, u32[]{:S(2)}, u32[]{:S(2)}) collective-permute-start(bf16[2,4,8320]{2,1,0:T(4,128)(2,1)S(1)} %get-tuple-element.15), channel_id=1, source_target_pairs={{0,4},{4,0},{8,12},{12,8},{16,20},{20,16},{24,28},{28,24},{1,5},{5... | collective-permute-start | bytes 399368 | tf_op jit(solution)/shard_map/ppermute | solution.py:186
  30.4 5.1 %collective-permute-start.3 = (bf16[2,4,8320]{2,1,0:T(4,128)(2,1)S(1)}, bf16[2,4,8320]{2,1,0:T(4,128)(2,1)S(1)}, u32[]{:S(2)}, u32[]{:S(2)}) collective-permute-start(bf16[2,4,8320]{2,1,0:T(4,128)(2,1)S(1)} %get-tuple-element.16), channel_id=1, source_target_pairs={{0,8},{4,12},{8,0},{12,4},{16,24},{20,28},{24,16},{28,20},{1,9},{5... | collective-permute-start | bytes 399368 | tf_op jit(solution)/shard_map/ppermute | solution.py:186
  34.1 7.0 %collective-permute-start.6 = (bf16[2,2,4,8320]{3,2,0,1:T(4,128)(2,1)S(1)}, bf16[2,2,4,8320]{3,2,0,1:T(4,128)(2,1)S(1)}, u32[]{:S(2)}, u32[]{:S(2)}) collective-permute-start(bf16[2,2,4,8320]{3,2,0,1:T(4,128)(2,1)S(1)} %get-tuple-element.14), channel_id=1, source_target_pairs={{0,8},{4,12},{8,0},{12,4},{16,24},{20,28},{24,16},{28,20},{1,9},{5... | collective-permute-start | bytes 798728 | tf_op jit(solution)/shard_map/ppermute | solution.py:186
  35.7 7.0 %collective-permute-start.4 = (bf16[2,2,4,8320]{3,2,0,1:T(4,128)(2,1)S(1)}, bf16[2,2,4,8320]{3,2,0,1:T(4,128)(2,1)S(1)}, u32[]{:S(2)}, u32[]{:S(2)}) collective-permute-start(bf16[2,2,4,8320]{3,2,0,1:T(4,128)(2,1)S(1)} %get-tuple-element.18), channel_id=1, source_target_pairs={{0,4},{4,0},{8,12},{12,8},{16,20},{20,16},{24,28},{28,24},{1,5},{5... | collective-permute-start | bytes 798728 | tf_op jit(solution)/shard_map/ppermute | solution.py:186

commit v13 on v12

--- a/solution.py
+++ b/solution.py
@@ -286,18 +286,20 @@
         pairs = [(source, (source + shift) % seg_count) for source in range(seg_count)]
         flat = outgoing.reshape(sections, -1)
         pieces.append(lax.ppermute(flat, "seg", pairs).reshape(outgoing.shape))
-    local = jnp.stack(pieces, axis=3).reshape(sections, block_bins, -1)
     all_segs = seg_dev * seg_count
-    table_width = local.shape[-1]
     table = jnp.concatenate([send_list[0], recv_row[0]], axis=1).reshape(-1)
     table_len = table.shape[0]
-    slab = jnp.pad(table.astype(jnp.bfloat16), (0, sections * table_width - table_len))
-    carried = jnp.concatenate([local, slab.reshape(sections, 1, table_width)], axis=1)
+    piece_width = block_bins * 2 * seg_dev
+    slab_width = 128
+    slab = jnp.pad(table.astype(jnp.bfloat16), (0, sections * slab_width - table_len))
     blk_rank = lax.axis_index("blk")
-    everything = gather_blocks(carried.reshape(sections, -1), owners_count, blk_rank)
-    everything = everything.reshape(owners_count, sections, block_bins + 1, table_width)
-    gathered = everything[:, :, :block_bins]
-    table_part = everything[:, :, block_bins].reshape(owners_count, -1)[:, :table_len]
+    moved = []
+    for index, piece in enumerate(pieces):
+        flat = piece.reshape(sections, -1)
+        if index == 0:
+            flat = jnp.concatenate([flat, slab.reshape(sections, slab_width)], axis=1)
+        moved.append(gather_blocks(flat, owners_count, blk_rank))
+    table_part = moved[0][:, :, piece_width:].reshape(owners_count, -1)[:, :table_len]
     table_part = table_part.astype(jnp.int32).reshape(owners_count, owners_count, 2 * capacity)
     position_ids = jnp.arange(owners_count, dtype=jnp.int32)
     if owners_count & (owners_count - 1) == 0:
@@ -326,15 +328,19 @@
         "er,ec->rc", row_hot, chan_hot, preferred_element_type=jnp.float32
     ).astype(jnp.bfloat16)
     selector = selector.reshape(rows_count, owners_count, sections)
-    routed = jnp.einsum(
-        "rsc,scbq->brq", selector, gathered, preferred_element_type=jnp.float32
-    ).astype(jnp.bfloat16)
-    own = lax.dynamic_slice_in_dim(routed, blk_rank * OWN, OWN, axis=1)
-    own_re = own[..., :all_segs]
-    own_im = own[..., all_segs:]
-    rotated = jnp.concatenate([own_im, -own_re], axis=-1)
-    lhs = jnp.concatenate([own, rotated], axis=1)
-    cross = jnp.einsum("bpq,bjq->bpj", lhs, routed, preferred_element_type=jnp.float32)
+    cross = None
+    for chain in moved:
+        data = chain[:, :, :piece_width].reshape(owners_count, sections, block_bins, 2 * seg_dev)
+        routed = jnp.einsum(
+            "rsc,scbq->brq", selector, data, preferred_element_type=jnp.float32
+        ).astype(jnp.bfloat16)
+        own = lax.dynamic_slice_in_dim(routed, blk_rank * OWN, OWN, axis=1)
+        own_re = own[..., :seg_dev]
+        own_im = own[..., seg_dev:]
+        rotated = jnp.concatenate([own_im, -own_re], axis=-1)
+        lhs = jnp.concatenate([own, rotated], axis=1)
+        part = jnp.einsum("bpq,bjq->bpj", lhs, routed, preferred_element_type=jnp.float32)
+        cross = part if cross is None else cross + part
     cross = cross.reshape(block_bins, 2, OWN, rows_count)
     return jnp.transpose(cross, (1, 0, 2, 3)) / jnp.float32(all_segs)
 

time: 48.7 us -> 49.5 us (1.016)
  waiting for transfers between devices: 16.5 us -> 6.14 us
  starting transfers between devices: 10.8 us -> 15.9 us
  local copies, waits for them, and re-layouts: 5.67 us -> 8.6 us
  other arithmetic: 5.42 us -> 6.97 us
  matrix products: 3.27 us -> 4.77 us
    ppermute x4 -> x8, waiting for transfers between devices: 7.95 us -> 1.79 us  [gather_blocks(): arrived = lax.ppermute(part, 'blk', pairs)]
    ppermute x4 -> x8, starting transfers between devices: 4.64 us -> 9.87 us  [gather_blocks(): arrived = lax.ppermute(part, 'blk', pairs)]
    ppermute x1 -> x2, waiting for transfers between devices: 6.2 us -> 1.65 us  [gather_blocks(): held = jnp.stack([carried, lax.ppermute(carried, 'blk', pairs)], axis=0)]
    dynamic_slice x0 -> x1, other arithmetic: none -> 1.39 us  [per_device(): lax.dynamic_index_in_dim(whitened, (seg_rank + shift) % seg_count, axis=0...]
    reshape x2 -> x4, local copies, waits for them, and re-layouts: 0.24 us -> 1.62 us  [the longest x1 1.13 us: per_device(): chain[:, :, :piece_width]]
    ppermute x1, starting transfers between devices: 2.74 us -> 1.56 us  [per_device(): pieces.append(lax.ppermute(flat, 'seg', pairs).reshape(outgoing.shape))]
    ppermute x1 -> x2, starting transfers between devices: 2.89 us -> 3.9 us  [gather_blocks(): held = jnp.stack([carried, lax.ppermute(carried, 'blk', pairs)], axis=0)]
    another operation x3 -> x4, local copies, waits for them, and re-layouts: 0.24 us -> 1.2 us  [per_device(): whitened = jnp.stack([white_re, white_im], axis=1).astype(jnp.bfloat16)]
  transfers between devices with their start and end apart: 7 -> 12, of which waited for: 6 -> 6; matrix products, arithmetic and copies ran while one was open for 6% -> 19% of each run, Pallas kernels for 0% -> 0%
where the time goes in v13:
time: 49.5 us; the launch traced here: 49.2 us
  starting transfers between devices  15.9 us (32%)
  local copies, waits for them, and re-layouts  8.6 us (17%)
  other arithmetic  6.97 us (14%)
  Pallas kernels  6.39 us (13%)
  waiting for transfers between devices  6.14 us (12%)
  matrix products  4.77 us (10%)
  between operations  0.52 us (1%)
    ppermute x8, starting transfers between devices, gather_blocks(): arrived = lax.ppermute(part, 'blk', pairs)  9.87 us
    pallas_call x1, Pallas kernels, dft_fused(): pl.pallas_call(dft_kernel, grid=(count // chunk,), in_specs=[pl.BlockSpec...  6.39 us
    ppermute x2, starting transfers between devices, gather_blocks(): held = jnp.stack([carried, lax.ppermute(carried, 'blk', pairs)], axis=0)  3.9 us
    ppermute x1, waiting for transfers between devices, per_device(): pieces.append(lax.ppermute(flat, 'seg', pairs).reshape(outgoing.shape))  2.69 us
    dot_general x2, matrix products, per_device(): jnp.einsum('bpq,bjq->bpj', lhs, routed, preferred_element_type=jnp.float32)  2.04 us
    ppermute x8, waiting for transfers between devices, gather_blocks(): arrived = lax.ppermute(part, 'blk', pairs)  1.79 us
    ppermute x2, waiting for transfers between devices, gather_blocks(): held = jnp.stack([carried, lax.ppermute(carried, 'blk', pairs)], axis=0)  1.65 us
    concatenate x4, local copies, waits for them, and re-layouts, gather_blocks(): return jnp.concatenate(results, axis=1)  1.57 us
  transfers between devices with their start and end apart: 12, of which 6 were waited for; matrix products, arithmetic and copies ran while one was open for 19% of the time, Pallas kernels for 0%

profile of v13, /device:TPU:0, one launch (start us, length us, event | category | flops | bytes accessed | tf_op | source)
XLA Modules:
  0.0 49.2 jit_solution(11344960117942429969)
XLA Ops:
  0.1 0.2 fusion.77
  0.3 0.7 %negate_bitcast_fusion = (f32[64,256]{1,0:T(8,128)}, f32[64,256]{1,0:T(8,128)}) fusion(f32[8,256]{1,0:T(8,128)S(1)} %get-tuple-element.53, f32[8,256]{1,0:T(8,128)S(1)} %get-tuple-element.55, f32[8,256]{1,0:T(8,128)S(1)} %get-tuple-element.54, f32[8,256]{1,0:T(8,128)S(1)} %get-tuple-element.56), kind=kLoop, calls=%fused_computation.115 | loop fusion | flops 114688 | bytes 163840 | tf_op jit(solution)/shard_map/neg | solution.py:136
  1.0 0.7 %add_multiply_fusion = (f32[8,16,256]{2,1,0:T(8,128)}, f32[8,16,256]{2,1,0:T(8,128)}) fusion(f32[16,256]{1,0:T(8,128)S(1)} %get-tuple-element.58, f32[8,256]{1,0:T(8,128)S(1)} %get-tuple-element.48, f32[16,256]{1,0:T(8,128)S(1)} %get-tuple-element.57, f32[8,256]{1,0:T(8,128)S(1)} %get-tuple-element.47), kind=kLoop, calls=%fused_computation.91 | loop fusion | flops 262144 | bytes 311296 | tf_op jit(solution)/shard_map/mul | solution.py:141
  1.7 6.4 %shard_map.46 = (f32[256,256]{1,0:T(8,128)}, f32[256,256]{1,0:T(8,128)}) custom-call(bf16[256,8192]{1,0:T(8,128)(2,1)} %bitcast.134, f32[64,256]{1,0:T(8,128)} %get-tuple-element.40.cos_a_ref, f32[64,256]{1,0:T(8,128)} %get-tuple-element.39.nsin_a_ref, f32[128,256]{1,0:T(8,128)} %bitcast.140, f32[128,256]{1,0:T(8,128)} %bitcast.139), custom_call_target="tpu_custom_call" | custom-call | tf_op jit(solution)/shard_map/pallas_call | solution.py:145
  8.1 1.3 %broadcast_select_fusion = (f32[128,2,256]{0,2,1:T(8,128)S(1)}, f32[128,2,256]{0,2,1:T(8,128)S(1)}) fusion(pred[]{:T(512)S(6)} %eq.66, f32[256,1,256]{0,2,1:T(8,128)} %bitcast.149, f32[256,1,256]{0,2,1:T(8,128)} %bitcast.148), kind=kLoop, calls=%fused_computation.93 | loop fusion | flops 327680 | bytes 1048577 | tf_op jit(solution)/shard_map/jit(_where)/select_n | solution.py:220
  9.4 0.1 copy.110
  9.6 0.1 copy.111
  9.7 0.5 %collective-permute-start = (f32[144,2,256]{0,2,1:T(8,128)S(1)}, f32[144,2,256]{0,2,1:T(8,128)S(1)}, u32[]{:S(2)}, u32[]{:S(2)}) collective-permute-start(f32[144,2,256]{0,2,1:T(8,128)S(1)} %pad_maximum_fusion), channel_id=1, source_target_pairs={{0,1},{1,0},{2,3},{3,2},{4,5},{5,4},{6,7},{7,6},{8,9},{9,8},{10,11... | collective-permute-start | bytes 884744 | tf_op jit(solution)/shard_map/ppermute | solution.py:24
  10.3 0.5 convolution_bitcast_fusion
  10.8 0.5 %convolution_bitcast_fusion.1 = f32[128]{0:T(128)S(1)} fusion(s32[128]{0:T(128)S(1)} %fusion.94, f32[128]{0:T(128)S(1)} %copy-done), kind=kOutput, calls=%fused_computation.6 | convolution fusion | flops 425984 | bytes 1536 | tf_op jit(solution)/shard_map/dot_general | solution.py:66
  11.3 0.2 copy.112
  11.8 0.1 copy.113
  12.5 0.1 fusion.26
  12.9 0.4 copy.122
  13.4 0.6 %copy.121 = bf16[2,64,1,8,32]{4,2,1,3,0:T(2,128)(2,1)S(1)} copy(bf16[2,64,1,8,32]{1,0,4,3,2:T(2,128)(2,1)S(1)} %stack.108) | data formatting | bytes 131072 | tf_op jit(solution)/shard_map/stack | solution.py:277
  14.0 1.4 %fusion.21 = (bf16[1,8,64,2,32]{4,3,2,1,0:T(2,128)(2,1)S(1)}, bf16[1,8,64,2,32]{4,3,2,1,0:T(2,128)(2,1)S(1)}) fusion(s32[]{:T(128)S(6)} %select_n.253, bf16[2,64,1,8,32]{4,2,1,3,0:T(2,128)(2,1)S(1)} %copy.122, bf16[2,64,1,8,32]{4,2,1,3,0:T(2,128)(2,1)S(1)} %copy.121, s32[]{:T(128)S(6)} %select_n.248), kind=kLoop, calls=%fused_computation.54 | loop fusion | flops 262144 | bytes 262152 | tf_op jit(solution)/shard_map/jit(dynamic_index_in_dim)/dynamic_slice | solution.py:283
  15.4 0.3 reshape.593
  15.7 3.8 %collective-permute-start.1 = (bf16[8,4224]{1,0:T(8,128)(2,1)S(1)}, bf16[8,4224]{1,0:T(8,128)(2,1)S(1)}, u32[]{:S(2)}, u32[]{:S(2)}) collective-permute-start(bf16[8,4224]{1,0:T(8,128)(2,1)S(1)} %get-tuple-element.35), channel_id=1, source_target_pairs={{0,16},{4,20},{8,24},{12,28},{16,0},{20,4},{24,8},{28,12},{1,17},{... | collective-permute-start | bytes 202760 | tf_op jit(solution)/shard_map/ppermute | solution.py:177
  19.5 0.3 reshape.600
  19.8 1.6 %collective-permute-start.6 = (bf16[8,4096]{1,0:T(8,128)(2,1)S(1)}, bf16[8,4096]{1,0:T(8,128)(2,1)S(1)}, u32[]{:S(2)}, u32[]{:S(2)}) collective-permute-start(bf16[8,4096]{1,0:T(8,128)(2,1)S(1)} %reshape.600), channel_id=1, source_target_pairs={{0,2},{2,0},{1,3},{3,1},{4,6},{6,4},{5,7},{7,5},{8,10},{10,8},{9,1... | collective-permute-start | bytes 196616 | tf_op jit(solution)/shard_map/ppermute | solution.py:288
  21.4 2.7 %collective-permute-done.6 = bf16[8,4096]{1,0:T(8,128)(2,1)S(1)} collective-permute-done((bf16[8,4096]{1,0:T(8,128)(2,1)S(1)}, bf16[8,4096]{1,0:T(8,128)(2,1)S(1)}, u32[]{:S(2)}, u32[]{:S(2)}) %collective-permute-start.6) | collective-permute-done | bytes 65568 | tf_op jit(solution)/shard_map/ppermute | solution.py:288
  24.3 1.9 %collective-permute-start.2 = (bf16[2,4,4224]{2,1,0:T(4,128)(2,1)S(1)}, bf16[2,4,4224]{2,1,0:T(4,128)(2,1)S(1)}, u32[]{:S(2)}, u32[]{:S(2)}) collective-permute-start(bf16[2,4,4224]{2,1,0:T(4,128)(2,1)S(1)} %get-tuple-element.26), channel_id=1, source_target_pairs={{0,8},{4,12},{8,0},{12,4},{16,24},{20,28},{24,16},{28,20},{1,9},{5... | collective-permute-start | bytes 202760 | tf_op jit(solution)/shard_map/ppermute | solution.py:186
  26.1 1.5 %collective-permute-start.4 = (bf16[2,4,4224]{2,1,0:T(4,128)(2,1)S(1)}, bf16[2,4,4224]{2,1,0:T(4,128)(2,1)S(1)}, u32[]{:S(2)}, u32[]{:S(2)}) collective-permute-start(bf16[2,4,4224]{2,1,0:T(4,128)(2,1)S(1)} %get-tuple-element.25), channel_id=1, source_target_pairs={{0,4},{4,0},{8,12},{12,8},{16,20},{20,16},{24,28},{28,24},{1,5},{5... | collective-permute-start | bytes 202760 | tf_op jit(solution)/shard_map/ppermute | solution.py:186
  27.7 1.6 %collective-permute-done.7 = bf16[8,4096]{1,0:T(8,128)(2,1)S(1)} collective-permute-done((bf16[8,4096]{1,0:T(8,128)(2,1)S(1)}, bf16[8,4096]{1,0:T(8,128)(2,1)S(1)}, u32[]{:S(2)}, u32[]{:S(2)}) %collective-permute-start.7) | collective-permute-done | bytes 65568 | tf_op jit(solution)/shard_map/ppermute | solution.py:177
  29.4 1.7 %collective-permute-start.10 = (bf16[2,4,4096]{2,1,0:T(4,128)(2,1)S(1)}, bf16[2,4,4096]{2,1,0:T(4,128)(2,1)S(1)}, u32[]{:S(2)}, u32[]{:S(2)}) collective-permute-start(bf16[2,4,4096]{2,1,0:T(4,128)(2,1)S(1)} %get-tuple-element.32), channel_id=1, source_target_pairs={{0,4},{4,0},{8,12},{12,8},{16,20},{20,16},{24,28},{28,24},{1,5},{5... | collective-permute-start | bytes 196616 | tf_op jit(solution)/shard_map/ppermute | solution.py:186
  31.0 1.5 %collective-permute-start.8 = (bf16[2,4,4096]{2,1,0:T(4,128)(2,1)S(1)}, bf16[2,4,4096]{2,1,0:T(4,128)(2,1)S(1)}, u32[]{:S(2)}, u32[]{:S(2)}) collective-permute-start(bf16[2,4,4096]{2,1,0:T(4,128)(2,1)S(1)} %get-tuple-element.31), channel_id=1, source_target_pairs={{0,8},{4,12},{8,0},{12,4},{16,24},{20,28},{24,16},{28,20},{1,9},{5... | collective-permute-start | bytes 196616 | tf_op jit(solution)/shard_map/ppermute | solution.py:186
  32.5 0.1 fusion.108
  32.6 0.6 %collective-permute-start.3 = (bf16[2,2,4,4224]{3,2,0,1:T(4,128)(2,1)S(1)}, bf16[2,2,4,4224]{3,2,0,1:T(4,128)(2,1)S(1)}, u32[]{:S(2)}, u32[]{:S(2)}) collective-permute-start(bf16[2,2,4,4224]{3,2,0,1:T(4,128)(2,1)S(1)} %get-tuple-element.28), channel_id=1, source_target_pairs={{0,4},{4,0},{8,12},{12,8},{16,20},{20,16},{24,28},{28,24},{1,5},{5... | collective-permute-start | bytes 405512 | tf_op jit(solution)/shard_map/ppermute | solution.py:186
  33.2 0.1 fusion.107
  33.3 0.6 %collective-permute-start.5 = (bf16[2,2,4,4224]{3,2,0,1:T(4,128)(2,1)S(1)}, bf16[2,2,4,4224]{3,2,0,1:T(4,128)(2,1)S(1)}, u32[]{:S(2)}, u32[]{:S(2)}) collective-permute-start(bf16[2,2,4,4224]{3,2,0,1:T(4,128)(2,1)S(1)} %get-tuple-element.24), channel_id=1, source_target_pairs={{0,8},{4,12},{8,0},{12,4},{16,24},{20,28},{24,16},{28,20},{1,9},{5... | collective-permute-start | bytes 405512 | tf_op jit(solution)/shard_map/ppermute | solution.py:186
  33.8 0.5 collective-permute-done.10
  34.3 0.1 fusion.105
  34.4 1.1 %collective-permute-start.11 = (bf16[2,2,4,4096]{3,2,0,1:T(4,128)(2,1)S(1)}, bf16[2,2,4,4096]{3,2,0,1:T(4,128)(2,1)S(1)}, u32[]{:S(2)}, u32[]{:S(2)}) collective-permute-start(bf16[2,2,4,4096]{3,2,0,1:T(4,128)(2,1)S(1)} %get-tuple-element.34), channel_id=1, source_target_pairs={{0,8},{4,12},{8,0},{12,4},{16,24},{20,28},{24,16},{28,20},{1,9},{5... | collective-permute-start | bytes 393224 | tf_op jit(solution)/shard_map/ppermute | solution.py:186
  35.6 0.5 collective-permute-done.8
  36.0 0.1 fusion.106
  36.2 1.1 %collective-permute-start.9 = (bf16[2,2,4,4096]{3,2,0,1:T(4,128)(2,1)S(1)}, bf16[2,2,4,4096]{3,2,0,1:T(4,128)(2,1)S(1)}, u32[]{:S(2)}, u32[]{:S(2)}) collective-permute-start(bf16[2,2,4,4096]{3,2,0,1:T(4,128)(2,1)S(1)} %get-tuple-element.30), channel_id=1, source_target_pairs={{0,4},{4,0},{8,12},{12,8},{16,20},{20,16},{24,28},{28,24},{1,5},{5... | collective-permute-start | bytes 393224 | tf_op jit(solution)/shard_map/ppermute | solution.py:186
  37.3 0.4 collective-permute-done.3
  37.7 0.2 pad_maximum_fusion.1
  38.0 0.4 collective-permute-done.5
  38.4 0.2 pad_maximum_fusion.2
  38.7 0.3 fusion.16
  38.9 1.1 %reshape.597 = bf16[8,8,64,64]{3,2,1,0:T(8,128)(2,1)S(1)} reshape(bf16[8,8,4096]{2,1,0:T(8,128)(2,1)S(1)} %fusion.16) | data formatting | bytes 1048576 | tf_op jit(solution)/shard_map/reshape | solution.py:333
  40.1 0.2 copy.144
  40.4 0.1 multiply_reduce_fusion
  40.7 0.1 copy.130
  40.8 0.1 eq.73
  40.9 0.1 copy.129
  41.1 0.1 eq.70
  41.2 0.3 convolution_convert_fusion
  41.5 0.8 %bitcast_convert_fusion.1 = bf16[64,64,128]{2,1,0:T(8,128)(2,1)S(1)} fusion(bf16[8,8,64,64]{3,2,1,0:T(8,128)(2,1)S(1)} %reshape.597, bf16[128,64]{0,1:T(8,128)(2,1)S(1)} %convolution_convert_fusion), kind=kOutput, calls=%fused_computation.1 | convolution fusion | flops 67633152 | bytes 1589248 | tf_op jit(solution)/shard_map/rsc,scbq->brq/dot_general | solution.py:334
  42.3 0.4 dynamic-slice_bitcast_fusion.1
  42.7 0.1 fusion.110
  42.8 1.0 %fusion.1 = f32[64,32,128]{2,1,0:T(8,128)S(1)} fusion(bf16[64,64,128]{2,1,0:T(8,128)(2,1)S(1)} %bitcast_convert_fusion.1, bf16[64,16,32]{1,2,0:T(8,128)(2,1)S(1)} %get-tuple-element.14, bf16[64,16,32]{1,2,0:T(8,128)(2,1)S(1)} %get-tuple-element.13, bf16[64,16,64]{1,2,0:T(8,128)(2,1)S(1)} %dynamic-slice_bitcast_fusion.1), kind=kOutput, calls=%fused_computation.7 | convolution fusion | flops 34340864 | bytes 2359296 | tf_op jit(solution)/shard_map/bpq,bjq->bpj/dot_general | solution.py:342
  43.9 0.2 pad_maximum_fusion.5
  44.1 0.4 concatenate.73
  44.6 0.3 copy.136
  45.0 0.2 pad_maximum_fusion.4
  45.2 0.4 concatenate.72
  45.7 0.3 copy.135
  46.0 0.6 %bitcast_convert_fusion = bf16[64,64,128]{2,1,0:T(8,128)(2,1)S(1)} fusion(bf16[8,4,64,64]{3,0,1,2:T(8,128)(2,1)S(1)} %copy.136, bf16[8,4,64,64]{3,0,1,2:T(8,128)(2,1)S(1)} %copy.135, bf16[128,8,8]{0,2,1:T(8,128)(2,1)S(1)} %bitcast.167), kind=kOutput, calls=%fused_computation | convolution fusion | flops 67895296 | bytes 1589248 | tf_op jit(solution)/shard_map/rsc,scbq->brq/dot_general | solution.py:334
  46.7 0.4 dynamic-slice_bitcast_fusion
  47.0 0.1 fusion.109
  47.2 1.0 %fusion = f32[64,32,128]{2,1,0:T(8,128)S(1)} fusion(f32[64,32,128]{2,1,0:T(8,128)S(1)} %fusion.1, bf16[64,64,128]{2,1,0:T(8,128)(2,1)S(1)} %bitcast_convert_fusion, bf16[64,16,32]{1,2,0:T(8,128)(2,1)S(1)} %get-tuple-element.10, bf16[64,16,32]{1,2,0:T(8,128)(2,1)S(1)} %get-tuple-element.9, bf16[64,16,64]{1,2,0:T(8,128)(2,1)S(1)} %dynamic-slice_bitcast_fusion), kind=kOutput, calls=%fused_computation.3 | convolution fusion | flops 34865152 | bytes 3407872 | tf_op jit(solution)/shard_map/bpq,bjq->bpj/dot_general | solution.py:342
  48.2 1.1 %copy.159 = f32[64,2,16,128]{3,2,0,1:T(8,128)} copy(f32[64,2,16,128]{3,2,1,0:T(8,128)S(1)} %bitcast.133) | data formatting | bytes 2097152 | tf_op jit(solution)/shard_map/div | solution.py:345
  (58 shorter events, 2.2 us)
Async XLA Ops:
  0.0 10.3 %copy-start = (f32[128]{0:T(128)S(1)}, f32[128]{0:T(128)}, u32[]{:S(2)}) copy-start(f32[128]{0:T(128)} %param.5) | copy-start | bytes 1540
  8.1 3.4 %copy-start.1 = (s32[1,8,2]{1,2,0:T(2,128)S(1)}, s32[1,8,2]{1,2,0:T(2,128)}, u32[]{:S(2)}) copy-start(s32[1,8,2]{1,2,0:T(2,128)} %param.7) | copy-start | bytes 196
  8.1 3.4 %copy-start.2 = (s32[1,8,2]{1,2,0:T(2,128)S(1)}, s32[1,8,2]{1,2,0:T(2,128)}, u32[]{:S(2)}) copy-start(s32[1,8,2]{1,2,0:T(2,128)} %param.6) | copy-start | bytes 196
  9.7 2.3 %collective-permute-start = (f32[144,2,256]{0,2,1:T(8,128)S(1)}, f32[144,2,256]{0,2,1:T(8,128)S(1)}, u32[]{:S(2)}, u32[]{:S(2)}) collective-permute-start(f32[144,2,256]{0,2,1:T(8,128)S(1)} %pad_maximum_fusion), channel_id=1, source_target_pairs={{0,1},{1,0},{2,3},{3,2},{4,5},{5,4},{6,7},{7,6},{8,9},{9,8},{10,11... | collective-permute-start | bytes 884744 | tf_op jit(solution)/shard_map/ppermute | solution.py:24
  15.7 8.5 %collective-permute-start.1 = (bf16[8,4224]{1,0:T(8,128)(2,1)S(1)}, bf16[8,4224]{1,0:T(8,128)(2,1)S(1)}, u32[]{:S(2)}, u32[]{:S(2)}) collective-permute-start(bf16[8,4224]{1,0:T(8,128)(2,1)S(1)} %get-tuple-element.35), channel_id=1, source_target_pairs={{0,16},{4,20},{8,24},{12,28},{16,0},{20,4},{24,8},{28,12},{1,17},{... | collective-permute-start | bytes 202760 | tf_op jit(solution)/shard_map/ppermute | solution.py:177
  19.8 4.3 %collective-permute-start.6 = (bf16[8,4096]{1,0:T(8,128)(2,1)S(1)}, bf16[8,4096]{1,0:T(8,128)(2,1)S(1)}, u32[]{:S(2)}, u32[]{:S(2)}) collective-permute-start(bf16[8,4096]{1,0:T(8,128)(2,1)S(1)} %reshape.600), channel_id=1, source_target_pairs={{0,2},{2,0},{1,3},{3,1},{4,6},{6,4},{5,7},{7,5},{8,10},{10,8},{9,1... | collective-permute-start | bytes 196616 | tf_op jit(solution)/shard_map/ppermute | solution.py:288
  24.1 5.2 %collective-permute-start.7 = (bf16[8,4096]{1,0:T(8,128)(2,1)S(1)}, bf16[8,4096]{1,0:T(8,128)(2,1)S(1)}, u32[]{:S(2)}, u32[]{:S(2)}) collective-permute-start(bf16[8,4096]{1,0:T(8,128)(2,1)S(1)} %collective-permute-done.6), channel_id=1, source_target_pairs={{0,16},{4,20},{8,24},{12,28},{16,0},{20,4},{24,8},{28,12},{1,17},{... | collective-permute-start | bytes 196616 | tf_op jit(solution)/shard_map/ppermute | solution.py:177
  24.3 8.2 %collective-permute-start.2 = (bf16[2,4,4224]{2,1,0:T(4,128)(2,1)S(1)}, bf16[2,4,4224]{2,1,0:T(4,128)(2,1)S(1)}, u32[]{:S(2)}, u32[]{:S(2)}) collective-permute-start(bf16[2,4,4224]{2,1,0:T(4,128)(2,1)S(1)} %get-tuple-element.26), channel_id=1, source_target_pairs={{0,8},{4,12},{8,0},{12,4},{16,24},{20,28},{24,16},{28,20},{1,9},{5... | collective-permute-start | bytes 202760 | tf_op jit(solution)/shard_map/ppermute | solution.py:186
  26.1 7.0 %collective-permute-start.4 = (bf16[2,4,4224]{2,1,0:T(4,128)(2,1)S(1)}, bf16[2,4,4224]{2,1,0:T(4,128)(2,1)S(1)}, u32[]{:S(2)}, u32[]{:S(2)}) collective-permute-start(bf16[2,4,4224]{2,1,0:T(4,128)(2,1)S(1)} %get-tuple-element.25), channel_id=1, source_target_pairs={{0,4},{4,0},{8,12},{12,8},{16,20},{20,16},{24,28},{28,24},{1,5},{5... | collective-permute-start | bytes 202760 | tf_op jit(solution)/shard_map/ppermute | solution.py:186
  29.4 5.0 %collective-permute-start.10 = (bf16[2,4,4096]{2,1,0:T(4,128)(2,1)S(1)}, bf16[2,4,4096]{2,1,0:T(4,128)(2,1)S(1)}, u32[]{:S(2)}, u32[]{:S(2)}) collective-permute-start(bf16[2,4,4096]{2,1,0:T(4,128)(2,1)S(1)} %get-tuple-element.32), channel_id=1, source_target_pairs={{0,4},{4,0},{8,12},{12,8},{16,20},{20,16},{24,28},{28,24},{1,5},{5... | collective-permute-start | bytes 196616 | tf_op jit(solution)/shard_map/ppermute | solution.py:186
  31.0 5.0 %collective-permute-start.8 = (bf16[2,4,4096]{2,1,0:T(4,128)(2,1)S(1)}, bf16[2,4,4096]{2,1,0:T(4,128)(2,1)S(1)}, u32[]{:S(2)}, u32[]{:S(2)}) collective-permute-start(bf16[2,4,4096]{2,1,0:T(4,128)(2,1)S(1)} %get-tuple-element.31), channel_id=1, source_target_pairs={{0,8},{4,12},{8,0},{12,4},{16,24},{20,28},{24,16},{28,20},{1,9},{5... | collective-permute-start | bytes 196616 | tf_op jit(solution)/shard_map/ppermute | solution.py:186
  32.6 5.1 %collective-permute-start.3 = (bf16[2,2,4,4224]{3,2,0,1:T(4,128)(2,1)S(1)}, bf16[2,2,4,4224]{3,2,0,1:T(4,128)(2,1)S(1)}, u32[]{:S(2)}, u32[]{:S(2)}) collective-permute-start(bf16[2,2,4,4224]{3,2,0,1:T(4,128)(2,1)S(1)} %get-tuple-element.28), channel_id=1, source_target_pairs={{0,4},{4,0},{8,12},{12,8},{16,20},{20,16},{24,28},{28,24},{1,5},{5... | collective-permute-start | bytes 405512 | tf_op jit(solution)/shard_map/ppermute | solution.py:186
  33.3 5.1 %collective-permute-start.5 = (bf16[2,2,4,4224]{3,2,0,1:T(4,128)(2,1)S(1)}, bf16[2,2,4,4224]{3,2,0,1:T(4,128)(2,1)S(1)}, u32[]{:S(2)}, u32[]{:S(2)}) collective-permute-start(bf16[2,2,4,4224]{3,2,0,1:T(4,128)(2,1)S(1)} %get-tuple-element.24), channel_id=1, source_target_pairs={{0,8},{4,12},{8,0},{12,4},{16,24},{20,28},{24,16},{28,20},{1,9},{5... | collective-permute-start | bytes 405512 | tf_op jit(solution)/shard_map/ppermute | solution.py:186
  34.4 9.4 %collective-permute-start.11 = (bf16[2,2,4,4096]{3,2,0,1:T(4,128)(2,1)S(1)}, bf16[2,2,4,4096]{3,2,0,1:T(4,128)(2,1)S(1)}, u32[]{:S(2)}, u32[]{:S(2)}) collective-permute-start(bf16[2,2,4,4096]{3,2,0,1:T(4,128)(2,1)S(1)} %get-tuple-element.34), channel_id=1, source_target_pairs={{0,8},{4,12},{8,0},{12,4},{16,24},{20,28},{24,16},{28,20},{1,9},{5... | collective-permute-start | bytes 393224 | tf_op jit(solution)/shard_map/ppermute | solution.py:186
  36.2 8.8 %collective-permute-start.9 = (bf16[2,2,4,4096]{3,2,0,1:T(4,128)(2,1)S(1)}, bf16[2,2,4,4096]{3,2,0,1:T(4,128)(2,1)S(1)}, u32[]{:S(2)}, u32[]{:S(2)}) collective-permute-start(bf16[2,2,4,4096]{3,2,0,1:T(4,128)(2,1)S(1)} %get-tuple-element.30), channel_id=1, source_target_pairs={{0,4},{4,0},{8,12},{12,8},{16,20},{20,16},{24,28},{28,24},{1,5},{5... | collective-permute-start | bytes 393224 | tf_op jit(solution)/shard_map/ppermute | solution.py:186

commit v14 on v13

--- a/solution.py
+++ b/solution.py
@@ -161,7 +161,7 @@
     )(records, cos_a, nsin_a, cos_b, sin_b)
 
 
-def gather_blocks(carried, count, rank):
+def gather_blocks(carried, count, rank, held=None):
     if count & (count - 1) != 0:
         return lax.all_gather(carried, "blk", axis=0, tiled=False)
     masks = []
@@ -173,8 +173,9 @@
         return carried[None]
     first = masks[0]
     rest = masks[1:]
-    pairs = [(source, source ^ first) for source in range(count)]
-    held = jnp.stack([carried, lax.ppermute(carried, "blk", pairs)], axis=0)
+    if held is None:
+        pairs = [(source, source ^ first) for source in range(count)]
+        held = jnp.stack([carried, lax.ppermute(carried, "blk", pairs)], axis=0)
     split = (held.shape[1] + 1) // 2
     halves = [held[:, :split], held[:, split:]]
     orders = [rest, rest[::-1]]
@@ -278,28 +279,62 @@
     whitened = whitened.reshape(seg_count, block_bins, 2, sections, seg_dev)
     whitened = jnp.transpose(whitened, (0, 3, 1, 2, 4))
     seg_rank = lax.axis_index("seg")
-    pieces = [lax.dynamic_index_in_dim(whitened, seg_rank, axis=0, keepdims=False)]
-    for shift in range(1, seg_count):
-        outgoing = lax.dynamic_index_in_dim(
-            whitened, (seg_rank + shift) % seg_count, axis=0, keepdims=False
-        )
-        pairs = [(source, (source + shift) % seg_count) for source in range(seg_count)]
-        flat = outgoing.reshape(sections, -1)
-        pieces.append(lax.ppermute(flat, "seg", pairs).reshape(outgoing.shape))
     all_segs = seg_dev * seg_count
     table = jnp.concatenate([send_list[0], recv_row[0]], axis=1).reshape(-1)
     table_len = table.shape[0]
-    piece_width = block_bins * 2 * seg_dev
-    slab_width = 128
-    slab = jnp.pad(table.astype(jnp.bfloat16), (0, sections * slab_width - table_len))
     blk_rank = lax.axis_index("blk")
-    moved = []
-    for index, piece in enumerate(pieces):
-        flat = piece.reshape(sections, -1)
-        if index == 0:
-            flat = jnp.concatenate([flat, slab.reshape(sections, slab_width)], axis=1)
-        moved.append(gather_blocks(flat, owners_count, blk_rank))
-    table_part = moved[0][:, :, piece_width:].reshape(owners_count, -1)[:, :table_len]
+    fused_round = seg_count == 2 and owners_count >= 2 and owners_count & (owners_count - 1) == 0
+    if fused_round:
+        piece_width = block_bins * 2 * seg_dev
+        slab_width = 128
+        slab = jnp.pad(table.astype(jnp.bfloat16), (0, sections * slab_width - table_len))
+        keep = lax.dynamic_index_in_dim(whitened, seg_rank, axis=0, keepdims=False)
+        other = lax.dynamic_index_in_dim(whitened, 1 - seg_rank, axis=0, keepdims=False)
+        keep_flat = jnp.concatenate(
+            [keep.reshape(sections, -1), slab.reshape(sections, slab_width)], axis=1
+        )
+        other_flat = other.reshape(sections, -1)
+        first = owners_count // 2
+        from_blk = lax.ppermute(
+            keep_flat, "blk", [(source, source ^ first) for source in range(owners_count)]
+        )
+        from_seg = lax.ppermute(other_flat, "seg", [(0, 1), (1, 0)])
+        diagonal = [
+            (source * 2 + side, (source ^ first) * 2 + 1 - side)
+            for source in range(owners_count)
+            for side in range(2)
+        ]
+        from_diagonal = lax.ppermute(other_flat, ("blk", "seg"), diagonal)
+        held = jnp.stack(
+            [
+                jnp.concatenate([keep_flat, from_seg], axis=1),
+                jnp.concatenate([from_blk, from_diagonal], axis=1),
+            ],
+            axis=0,
+        )
+        moved = gather_blocks(None, owners_count, blk_rank, held=held)
+        halves = [moved[:, :, :piece_width], moved[:, :, piece_width + slab_width :]]
+        table_part = moved[:, :, piece_width : piece_width + slab_width]
+        table_part = table_part.reshape(owners_count, -1)[:, :table_len]
+        half_segs = seg_dev
+    else:
+        pieces = [lax.dynamic_index_in_dim(whitened, seg_rank, axis=0, keepdims=False)]
+        for shift in range(1, seg_count):
+            outgoing = lax.dynamic_index_in_dim(
+                whitened, (seg_rank + shift) % seg_count, axis=0, keepdims=False
+            )
+            pairs = [(source, (source + shift) % seg_count) for source in range(seg_count)]
+            flat = outgoing.reshape(sections, -1)
+            pieces.append(lax.ppermute(flat, "seg", pairs).reshape(outgoing.shape))
+        local = jnp.stack(pieces, axis=3).reshape(sections, block_bins, -1)
+        table_width = local.shape[-1]
+        slab = jnp.pad(table.astype(jnp.bfloat16), (0, sections * table_width - table_len))
+        carried = jnp.concatenate([local, slab.reshape(sections, 1, table_width)], axis=1)
+        everything = gather_blocks(carried.reshape(sections, -1), owners_count, blk_rank)
+        everything = everything.reshape(owners_count, sections, block_bins + 1, table_width)
+        halves = [everything[:, :, :block_bins]]
+        table_part = everything[:, :, block_bins].reshape(owners_count, -1)[:, :table_len]
+        half_segs = all_segs
     table_part = table_part.astype(jnp.int32).reshape(owners_count, owners_count, 2 * capacity)
     position_ids = jnp.arange(owners_count, dtype=jnp.int32)
     if owners_count & (owners_count - 1) == 0:
@@ -329,14 +364,14 @@
     ).astype(jnp.bfloat16)
     selector = selector.reshape(rows_count, owners_count, sections)
     cross = None
-    for chain in moved:
-        data = chain[:, :, :piece_width].reshape(owners_count, sections, block_bins, 2 * seg_dev)
+    for half in halves:
+        data = half.reshape(owners_count, sections, block_bins, 2 * half_segs)
         routed = jnp.einsum(
             "rsc,scbq->brq", selector, data, preferred_element_type=jnp.float32
         ).astype(jnp.bfloat16)
         own = lax.dynamic_slice_in_dim(routed, blk_rank * OWN, OWN, axis=1)
-        own_re = own[..., :seg_dev]
-        own_im = own[..., seg_dev:]
+        own_re = own[..., :half_segs]
+        own_im = own[..., half_segs:]
         rotated = jnp.concatenate([own_im, -own_re], axis=-1)
         lhs = jnp.concatenate([own, rotated], axis=1)
         part = jnp.einsum("bpq,bjq->bpj", lhs, routed, preferred_element_type=jnp.float32)

time: 49.5 us -> 55.8 us (1.13)
  waiting for transfers between devices: 6.14 us -> 14.5 us
  starting transfers between devices: 15.9 us -> 10.3 us
  matrix products: 4.77 us -> 6.2 us
  other arithmetic: 6.97 us -> 8.06 us
  local copies, waits for them, and re-layouts: 8.6 us -> 9.63 us
    ppermute x8 -> x4, waiting for transfers between devices: 1.79 us -> 8.16 us  [gather_blocks(): arrived = lax.ppermute(part, 'blk', pairs)]
    ppermute x8 -> x4, starting transfers between devices: 9.87 us -> 4.32 us  [gather_blocks(): arrived = lax.ppermute(part, 'blk', pairs)]
    reshape x5 -> x6, local copies, waits for them, and re-layouts: 1.9 us -> 3.96 us  [the longest x2 3.22 us: per_device(): data = half.reshape(owners_count, sections, block_bins, 2 * half_segs)]
    ppermute x3, waiting for transfers between devices: 4.34 us -> 6.33 us  [the longest x1 3.53 us: per_device(): from_seg = lax.ppermute(other_flat, 'seg', [(0, 1), (1, 0)])]
    concatenate x4 -> x0, local copies, waits for them, and re-layouts: 1.57 us -> none  [gather_blocks(): return jnp.concatenate(results, axis=1)]
    dot_general x2, matrix products: 1.45 us -> 2.89 us  [per_device(): jnp.einsum('rsc,scbq->brq', selector, data, preferred_element_type=jnp.fl...]
    slice x2, other arithmetic: 0.21 us -> 1.02 us  [per_device(): own_im = own[..., half_segs:]]
    another operation x8 -> x4, other arithmetic: 1.18 us -> 1.18 us  [gather_blocks(): part = jnp.stack([part, arrived], axis=axis)]
  transfers between devices with their start and end apart: 12 -> 8, of which waited for: 6 -> 5; matrix products, arithmetic and copies ran while one was open for 19% -> 5% of each run, Pallas kernels for 0% -> 0%
where the time goes in v14:
time: 55.8 us; the launch traced here: 55.5 us
  waiting for transfers between devices  14.5 us (26%)
  starting transfers between devices  10.3 us (18%)
  local copies, waits for them, and re-layouts  9.63 us (17%)
  other arithmetic  8.06 us (14%)
  Pallas kernels  6.39 us (11%)
  matrix products  6.2 us (11%)
    ppermute x4, waiting for transfers between devices, gather_blocks(): arrived = lax.ppermute(part, 'blk', pairs)  8.16 us
    pallas_call x1, Pallas kernels, dft_fused(): pl.pallas_call(dft_kernel, grid=(count // chunk,), in_specs=[pl.BlockSpec...  6.39 us
    ppermute x1, starting transfers between devices, per_device(): from_diagonal = lax.ppermute(other_flat, ('blk', 'seg'), diagonal)  4.73 us
    ppermute x4, starting transfers between devices, gather_blocks(): arrived = lax.ppermute(part, 'blk', pairs)  4.32 us
    ppermute x1, waiting for transfers between devices, per_device(): from_seg = lax.ppermute(other_flat, 'seg', [(0, 1), (1, 0)])  3.53 us
    reshape x2, local copies, waits for them, and re-layouts, per_device(): data = half.reshape(owners_count, sections, block_bins, 2 * half_segs)  3.22 us
    dot_general x2, matrix products, per_device(): jnp.einsum('rsc,scbq->brq', selector, data, preferred_element_type=jnp.fl...  2.89 us
    ppermute x1, waiting for transfers between devices, per_device(): lax.ppermute(keep_flat, 'blk', [(source, source ^ first) for source in ra...  2.79 us
  transfers between devices with their start and end apart: 8, of which 5 were waited for; matrix products, arithmetic and copies ran while one was open for 5% of the time, Pallas kernels for 0%

profile of v14, /device:TPU:0, one launch (start us, length us, event | category | flops | bytes accessed | tf_op | source)
XLA Modules:
  0.0 55.5 jit_solution(1014640065288864273)
XLA Ops:
  0.1 0.2 fusion.73
  0.3 0.7 %negate_bitcast_fusion = (f32[64,256]{1,0:T(8,128)}, f32[64,256]{1,0:T(8,128)}) fusion(f32[8,256]{1,0:T(8,128)S(1)} %get-tuple-element.47, f32[8,256]{1,0:T(8,128)S(1)} %get-tuple-element.49, f32[8,256]{1,0:T(8,128)S(1)} %get-tuple-element.48, f32[8,256]{1,0:T(8,128)S(1)} %get-tuple-element.50), kind=kLoop, calls=%fused_computation.111 | loop fusion | flops 114688 | bytes 163840 | tf_op jit(solution)/shard_map/neg | solution.py:136
  1.0 0.8 %add_multiply_fusion = (f32[8,16,256]{2,1,0:T(8,128)}, f32[8,16,256]{2,1,0:T(8,128)}) fusion(f32[16,256]{1,0:T(8,128)S(1)} %get-tuple-element.52, f32[8,256]{1,0:T(8,128)S(1)} %get-tuple-element.42, f32[16,256]{1,0:T(8,128)S(1)} %get-tuple-element.51, f32[8,256]{1,0:T(8,128)S(1)} %get-tuple-element.41), kind=kLoop, calls=%fused_computation.91 | loop fusion | flops 262144 | bytes 311296 | tf_op jit(solution)/shard_map/mul | solution.py:141
  1.7 6.4 %shard_map.46 = (f32[256,256]{1,0:T(8,128)}, f32[256,256]{1,0:T(8,128)}) custom-call(bf16[256,8192]{1,0:T(8,128)(2,1)} %bitcast.125, f32[64,256]{1,0:T(8,128)} %get-tuple-element.34.cos_a_ref, f32[64,256]{1,0:T(8,128)} %get-tuple-element.33.nsin_a_ref, f32[128,256]{1,0:T(8,128)} %bitcast.129, f32[128,256]{1,0:T(8,128)} %bitcast.128), custom_call_target="tpu_custom_call" | custom-call | tf_op jit(solution)/shard_map/pallas_call | solution.py:145
  8.1 1.3 %broadcast_select_fusion = (f32[128,2,256]{0,2,1:T(8,128)S(1)}, f32[128,2,256]{0,2,1:T(8,128)S(1)}) fusion(pred[]{:T(512)S(6)} %eq.64, f32[256,1,256]{0,2,1:T(8,128)} %bitcast.138, f32[256,1,256]{0,2,1:T(8,128)} %bitcast.137), kind=kLoop, calls=%fused_computation.93 | loop fusion | flops 327680 | bytes 1048577 | tf_op jit(solution)/shard_map/jit(_where)/select_n | solution.py:221
  9.4 0.1 copy.99
  9.6 0.1 copy.100
  9.8 0.5 collective-permute-start
  10.3 0.5 convolution_bitcast_fusion
  10.8 0.5 convolution_bitcast_fusion.1
  11.3 0.2 copy.101
  11.6 0.1 copy.102
  11.7 0.1 copy.112
  11.8 0.1 convert_element_type.95
  12.1 0.1 copy.106
  12.3 0.1 copy.103
  12.5 0.1 fusion.26
  12.6 0.1 copy.108
  12.8 0.1 stack.67
  12.9 0.4 copy.111
  13.3 0.1 stack.66
  13.4 0.6 %copy.110 = bf16[2,64,1,8,32]{4,2,1,3,0:T(2,128)(2,1)S(1)} copy(bf16[2,64,1,8,32]{1,0,4,3,2:T(2,128)(2,1)S(1)} %stack.66) | data formatting | bytes 131072 | tf_op jit(solution)/shard_map/stack | solution.py:278
  14.0 1.4 %fusion.19 = (bf16[1,8,64,2,32]{4,3,2,1,0:T(2,128)(2,1)S(1)}, bf16[1,8,64,2,32]{4,3,2,1,0:T(2,128)(2,1)S(1)}) fusion(s32[]{:T(128)S(6)} %select_n.242, bf16[2,64,1,8,32]{4,2,1,3,0:T(2,128)(2,1)S(1)} %copy.111, bf16[2,64,1,8,32]{4,2,1,3,0:T(2,128)(2,1)S(1)} %copy.110, s32[]{:T(128)S(6)} %select_n.243), kind=kLoop, calls=%fused_computation.57 | loop fusion | flops 262144 | bytes 262152 | tf_op jit(solution)/shard_map/jit(dynamic_index_in_dim)/dynamic_slice | solution.py:291
  15.4 0.3 reshape.591
  15.7 4.7 %collective-permute-start.3 = (bf16[8,4096]{1,0:T(8,128)(2,1)S(1)}, bf16[8,4096]{1,0:T(8,128)(2,1)S(1)}, u32[]{:S(2)}, u32[]{:S(2)}) collective-permute-start(bf16[8,4096]{1,0:T(8,128)(2,1)S(1)} %reshape.591), channel_id=1, source_target_pairs={{0,18},{2,16},{4,22},{6,20},{8,26},{10,24},{12,30},{14,28},{16,2},... | collective-permute-start | bytes 196616 | tf_op jit(solution)/shard_map/ppermute | solution.py:307
  20.4 0.5 collective-permute-start.1
  20.9 0.3 reshape.589
  21.2 0.2 collective-permute-start.2
  21.4 3.5 %collective-permute-done.1 = bf16[8,4096]{1,0:T(8,128)(2,1)S(1)} collective-permute-done((bf16[8,4096]{1,0:T(8,128)(2,1)S(1)}, bf16[8,4096]{1,0:T(8,128)(2,1)S(1)}, u32[]{:S(2)}, u32[]{:S(2)}) %collective-permute-start.1) | collective-permute-done | bytes 65568 | tf_op jit(solution)/shard_map/ppermute | solution.py:301
  25.0 2.8 %collective-permute-done.2 = bf16[8,4224]{1,0:T(8,128)(2,1)S(1)} collective-permute-done((bf16[8,4224]{1,0:T(8,128)(2,1)S(1)}, bf16[8,4224]{1,0:T(8,128)(2,1)S(1)}, u32[]{:S(2)}, u32[]{:S(2)}) %collective-permute-start.2) | collective-permute-done | bytes 67616 | tf_op jit(solution)/shard_map/ppermute | solution.py:298
  27.8 0.1 pad_maximum_fusion.7
  27.9 0.4 collective-permute-start.4
  28.3 1.5 %collective-permute-start.6 = (bf16[2,4,8320]{2,1,0:T(4,128)(2,1)S(1)}, bf16[2,4,8320]{2,1,0:T(4,128)(2,1)S(1)}, u32[]{:S(2)}, u32[]{:S(2)}) collective-permute-start(bf16[2,4,8320]{2,1,0:T(4,128)(2,1)S(1)} %get-tuple-element.23), channel_id=1, source_target_pairs={{0,4},{4,0},{8,12},{12,8},{16,20},{20,16},{24,28},{28,24},{1,5},{5... | collective-permute-start | bytes 399368 | tf_op jit(solution)/shard_map/ppermute | solution.py:187
  29.8 3.1 %collective-permute-done.4 = bf16[2,4,8320]{2,1,0:T(4,128)(2,1)S(1)} collective-permute-done((bf16[2,4,8320]{2,1,0:T(4,128)(2,1)S(1)}, bf16[2,4,8320]{2,1,0:T(4,128)(2,1)S(1)}, u32[]{:S(2)}, u32[]{:S(2)}) %collective-permute-start.4) | collective-permute-done | bytes 133152 | tf_op jit(solution)/shard_map/ppermute | solution.py:187
  32.9 0.2 fusion.100
  33.2 1.6 %collective-permute-start.5 = (bf16[2,2,4,8320]{3,2,0,1:T(4,128)(2,1)S(1)}, bf16[2,2,4,8320]{3,2,0,1:T(4,128)(2,1)S(1)}, u32[]{:S(2)}, u32[]{:S(2)}) collective-permute-start(bf16[2,2,4,8320]{3,2,0,1:T(4,128)(2,1)S(1)} %get-tuple-element.26), channel_id=1, source_target_pairs={{0,4},{4,0},{8,12},{12,8},{16,20},{20,16},{24,28},{28,24},{1,5},{5... | collective-permute-start | bytes 798728 | tf_op jit(solution)/shard_map/ppermute | solution.py:187
  34.7 0.2 fusion.99
  35.0 0.9 %collective-permute-start.7 = (bf16[2,2,4,8320]{3,2,0,1:T(4,128)(2,1)S(1)}, bf16[2,2,4,8320]{3,2,0,1:T(4,128)(2,1)S(1)}, u32[]{:S(2)}, u32[]{:S(2)}) collective-permute-start(bf16[2,2,4,8320]{3,2,0,1:T(4,128)(2,1)S(1)} %get-tuple-element.22), channel_id=1, source_target_pairs={{0,8},{4,12},{8,0},{12,4},{16,24},{20,28},{24,16},{28,20},{1,9},{5... | collective-permute-start | bytes 798728 | tf_op jit(solution)/shard_map/ppermute | solution.py:187
  35.8 3.8 %collective-permute-done.5 = bf16[2,2,4,8320]{3,2,0,1:T(4,128)(2,1)S(1)} collective-permute-done((bf16[2,2,4,8320]{3,2,0,1:T(4,128)(2,1)S(1)}, bf16[2,2,4,8320]{3,2,0,1:T(4,128)(2,1)S(1)}, u32[]{:S(2)}, u32[]{:S(2)}) %collective-permute-start.5) | collective-permute-done | bytes 266272 | tf_op jit(solution)/shard_map/ppermute | solution.py:187
  39.6 0.4 pad_maximum_fusion
  40.0 0.2 copy.113
  40.2 1.2 %collective-permute-done.7 = bf16[2,2,4,8320]{3,2,0,1:T(4,128)(2,1)S(1)} collective-permute-done((bf16[2,2,4,8320]{3,2,0,1:T(4,128)(2,1)S(1)}, bf16[2,2,4,8320]{3,2,0,1:T(4,128)(2,1)S(1)}, u32[]{:S(2)}, u32[]{:S(2)}) %collective-permute-start.7) | collective-permute-done | bytes 266272 | tf_op jit(solution)/shard_map/ppermute | solution.py:187
  41.4 0.4 pad_maximum_fusion.1
  41.8 0.2 copy.114
  42.0 0.5 pad_maximum_fusion.2
  42.6 0.2 copy.129
  42.8 0.1 multiply_reduce_fusion
  43.1 0.1 copy.119
  43.3 0.1 eq.71
  43.4 0.1 copy.118
  43.5 0.1 eq.68
  43.7 1.1 %reshape.594 = bf16[8,8,64,64]{3,2,1,0:T(8,128)(2,1)S(1)} reshape(bf16[8,8,4096]{2,1,0:T(8,128)(2,1)S(1)} %get-tuple-element.10) | data formatting | bytes 1048576 | tf_op jit(solution)/shard_map/reshape | solution.py:368
  44.8 0.3 fusion.1
  45.1 0.8 %bitcast_convert_fusion.1 = bf16[64,64,128]{2,1,0:T(8,128)(2,1)S(1)} fusion(bf16[128,8,8,1]{0,2,1,3:T(8,128)(2,1)S(1)} %fusion.1, bf16[8,8,64,64]{3,2,1,0:T(8,128)(2,1)S(1)} %reshape.594), kind=kOutput, calls=%fused_computation.1 | convolution fusion | flops 67633152 | bytes 1589248 | tf_op jit(solution)/shard_map/rsc,scbq->brq/dot_general | solution.py:369
  45.9 0.4 dynamic-slice_bitcast_fusion.1
  46.3 0.9 %fusion.102 = (bf16[64,16,32]{1,2,0:T(8,128)(2,1)S(1)}, bf16[64,16,32]{1,2,0:T(8,128)(2,1)}) fusion(bf16[64,16,64]{1,2,0:T(8,128)(2,1)S(1)} %dynamic-slice_bitcast_fusion.1), kind=kLoop, calls=%fused_computation.231 | loop fusion | flops 32768 | bytes 262144 | tf_op jit(solution)/shard_map/slice | solution.py:374
  47.2 2.1 %reshape.597 = bf16[8,8,64,64]{3,2,1,0:T(8,128)(2,1)} reshape(bf16[8,8,4096]{2,1,0:T(8,128)(2,1)S(1)} %get-tuple-element.9) | data formatting | bytes 1048576 | tf_op jit(solution)/shard_map/reshape | solution.py:368
  49.3 2.1 %bitcast_convert_fusion = bf16[64,64,128]{2,1,0:T(8,128)(2,1)S(1)} fusion(bf16[128,8,8,1]{0,2,1,3:T(8,128)(2,1)S(1)} %fusion.1, bf16[8,8,64,64]{3,2,1,0:T(8,128)(2,1)} %reshape.597), kind=kOutput, calls=%fused_computation | convolution fusion | flops 67633152 | bytes 1589248 | tf_op jit(solution)/shard_map/rsc,scbq->brq/dot_general | solution.py:369
  51.4 0.4 dynamic-slice_bitcast_fusion
  51.8 0.1 fusion.101
  51.9 0.5 copy-done.1
  52.4 1.0 %fusion.2 = f32[64,32,128]{2,1,0:T(8,128)S(1)} fusion(bf16[64,64,128]{2,1,0:T(8,128)(2,1)S(1)} %bitcast_convert_fusion.1, bf16[64,16,32]{1,2,0:T(8,128)(2,1)S(1)} %copy-done.1, bf16[64,16,32]{1,2,0:T(8,128)(2,1)S(1)} %get-tuple-element.13, bf16[64,16,64]{1,2,0:T(8,128)(2,1)S(1)} %dynamic-slice_bitcast_fusion.1), kind=kOutput, calls=%fused_computation.12 | convolution fusion | flops 34340864 | bytes 2359296 | tf_op jit(solution)/shard_map/bpq,bjq->bpj/dot_general | solution.py:377
  53.4 1.0 %fusion = f32[64,32,128]{2,1,0:T(8,128)S(1)} fusion(f32[64,32,128]{2,1,0:T(8,128)S(1)} %fusion.2, bf16[64,64,128]{2,1,0:T(8,128)(2,1)S(1)} %bitcast_convert_fusion, bf16[64,16,32]{1,2,0:T(8,128)(2,1)S(1)} %get-tuple-element.12, bf16[64,16,32]{1,2,0:T(8,128)(2,1)S(1)} %get-tuple-element.11, bf16[64,16,64]{1,2,0:T(8,128)(2,1)S(1)} %dynamic-slice_bitcast_fusion), kind=kOutput, calls=%fused_computation.3 | convolution fusion | flops 34865152 | bytes 3407872 | tf_op jit(solution)/shard_map/bpq,bjq->bpj/dot_general | solution.py:377
  54.5 1.1 %copy.142 = f32[64,2,16,128]{3,2,0,1:T(8,128)} copy(f32[64,2,16,128]{3,2,1,0:T(8,128)S(1)} %bitcast.124) | data formatting | bytes 2097152 | tf_op jit(solution)/shard_map/div | solution.py:380
  (44 shorter events, 1.0 us)
Async XLA Ops:
  0.0 10.3 %copy-start = (f32[128]{0:T(128)S(1)}, f32[128]{0:T(128)}, u32[]{:S(2)}) copy-start(f32[128]{0:T(128)} %param.5) | copy-start | bytes 1540
  8.1 3.6 %copy-start.2 = (s32[1,8,2]{1,2,0:T(2,128)S(1)}, s32[1,8,2]{1,2,0:T(2,128)}, u32[]{:S(2)}) copy-start(s32[1,8,2]{1,2,0:T(2,128)} %param.7) | copy-start | bytes 196
  8.1 3.6 %copy-start.3 = (s32[1,8,2]{1,2,0:T(2,128)S(1)}, s32[1,8,2]{1,2,0:T(2,128)}, u32[]{:S(2)}) copy-start(s32[1,8,2]{1,2,0:T(2,128)} %param.6) | copy-start | bytes 196
  9.8 2.3 %collective-permute-start = (f32[144,2,256]{0,2,1:T(8,128)S(1)}, f32[144,2,256]{0,2,1:T(8,128)S(1)}, u32[]{:S(2)}, u32[]{:S(2)}) collective-permute-start(f32[144,2,256]{0,2,1:T(8,128)S(1)} %pad_maximum_fusion.3), channel_id=1, source_target_pairs={{0,1},{1,0},{2,3},{3,2},{4,5},{5,4},{6,7},{7,6},{8,9},{9,8},{10,11... | collective-permute-start | bytes 884744 | tf_op jit(solution)/shard_map/ppermute | solution.py:24
  15.7 9.3 %collective-permute-start.3 = (bf16[8,4096]{1,0:T(8,128)(2,1)S(1)}, bf16[8,4096]{1,0:T(8,128)(2,1)S(1)}, u32[]{:S(2)}, u32[]{:S(2)}) collective-permute-start(bf16[8,4096]{1,0:T(8,128)(2,1)S(1)} %reshape.591), channel_id=1, source_target_pairs={{0,18},{2,16},{4,22},{6,20},{8,26},{10,24},{12,30},{14,28},{16,2},... | collective-permute-start | bytes 196616 | tf_op jit(solution)/shard_map/ppermute | solution.py:307
  20.4 4.5 %collective-permute-start.1 = (bf16[8,4096]{1,0:T(8,128)(2,1)S(1)}, bf16[8,4096]{1,0:T(8,128)(2,1)S(1)}, u32[]{:S(2)}, u32[]{:S(2)}) collective-permute-start(bf16[8,4096]{1,0:T(8,128)(2,1)S(1)} %reshape.591), channel_id=1, source_target_pairs={{0,2},{2,0},{1,3},{3,1},{4,6},{6,4},{5,7},{7,5},{8,10},{10,8},{9,1... | collective-permute-start | bytes 196616 | tf_op jit(solution)/shard_map/ppermute | solution.py:301
  21.2 6.5 %collective-permute-start.2 = (bf16[8,4224]{1,0:T(8,128)(2,1)S(1)}, bf16[8,4224]{1,0:T(8,128)(2,1)S(1)}, u32[]{:S(2)}, u32[]{:S(2)}) collective-permute-start(bf16[8,4224]{1,0:T(8,128)(2,1)S(1)} %pad_maximum_fusion.10), channel_id=1, source_target_pairs={{0,16},{4,20},{8,24},{12,28},{16,0},{20,4},{24,8},{28,12},{1,17},{... | collective-permute-start | bytes 202760 | tf_op jit(solution)/shard_map/ppermute | solution.py:298
  27.9 5.1 %collective-permute-start.4 = (bf16[2,4,8320]{2,1,0:T(4,128)(2,1)S(1)}, bf16[2,4,8320]{2,1,0:T(4,128)(2,1)S(1)}, u32[]{:S(2)}, u32[]{:S(2)}) collective-permute-start(bf16[2,4,8320]{2,1,0:T(4,128)(2,1)S(1)} %get-tuple-element.24), channel_id=1, source_target_pairs={{0,8},{4,12},{8,0},{12,4},{16,24},{20,28},{24,16},{28,20},{1,9},{5... | collective-permute-start | bytes 399368 | tf_op jit(solution)/shard_map/ppermute | solution.py:187
  28.3 6.4 %collective-permute-start.6 = (bf16[2,4,8320]{2,1,0:T(4,128)(2,1)S(1)}, bf16[2,4,8320]{2,1,0:T(4,128)(2,1)S(1)}, u32[]{:S(2)}, u32[]{:S(2)}) collective-permute-start(bf16[2,4,8320]{2,1,0:T(4,128)(2,1)S(1)} %get-tuple-element.23), channel_id=1, source_target_pairs={{0,4},{4,0},{8,12},{12,8},{16,20},{20,16},{24,28},{28,24},{1,5},{5... | collective-permute-start | bytes 399368 | tf_op jit(solution)/shard_map/ppermute | solution.py:187
  33.2 6.5 %collective-permute-start.5 = (bf16[2,2,4,8320]{3,2,0,1:T(4,128)(2,1)S(1)}, bf16[2,2,4,8320]{3,2,0,1:T(4,128)(2,1)S(1)}, u32[]{:S(2)}, u32[]{:S(2)}) collective-permute-start(bf16[2,2,4,8320]{3,2,0,1:T(4,128)(2,1)S(1)} %get-tuple-element.26), channel_id=1, source_target_pairs={{0,4},{4,0},{8,12},{12,8},{16,20},{20,16},{24,28},{28,24},{1,5},{5... | collective-permute-start | bytes 798728 | tf_op jit(solution)/shard_map/ppermute | solution.py:187
  35.0 6.5 %collective-permute-start.7 = (bf16[2,2,4,8320]{3,2,0,1:T(4,128)(2,1)S(1)}, bf16[2,2,4,8320]{3,2,0,1:T(4,128)(2,1)S(1)}, u32[]{:S(2)}, u32[]{:S(2)}) collective-permute-start(bf16[2,2,4,8320]{3,2,0,1:T(4,128)(2,1)S(1)} %get-tuple-element.22), channel_id=1, source_target_pairs={{0,8},{4,12},{8,0},{12,4},{16,24},{20,28},{24,16},{28,20},{1,9},{5... | collective-permute-start | bytes 798728 | tf_op jit(solution)/shard_map/ppermute | solution.py:187
  51.4 1.0 %copy-start.1 = (bf16[64,16,32]{1,2,0:T(8,128)(2,1)S(1)}, bf16[64,16,32]{1,2,0:T(8,128)(2,1)}, u32[]{:S(2)}) copy-start(bf16[64,16,32]{1,2,0:T(8,128)(2,1)} %get-tuple-element.14) | copy-start | bytes 196612

commit v15 on v14

--- a/solution.py
+++ b/solution.py
@@ -305,18 +305,31 @@
             for side in range(2)
         ]
         from_diagonal = lax.ppermute(other_flat, ("blk", "seg"), diagonal)
+
+        def interleave(mine_segs, their_segs, table_slab):
+            lanes_in = 2 * seg_dev
+            joined = jnp.concatenate(
+                [
+                    mine_segs.reshape(sections, block_bins, lanes_in),
+                    their_segs.reshape(sections, block_bins, lanes_in),
+                ],
+                axis=2,
+            ).reshape(sections, -1)
+            return jnp.concatenate([joined, table_slab], axis=1)
+
         held = jnp.stack(
             [
-                jnp.concatenate([keep_flat, from_seg], axis=1),
-                jnp.concatenate([from_blk, from_diagonal], axis=1),
+                interleave(keep_flat[:, :piece_width], from_seg, keep_flat[:, piece_width:]),
+                interleave(from_blk[:, :piece_width], from_diagonal, from_blk[:, piece_width:]),
             ],
             axis=0,
         )
         moved = gather_blocks(None, owners_count, blk_rank, held=held)
-        halves = [moved[:, :, :piece_width], moved[:, :, piece_width + slab_width :]]
-        table_part = moved[:, :, piece_width : piece_width + slab_width]
+        halves = [moved[:, :, : 2 * piece_width]]
+        table_part = moved[:, :, 2 * piece_width :]
         table_part = table_part.reshape(owners_count, -1)[:, :table_len]
-        half_segs = seg_dev
+        half_segs = all_segs
+        chunk_segs = seg_dev
     else:
         pieces = [lax.dynamic_index_in_dim(whitened, seg_rank, axis=0, keepdims=False)]
         for shift in range(1, seg_count):
@@ -335,6 +348,7 @@
         halves = [everything[:, :, :block_bins]]
         table_part = everything[:, :, block_bins].reshape(owners_count, -1)[:, :table_len]
         half_segs = all_segs
+        chunk_segs = all_segs
     table_part = table_part.astype(jnp.int32).reshape(owners_count, owners_count, 2 * capacity)
     position_ids = jnp.arange(owners_count, dtype=jnp.int32)
     if owners_count & (owners_count - 1) == 0:
@@ -370,9 +384,9 @@
             "rsc,scbq->brq", selector, data, preferred_element_type=jnp.float32
         ).astype(jnp.bfloat16)
         own = lax.dynamic_slice_in_dim(routed, blk_rank * OWN, OWN, axis=1)
-        own_re = own[..., :half_segs]
-        own_im = own[..., half_segs:]
-        rotated = jnp.concatenate([own_im, -own_re], axis=-1)
+        own_parts = own.reshape(own.shape[:-1] + (-1, 2, chunk_segs))
+        rotated = jnp.stack([own_parts[..., 1, :], -own_parts[..., 0, :]], axis=-2)
+        rotated = rotated.reshape(own.shape)
         lhs = jnp.concatenate([own, rotated], axis=1)
         part = jnp.einsum("bpq,bjq->bpj", lhs, routed, preferred_element_type=jnp.float32)
         cross = part if cross is None else cross + part

time: 55.8 us -> 46.8 us (0.84)
  local copies, waits for them, and re-layouts: 9.63 us -> 6.23 us
  matrix products: 6.2 us -> 3.25 us
  other arithmetic: 8.06 us -> 5.46 us
  starting transfers between devices: 10.3 us -> 8.61 us
  waiting for transfers between devices: 14.5 us -> 16.1 us
    ppermute x4, waiting for transfers between devices: 8.16 us -> 10.6 us  [gather_blocks(): arrived = lax.ppermute(part, 'blk', pairs)]
    reshape x2 -> x5, local copies, waits for them, and re-layouts: 3.22 us -> 0.94 us  [the longest x3 0.48 us: interleave(): their_segs.reshape(sections, block_bins, lanes_in)]
    dot_general x2 -> x1, matrix products: 2.89 us -> 1.05 us  [per_device(): jnp.einsum('rsc,scbq->brq', selector, data, preferred_element_type=jnp.fl...]
    ppermute x4, starting transfers between devices: 4.32 us -> 2.64 us  [gather_blocks(): arrived = lax.ppermute(part, 'blk', pairs)]
    dynamic_slice x1 -> x0, other arithmetic: 1.39 us -> none  [per_device(): keep = lax.dynamic_index_in_dim(whitened, seg_rank, axis=0, keepdims=False)]
    slice x2 -> x1, other arithmetic: 1.02 us -> 0.06 us  [per_device(): rotated = jnp.stack([own_parts[..., 1, :], -own_parts[..., 0, :]], axis=-2)]
    another operation x4 -> x3, local copies, waits for them, and re-layouts: 1.2 us -> 0.24 us  [per_device(): whitened = jnp.stack([white_re, white_im], axis=1).astype(jnp.bfloat16)]
    dot_general x2 -> x1, matrix products: 2.03 us -> 1.19 us  [per_device(): jnp.einsum('bpq,bjq->bpj', lhs, routed, preferred_element_type=jnp.float32)]
  transfers between devices with their start and end apart: 8 -> 8, of which waited for: 5 -> 6; matrix products, arithmetic and copies ran while one was open for 5% -> 8% of each run, Pallas kernels for 0% -> 0%
where the time goes in v15:
time: 46.8 us; the launch traced here: 46.6 us
  waiting for transfers between devices  16.1 us (34%)
  starting transfers between devices  8.61 us (18%)
  Pallas kernels  6.41 us (14%)
  local copies, waits for them, and re-layouts  6.23 us (13%)
  other arithmetic  5.46 us (12%)
  matrix products  3.25 us (7%)
  between operations  0.53 us (1%)
    ppermute x4, waiting for transfers between devices, gather_blocks(): arrived = lax.ppermute(part, 'blk', pairs)  10.6 us
    pallas_call x1, Pallas kernels, dft_fused(): pl.pallas_call(dft_kernel, grid=(count // chunk,), in_specs=[pl.BlockSpec...  6.41 us
    ppermute x1, starting transfers between devices, per_device(): from_diagonal = lax.ppermute(other_flat, ('blk', 'seg'), diagonal)  4.75 us
    ppermute x1, waiting for transfers between devices, per_device(): from_seg = lax.ppermute(other_flat, 'seg', [(0, 1), (1, 0)])  3.35 us
    ppermute x4, starting transfers between devices, gather_blocks(): arrived = lax.ppermute(part, 'blk', pairs)  2.64 us
    ppermute x1, waiting for transfers between devices, per_device(): lax.ppermute(keep_flat, 'blk', [(source, source ^ first) for source in ra...  2.16 us
    select_n x1, other arithmetic, per_device(): sent = jnp.where(freq_rank == 0, blocks[1], blocks[0])  1.27 us
    dot_general x1, matrix products, per_device(): jnp.einsum('bpq,bjq->bpj', lhs, routed, preferred_element_type=jnp.float32)  1.19 us
  transfers between devices with their start and end apart: 8, of which 6 were waited for; matrix products, arithmetic and copies ran while one was open for 8% of the time, Pallas kernels for 0%

profile of v15, /device:TPU:0, one launch (start us, length us, event | category | flops | bytes accessed | tf_op | source)
XLA Modules:
  0.0 46.6 jit_solution(2780879221544841372)
XLA Ops:
  0.0 0.1 fusion.60
  0.1 0.2 fusion.62
  0.3 0.7 %negate_bitcast_fusion = (f32[64,256]{1,0:T(8,128)}, f32[64,256]{1,0:T(8,128)}) fusion(f32[8,256]{1,0:T(8,128)S(1)} %get-tuple-element.43, f32[8,256]{1,0:T(8,128)S(1)} %get-tuple-element.45, f32[8,256]{1,0:T(8,128)S(1)} %get-tuple-element.44, f32[8,256]{1,0:T(8,128)S(1)} %get-tuple-element.46), kind=kLoop, calls=%fused_computation.97 | loop fusion | flops 114688 | bytes 163840 | tf_op jit(solution)/shard_map/neg | solution.py:136
  1.0 0.7 %add_multiply_fusion = (f32[8,16,256]{2,1,0:T(8,128)}, f32[8,16,256]{2,1,0:T(8,128)}) fusion(f32[16,256]{1,0:T(8,128)S(1)} %get-tuple-element.48, f32[8,256]{1,0:T(8,128)S(1)} %get-tuple-element.38, f32[16,256]{1,0:T(8,128)S(1)} %get-tuple-element.47, f32[8,256]{1,0:T(8,128)S(1)} %get-tuple-element.37), kind=kLoop, calls=%fused_computation.77 | loop fusion | flops 262144 | bytes 311296 | tf_op jit(solution)/shard_map/mul | solution.py:141
  1.7 6.4 %shard_map.46 = (f32[256,256]{1,0:T(8,128)}, f32[256,256]{1,0:T(8,128)}) custom-call(bf16[256,8192]{1,0:T(8,128)(2,1)} %bitcast.134, f32[64,256]{1,0:T(8,128)} %get-tuple-element.30.cos_a_ref, f32[64,256]{1,0:T(8,128)} %get-tuple-element.29.nsin_a_ref, f32[128,256]{1,0:T(8,128)} %bitcast.146, f32[128,256]{1,0:T(8,128)} %bitcast.145), custom_call_target="tpu_custom_call" | custom-call | tf_op jit(solution)/shard_map/pallas_call | solution.py:145
  8.1 1.3 %broadcast_select_fusion = (f32[128,2,256]{0,2,1:T(8,128)S(1)}, f32[128,2,256]{0,2,1:T(8,128)S(1)}) fusion(pred[]{:T(512)S(6)} %eq.64, f32[256,1,256]{0,2,1:T(8,128)} %bitcast.158, f32[256,1,256]{0,2,1:T(8,128)} %bitcast.157), kind=kLoop, calls=%fused_computation.79 | loop fusion | flops 327680 | bytes 1048577 | tf_op jit(solution)/shard_map/jit(_where)/select_n | solution.py:221
  9.4 0.1 copy.101
  9.6 0.1 copy.102
  9.8 0.5 %collective-permute-start = (f32[144,2,256]{0,2,1:T(8,128)S(1)}, f32[144,2,256]{0,2,1:T(8,128)S(1)}, u32[]{:S(2)}, u32[]{:S(2)}) collective-permute-start(f32[144,2,256]{0,2,1:T(8,128)S(1)} %pad_maximum_fusion.2), channel_id=1, source_target_pairs={{0,1},{1,0},{2,3},{3,2},{4,5},{5,4},{6,7},{7,6},{8,9},{9,8},{10,11... | collective-permute-start | bytes 884744 | tf_op jit(solution)/shard_map/ppermute | solution.py:24
  10.3 0.5 %convolution_bitcast_fusion = f32[128]{0:T(128)S(1)} fusion(s32[128]{0:T(128)S(1)} %fusion.79, f32[128]{0:T(128)S(1)} %copy-done), kind=kOutput, calls=%fused_computation.4 | convolution fusion | flops 442368 | bytes 1536 | tf_op jit(solution)/shard_map/dot_general | solution.py:67
  10.8 0.5 %convolution_bitcast_fusion.1 = f32[128]{0:T(128)S(1)} fusion(s32[128]{0:T(128)S(1)} %fusion.79, f32[128]{0:T(128)S(1)} %copy-done), kind=kOutput, calls=%fused_computation.5 | convolution fusion | flops 425984 | bytes 1536 | tf_op jit(solution)/shard_map/dot_general | solution.py:66
  11.3 0.2 copy.103
  11.6 0.1 copy.117
  11.7 0.1 convert_element_type.91
  11.8 0.1 copy.104
  12.1 0.1 copy.105
  12.4 0.1 copy.108
  12.5 0.1 fusion.14
  12.6 0.1 copy.110
  12.8 0.1 stack.71
  12.9 0.1 stack.70
  13.1 0.2 copy.114
  13.3 0.3 reshape.608
  13.6 4.7 %collective-permute-start.3 = (bf16[8,4096]{1,0:T(8,128)(2,1)S(1)}, bf16[8,4096]{1,0:T(8,128)(2,1)S(1)}, u32[]{:S(2)}, u32[]{:S(2)}) collective-permute-start(bf16[8,4096]{1,0:T(8,128)(2,1)S(1)} %reshape.608), channel_id=1, source_target_pairs={{0,18},{2,16},{4,22},{6,20},{8,26},{10,24},{12,30},{14,28},{16,2},... | collective-permute-start | bytes 196616 | tf_op jit(solution)/shard_map/ppermute | solution.py:307
  18.3 0.5 %collective-permute-start.1 = (bf16[8,4096]{1,0:T(8,128)(2,1)S(1)}, bf16[8,4096]{1,0:T(8,128)(2,1)S(1)}, u32[]{:S(2)}, u32[]{:S(2)}) collective-permute-start(bf16[8,4096]{1,0:T(8,128)(2,1)S(1)} %reshape.608), channel_id=1, source_target_pairs={{0,2},{2,0},{1,3},{3,1},{4,6},{6,4},{5,7},{7,5},{8,10},{10,8},{9,1... | collective-permute-start | bytes 196616 | tf_op jit(solution)/shard_map/ppermute | solution.py:301
  18.8 0.2 copy.118
  19.0 0.3 reshape.612
  19.3 0.2 collective-permute-start.2
  19.5 3.3 %collective-permute-done.1 = bf16[8,4096]{1,0:T(8,128)(2,1)S(1)} collective-permute-done((bf16[8,4096]{1,0:T(8,128)(2,1)S(1)}, bf16[8,4096]{1,0:T(8,128)(2,1)S(1)}, u32[]{:S(2)}, u32[]{:S(2)}) %collective-permute-start.1) | collective-permute-done | bytes 65568 | tf_op jit(solution)/shard_map/ppermute | solution.py:301
  22.8 0.2 reshape.609
  23.0 0.1 copy.115
  23.2 0.1 copy.116
  23.4 0.1 copy.155
  23.5 0.2 reshape.614
  23.7 2.2 %collective-permute-done.2 = bf16[8,4224]{1,0:T(8,128)(2,1)S(1)} collective-permute-done((bf16[8,4224]{1,0:T(8,128)(2,1)S(1)}, bf16[8,4224]{1,0:T(8,128)(2,1)S(1)}, u32[]{:S(2)}, u32[]{:S(2)}) %collective-permute-start.2) | collective-permute-done | bytes 67616 | tf_op jit(solution)/shard_map/ppermute | solution.py:298
  25.8 0.2 reshape.613
  26.0 0.1 maximum_bitcast_fusion.2
  26.1 0.1 copy.154
  26.3 0.1 pad_maximum_fusion.8
  26.4 1.6 %collective-permute-start.6 = (bf16[2,4,8320]{2,1,0:T(4,128)(2,1)S(1)}, bf16[2,4,8320]{2,1,0:T(4,128)(2,1)S(1)}, u32[]{:S(2)}, u32[]{:S(2)}) collective-permute-start(bf16[2,4,8320]{2,1,0:T(4,128)(2,1)S(1)} %get-tuple-element.17), channel_id=1, source_target_pairs={{0,4},{4,0},{8,12},{12,8},{16,20},{20,16},{24,28},{28,24},{1,5},{5... | collective-permute-start | bytes 399368 | tf_op jit(solution)/shard_map/ppermute | solution.py:187
  28.0 0.3 collective-permute-start.4
  28.3 3.1 %collective-permute-done.6 = bf16[2,4,8320]{2,1,0:T(4,128)(2,1)S(1)} collective-permute-done((bf16[2,4,8320]{2,1,0:T(4,128)(2,1)S(1)}, bf16[2,4,8320]{2,1,0:T(4,128)(2,1)S(1)}, u32[]{:S(2)}, u32[]{:S(2)}) %collective-permute-start.6) | collective-permute-done | bytes 133152 | tf_op jit(solution)/shard_map/ppermute | solution.py:187
  31.4 0.2 fusion.87
  31.6 0.7 %collective-permute-start.7 = (bf16[2,2,4,8320]{3,2,0,1:T(4,128)(2,1)S(1)}, bf16[2,2,4,8320]{3,2,0,1:T(4,128)(2,1)S(1)}, u32[]{:S(2)}, u32[]{:S(2)}) collective-permute-start(bf16[2,2,4,8320]{3,2,0,1:T(4,128)(2,1)S(1)} %get-tuple-element.16), channel_id=1, source_target_pairs={{0,8},{4,12},{8,0},{12,4},{16,24},{20,28},{24,16},{28,20},{1,9},{5... | collective-permute-start | bytes 798728 | tf_op jit(solution)/shard_map/ppermute | solution.py:187
  32.3 1.6 %collective-permute-done.4 = bf16[2,4,8320]{2,1,0:T(4,128)(2,1)S(1)} collective-permute-done((bf16[2,4,8320]{2,1,0:T(4,128)(2,1)S(1)}, bf16[2,4,8320]{2,1,0:T(4,128)(2,1)S(1)}, u32[]{:S(2)}, u32[]{:S(2)}) %collective-permute-start.4) | collective-permute-done | bytes 133152 | tf_op jit(solution)/shard_map/ppermute | solution.py:187
  34.0 0.2 fusion.88
  34.3 4.5 %collective-permute-done.7 = bf16[2,2,4,8320]{3,2,0,1:T(4,128)(2,1)S(1)} collective-permute-done((bf16[2,2,4,8320]{3,2,0,1:T(4,128)(2,1)S(1)}, bf16[2,2,4,8320]{3,2,0,1:T(4,128)(2,1)S(1)}, u32[]{:S(2)}, u32[]{:S(2)}) %collective-permute-start.7) | collective-permute-done | bytes 266272 | tf_op jit(solution)/shard_map/ppermute | solution.py:187
  38.7 0.4 pad_maximum_fusion.1
  39.1 0.2 copy.120
  39.3 1.4 %collective-permute-done.5 = bf16[2,2,4,8320]{3,2,0,1:T(4,128)(2,1)S(1)} collective-permute-done((bf16[2,2,4,8320]{3,2,0,1:T(4,128)(2,1)S(1)}, bf16[2,2,4,8320]{3,2,0,1:T(4,128)(2,1)S(1)}, u32[]{:S(2)}, u32[]{:S(2)}) %collective-permute-start.5) | collective-permute-done | bytes 266272 | tf_op jit(solution)/shard_map/ppermute | solution.py:187
  40.7 0.4 pad_maximum_fusion
  41.0 0.2 copy.119
  41.3 0.2 copy.133
  41.5 0.1 multiply_reduce_fusion
  41.9 0.1 copy.124
  42.0 0.1 eq.68
  42.1 0.1 copy.125
  42.2 0.1 eq.71
  42.4 1.0 %bitcast_convert_fusion = bf16[64,128,128]{1,2,0:T(8,128)(2,1)S(1)} fusion(s32[128]{0:T(128)S(1)} %eq.71, s32[128]{0:T(128)S(1)} %eq.68, bf16[8,4,8320]{2,1,0:T(4,128)(2,1)S(1)} %bitcast.138, bf16[8,4,8320]{2,1,0:T(4,128)(2,1)S(1)} %bitcast.136), kind=kOutput, calls=%fused_computation | convolution fusion | flops 139493376 | bytes 3163136 | tf_op jit(solution)/shard_map/rsc,scbq->brq/dot_general | solution.py:383
  43.5 0.3 copy.127
  43.9 0.1 pad_maximum_fusion.3
  44.0 0.3 copy.128
  44.3 1.2 %convolution_multiply_fusion = f32[64,32,128]{2,1,0:T(8,128)S(1)} fusion(bf16[64,128,128]{1,2,0:T(8,128)(2,1)S(1)} %bitcast_convert_fusion, bf16[64,16,128]{2,1,0:T(8,128)(2,1)S(1)} %copy.128, bf16[64,16,128]{2,1,0:T(8,128)(2,1)S(1)} %dynamic-slice_bitcast_fusion), kind=kOutput, calls=%fused_computation.1 | convolution fusion | flops 68419584 | bytes 3670016 | tf_op jit(solution)/shard_map/bpq,bjq->bpj/dot_general | solution.py:391
  45.5 1.1 %copy.153 = f32[64,2,16,128]{3,2,0,1:T(8,128)} copy(f32[64,2,16,128]{3,2,1,0:T(8,128)S(1)} %bitcast.133) | data formatting | bytes 2097152 | tf_op jit(solution)/shard_map/div | solution.py:394
  (50 shorter events, 1.2 us)
Async XLA Ops:
  0.0 10.3 %copy-start = (f32[128]{0:T(128)S(1)}, f32[128]{0:T(128)}, u32[]{:S(2)}) copy-start(f32[128]{0:T(128)} %param.5) | copy-start | bytes 1540
  8.1 3.4 %copy-start.1 = (s32[1,8,2]{1,2,0:T(2,128)S(1)}, s32[1,8,2]{1,2,0:T(2,128)}, u32[]{:S(2)}) copy-start(s32[1,8,2]{1,2,0:T(2,128)} %param.7) | copy-start | bytes 196
  8.1 3.4 %copy-start.2 = (s32[1,8,2]{1,2,0:T(2,128)S(1)}, s32[1,8,2]{1,2,0:T(2,128)}, u32[]{:S(2)}) copy-start(s32[1,8,2]{1,2,0:T(2,128)} %param.6) | copy-start | bytes 196
  9.8 2.3 %collective-permute-start = (f32[144,2,256]{0,2,1:T(8,128)S(1)}, f32[144,2,256]{0,2,1:T(8,128)S(1)}, u32[]{:S(2)}, u32[]{:S(2)}) collective-permute-start(f32[144,2,256]{0,2,1:T(8,128)S(1)} %pad_maximum_fusion.2), channel_id=1, source_target_pairs={{0,1},{1,0},{2,3},{3,2},{4,5},{5,4},{6,7},{7,6},{8,9},{9,8},{10,11... | collective-permute-start | bytes 884744 | tf_op jit(solution)/shard_map/ppermute | solution.py:24
  13.6 9.9 %collective-permute-start.3 = (bf16[8,4096]{1,0:T(8,128)(2,1)S(1)}, bf16[8,4096]{1,0:T(8,128)(2,1)S(1)}, u32[]{:S(2)}, u32[]{:S(2)}) collective-permute-start(bf16[8,4096]{1,0:T(8,128)(2,1)S(1)} %reshape.608), channel_id=1, source_target_pairs={{0,18},{2,16},{4,22},{6,20},{8,26},{10,24},{12,30},{14,28},{16,2},... | collective-permute-start | bytes 196616 | tf_op jit(solution)/shard_map/ppermute | solution.py:307
  18.3 4.5 %collective-permute-start.1 = (bf16[8,4096]{1,0:T(8,128)(2,1)S(1)}, bf16[8,4096]{1,0:T(8,128)(2,1)S(1)}, u32[]{:S(2)}, u32[]{:S(2)}) collective-permute-start(bf16[8,4096]{1,0:T(8,128)(2,1)S(1)} %reshape.608), channel_id=1, source_target_pairs={{0,2},{2,0},{1,3},{3,1},{4,6},{6,4},{5,7},{7,5},{8,10},{10,8},{9,1... | collective-permute-start | bytes 196616 | tf_op jit(solution)/shard_map/ppermute | solution.py:301
  19.3 6.5 %collective-permute-start.2 = (bf16[8,4224]{1,0:T(8,128)(2,1)S(1)}, bf16[8,4224]{1,0:T(8,128)(2,1)S(1)}, u32[]{:S(2)}, u32[]{:S(2)}) collective-permute-start(bf16[8,4224]{1,0:T(8,128)(2,1)S(1)} %pad_maximum_fusion.11), channel_id=1, source_target_pairs={{0,16},{4,20},{8,24},{12,28},{16,0},{20,4},{24,8},{28,12},{1,17},{... | collective-permute-start | bytes 202760 | tf_op jit(solution)/shard_map/ppermute | solution.py:298
  26.4 5.1 %collective-permute-start.6 = (bf16[2,4,8320]{2,1,0:T(4,128)(2,1)S(1)}, bf16[2,4,8320]{2,1,0:T(4,128)(2,1)S(1)}, u32[]{:S(2)}, u32[]{:S(2)}) collective-permute-start(bf16[2,4,8320]{2,1,0:T(4,128)(2,1)S(1)} %get-tuple-element.17), channel_id=1, source_target_pairs={{0,4},{4,0},{8,12},{12,8},{16,20},{20,16},{24,28},{28,24},{1,5},{5... | collective-permute-start | bytes 399368 | tf_op jit(solution)/shard_map/ppermute | solution.py:187
  28.0 5.9 %collective-permute-start.4 = (bf16[2,4,8320]{2,1,0:T(4,128)(2,1)S(1)}, bf16[2,4,8320]{2,1,0:T(4,128)(2,1)S(1)}, u32[]{:S(2)}, u32[]{:S(2)}) collective-permute-start(bf16[2,4,8320]{2,1,0:T(4,128)(2,1)S(1)} %get-tuple-element.18), channel_id=1, source_target_pairs={{0,8},{4,12},{8,0},{12,4},{16,24},{20,28},{24,16},{28,20},{1,9},{5... | collective-permute-start | bytes 399368 | tf_op jit(solution)/shard_map/ppermute | solution.py:187
  31.6 7.1 %collective-permute-start.7 = (bf16[2,2,4,8320]{3,2,0,1:T(4,128)(2,1)S(1)}, bf16[2,2,4,8320]{3,2,0,1:T(4,128)(2,1)S(1)}, u32[]{:S(2)}, u32[]{:S(2)}) collective-permute-start(bf16[2,2,4,8320]{3,2,0,1:T(4,128)(2,1)S(1)} %get-tuple-element.16), channel_id=1, source_target_pairs={{0,8},{4,12},{8,0},{12,4},{16,24},{20,28},{24,16},{28,20},{1,9},{5... | collective-permute-start | bytes 798728 | tf_op jit(solution)/shard_map/ppermute | solution.py:187
  34.2 6.5 %collective-permute-start.5 = (bf16[2,2,4,8320]{3,2,0,1:T(4,128)(2,1)S(1)}, bf16[2,2,4,8320]{3,2,0,1:T(4,128)(2,1)S(1)}, u32[]{:S(2)}, u32[]{:S(2)}) collective-permute-start(bf16[2,2,4,8320]{3,2,0,1:T(4,128)(2,1)S(1)} %get-tuple-element.20), channel_id=1, source_target_pairs={{0,4},{4,0},{8,12},{12,8},{16,20},{20,16},{24,28},{28,24},{1,5},{5... | collective-permute-start | bytes 798728 | tf_op jit(solution)/shard_map/ppermute | solution.py:187

commit v16 on v15

--- a/solution.py
+++ b/solution.py
@@ -98,8 +98,8 @@
             sin_tile = jnp.concatenate(sin_parts, axis=0).astype(jnp.bfloat16)
             first = pl.multiple_of((index * group + 2 * pair) * lanes, 2 * lanes)
             rec = rec_ref[:, pl.ds(first, 2 * lanes)]
-            re_ref[...] += jnp.dot(rec, cos_tile, preferred_element_type=jnp.float32)
-            im_ref[...] += jnp.dot(rec, sin_tile, preferred_element_type=jnp.float32)
+            re_ref[...] += lax.dot_general(cos_tile, rec, (((0,), (1,)), ((), ())), preferred_element_type=jnp.float32)
+            im_ref[...] += lax.dot_general(sin_tile, rec, (((0,), (1,)), ((), ())), preferred_element_type=jnp.float32)
         return carry
 
     lax.fori_loop(0, groups, one_group, 0)
@@ -152,10 +152,10 @@
             pl.BlockSpec(cos_b.shape, full),
             pl.BlockSpec(sin_b.shape, full),
         ],
-        out_specs=[pl.BlockSpec((rows, bins), full), pl.BlockSpec((rows, bins), full)],
+        out_specs=[pl.BlockSpec((bins, rows), full), pl.BlockSpec((bins, rows), full)],
         out_shape=[
-            jax.ShapeDtypeStruct((rows, bins), jnp.float32),
-            jax.ShapeDtypeStruct((rows, bins), jnp.float32),
+            jax.ShapeDtypeStruct((bins, rows), jnp.float32),
+            jax.ShapeDtypeStruct((bins, rows), jnp.float32),
         ],
         compiler_params=pltpu.CompilerParams(dimension_semantics=("arbitrary",)),
     )(records, cos_a, nsin_a, cos_b, sin_b)
@@ -211,9 +211,7 @@
         ) * block_bins + local_row % block_bins
 
     band_rows = band_of(jnp.arange(device_bins * freq_count, dtype=jnp.int32))
-    real_t, imag_t = dft_fused(records, band_rows, freq_rank * half_len)
-    real_all = real_t.T
-    imag_all = imag_t.T
+    real_all, imag_all = dft_fused(records, band_rows, freq_rank * half_len)
     blocks = jnp.stack([real_all, imag_all], axis=1)
     blocks = blocks.reshape(freq_count, device_bins, 2, records.shape[0])
     if freq_count == 2:

time: 46.8 us -> 47.7 us (1.019)
  local copies, waits for them, and re-layouts: 6.23 us -> 6.76 us
  waiting for transfers between devices: 16.1 us -> 16.6 us
    dynamic_slice x1 -> x3, local copies, waits for them, and re-layouts: 0.17 us -> 0.96 us  [per_device(): keep = lax.dynamic_index_in_dim(whitened, seg_rank, axis=0, keepdims=False)]
    ppermute x4, waiting for transfers between devices: 10.6 us -> 11.1 us  [gather_blocks(): arrived = lax.ppermute(part, 'blk', pairs)]
where the time goes in v16:
time: 47.7 us; the launch traced here: 47.5 us
  waiting for transfers between devices  16.6 us (35%)
  starting transfers between devices  8.38 us (18%)
  local copies, waits for them, and re-layouts  6.76 us (14%)
  Pallas kernels  6.55 us (14%)
  other arithmetic  5.42 us (11%)
  matrix products  3.25 us (7%)
  between operations  0.49 us (1%)
    ppermute x4, waiting for transfers between devices, gather_blocks(): arrived = lax.ppermute(part, 'blk', pairs)  11.1 us
    pallas_call x1, Pallas kernels, dft_fused(): pl.pallas_call(dft_kernel, grid=(count // chunk,), in_specs=[pl.BlockSpec...  6.55 us
    ppermute x1, starting transfers between devices, per_device(): from_diagonal = lax.ppermute(other_flat, ('blk', 'seg'), diagonal)  4.72 us
    ppermute x1, waiting for transfers between devices, per_device(): from_seg = lax.ppermute(other_flat, 'seg', [(0, 1), (1, 0)])  3.17 us
    ppermute x4, starting transfers between devices, gather_blocks(): arrived = lax.ppermute(part, 'blk', pairs)  2.43 us
    ppermute x1, waiting for transfers between devices, per_device(): lax.ppermute(keep_flat, 'blk', [(source, source ^ first) for source in ra...  2.36 us
    select_n x1, other arithmetic, per_device(): sent = jnp.where(freq_rank == 0, blocks[1], blocks[0])  1.27 us
    dot_general x1, matrix products, per_device(): jnp.einsum('bpq,bjq->bpj', lhs, routed, preferred_element_type=jnp.float32)  1.19 us
  transfers between devices with their start and end apart: 8, of which 6 were waited for; matrix products, arithmetic and copies ran while one was open for 8% of the time, Pallas kernels for 0%

profile of v16, /device:TPU:0, one launch (start us, length us, event | category | flops | bytes accessed | tf_op | source)
XLA Modules:
  0.0 47.5 jit_solution(14195520053085987311)
XLA Ops:
  0.0 0.1 fusion.63
  0.1 0.2 fusion.65
  0.3 0.7 %negate_bitcast_fusion = (f32[64,256]{1,0:T(8,128)}, f32[64,256]{1,0:T(8,128)}) fusion(f32[8,256]{1,0:T(8,128)S(1)} %get-tuple-element.43, f32[8,256]{1,0:T(8,128)S(1)} %get-tuple-element.45, f32[8,256]{1,0:T(8,128)S(1)} %get-tuple-element.44, f32[8,256]{1,0:T(8,128)S(1)} %get-tuple-element.46), kind=kLoop, calls=%fused_computation.95 | loop fusion | flops 114688 | bytes 163840 | tf_op jit(solution)/shard_map/neg | solution.py:136
  1.0 0.7 %add_multiply_fusion = (f32[8,16,256]{2,1,0:T(8,128)}, f32[8,16,256]{2,1,0:T(8,128)}) fusion(f32[16,256]{1,0:T(8,128)S(1)} %get-tuple-element.48, f32[8,256]{1,0:T(8,128)S(1)} %get-tuple-element.38, f32[16,256]{1,0:T(8,128)S(1)} %get-tuple-element.47, f32[8,256]{1,0:T(8,128)S(1)} %get-tuple-element.37), kind=kLoop, calls=%fused_computation.77 | loop fusion | flops 262144 | bytes 311296 | tf_op jit(solution)/shard_map/mul | solution.py:141
  1.7 6.6 %shard_map.46 = (f32[256,256]{1,0:T(8,128)}, f32[256,256]{1,0:T(8,128)}) custom-call(bf16[256,8192]{1,0:T(8,128)(2,1)} %bitcast.141, f32[64,256]{1,0:T(8,128)} %get-tuple-element.30.cos_a_ref, f32[64,256]{1,0:T(8,128)} %get-tuple-element.29.nsin_a_ref, f32[128,256]{1,0:T(8,128)} %bitcast.153, f32[128,256]{1,0:T(8,128)} %bitcast.152), custom_call_target="tpu_custom_call" | custom-call | tf_op jit(solution)/shard_map/pallas_call | solution.py:145
  8.3 1.3 %broadcast_select_fusion = (f32[128,2,256]{2,0,1:T(8,128)S(1)}, f32[128,2,256]{2,0,1:T(8,128)S(1)}) fusion(pred[]{:T(512)S(6)} %eq.64, f32[256,1,256]{2,0,1:T(8,128)} %bitcast.163, f32[256,1,256]{2,0,1:T(8,128)} %bitcast.162), kind=kLoop, calls=%fused_computation.79 | loop fusion | flops 327680 | bytes 1048577 | tf_op jit(solution)/shard_map/jit(_where)/select_n | solution.py:219
  9.6 0.5 %collective-permute-start = (f32[144,2,256]{2,0,1:T(8,128)S(1)}, f32[144,2,256]{2,0,1:T(8,128)S(1)}, u32[]{:S(2)}, u32[]{:S(2)}) collective-permute-start(f32[144,2,256]{2,0,1:T(8,128)S(1)} %pad_maximum_fusion.3), channel_id=1, source_target_pairs={{0,1},{1,0},{2,3},{3,2},{4,5},{5,4},{6,7},{7,6},{8,9},{9,8},{10,11... | collective-permute-start | bytes 884744 | tf_op jit(solution)/shard_map/ppermute | solution.py:24
  10.2 0.5 %convolution_bitcast_fusion = f32[128]{0:T(128)S(1)} fusion(s32[128]{0:T(128)S(1)} %fusion.82, f32[128]{0:T(128)S(1)} %copy-done), kind=kOutput, calls=%fused_computation.4 | convolution fusion | flops 442368 | bytes 1536 | tf_op jit(solution)/shard_map/dot_general | solution.py:67
  10.7 0.5 %convolution_bitcast_fusion.1 = f32[128]{0:T(128)S(1)} fusion(s32[128]{0:T(128)S(1)} %fusion.82, f32[128]{0:T(128)S(1)} %copy-done), kind=kOutput, calls=%fused_computation.5 | convolution fusion | flops 425984 | bytes 1536 | tf_op jit(solution)/shard_map/dot_general | solution.py:66
  11.4 0.1 copy.64
  11.5 0.1 convert_element_type.91
  11.8 0.1 fusion.14
  11.9 0.1 add_convert_fusion
  12.0 0.1 copy.59
  12.2 0.1 stack.71
  12.3 0.1 copy.58
  12.4 0.1 stack.70
  12.5 0.1 constant_dynamic-update-slice_fusion.1
  12.6 0.1 constant_dynamic-update-slice_fusion
  12.7 0.6 %dynamic-slice_bitcast_fusion.2 = (bf16[1,8,64,2,32]{2,0,4,1,3:T(2,128)(2,1)S(1)}, bf16[1,8,64,2,32]{2,0,4,1,3:T(2,128)(2,1)S(1)}) fusion(bf16[2,64,2,8,32]{1,0,4,3,2:T(2,128)(2,1)S(1)} %constant_dynamic-update-slice_fusion, s32[]{:T(128)S(6)} %select_n.241, s32[]{:T(128)S(6)} %select_n.242), kind=kLoop, calls=%fused_computation.39 | loop fusion | bytes 262152 | tf_op jit(solution)/shard_map/jit(dynamic_index_in_dim)/dynamic_slice | solution.py:289
  13.3 0.3 copy.61
  13.7 0.3 reshape.608
  14.0 4.7 %collective-permute-start.3 = (bf16[8,4096]{1,0:T(8,128)(2,1)S(1)}, bf16[8,4096]{1,0:T(8,128)(2,1)S(1)}, u32[]{:S(2)}, u32[]{:S(2)}) collective-permute-start(bf16[8,4096]{1,0:T(8,128)(2,1)S(1)} %reshape.608), channel_id=1, source_target_pairs={{0,18},{2,16},{4,22},{6,20},{8,26},{10,24},{12,30},{14,28},{16,2},... | collective-permute-start | bytes 196616 | tf_op jit(solution)/shard_map/ppermute | solution.py:305
  18.7 0.5 %collective-permute-start.1 = (bf16[8,4096]{1,0:T(8,128)(2,1)S(1)}, bf16[8,4096]{1,0:T(8,128)(2,1)S(1)}, u32[]{:S(2)}, u32[]{:S(2)}) collective-permute-start(bf16[8,4096]{1,0:T(8,128)(2,1)S(1)} %reshape.608), channel_id=1, source_target_pairs={{0,2},{2,0},{1,3},{3,1},{4,6},{6,4},{5,7},{7,5},{8,10},{10,8},{9,1... | collective-permute-start | bytes 196616 | tf_op jit(solution)/shard_map/ppermute | solution.py:299
  19.2 0.3 copy.65
  19.6 0.3 reshape.612
  19.9 0.2 collective-permute-start.2
  20.1 3.2 %collective-permute-done.1 = bf16[8,4096]{1,0:T(8,128)(2,1)S(1)} collective-permute-done((bf16[8,4096]{1,0:T(8,128)(2,1)S(1)}, bf16[8,4096]{1,0:T(8,128)(2,1)S(1)}, u32[]{:S(2)}, u32[]{:S(2)}) %collective-permute-start.1) | collective-permute-done | bytes 65568 | tf_op jit(solution)/shard_map/ppermute | solution.py:299
  23.2 0.2 reshape.609
  23.4 0.1 copy.62
  23.6 0.1 copy.63
  23.8 0.1 copy.97
  23.9 0.2 reshape.614
  24.1 2.4 %collective-permute-done.2 = bf16[8,4224]{1,0:T(8,128)(2,1)S(1)} collective-permute-done((bf16[8,4224]{1,0:T(8,128)(2,1)S(1)}, bf16[8,4224]{1,0:T(8,128)(2,1)S(1)}, u32[]{:S(2)}, u32[]{:S(2)}) %collective-permute-start.2) | collective-permute-done | bytes 67616 | tf_op jit(solution)/shard_map/ppermute | solution.py:296
  26.4 0.2 reshape.613
  26.6 0.1 maximum_bitcast_fusion.2
  26.7 0.1 copy.96
  26.9 0.1 pad_maximum_fusion.8
  27.0 1.6 %collective-permute-start.6 = (bf16[2,4,8320]{2,1,0:T(4,128)(2,1)S(1)}, bf16[2,4,8320]{2,1,0:T(4,128)(2,1)S(1)}, u32[]{:S(2)}, u32[]{:S(2)}) collective-permute-start(bf16[2,4,8320]{2,1,0:T(4,128)(2,1)S(1)} %get-tuple-element.17), channel_id=1, source_target_pairs={{0,4},{4,0},{8,12},{12,8},{16,20},{20,16},{24,28},{28,24},{1,5},{5... | collective-permute-start | bytes 399368 | tf_op jit(solution)/shard_map/ppermute | solution.py:187
  28.6 0.3 collective-permute-start.4
  28.9 3.1 %collective-permute-done.6 = bf16[2,4,8320]{2,1,0:T(4,128)(2,1)S(1)} collective-permute-done((bf16[2,4,8320]{2,1,0:T(4,128)(2,1)S(1)}, bf16[2,4,8320]{2,1,0:T(4,128)(2,1)S(1)}, u32[]{:S(2)}, u32[]{:S(2)}) %collective-permute-start.6) | collective-permute-done | bytes 133152 | tf_op jit(solution)/shard_map/ppermute | solution.py:187
  32.0 0.2 fusion.90
  32.2 0.5 %collective-permute-start.7 = (bf16[2,2,4,8320]{3,2,0,1:T(4,128)(2,1)S(1)}, bf16[2,2,4,8320]{3,2,0,1:T(4,128)(2,1)S(1)}, u32[]{:S(2)}, u32[]{:S(2)}) collective-permute-start(bf16[2,2,4,8320]{3,2,0,1:T(4,128)(2,1)S(1)} %get-tuple-element.16), channel_id=1, source_target_pairs={{0,8},{4,12},{8,0},{12,4},{16,24},{20,28},{24,16},{28,20},{1,9},{5... | collective-permute-start | bytes 798728 | tf_op jit(solution)/shard_map/ppermute | solution.py:187
  32.7 2.2 %collective-permute-done.4 = bf16[2,4,8320]{2,1,0:T(4,128)(2,1)S(1)} collective-permute-done((bf16[2,4,8320]{2,1,0:T(4,128)(2,1)S(1)}, bf16[2,4,8320]{2,1,0:T(4,128)(2,1)S(1)}, u32[]{:S(2)}, u32[]{:S(2)}) %collective-permute-start.4) | collective-permute-done | bytes 133152 | tf_op jit(solution)/shard_map/ppermute | solution.py:187
  34.9 0.2 fusion.91
  35.2 4.1 %collective-permute-done.7 = bf16[2,2,4,8320]{3,2,0,1:T(4,128)(2,1)S(1)} collective-permute-done((bf16[2,2,4,8320]{3,2,0,1:T(4,128)(2,1)S(1)}, bf16[2,2,4,8320]{3,2,0,1:T(4,128)(2,1)S(1)}, u32[]{:S(2)}, u32[]{:S(2)}) %collective-permute-start.7) | collective-permute-done | bytes 266272 | tf_op jit(solution)/shard_map/ppermute | solution.py:187
  39.3 0.4 pad_maximum_fusion.1
  39.7 0.2 copy.67
  39.9 1.7 %collective-permute-done.5 = bf16[2,2,4,8320]{3,2,0,1:T(4,128)(2,1)S(1)} collective-permute-done((bf16[2,2,4,8320]{3,2,0,1:T(4,128)(2,1)S(1)}, bf16[2,2,4,8320]{3,2,0,1:T(4,128)(2,1)S(1)}, u32[]{:S(2)}, u32[]{:S(2)}) %collective-permute-start.5) | collective-permute-done | bytes 266272 | tf_op jit(solution)/shard_map/ppermute | solution.py:187
  41.6 0.4 pad_maximum_fusion
  41.9 0.2 copy.66
  42.2 0.2 copy.80
  42.5 0.1 multiply_reduce_fusion
  42.6 0.1 copy.84
  42.8 0.1 copy.71
  42.9 0.1 eq.68
  43.0 0.1 copy.72
  43.2 0.1 eq.71
  43.3 1.0 %bitcast_convert_fusion = bf16[64,128,128]{1,2,0:T(8,128)(2,1)S(1)} fusion(s32[128]{0:T(128)S(1)} %eq.71, s32[128]{0:T(128)S(1)} %eq.68, bf16[8,4,8320]{2,1,0:T(4,128)(2,1)S(1)} %bitcast.145, bf16[8,4,8320]{2,1,0:T(4,128)(2,1)S(1)} %bitcast.143), kind=kOutput, calls=%fused_computation | convolution fusion | flops 139493376 | bytes 3163136 | tf_op jit(solution)/shard_map/rsc,scbq->brq/dot_general | solution.py:381
  44.4 0.3 copy.74
  44.8 0.1 pad_maximum_fusion.2
  44.9 0.3 copy.75
  45.2 1.2 %convolution_multiply_fusion = f32[64,32,128]{2,1,0:T(8,128)S(1)} fusion(bf16[64,128,128]{1,2,0:T(8,128)(2,1)S(1)} %bitcast_convert_fusion, bf16[64,16,128]{2,1,0:T(8,128)(2,1)S(1)} %copy.75, bf16[64,16,128]{2,1,0:T(8,128)(2,1)S(1)} %dynamic-slice_bitcast_fusion), kind=kOutput, calls=%fused_computation.1 | convolution fusion | flops 68419584 | bytes 3670016 | tf_op jit(solution)/shard_map/bpq,bjq->bpj/dot_general | solution.py:389
  46.4 1.1 %copy.95 = f32[64,2,16,128]{3,2,0,1:T(8,128)} copy(f32[64,2,16,128]{3,2,1,0:T(8,128)S(1)} %bitcast.140) | data formatting | bytes 2097152 | tf_op jit(solution)/shard_map/div | solution.py:392
  (45 shorter events, 0.9 us)
Async XLA Ops:
  0.0 10.2 %copy-start = (f32[128]{0:T(128)S(1)}, f32[128]{0:T(128)}, u32[]{:S(2)}) copy-start(f32[128]{0:T(128)} %param.5) | copy-start | bytes 1540
  8.3 3.0 %copy-start.1 = (s32[1,8,2]{1,2,0:T(2,128)S(1)}, s32[1,8,2]{1,2,0:T(2,128)}, u32[]{:S(2)}) copy-start(s32[1,8,2]{1,2,0:T(2,128)} %param.7) | copy-start | bytes 196
  8.3 3.0 %copy-start.2 = (s32[1,8,2]{1,2,0:T(2,128)S(1)}, s32[1,8,2]{1,2,0:T(2,128)}, u32[]{:S(2)}) copy-start(s32[1,8,2]{1,2,0:T(2,128)} %param.6) | copy-start | bytes 196
  9.6 2.0 %collective-permute-start = (f32[144,2,256]{2,0,1:T(8,128)S(1)}, f32[144,2,256]{2,0,1:T(8,128)S(1)}, u32[]{:S(2)}, u32[]{:S(2)}) collective-permute-start(f32[144,2,256]{2,0,1:T(8,128)S(1)} %pad_maximum_fusion.3), channel_id=1, source_target_pairs={{0,1},{1,0},{2,3},{3,2},{4,5},{5,4},{6,7},{7,6},{8,9},{9,8},{10,11... | collective-permute-start | bytes 884744 | tf_op jit(solution)/shard_map/ppermute | solution.py:24
  14.0 9.9 %collective-permute-start.3 = (bf16[8,4096]{1,0:T(8,128)(2,1)S(1)}, bf16[8,4096]{1,0:T(8,128)(2,1)S(1)}, u32[]{:S(2)}, u32[]{:S(2)}) collective-permute-start(bf16[8,4096]{1,0:T(8,128)(2,1)S(1)} %reshape.608), channel_id=1, source_target_pairs={{0,18},{2,16},{4,22},{6,20},{8,26},{10,24},{12,30},{14,28},{16,2},... | collective-permute-start | bytes 196616 | tf_op jit(solution)/shard_map/ppermute | solution.py:305
  18.7 4.5 %collective-permute-start.1 = (bf16[8,4096]{1,0:T(8,128)(2,1)S(1)}, bf16[8,4096]{1,0:T(8,128)(2,1)S(1)}, u32[]{:S(2)}, u32[]{:S(2)}) collective-permute-start(bf16[8,4096]{1,0:T(8,128)(2,1)S(1)} %reshape.608), channel_id=1, source_target_pairs={{0,2},{2,0},{1,3},{3,1},{4,6},{6,4},{5,7},{7,5},{8,10},{10,8},{9,1... | collective-permute-start | bytes 196616 | tf_op jit(solution)/shard_map/ppermute | solution.py:299
  19.9 6.5 %collective-permute-start.2 = (bf16[8,4224]{1,0:T(8,128)(2,1)S(1)}, bf16[8,4224]{1,0:T(8,128)(2,1)S(1)}, u32[]{:S(2)}, u32[]{:S(2)}) collective-permute-start(bf16[8,4224]{1,0:T(8,128)(2,1)S(1)} %pad_maximum_fusion.11), channel_id=1, source_target_pairs={{0,16},{4,20},{8,24},{12,28},{16,0},{20,4},{24,8},{28,12},{1,17},{... | collective-permute-start | bytes 202760 | tf_op jit(solution)/shard_map/ppermute | solution.py:296
  27.0 5.1 %collective-permute-start.6 = (bf16[2,4,8320]{2,1,0:T(4,128)(2,1)S(1)}, bf16[2,4,8320]{2,1,0:T(4,128)(2,1)S(1)}, u32[]{:S(2)}, u32[]{:S(2)}) collective-permute-start(bf16[2,4,8320]{2,1,0:T(4,128)(2,1)S(1)} %get-tuple-element.17), channel_id=1, source_target_pairs={{0,4},{4,0},{8,12},{12,8},{16,20},{20,16},{24,28},{28,24},{1,5},{5... | collective-permute-start | bytes 399368 | tf_op jit(solution)/shard_map/ppermute | solution.py:187
  28.6 6.3 %collective-permute-start.4 = (bf16[2,4,8320]{2,1,0:T(4,128)(2,1)S(1)}, bf16[2,4,8320]{2,1,0:T(4,128)(2,1)S(1)}, u32[]{:S(2)}, u32[]{:S(2)}) collective-permute-start(bf16[2,4,8320]{2,1,0:T(4,128)(2,1)S(1)} %get-tuple-element.18), channel_id=1, source_target_pairs={{0,8},{4,12},{8,0},{12,4},{16,24},{20,28},{24,16},{28,20},{1,9},{5... | collective-permute-start | bytes 399368 | tf_op jit(solution)/shard_map/ppermute | solution.py:187
  32.2 7.1 %collective-permute-start.7 = (bf16[2,2,4,8320]{3,2,0,1:T(4,128)(2,1)S(1)}, bf16[2,2,4,8320]{3,2,0,1:T(4,128)(2,1)S(1)}, u32[]{:S(2)}, u32[]{:S(2)}) collective-permute-start(bf16[2,2,4,8320]{3,2,0,1:T(4,128)(2,1)S(1)} %get-tuple-element.16), channel_id=1, source_target_pairs={{0,8},{4,12},{8,0},{12,4},{16,24},{20,28},{24,16},{28,20},{1,9},{5... | collective-permute-start | bytes 798728 | tf_op jit(solution)/shard_map/ppermute | solution.py:187
  35.1 6.5 %collective-permute-start.5 = (bf16[2,2,4,8320]{3,2,0,1:T(4,128)(2,1)S(1)}, bf16[2,2,4,8320]{3,2,0,1:T(4,128)(2,1)S(1)}, u32[]{:S(2)}, u32[]{:S(2)}) collective-permute-start(bf16[2,2,4,8320]{3,2,0,1:T(4,128)(2,1)S(1)} %get-tuple-element.20), channel_id=1, source_target_pairs={{0,4},{4,0},{8,12},{12,8},{16,20},{20,16},{24,28},{28,24},{1,5},{5... | collective-permute-start | bytes 798728 | tf_op jit(solution)/shard_map/ppermute | solution.py:187

commit v17 on v15

--- a/solution.py
+++ b/solution.py
@@ -217,8 +217,8 @@
     blocks = jnp.stack([real_all, imag_all], axis=1)
     blocks = blocks.reshape(freq_count, device_bins, 2, records.shape[0])
     if freq_count == 2:
-        kept = jnp.where(freq_rank == 0, blocks[0], blocks[1])
-        sent = jnp.where(freq_rank == 0, blocks[1], blocks[0])
+        kept = lax.dynamic_index_in_dim(blocks, freq_rank, axis=0, keepdims=False)
+        sent = lax.dynamic_index_in_dim(blocks, 1 - freq_rank, axis=0, keepdims=False)
         kept_blocks = kept.reshape(seg_count, block_bins, 2, -1)
         sent_blocks = sent.reshape(seg_count, block_bins, 2, -1)
         own_edges = jnp.concatenate(

time: 46.8 us -> 48.6 us (1.038)
  local copies, waits for them, and re-layouts: 6.23 us -> 8.96 us
  other arithmetic: 5.46 us -> 4.23 us
  waiting for transfers between devices: 16.1 us -> 16.6 us
    another operation x1 -> x4, local copies, waits for them, and re-layouts: 0.03 us -> 2.41 us  [the longest x2 2.18 us: per_device(): blocks = jnp.stack([real_all, imag_all], axis=1)]
    select_n x1 -> x0, other arithmetic: 1.27 us -> none  [per_device(): sent = jnp.where(freq_rank == 0, blocks[1], blocks[0])]
    dynamic_slice x1 -> x3, local copies, waits for them, and re-layouts: 0.17 us -> 0.96 us  [per_device(): keep = lax.dynamic_index_in_dim(whitened, seg_rank, axis=0, keepdims=False)]
    ppermute x4, waiting for transfers between devices: 10.6 us -> 11.1 us  [gather_blocks(): arrived = lax.ppermute(part, 'blk', pairs)]
where the time goes in v17:
time: 48.6 us; the launch traced here: 48.4 us
  waiting for transfers between devices  16.6 us (34%)
  local copies, waits for them, and re-layouts  8.96 us (18%)
  starting transfers between devices  8.38 us (17%)
  Pallas kernels  6.41 us (13%)
  other arithmetic  4.23 us (9%)
  matrix products  3.25 us (7%)
  between operations  0.52 us (1%)
    ppermute x4, waiting for transfers between devices, gather_blocks(): arrived = lax.ppermute(part, 'blk', pairs)  11.1 us
    pallas_call x1, Pallas kernels, dft_fused(): pl.pallas_call(dft_kernel, grid=(count // chunk,), in_specs=[pl.BlockSpec...  6.41 us
    ppermute x1, starting transfers between devices, per_device(): from_diagonal = lax.ppermute(other_flat, ('blk', 'seg'), diagonal)  4.72 us
    ppermute x1, waiting for transfers between devices, per_device(): from_seg = lax.ppermute(other_flat, 'seg', [(0, 1), (1, 0)])  3.17 us
    ppermute x4, starting transfers between devices, gather_blocks(): arrived = lax.ppermute(part, 'blk', pairs)  2.42 us
    ppermute x1, waiting for transfers between devices, per_device(): lax.ppermute(keep_flat, 'blk', [(source, source ^ first) for source in ra...  2.36 us
    another operation x2, local copies, waits for them, and re-layouts, per_device(): blocks = jnp.stack([real_all, imag_all], axis=1)  2.18 us
    dot_general x1, matrix products, per_device(): jnp.einsum('bpq,bjq->bpj', lhs, routed, preferred_element_type=jnp.float32)  1.19 us
  transfers between devices with their start and end apart: 8, of which 6 were waited for; matrix products, arithmetic and copies ran while one was open for 8% of the time, Pallas kernels for 0%

profile of v17, /device:TPU:0, one launch (start us, length us, event | category | flops | bytes accessed | tf_op | source)
XLA Modules:
  0.0 48.4 jit_solution(8592617448566352976)
XLA Ops:
  0.0 0.1 fusion.61
  0.1 0.2 fusion.63
  0.3 0.7 %negate_bitcast_fusion = (f32[64,256]{1,0:T(8,128)}, f32[64,256]{1,0:T(8,128)}) fusion(f32[8,256]{1,0:T(8,128)S(1)} %get-tuple-element.43, f32[8,256]{1,0:T(8,128)S(1)} %get-tuple-element.45, f32[8,256]{1,0:T(8,128)S(1)} %get-tuple-element.44, f32[8,256]{1,0:T(8,128)S(1)} %get-tuple-element.46), kind=kLoop, calls=%fused_computation.95 | loop fusion | flops 114688 | bytes 163840 | tf_op jit(solution)/shard_map/neg | solution.py:136
  1.0 0.7 %add_multiply_fusion = (f32[8,16,256]{2,1,0:T(8,128)}, f32[8,16,256]{2,1,0:T(8,128)}) fusion(f32[16,256]{1,0:T(8,128)S(1)} %get-tuple-element.48, f32[8,256]{1,0:T(8,128)S(1)} %get-tuple-element.38, f32[16,256]{1,0:T(8,128)S(1)} %get-tuple-element.47, f32[8,256]{1,0:T(8,128)S(1)} %get-tuple-element.37), kind=kLoop, calls=%fused_computation.79 | loop fusion | flops 262144 | bytes 311296 | tf_op jit(solution)/shard_map/mul | solution.py:141
  1.7 6.4 %shard_map.46 = (f32[256,256]{1,0:T(8,128)}, f32[256,256]{1,0:T(8,128)}) custom-call(bf16[256,8192]{1,0:T(8,128)(2,1)} %bitcast.147, f32[64,256]{1,0:T(8,128)} %get-tuple-element.30.cos_a_ref, f32[64,256]{1,0:T(8,128)} %get-tuple-element.29.nsin_a_ref, f32[128,256]{1,0:T(8,128)} %bitcast.162, f32[128,256]{1,0:T(8,128)} %bitcast.161), custom_call_target="tpu_custom_call" | custom-call | tf_op jit(solution)/shard_map/pallas_call | solution.py:145
  8.1 1.1 %copy.89 = f32[256,256]{1,0:T(8,128)S(1)} copy(f32[256,256]{0,1:T(8,128)} %bitcast.172) | data formatting | bytes 524288 | tf_op jit(solution)/shard_map/stack | solution.py:217
  9.2 1.1 %copy.90 = f32[256,256]{1,0:T(8,128)S(1)} copy(f32[256,256]{0,1:T(8,128)} %bitcast.171) | data formatting | bytes 524288 | tf_op jit(solution)/shard_map/stack | solution.py:217
  10.5 0.5 %collective-permute-start = (f32[144,2,256]{2,0,1:T(8,128)S(1)}, f32[144,2,256]{2,0,1:T(8,128)S(1)}, u32[]{:S(2)}, u32[]{:S(2)}) collective-permute-start(f32[144,2,256]{2,0,1:T(8,128)S(1)} %pad_maximum_fusion.3), channel_id=1, source_target_pairs={{0,1},{1,0},{2,3},{3,2},{4,5},{5,4},{6,7},{7,6},{8,9},{9,8},{10,11... | collective-permute-start | bytes 884744 | tf_op jit(solution)/shard_map/ppermute | solution.py:24
  11.0 0.5 %convolution_bitcast_fusion = f32[128]{0:T(128)S(1)} fusion(s32[128]{0:T(128)S(1)} %fusion.80, f32[128]{0:T(128)S(1)} %copy-done), kind=kOutput, calls=%fused_computation.4 | convolution fusion | flops 442368 | bytes 1536 | tf_op jit(solution)/shard_map/dot_general | solution.py:67
  11.5 0.5 %convolution_bitcast_fusion.1 = f32[128]{0:T(128)S(1)} fusion(s32[128]{0:T(128)S(1)} %fusion.80, f32[128]{0:T(128)S(1)} %copy-done), kind=kOutput, calls=%fused_computation.5 | convolution fusion | flops 425984 | bytes 1536 | tf_op jit(solution)/shard_map/dot_general | solution.py:66
  12.2 0.1 copy.73
  12.3 0.1 convert_element_type.91
  12.7 0.1 fusion.15
  12.8 0.1 add_convert_fusion
  12.9 0.1 copy.68
  13.1 0.1 stack.71
  13.2 0.1 copy.67
  13.3 0.1 stack.70
  13.4 0.1 constant_dynamic-update-slice_fusion.1
  13.5 0.1 constant_dynamic-update-slice_fusion
  13.6 0.6 %dynamic-slice_bitcast_fusion.2 = (bf16[1,8,64,2,32]{2,0,4,1,3:T(2,128)(2,1)S(1)}, bf16[1,8,64,2,32]{2,0,4,1,3:T(2,128)(2,1)S(1)}) fusion(bf16[2,64,2,8,32]{1,0,4,3,2:T(2,128)(2,1)S(1)} %constant_dynamic-update-slice_fusion, s32[]{:T(128)S(6)} %select_n.235, s32[]{:T(128)S(6)} %select_n.236), kind=kLoop, calls=%fused_computation.41 | loop fusion | bytes 262152 | tf_op jit(solution)/shard_map/jit(dynamic_index_in_dim)/dynamic_slice | solution.py:291
  14.2 0.3 copy.70
  14.6 0.3 reshape.610
  14.9 4.7 %collective-permute-start.3 = (bf16[8,4096]{1,0:T(8,128)(2,1)S(1)}, bf16[8,4096]{1,0:T(8,128)(2,1)S(1)}, u32[]{:S(2)}, u32[]{:S(2)}) collective-permute-start(bf16[8,4096]{1,0:T(8,128)(2,1)S(1)} %reshape.610), channel_id=1, source_target_pairs={{0,18},{2,16},{4,22},{6,20},{8,26},{10,24},{12,30},{14,28},{16,2},... | collective-permute-start | bytes 196616 | tf_op jit(solution)/shard_map/ppermute | solution.py:307
  19.6 0.5 %collective-permute-start.1 = (bf16[8,4096]{1,0:T(8,128)(2,1)S(1)}, bf16[8,4096]{1,0:T(8,128)(2,1)S(1)}, u32[]{:S(2)}, u32[]{:S(2)}) collective-permute-start(bf16[8,4096]{1,0:T(8,128)(2,1)S(1)} %reshape.610), channel_id=1, source_target_pairs={{0,2},{2,0},{1,3},{3,1},{4,6},{6,4},{5,7},{7,5},{8,10},{10,8},{9,1... | collective-permute-start | bytes 196616 | tf_op jit(solution)/shard_map/ppermute | solution.py:301
  20.1 0.3 copy.74
  20.5 0.3 reshape.614
  20.8 0.2 collective-permute-start.2
  21.0 3.2 %collective-permute-done.1 = bf16[8,4096]{1,0:T(8,128)(2,1)S(1)} collective-permute-done((bf16[8,4096]{1,0:T(8,128)(2,1)S(1)}, bf16[8,4096]{1,0:T(8,128)(2,1)S(1)}, u32[]{:S(2)}, u32[]{:S(2)}) %collective-permute-start.1) | collective-permute-done | bytes 65568 | tf_op jit(solution)/shard_map/ppermute | solution.py:301
  24.1 0.2 reshape.611
  24.3 0.1 copy.71
  24.5 0.1 copy.72
  24.7 0.1 copy.111
  24.8 0.2 reshape.616
  25.0 2.4 %collective-permute-done.2 = bf16[8,4224]{1,0:T(8,128)(2,1)S(1)} collective-permute-done((bf16[8,4224]{1,0:T(8,128)(2,1)S(1)}, bf16[8,4224]{1,0:T(8,128)(2,1)S(1)}, u32[]{:S(2)}, u32[]{:S(2)}) %collective-permute-start.2) | collective-permute-done | bytes 67616 | tf_op jit(solution)/shard_map/ppermute | solution.py:298
  27.3 0.2 reshape.615
  27.5 0.1 maximum_bitcast_fusion.2
  27.6 0.1 copy.110
  27.8 0.1 pad_maximum_fusion.7
  27.9 1.6 %collective-permute-start.6 = (bf16[2,4,8320]{2,1,0:T(4,128)(2,1)S(1)}, bf16[2,4,8320]{2,1,0:T(4,128)(2,1)S(1)}, u32[]{:S(2)}, u32[]{:S(2)}) collective-permute-start(bf16[2,4,8320]{2,1,0:T(4,128)(2,1)S(1)} %get-tuple-element.17), channel_id=1, source_target_pairs={{0,4},{4,0},{8,12},{12,8},{16,20},{20,16},{24,28},{28,24},{1,5},{5... | collective-permute-start | bytes 399368 | tf_op jit(solution)/shard_map/ppermute | solution.py:187
  29.5 0.3 collective-permute-start.4
  29.8 3.1 %collective-permute-done.6 = bf16[2,4,8320]{2,1,0:T(4,128)(2,1)S(1)} collective-permute-done((bf16[2,4,8320]{2,1,0:T(4,128)(2,1)S(1)}, bf16[2,4,8320]{2,1,0:T(4,128)(2,1)S(1)}, u32[]{:S(2)}, u32[]{:S(2)}) %collective-permute-start.6) | collective-permute-done | bytes 133152 | tf_op jit(solution)/shard_map/ppermute | solution.py:187
  32.9 0.2 fusion.88
  33.1 0.5 collective-permute-start.7
  33.6 2.2 %collective-permute-done.4 = bf16[2,4,8320]{2,1,0:T(4,128)(2,1)S(1)} collective-permute-done((bf16[2,4,8320]{2,1,0:T(4,128)(2,1)S(1)}, bf16[2,4,8320]{2,1,0:T(4,128)(2,1)S(1)}, u32[]{:S(2)}, u32[]{:S(2)}) %collective-permute-start.4) | collective-permute-done | bytes 133152 | tf_op jit(solution)/shard_map/ppermute | solution.py:187
  35.8 0.2 fusion.89
  36.1 4.1 %collective-permute-done.7 = bf16[2,2,4,8320]{3,2,0,1:T(4,128)(2,1)S(1)} collective-permute-done((bf16[2,2,4,8320]{3,2,0,1:T(4,128)(2,1)S(1)}, bf16[2,2,4,8320]{3,2,0,1:T(4,128)(2,1)S(1)}, u32[]{:S(2)}, u32[]{:S(2)}) %collective-permute-start.7) | collective-permute-done | bytes 266272 | tf_op jit(solution)/shard_map/ppermute | solution.py:187
  40.2 0.4 pad_maximum_fusion.1
  40.6 0.2 copy.76
  40.8 1.7 %collective-permute-done.5 = bf16[2,2,4,8320]{3,2,0,1:T(4,128)(2,1)S(1)} collective-permute-done((bf16[2,2,4,8320]{3,2,0,1:T(4,128)(2,1)S(1)}, bf16[2,2,4,8320]{3,2,0,1:T(4,128)(2,1)S(1)}, u32[]{:S(2)}, u32[]{:S(2)}) %collective-permute-start.5) | collective-permute-done | bytes 266272 | tf_op jit(solution)/shard_map/ppermute | solution.py:187
  42.5 0.4 pad_maximum_fusion
  42.8 0.2 copy.75
  43.1 0.2 copy.91
  43.4 0.1 multiply_reduce_fusion
  43.7 0.1 copy.80
  43.8 0.1 eq.66
  43.9 0.1 copy.81
  44.1 0.1 eq.69
  44.2 1.0 %bitcast_convert_fusion = bf16[64,128,128]{1,2,0:T(8,128)(2,1)S(1)} fusion(s32[128]{0:T(128)S(1)} %eq.69, s32[128]{0:T(128)S(1)} %eq.66, bf16[8,4,8320]{2,1,0:T(4,128)(2,1)S(1)} %bitcast.151, bf16[8,4,8320]{2,1,0:T(4,128)(2,1)S(1)} %bitcast.149), kind=kOutput, calls=%fused_computation | convolution fusion | flops 139493376 | bytes 3163136 | tf_op jit(solution)/shard_map/rsc,scbq->brq/dot_general | solution.py:383
  45.3 0.3 copy.83
  45.7 0.1 pad_maximum_fusion.2
  45.8 0.3 copy.84
  46.1 1.2 %convolution_multiply_fusion = f32[64,32,128]{2,1,0:T(8,128)S(1)} fusion(bf16[64,128,128]{1,2,0:T(8,128)(2,1)S(1)} %bitcast_convert_fusion, bf16[64,16,128]{2,1,0:T(8,128)(2,1)S(1)} %copy.84, bf16[64,16,128]{2,1,0:T(8,128)(2,1)S(1)} %dynamic-slice_bitcast_fusion), kind=kOutput, calls=%fused_computation.1 | convolution fusion | flops 68419584 | bytes 3670016 | tf_op jit(solution)/shard_map/bpq,bjq->bpj/dot_general | solution.py:391
  47.3 1.1 %copy.109 = f32[64,2,16,128]{3,2,0,1:T(8,128)} copy(f32[64,2,16,128]{3,2,1,0:T(8,128)S(1)} %bitcast.146) | data formatting | bytes 2097152 | tf_op jit(solution)/shard_map/div | solution.py:394
  (48 shorter events, 1.1 us)
Async XLA Ops:
  0.0 11.0 %copy-start = (f32[128]{0:T(128)S(1)}, f32[128]{0:T(128)}, u32[]{:S(2)}) copy-start(f32[128]{0:T(128)} %param.5) | copy-start | bytes 1540
  8.1 4.0 %copy-start.1 = (s32[1,8,2]{1,2,0:T(2,128)S(1)}, s32[1,8,2]{1,2,0:T(2,128)}, u32[]{:S(2)}) copy-start(s32[1,8,2]{1,2,0:T(2,128)} %param.7) | copy-start | bytes 196
  8.1 4.0 %copy-start.2 = (s32[1,8,2]{1,2,0:T(2,128)S(1)}, s32[1,8,2]{1,2,0:T(2,128)}, u32[]{:S(2)}) copy-start(s32[1,8,2]{1,2,0:T(2,128)} %param.6) | copy-start | bytes 196
  10.5 2.0 %collective-permute-start = (f32[144,2,256]{2,0,1:T(8,128)S(1)}, f32[144,2,256]{2,0,1:T(8,128)S(1)}, u32[]{:S(2)}, u32[]{:S(2)}) collective-permute-start(f32[144,2,256]{2,0,1:T(8,128)S(1)} %pad_maximum_fusion.3), channel_id=1, source_target_pairs={{0,1},{1,0},{2,3},{3,2},{4,5},{5,4},{6,7},{7,6},{8,9},{9,8},{10,11... | collective-permute-start | bytes 884744 | tf_op jit(solution)/shard_map/ppermute | solution.py:24
  14.9 9.9 %collective-permute-start.3 = (bf16[8,4096]{1,0:T(8,128)(2,1)S(1)}, bf16[8,4096]{1,0:T(8,128)(2,1)S(1)}, u32[]{:S(2)}, u32[]{:S(2)}) collective-permute-start(bf16[8,4096]{1,0:T(8,128)(2,1)S(1)} %reshape.610), channel_id=1, source_target_pairs={{0,18},{2,16},{4,22},{6,20},{8,26},{10,24},{12,30},{14,28},{16,2},... | collective-permute-start | bytes 196616 | tf_op jit(solution)/shard_map/ppermute | solution.py:307
  19.6 4.5 %collective-permute-start.1 = (bf16[8,4096]{1,0:T(8,128)(2,1)S(1)}, bf16[8,4096]{1,0:T(8,128)(2,1)S(1)}, u32[]{:S(2)}, u32[]{:S(2)}) collective-permute-start(bf16[8,4096]{1,0:T(8,128)(2,1)S(1)} %reshape.610), channel_id=1, source_target_pairs={{0,2},{2,0},{1,3},{3,1},{4,6},{6,4},{5,7},{7,5},{8,10},{10,8},{9,1... | collective-permute-start | bytes 196616 | tf_op jit(solution)/shard_map/ppermute | solution.py:301
  20.8 6.5 %collective-permute-start.2 = (bf16[8,4224]{1,0:T(8,128)(2,1)S(1)}, bf16[8,4224]{1,0:T(8,128)(2,1)S(1)}, u32[]{:S(2)}, u32[]{:S(2)}) collective-permute-start(bf16[8,4224]{1,0:T(8,128)(2,1)S(1)} %pad_maximum_fusion.10), channel_id=1, source_target_pairs={{0,16},{4,20},{8,24},{12,28},{16,0},{20,4},{24,8},{28,12},{1,17},{... | collective-permute-start | bytes 202760 | tf_op jit(solution)/shard_map/ppermute | solution.py:298
  27.9 5.1 %collective-permute-start.6 = (bf16[2,4,8320]{2,1,0:T(4,128)(2,1)S(1)}, bf16[2,4,8320]{2,1,0:T(4,128)(2,1)S(1)}, u32[]{:S(2)}, u32[]{:S(2)}) collective-permute-start(bf16[2,4,8320]{2,1,0:T(4,128)(2,1)S(1)} %get-tuple-element.17), channel_id=1, source_target_pairs={{0,4},{4,0},{8,12},{12,8},{16,20},{20,16},{24,28},{28,24},{1,5},{5... | collective-permute-start | bytes 399368 | tf_op jit(solution)/shard_map/ppermute | solution.py:187
  29.5 6.3 %collective-permute-start.4 = (bf16[2,4,8320]{2,1,0:T(4,128)(2,1)S(1)}, bf16[2,4,8320]{2,1,0:T(4,128)(2,1)S(1)}, u32[]{:S(2)}, u32[]{:S(2)}) collective-permute-start(bf16[2,4,8320]{2,1,0:T(4,128)(2,1)S(1)} %get-tuple-element.18), channel_id=1, source_target_pairs={{0,8},{4,12},{8,0},{12,4},{16,24},{20,28},{24,16},{28,20},{1,9},{5... | collective-permute-start | bytes 399368 | tf_op jit(solution)/shard_map/ppermute | solution.py:187
  33.1 7.1 %collective-permute-start.7 = (bf16[2,2,4,8320]{3,2,0,1:T(4,128)(2,1)S(1)}, bf16[2,2,4,8320]{3,2,0,1:T(4,128)(2,1)S(1)}, u32[]{:S(2)}, u32[]{:S(2)}) collective-permute-start(bf16[2,2,4,8320]{3,2,0,1:T(4,128)(2,1)S(1)} %get-tuple-element.16), channel_id=1, source_target_pairs={{0,8},{4,12},{8,0},{12,4},{16,24},{20,28},{24,16},{28,20},{1,9},{5... | collective-permute-start | bytes 798728 | tf_op jit(solution)/shard_map/ppermute | solution.py:187
  36.0 6.5 %collective-permute-start.5 = (bf16[2,2,4,8320]{3,2,0,1:T(4,128)(2,1)S(1)}, bf16[2,2,4,8320]{3,2,0,1:T(4,128)(2,1)S(1)}, u32[]{:S(2)}, u32[]{:S(2)}) collective-permute-start(bf16[2,2,4,8320]{3,2,0,1:T(4,128)(2,1)S(1)} %get-tuple-element.20), channel_id=1, source_target_pairs={{0,4},{4,0},{8,12},{12,8},{16,20},{20,16},{24,28},{28,24},{1,5},{5... | collective-permute-start | bytes 798728 | tf_op jit(solution)/shard_map/ppermute | solution.py:187

commit v18 on v15

--- a/solution.py
+++ b/solution.py
@@ -119,8 +119,9 @@
         return jnp.cos(angle), jnp.sin(angle)
 
     def combined(outer_steps, inner_steps):
-        outer_cos, outer_sin = cos_sin(outer_steps)
-        inner_cos, inner_sin = cos_sin(inner_steps)
+        outer_cos, outer_sin, inner_cos, inner_sin = lax.optimization_barrier(
+            cos_sin(outer_steps) + cos_sin(inner_steps)
+        )
         width = wavenumber.shape[0]
         cos_sum = outer_cos[:, None] * inner_cos[None] - outer_sin[:, None] * inner_sin[None]
         sin_sum = outer_sin[:, None] * inner_cos[None] + outer_cos[:, None] * inner_sin[None]

time: 46.8 us -> 46.8 us (level)
  no operation moved by 1% of the time
where the time goes in v18:
time: 46.8 us; the launch traced here: 46.6 us
  waiting for transfers between devices  16.1 us (34%)
  starting transfers between devices  8.58 us (18%)
  Pallas kernels  6.41 us (14%)
  local copies, waits for them, and re-layouts  6.23 us (13%)
  other arithmetic  5.46 us (12%)
  matrix products  3.25 us (7%)
  between operations  0.53 us (1%)
    ppermute x4, waiting for transfers between devices, gather_blocks(): arrived = lax.ppermute(part, 'blk', pairs)  10.6 us
    pallas_call x1, Pallas kernels, dft_fused(): pl.pallas_call(dft_kernel, grid=(count // chunk,), in_specs=[pl.BlockSpec...  6.41 us
    ppermute x1, starting transfers between devices, per_device(): from_diagonal = lax.ppermute(other_flat, ('blk', 'seg'), diagonal)  4.74 us
    ppermute x1, waiting for transfers between devices, per_device(): from_seg = lax.ppermute(other_flat, 'seg', [(0, 1), (1, 0)])  3.35 us
    ppermute x4, starting transfers between devices, gather_blocks(): arrived = lax.ppermute(part, 'blk', pairs)  2.62 us
    ppermute x1, waiting for transfers between devices, per_device(): lax.ppermute(keep_flat, 'blk', [(source, source ^ first) for source in ra...  2.16 us
    select_n x1, other arithmetic, per_device(): sent = jnp.where(freq_rank == 0, blocks[1], blocks[0])  1.27 us
    dot_general x1, matrix products, per_device(): jnp.einsum('bpq,bjq->bpj', lhs, routed, preferred_element_type=jnp.float32)  1.19 us
  transfers between devices with their start and end apart: 8, of which 6 were waited for; matrix products, arithmetic and copies ran while one was open for 8% of the time, Pallas kernels for 0%

profile of v18, /device:TPU:0, one launch (start us, length us, event | category | flops | bytes accessed | tf_op | source)
XLA Modules:
  0.0 46.6 jit_solution(12672724260275201876)
XLA Ops:
  0.0 0.1 fusion.59
  0.1 0.2 fusion.61
  0.3 0.7 %negate_bitcast_fusion = (f32[64,256]{1,0:T(8,128)}, f32[64,256]{1,0:T(8,128)}) fusion(f32[8,256]{1,0:T(8,128)S(1)} %get-tuple-element.18, f32[8,256]{1,0:T(8,128)S(1)} %get-tuple-element.17, f32[8,256]{1,0:T(8,128)S(1)} %get-tuple-element.16, f32[8,256]{1,0:T(8,128)S(1)} %get-tuple-element.15), kind=kLoop, calls=%fused_computation.97 | loop fusion | flops 114688 | bytes 163840 | tf_op jit(solution)/shard_map/neg | solution.py:137
  1.0 0.7 %add_multiply_fusion = (f32[8,16,256]{2,1,0:T(8,128)}, f32[8,16,256]{2,1,0:T(8,128)}) fusion(f32[16,256]{1,0:T(8,128)S(1)} %get-tuple-element.22, f32[8,256]{1,0:T(8,128)S(1)} %get-tuple-element.21, f32[16,256]{1,0:T(8,128)S(1)} %get-tuple-element.20, f32[8,256]{1,0:T(8,128)S(1)} %get-tuple-element.19), kind=kLoop, calls=%fused_computation.77 | loop fusion | flops 262144 | bytes 311296 | tf_op jit(solution)/shard_map/mul | solution.py:142
  1.7 6.4 %shard_map.46 = (f32[256,256]{1,0:T(8,128)}, f32[256,256]{1,0:T(8,128)}) custom-call(bf16[256,8192]{1,0:T(8,128)(2,1)} %bitcast.134, f32[64,256]{1,0:T(8,128)} %get-tuple-element.46.cos_a_ref, f32[64,256]{1,0:T(8,128)} %get-tuple-element.45.nsin_a_ref, f32[128,256]{1,0:T(8,128)} %bitcast.146, f32[128,256]{1,0:T(8,128)} %bitcast.145), custom_call_target="tpu_custom_call" | custom-call | tf_op jit(solution)/shard_map/pallas_call | solution.py:146
  8.1 1.3 %broadcast_select_fusion = (f32[128,2,256]{0,2,1:T(8,128)S(1)}, f32[128,2,256]{0,2,1:T(8,128)S(1)}) fusion(pred[]{:T(512)S(6)} %eq.64, f32[256,1,256]{0,2,1:T(8,128)} %bitcast.158, f32[256,1,256]{0,2,1:T(8,128)} %bitcast.157), kind=kLoop, calls=%fused_computation.79 | loop fusion | flops 327680 | bytes 1048577 | tf_op jit(solution)/shard_map/jit(_where)/select_n | solution.py:222
  9.4 0.1 copy.101
  9.6 0.1 copy.102
  9.8 0.5 %collective-permute-start = (f32[144,2,256]{0,2,1:T(8,128)S(1)}, f32[144,2,256]{0,2,1:T(8,128)S(1)}, u32[]{:S(2)}, u32[]{:S(2)}) collective-permute-start(f32[144,2,256]{0,2,1:T(8,128)S(1)} %pad_maximum_fusion.2), channel_id=1, source_target_pairs={{0,1},{1,0},{2,3},{3,2},{4,5},{5,4},{6,7},{7,6},{8,9},{9,8},{10,11... | collective-permute-start | bytes 884744 | tf_op jit(solution)/shard_map/ppermute | solution.py:24
  10.3 0.5 %convolution_bitcast_fusion = f32[128]{0:T(128)S(1)} fusion(s32[128]{0:T(128)S(1)} %fusion.79, f32[128]{0:T(128)S(1)} %copy-done), kind=kOutput, calls=%fused_computation.4 | convolution fusion | flops 442368 | bytes 1536 | tf_op jit(solution)/shard_map/dot_general | solution.py:67
  10.8 0.5 %convolution_bitcast_fusion.1 = f32[128]{0:T(128)S(1)} fusion(s32[128]{0:T(128)S(1)} %fusion.79, f32[128]{0:T(128)S(1)} %copy-done), kind=kOutput, calls=%fused_computation.5 | convolution fusion | flops 425984 | bytes 1536 | tf_op jit(solution)/shard_map/dot_general | solution.py:66
  11.3 0.2 copy.103
  11.6 0.1 copy.117
  11.7 0.1 convert_element_type.59
  11.8 0.1 copy.104
  12.1 0.1 copy.105
  12.4 0.1 copy.108
  12.5 0.1 fusion.14
  12.6 0.1 copy.110
  12.8 0.1 stack.71
  12.9 0.1 stack.70
  13.1 0.2 copy.114
  13.3 0.3 reshape.375
  13.6 4.7 %collective-permute-start.3 = (bf16[8,4096]{1,0:T(8,128)(2,1)S(1)}, bf16[8,4096]{1,0:T(8,128)(2,1)S(1)}, u32[]{:S(2)}, u32[]{:S(2)}) collective-permute-start(bf16[8,4096]{1,0:T(8,128)(2,1)S(1)} %reshape.375), channel_id=1, source_target_pairs={{0,18},{2,16},{4,22},{6,20},{8,26},{10,24},{12,30},{14,28},{16,2},... | collective-permute-start | bytes 196616 | tf_op jit(solution)/shard_map/ppermute | solution.py:308
  18.3 0.5 %collective-permute-start.1 = (bf16[8,4096]{1,0:T(8,128)(2,1)S(1)}, bf16[8,4096]{1,0:T(8,128)(2,1)S(1)}, u32[]{:S(2)}, u32[]{:S(2)}) collective-permute-start(bf16[8,4096]{1,0:T(8,128)(2,1)S(1)} %reshape.375), channel_id=1, source_target_pairs={{0,2},{2,0},{1,3},{3,1},{4,6},{6,4},{5,7},{7,5},{8,10},{10,8},{9,1... | collective-permute-start | bytes 196616 | tf_op jit(solution)/shard_map/ppermute | solution.py:302
  18.8 0.2 copy.118
  19.0 0.3 reshape.379
  19.3 0.2 collective-permute-start.2
  19.5 3.4 %collective-permute-done.1 = bf16[8,4096]{1,0:T(8,128)(2,1)S(1)} collective-permute-done((bf16[8,4096]{1,0:T(8,128)(2,1)S(1)}, bf16[8,4096]{1,0:T(8,128)(2,1)S(1)}, u32[]{:S(2)}, u32[]{:S(2)}) %collective-permute-start.1) | collective-permute-done | bytes 65568 | tf_op jit(solution)/shard_map/ppermute | solution.py:302
  22.8 0.2 reshape.376
  23.0 0.1 copy.115
  23.2 0.1 copy.116
  23.4 0.1 copy.155
  23.5 0.2 reshape.381
  23.7 2.2 %collective-permute-done.2 = bf16[8,4224]{1,0:T(8,128)(2,1)S(1)} collective-permute-done((bf16[8,4224]{1,0:T(8,128)(2,1)S(1)}, bf16[8,4224]{1,0:T(8,128)(2,1)S(1)}, u32[]{:S(2)}, u32[]{:S(2)}) %collective-permute-start.2) | collective-permute-done | bytes 67616 | tf_op jit(solution)/shard_map/ppermute | solution.py:299
  25.8 0.2 reshape.380
  26.0 0.1 maximum_bitcast_fusion.2
  26.1 0.1 copy.154
  26.3 0.1 pad_maximum_fusion.8
  26.4 1.6 %collective-permute-start.6 = (bf16[2,4,8320]{2,1,0:T(4,128)(2,1)S(1)}, bf16[2,4,8320]{2,1,0:T(4,128)(2,1)S(1)}, u32[]{:S(2)}, u32[]{:S(2)}) collective-permute-start(bf16[2,4,8320]{2,1,0:T(4,128)(2,1)S(1)} %get-tuple-element.33), channel_id=1, source_target_pairs={{0,4},{4,0},{8,12},{12,8},{16,20},{20,16},{24,28},{28,24},{1,5},{5... | collective-permute-start | bytes 399368 | tf_op jit(solution)/shard_map/ppermute | solution.py:188
  28.0 0.3 collective-permute-start.4
  28.3 3.1 %collective-permute-done.6 = bf16[2,4,8320]{2,1,0:T(4,128)(2,1)S(1)} collective-permute-done((bf16[2,4,8320]{2,1,0:T(4,128)(2,1)S(1)}, bf16[2,4,8320]{2,1,0:T(4,128)(2,1)S(1)}, u32[]{:S(2)}, u32[]{:S(2)}) %collective-permute-start.6) | collective-permute-done | bytes 133152 | tf_op jit(solution)/shard_map/ppermute | solution.py:188
  31.4 0.2 fusion.87
  31.6 0.7 %collective-permute-start.7 = (bf16[2,2,4,8320]{3,2,0,1:T(4,128)(2,1)S(1)}, bf16[2,2,4,8320]{3,2,0,1:T(4,128)(2,1)S(1)}, u32[]{:S(2)}, u32[]{:S(2)}) collective-permute-start(bf16[2,2,4,8320]{3,2,0,1:T(4,128)(2,1)S(1)} %get-tuple-element.32), channel_id=1, source_target_pairs={{0,8},{4,12},{8,0},{12,4},{16,24},{20,28},{24,16},{28,20},{1,9},{5... | collective-permute-start | bytes 798728 | tf_op jit(solution)/shard_map/ppermute | solution.py:188
  32.3 1.7 %collective-permute-done.4 = bf16[2,4,8320]{2,1,0:T(4,128)(2,1)S(1)} collective-permute-done((bf16[2,4,8320]{2,1,0:T(4,128)(2,1)S(1)}, bf16[2,4,8320]{2,1,0:T(4,128)(2,1)S(1)}, u32[]{:S(2)}, u32[]{:S(2)}) %collective-permute-start.4) | collective-permute-done | bytes 133152 | tf_op jit(solution)/shard_map/ppermute | solution.py:188
  34.0 0.2 fusion.88
  34.3 4.4 %collective-permute-done.7 = bf16[2,2,4,8320]{3,2,0,1:T(4,128)(2,1)S(1)} collective-permute-done((bf16[2,2,4,8320]{3,2,0,1:T(4,128)(2,1)S(1)}, bf16[2,2,4,8320]{3,2,0,1:T(4,128)(2,1)S(1)}, u32[]{:S(2)}, u32[]{:S(2)}) %collective-permute-start.7) | collective-permute-done | bytes 266272 | tf_op jit(solution)/shard_map/ppermute | solution.py:188
  38.7 0.4 pad_maximum_fusion.1
  39.1 0.2 copy.120
  39.3 1.4 %collective-permute-done.5 = bf16[2,2,4,8320]{3,2,0,1:T(4,128)(2,1)S(1)} collective-permute-done((bf16[2,2,4,8320]{3,2,0,1:T(4,128)(2,1)S(1)}, bf16[2,2,4,8320]{3,2,0,1:T(4,128)(2,1)S(1)}, u32[]{:S(2)}, u32[]{:S(2)}) %collective-permute-start.5) | collective-permute-done | bytes 266272 | tf_op jit(solution)/shard_map/ppermute | solution.py:188
  40.7 0.4 pad_maximum_fusion
  41.1 0.2 copy.119
  41.3 0.2 copy.133
  41.6 0.1 multiply_reduce_fusion
  41.9 0.1 copy.124
  42.0 0.1 eq.68
  42.1 0.1 copy.125
  42.3 0.1 eq.71
  42.4 1.0 %bitcast_convert_fusion = bf16[64,128,128]{1,2,0:T(8,128)(2,1)S(1)} fusion(s32[128]{0:T(128)S(1)} %eq.71, s32[128]{0:T(128)S(1)} %eq.68, bf16[8,4,8320]{2,1,0:T(4,128)(2,1)S(1)} %bitcast.138, bf16[8,4,8320]{2,1,0:T(4,128)(2,1)S(1)} %bitcast.136), kind=kOutput, calls=%fused_computation | convolution fusion | flops 139493376 | bytes 3163136 | tf_op jit(solution)/shard_map/rsc,scbq->brq/dot_general | solution.py:384
  43.5 0.3 copy.127
  43.9 0.1 pad_maximum_fusion.3
  44.0 0.3 copy.128
  44.3 1.2 %convolution_multiply_fusion = f32[64,32,128]{2,1,0:T(8,128)S(1)} fusion(bf16[64,128,128]{1,2,0:T(8,128)(2,1)S(1)} %bitcast_convert_fusion, bf16[64,16,128]{2,1,0:T(8,128)(2,1)S(1)} %copy.128, bf16[64,16,128]{2,1,0:T(8,128)(2,1)S(1)} %dynamic-slice_bitcast_fusion), kind=kOutput, calls=%fused_computation.1 | convolution fusion | flops 68419584 | bytes 3670016 | tf_op jit(solution)/shard_map/bpq,bjq->bpj/dot_general | solution.py:392
  45.5 1.1 %copy.153 = f32[64,2,16,128]{3,2,0,1:T(8,128)} copy(f32[64,2,16,128]{3,2,1,0:T(8,128)S(1)} %bitcast.133) | data formatting | bytes 2097152 | tf_op jit(solution)/shard_map/div | solution.py:395
  (50 shorter events, 1.2 us)
Async XLA Ops:
  0.0 10.3 %copy-start = (f32[128]{0:T(128)S(1)}, f32[128]{0:T(128)}, u32[]{:S(2)}) copy-start(f32[128]{0:T(128)} %param.5) | copy-start | bytes 1540
  8.1 3.4 %copy-start.1 = (s32[1,8,2]{1,2,0:T(2,128)S(1)}, s32[1,8,2]{1,2,0:T(2,128)}, u32[]{:S(2)}) copy-start(s32[1,8,2]{1,2,0:T(2,128)} %param.7) | copy-start | bytes 196
  8.1 3.4 %copy-start.2 = (s32[1,8,2]{1,2,0:T(2,128)S(1)}, s32[1,8,2]{1,2,0:T(2,128)}, u32[]{:S(2)}) copy-start(s32[1,8,2]{1,2,0:T(2,128)} %param.6) | copy-start | bytes 196
  9.8 2.3 %collective-permute-start = (f32[144,2,256]{0,2,1:T(8,128)S(1)}, f32[144,2,256]{0,2,1:T(8,128)S(1)}, u32[]{:S(2)}, u32[]{:S(2)}) collective-permute-start(f32[144,2,256]{0,2,1:T(8,128)S(1)} %pad_maximum_fusion.2), channel_id=1, source_target_pairs={{0,1},{1,0},{2,3},{3,2},{4,5},{5,4},{6,7},{7,6},{8,9},{9,8},{10,11... | collective-permute-start | bytes 884744 | tf_op jit(solution)/shard_map/ppermute | solution.py:24
  13.6 9.9 %collective-permute-start.3 = (bf16[8,4096]{1,0:T(8,128)(2,1)S(1)}, bf16[8,4096]{1,0:T(8,128)(2,1)S(1)}, u32[]{:S(2)}, u32[]{:S(2)}) collective-permute-start(bf16[8,4096]{1,0:T(8,128)(2,1)S(1)} %reshape.375), channel_id=1, source_target_pairs={{0,18},{2,16},{4,22},{6,20},{8,26},{10,24},{12,30},{14,28},{16,2},... | collective-permute-start | bytes 196616 | tf_op jit(solution)/shard_map/ppermute | solution.py:308
  18.3 4.5 %collective-permute-start.1 = (bf16[8,4096]{1,0:T(8,128)(2,1)S(1)}, bf16[8,4096]{1,0:T(8,128)(2,1)S(1)}, u32[]{:S(2)}, u32[]{:S(2)}) collective-permute-start(bf16[8,4096]{1,0:T(8,128)(2,1)S(1)} %reshape.375), channel_id=1, source_target_pairs={{0,2},{2,0},{1,3},{3,1},{4,6},{6,4},{5,7},{7,5},{8,10},{10,8},{9,1... | collective-permute-start | bytes 196616 | tf_op jit(solution)/shard_map/ppermute | solution.py:302
  19.3 6.5 %collective-permute-start.2 = (bf16[8,4224]{1,0:T(8,128)(2,1)S(1)}, bf16[8,4224]{1,0:T(8,128)(2,1)S(1)}, u32[]{:S(2)}, u32[]{:S(2)}) collective-permute-start(bf16[8,4224]{1,0:T(8,128)(2,1)S(1)} %pad_maximum_fusion.11), channel_id=1, source_target_pairs={{0,16},{4,20},{8,24},{12,28},{16,0},{20,4},{24,8},{28,12},{1,17},{... | collective-permute-start | bytes 202760 | tf_op jit(solution)/shard_map/ppermute | solution.py:299
  26.4 5.1 %collective-permute-start.6 = (bf16[2,4,8320]{2,1,0:T(4,128)(2,1)S(1)}, bf16[2,4,8320]{2,1,0:T(4,128)(2,1)S(1)}, u32[]{:S(2)}, u32[]{:S(2)}) collective-permute-start(bf16[2,4,8320]{2,1,0:T(4,128)(2,1)S(1)} %get-tuple-element.33), channel_id=1, source_target_pairs={{0,4},{4,0},{8,12},{12,8},{16,20},{20,16},{24,28},{28,24},{1,5},{5... | collective-permute-start | bytes 399368 | tf_op jit(solution)/shard_map/ppermute | solution.py:188
  28.0 6.0 %collective-permute-start.4 = (bf16[2,4,8320]{2,1,0:T(4,128)(2,1)S(1)}, bf16[2,4,8320]{2,1,0:T(4,128)(2,1)S(1)}, u32[]{:S(2)}, u32[]{:S(2)}) collective-permute-start(bf16[2,4,8320]{2,1,0:T(4,128)(2,1)S(1)} %get-tuple-element.34), channel_id=1, source_target_pairs={{0,8},{4,12},{8,0},{12,4},{16,24},{20,28},{24,16},{28,20},{1,9},{5... | collective-permute-start | bytes 399368 | tf_op jit(solution)/shard_map/ppermute | solution.py:188
  31.6 7.1 %collective-permute-start.7 = (bf16[2,2,4,8320]{3,2,0,1:T(4,128)(2,1)S(1)}, bf16[2,2,4,8320]{3,2,0,1:T(4,128)(2,1)S(1)}, u32[]{:S(2)}, u32[]{:S(2)}) collective-permute-start(bf16[2,2,4,8320]{3,2,0,1:T(4,128)(2,1)S(1)} %get-tuple-element.32), channel_id=1, source_target_pairs={{0,8},{4,12},{8,0},{12,4},{16,24},{20,28},{24,16},{28,20},{1,9},{5... | collective-permute-start | bytes 798728 | tf_op jit(solution)/shard_map/ppermute | solution.py:188
  34.2 6.5 %collective-permute-start.5 = (bf16[2,2,4,8320]{3,2,0,1:T(4,128)(2,1)S(1)}, bf16[2,2,4,8320]{3,2,0,1:T(4,128)(2,1)S(1)}, u32[]{:S(2)}, u32[]{:S(2)}) collective-permute-start(bf16[2,2,4,8320]{3,2,0,1:T(4,128)(2,1)S(1)} %get-tuple-element.36), channel_id=1, source_target_pairs={{0,4},{4,0},{8,12},{12,8},{16,20},{20,16},{24,28},{28,24},{1,5},{5... | collective-permute-start | bytes 798728 | tf_op jit(solution)/shard_map/ppermute | solution.py:188

commit v19 on v15

--- a/solution.py
+++ b/solution.py
@@ -105,6 +105,59 @@
     lax.fori_loop(0, groups, one_group, 0)
 
 
+def dft_kernel_inline(rec_ref, oca_ref, osa_ref, ica_ref, isa_ref, ocb_ref, osb_ref, icb_ref, isb_ref,
+                      re_ref, im_ref):
+    step = pl.program_id(0)
+    lanes = 128
+    group = ica_ref.shape[0]
+    groups = rec_ref.shape[1] // (group * lanes)
+    norm_scale = 1.0 / math.sqrt(SEG_LEN)
+
+    @pl.when(step == 0)
+    def _():
+        re_ref[...] = jnp.zeros_like(re_ref)
+        im_ref[...] = jnp.zeros_like(im_ref)
+
+    icb = icb_ref[...]
+    isb = isb_ref[...]
+    cos_rows = []
+    sin_rows = []
+    for outer in range(ocb_ref.shape[0]):
+        ocb = ocb_ref[outer : outer + 1, :]
+        osb = osb_ref[outer : outer + 1, :]
+        cos_rows.append(ocb * icb - osb * isb)
+        sin_rows.append(osb * icb + ocb * isb)
+    cos_b = jnp.concatenate(cos_rows, axis=0) * norm_scale
+    sin_b = jnp.concatenate(sin_rows, axis=0) * norm_scale
+    ica = ica_ref[...]
+    isa = isa_ref[...]
+
+    def one_group(index, carry):
+        outer = step * groups + index
+        oca = oca_ref[outer]
+        osa = osa_ref[outer]
+        cos_a = oca * ica - osa * isa
+        nsin_a = -(osa * ica + oca * isa)
+        for pair in range(group // 2):
+            cos_parts = []
+            sin_parts = []
+            for half in range(2):
+                at = 2 * pair + half
+                ca = cos_a[at : at + 1]
+                sa = nsin_a[at : at + 1]
+                cos_parts.append(ca * cos_b + sa * sin_b)
+                sin_parts.append(sa * cos_b - ca * sin_b)
+            cos_tile = jnp.concatenate(cos_parts, axis=0).astype(jnp.bfloat16)
+            sin_tile = jnp.concatenate(sin_parts, axis=0).astype(jnp.bfloat16)
+            first = pl.multiple_of((index * group + 2 * pair) * lanes, 2 * lanes)
+            rec = rec_ref[:, pl.ds(first, 2 * lanes)]
+            re_ref[...] += jnp.dot(rec, cos_tile, preferred_element_type=jnp.float32)
+            im_ref[...] += jnp.dot(rec, sin_tile, preferred_element_type=jnp.float32)
+        return carry
+
+    lax.fori_loop(0, groups, one_group, 0)
+
+
 def dft_fused(records, band_index, first_sample):
     lanes = 128
     chunk = 2048
@@ -127,6 +180,30 @@
         return cos_sum.reshape(-1, width), sin_sum.reshape(-1, width)
 
     coarse_count = count // lanes
+    rows = records.shape[0]
+    bins = band_index.shape[0]
+    full = lambda step: (0, 0)
+    if coarse_count == 64 and chunk == 2048:
+        outer_cos, outer_sin = cos_sin(first_sample + lanes * 8 * jnp.arange(8, dtype=jnp.int32))
+        inner_cos, inner_sin = cos_sin(lanes * jnp.arange(8, dtype=jnp.int32))
+        fine_outer_cos, fine_outer_sin = cos_sin(16 * jnp.arange(lanes // 16, dtype=jnp.int32))
+        fine_inner_cos, fine_inner_sin = cos_sin(jnp.arange(16, dtype=jnp.int32))
+        outer_cos = jnp.broadcast_to(outer_cos[:, None, :], (8, 8, bins))
+        outer_sin = jnp.broadcast_to(outer_sin[:, None, :], (8, 8, bins))
+        small = [inner_cos, inner_sin, fine_outer_cos, fine_outer_sin, fine_inner_cos, fine_inner_sin]
+        return pl.pallas_call(
+            dft_kernel_inline,
+            grid=(count // chunk,),
+            in_specs=[pl.BlockSpec((rows, chunk), lambda step: (0, step))]
+            + [pl.BlockSpec((8, 8, bins), lambda step: (0, 0, 0))] * 2
+            + [pl.BlockSpec(table.shape, full) for table in small],
+            out_specs=[pl.BlockSpec((rows, bins), full), pl.BlockSpec((rows, bins), full)],
+            out_shape=[
+                jax.ShapeDtypeStruct((rows, bins), jnp.float32),
+                jax.ShapeDtypeStruct((rows, bins), jnp.float32),
+            ],
+            compiler_params=pltpu.CompilerParams(dimension_semantics=("arbitrary",)),
+        )(records, outer_cos, outer_sin, *small)
     coarse_outer = coarse_count // 8 if coarse_count % 8 == 0 else 1
     coarse_inner = coarse_count // coarse_outer
     cos_a, sin_a = combined(

time: 46.8 us -> 48.2 us (1.030)
  local copies, waits for them, and re-layouts: 6.23 us -> 7.48 us
    sin x0 -> x2, other arithmetic: none -> 1.48 us  [cos_sin(): return (jnp.cos(angle), jnp.sin(angle))]
    broadcast_in_dim x0 -> x2, local copies, waits for them, and re-layouts: none -> 1.25 us  [the longest x1 0.63 us: dft_fused(): outer_cos = jnp.broadcast_to(outer_cos[:, None, :], (8, 8, bins))]
    mul x1 -> x0, other arithmetic: 0.73 us -> none  [dft_fused(): sin_b = sin_b * norm_scale]
    neg x1 -> x0, other arithmetic: 0.68 us -> none  [dft_fused(): nsin_a = -sin_a]
where the time goes in v19:
time: 48.2 us; the launch traced here: 48 us
  waiting for transfers between devices  16.1 us (33%)
  starting transfers between devices  8.6 us (18%)
  local copies, waits for them, and re-layouts  7.48 us (16%)
  Pallas kernels  6.75 us (14%)
  other arithmetic  5.27 us (11%)
  matrix products  3.25 us (7%)
  between operations  0.53 us (1%)
    ppermute x4, waiting for transfers between devices, gather_blocks(): arrived = lax.ppermute(part, 'blk', pairs)  10.6 us
    pallas_call x1, Pallas kernels, dft_fused(): pl.pallas_call(dft_kernel_inline, grid=(count // chunk,), in_specs=[pl.Bl...  6.75 us
    ppermute x1, starting transfers between devices, per_device(): from_diagonal = lax.ppermute(other_flat, ('blk', 'seg'), diagonal)  4.75 us
    ppermute x1, waiting for transfers between devices, per_device(): from_seg = lax.ppermute(other_flat, 'seg', [(0, 1), (1, 0)])  3.35 us
    ppermute x4, starting transfers between devices, gather_blocks(): arrived = lax.ppermute(part, 'blk', pairs)  2.63 us
    ppermute x1, waiting for transfers between devices, per_device(): lax.ppermute(keep_flat, 'blk', [(source, source ^ first) for source in ra...  2.16 us
    sin x2, other arithmetic, cos_sin(): return (jnp.cos(angle), jnp.sin(angle))  1.48 us
    select_n x1, other arithmetic, per_device(): sent = jnp.where(freq_rank == 0, blocks[1], blocks[0])  1.27 us
  transfers between devices with their start and end apart: 8, of which 6 were waited for; matrix products, arithmetic and copies ran while one was open for 8% of the time, Pallas kernels for 0%

profile of v19, /device:TPU:0, one launch (start us, length us, event | category | flops | bytes accessed | tf_op | source)
XLA Modules:
  0.0 48.0 jit_solution(9829665491655197165)
XLA Ops:
  0.0 0.7 %fusion.59 = (f32[16,256]{1,0:T(8,128)}, f32[16,256]{1,0:T(8,128)}) fusion(s32[256]{0:T(256)S(1)} %fusion.73), kind=kLoop, calls=%fused_computation.147 | loop fusion | flops 57344 | bytes 33792 | tf_op jit(solution)/shard_map/sin | solution.py:172
  0.8 0.8 %fusion.61 = (f32[8,256]{1,0:T(8,128)}, f32[8,256]{1,0:T(8,128)}, f32[8,256]{1,0:T(8,128)S(1)}, f32[8,256]{1,0:T(8,128)S(1)}, f32[8,256]{1,0:T(8,128)}, /*index=5*/f32[8,256]{1,0:T(8,128)}) fusion(s32[256]{0:T(256)S(1)} %fusion.73, s32[8]{0:T(128)S(1)} %get-tuple-element.45, s32[8]{0:T(128)S(1)} %multiply_add_fusion, s32[8]{0:T(128)S(1)} %get-tuple-element.46), kind=kLoop, calls=%fused_computation.152 | loop fusion | flops 86016 | bytes 50272 | tf_op jit(solution)/shard_map/sin | solution.py:172
  1.5 0.6 %broadcast_in_dim.8.oca_ref = f32[8,8,256]{2,1,0:T(8,128)} broadcast(f32[8,256]{1,0:T(8,128)S(1)} %get-tuple-element.41), dimensions={0,2} | broadcast | bytes 73728 | tf_op jit(solution)/shard_map/broadcast_in_dim | solution.py:191
  2.2 0.6 %broadcast_in_dim.9.osa_ref = f32[8,8,256]{2,1,0:T(8,128)} broadcast(f32[8,256]{1,0:T(8,128)S(1)} %get-tuple-element.42), dimensions={0,2} | broadcast | bytes 73728 | tf_op jit(solution)/shard_map/broadcast_in_dim | solution.py:192
  2.8 6.7 %shard_map.46 = (f32[256,256]{1,0:T(8,128)}, f32[256,256]{1,0:T(8,128)}) custom-call(bf16[256,8192]{1,0:T(8,128)(2,1)} %bitcast.128, f32[8,8,256]{2,1,0:T(8,128)} %broadcast_in_dim.8.oca_ref, f32[8,8,256]{2,1,0:T(8,128)} %broadcast_in_dim.9.osa_ref, f32[8,256]{1,0:T(8,128)} %get-tuple-element.43.ica_ref, f32[8,256]{1,0:T(8,128)} %get-tuple-element.44.isa_ref, ...), custom_call_target="tpu_custom_call" | custom-call | tf_op jit(solution)/shard_map/pallas_call | solution.py:194
  9.5 1.3 %broadcast_select_fusion = (f32[128,2,256]{0,2,1:T(8,128)S(1)}, f32[128,2,256]{0,2,1:T(8,128)S(1)}) fusion(pred[]{:T(512)S(6)} %eq.64, f32[256,1,256]{0,2,1:T(8,128)} %bitcast.150, f32[256,1,256]{0,2,1:T(8,128)} %bitcast.149), kind=kLoop, calls=%fused_computation.77 | loop fusion | flops 327680 | bytes 1048577 | tf_op jit(solution)/shard_map/jit(_where)/select_n | solution.py:298
  10.8 0.1 copy.101
  11.0 0.1 copy.102
  11.2 0.5 %collective-permute-start = (f32[144,2,256]{0,2,1:T(8,128)S(1)}, f32[144,2,256]{0,2,1:T(8,128)S(1)}, u32[]{:S(2)}, u32[]{:S(2)}) collective-permute-start(f32[144,2,256]{0,2,1:T(8,128)S(1)} %pad_maximum_fusion.2), channel_id=1, source_target_pairs={{0,1},{1,0},{2,3},{3,2},{4,5},{5,4},{6,7},{7,6},{8,9},{9,8},{10,11... | collective-permute-start | bytes 884744 | tf_op jit(solution)/shard_map/ppermute | solution.py:24
  11.7 0.5 %convolution_bitcast_fusion = f32[128]{0:T(128)S(1)} fusion(s32[128]{0:T(128)S(1)} %fusion.79, f32[128]{0:T(128)S(1)} %copy-done), kind=kOutput, calls=%fused_computation.4 | convolution fusion | flops 442368 | bytes 1536 | tf_op jit(solution)/shard_map/dot_general | solution.py:67
  12.2 0.5 %convolution_bitcast_fusion.1 = f32[128]{0:T(128)S(1)} fusion(s32[128]{0:T(128)S(1)} %fusion.79, f32[128]{0:T(128)S(1)} %copy-done), kind=kOutput, calls=%fused_computation.5 | convolution fusion | flops 425984 | bytes 1536 | tf_op jit(solution)/shard_map/dot_general | solution.py:66
  12.7 0.2 copy.103
  13.0 0.1 copy.117
  13.1 0.1 convert_element_type.66
  13.2 0.1 copy.104
  13.4 0.1 copy.105
  13.8 0.1 copy.108
  13.9 0.1 fusion.14
  14.0 0.1 copy.110
  14.2 0.1 stack.71
  14.3 0.1 stack.70
  14.5 0.2 copy.114
  14.7 0.3 reshape.390
  15.0 4.7 %collective-permute-start.3 = (bf16[8,4096]{1,0:T(8,128)(2,1)S(1)}, bf16[8,4096]{1,0:T(8,128)(2,1)S(1)}, u32[]{:S(2)}, u32[]{:S(2)}) collective-permute-start(bf16[8,4096]{1,0:T(8,128)(2,1)S(1)} %reshape.390), channel_id=1, source_target_pairs={{0,18},{2,16},{4,22},{6,20},{8,26},{10,24},{12,30},{14,28},{16,2},... | collective-permute-start | bytes 196616 | tf_op jit(solution)/shard_map/ppermute | solution.py:384
  19.7 0.5 %collective-permute-start.1 = (bf16[8,4096]{1,0:T(8,128)(2,1)S(1)}, bf16[8,4096]{1,0:T(8,128)(2,1)S(1)}, u32[]{:S(2)}, u32[]{:S(2)}) collective-permute-start(bf16[8,4096]{1,0:T(8,128)(2,1)S(1)} %reshape.390), channel_id=1, source_target_pairs={{0,2},{2,0},{1,3},{3,1},{4,6},{6,4},{5,7},{7,5},{8,10},{10,8},{9,1... | collective-permute-start | bytes 196616 | tf_op jit(solution)/shard_map/ppermute | solution.py:378
  20.2 0.2 copy.118
  20.4 0.3 reshape.394
  20.7 0.2 collective-permute-start.2
  20.9 3.4 %collective-permute-done.1 = bf16[8,4096]{1,0:T(8,128)(2,1)S(1)} collective-permute-done((bf16[8,4096]{1,0:T(8,128)(2,1)S(1)}, bf16[8,4096]{1,0:T(8,128)(2,1)S(1)}, u32[]{:S(2)}, u32[]{:S(2)}) %collective-permute-start.1) | collective-permute-done | bytes 65568 | tf_op jit(solution)/shard_map/ppermute | solution.py:378
  24.2 0.2 reshape.391
  24.4 0.1 copy.115
  24.6 0.1 copy.116
  24.8 0.1 copy.155
  24.9 0.2 reshape.396
  25.1 2.2 %collective-permute-done.2 = bf16[8,4224]{1,0:T(8,128)(2,1)S(1)} collective-permute-done((bf16[8,4224]{1,0:T(8,128)(2,1)S(1)}, bf16[8,4224]{1,0:T(8,128)(2,1)S(1)}, u32[]{:S(2)}, u32[]{:S(2)}) %collective-permute-start.2) | collective-permute-done | bytes 67616 | tf_op jit(solution)/shard_map/ppermute | solution.py:375
  27.2 0.2 reshape.395
  27.4 0.1 maximum_bitcast_fusion.2
  27.5 0.1 copy.154
  27.7 0.1 pad_maximum_fusion.8
  27.8 1.6 %collective-permute-start.6 = (bf16[2,4,8320]{2,1,0:T(4,128)(2,1)S(1)}, bf16[2,4,8320]{2,1,0:T(4,128)(2,1)S(1)}, u32[]{:S(2)}, u32[]{:S(2)}) collective-permute-start(bf16[2,4,8320]{2,1,0:T(4,128)(2,1)S(1)} %get-tuple-element.17), channel_id=1, source_target_pairs={{0,4},{4,0},{8,12},{12,8},{16,20},{20,16},{24,28},{28,24},{1,5},{5... | collective-permute-start | bytes 399368 | tf_op jit(solution)/shard_map/ppermute | solution.py:264
  29.4 0.3 collective-permute-start.4
  29.7 3.1 %collective-permute-done.6 = bf16[2,4,8320]{2,1,0:T(4,128)(2,1)S(1)} collective-permute-done((bf16[2,4,8320]{2,1,0:T(4,128)(2,1)S(1)}, bf16[2,4,8320]{2,1,0:T(4,128)(2,1)S(1)}, u32[]{:S(2)}, u32[]{:S(2)}) %collective-permute-start.6) | collective-permute-done | bytes 133152 | tf_op jit(solution)/shard_map/ppermute | solution.py:264
  32.8 0.2 fusion.87
  33.0 0.7 %collective-permute-start.7 = (bf16[2,2,4,8320]{3,2,0,1:T(4,128)(2,1)S(1)}, bf16[2,2,4,8320]{3,2,0,1:T(4,128)(2,1)S(1)}, u32[]{:S(2)}, u32[]{:S(2)}) collective-permute-start(bf16[2,2,4,8320]{3,2,0,1:T(4,128)(2,1)S(1)} %get-tuple-element.16), channel_id=1, source_target_pairs={{0,8},{4,12},{8,0},{12,4},{16,24},{20,28},{24,16},{28,20},{1,9},{5... | collective-permute-start | bytes 798728 | tf_op jit(solution)/shard_map/ppermute | solution.py:264
  33.7 1.7 %collective-permute-done.4 = bf16[2,4,8320]{2,1,0:T(4,128)(2,1)S(1)} collective-permute-done((bf16[2,4,8320]{2,1,0:T(4,128)(2,1)S(1)}, bf16[2,4,8320]{2,1,0:T(4,128)(2,1)S(1)}, u32[]{:S(2)}, u32[]{:S(2)}) %collective-permute-start.4) | collective-permute-done | bytes 133152 | tf_op jit(solution)/shard_map/ppermute | solution.py:264
  35.4 0.2 fusion.88
  35.7 4.5 %collective-permute-done.7 = bf16[2,2,4,8320]{3,2,0,1:T(4,128)(2,1)S(1)} collective-permute-done((bf16[2,2,4,8320]{3,2,0,1:T(4,128)(2,1)S(1)}, bf16[2,2,4,8320]{3,2,0,1:T(4,128)(2,1)S(1)}, u32[]{:S(2)}, u32[]{:S(2)}) %collective-permute-start.7) | collective-permute-done | bytes 266272 | tf_op jit(solution)/shard_map/ppermute | solution.py:264
  40.1 0.4 pad_maximum_fusion.1
  40.5 0.2 copy.120
  40.7 1.4 %collective-permute-done.5 = bf16[2,2,4,8320]{3,2,0,1:T(4,128)(2,1)S(1)} collective-permute-done((bf16[2,2,4,8320]{3,2,0,1:T(4,128)(2,1)S(1)}, bf16[2,2,4,8320]{3,2,0,1:T(4,128)(2,1)S(1)}, u32[]{:S(2)}, u32[]{:S(2)}) %collective-permute-start.5) | collective-permute-done | bytes 266272 | tf_op jit(solution)/shard_map/ppermute | solution.py:264
  42.1 0.4 pad_maximum_fusion
  42.4 0.2 copy.119
  42.7 0.2 copy.133
  43.0 0.1 multiply_reduce_fusion
  43.3 0.1 copy.124
  43.4 0.1 eq.68
  43.5 0.1 copy.125
  43.6 0.1 eq.71
  43.8 1.0 %bitcast_convert_fusion = bf16[64,128,128]{1,2,0:T(8,128)(2,1)S(1)} fusion(s32[128]{0:T(128)S(1)} %eq.71, s32[128]{0:T(128)S(1)} %eq.68, bf16[8,4,8320]{2,1,0:T(4,128)(2,1)S(1)} %bitcast.132, bf16[8,4,8320]{2,1,0:T(4,128)(2,1)S(1)} %bitcast.130), kind=kOutput, calls=%fused_computation | convolution fusion | flops 139493376 | bytes 3163136 | tf_op jit(solution)/shard_map/rsc,scbq->brq/dot_general | solution.py:460
  44.9 0.3 copy.127
  45.3 0.1 pad_maximum_fusion.3
  45.4 0.3 copy.128
  45.7 1.2 %convolution_multiply_fusion = f32[64,32,128]{2,1,0:T(8,128)S(1)} fusion(bf16[64,128,128]{1,2,0:T(8,128)(2,1)S(1)} %bitcast_convert_fusion, bf16[64,16,128]{2,1,0:T(8,128)(2,1)S(1)} %copy.128, bf16[64,16,128]{2,1,0:T(8,128)(2,1)S(1)} %dynamic-slice_bitcast_fusion), kind=kOutput, calls=%fused_computation.1 | convolution fusion | flops 68419584 | bytes 3670016 | tf_op jit(solution)/shard_map/bpq,bjq->bpj/dot_general | solution.py:468
  46.9 1.1 %copy.153 = f32[64,2,16,128]{3,2,0,1:T(8,128)} copy(f32[64,2,16,128]{3,2,1,0:T(8,128)S(1)} %bitcast.127) | data formatting | bytes 2097152 | tf_op jit(solution)/shard_map/div | solution.py:471
  (50 shorter events, 1.2 us)
Async XLA Ops:
  0.0 11.7 %copy-start = (f32[128]{0:T(128)S(1)}, f32[128]{0:T(128)}, u32[]{:S(2)}) copy-start(f32[128]{0:T(128)} %param.5) | copy-start | bytes 1540
  9.5 3.4 %copy-start.1 = (s32[1,8,2]{1,2,0:T(2,128)S(1)}, s32[1,8,2]{1,2,0:T(2,128)}, u32[]{:S(2)}) copy-start(s32[1,8,2]{1,2,0:T(2,128)} %param.7) | copy-start | bytes 196
  9.5 3.4 %copy-start.2 = (s32[1,8,2]{1,2,0:T(2,128)S(1)}, s32[1,8,2]{1,2,0:T(2,128)}, u32[]{:S(2)}) copy-start(s32[1,8,2]{1,2,0:T(2,128)} %param.6) | copy-start | bytes 196
  11.2 2.3 %collective-permute-start = (f32[144,2,256]{0,2,1:T(8,128)S(1)}, f32[144,2,256]{0,2,1:T(8,128)S(1)}, u32[]{:S(2)}, u32[]{:S(2)}) collective-permute-start(f32[144,2,256]{0,2,1:T(8,128)S(1)} %pad_maximum_fusion.2), channel_id=1, source_target_pairs={{0,1},{1,0},{2,3},{3,2},{4,5},{5,4},{6,7},{7,6},{8,9},{9,8},{10,11... | collective-permute-start | bytes 884744 | tf_op jit(solution)/shard_map/ppermute | solution.py:24
  15.0 9.9 %collective-permute-start.3 = (bf16[8,4096]{1,0:T(8,128)(2,1)S(1)}, bf16[8,4096]{1,0:T(8,128)(2,1)S(1)}, u32[]{:S(2)}, u32[]{:S(2)}) collective-permute-start(bf16[8,4096]{1,0:T(8,128)(2,1)S(1)} %reshape.390), channel_id=1, source_target_pairs={{0,18},{2,16},{4,22},{6,20},{8,26},{10,24},{12,30},{14,28},{16,2},... | collective-permute-start | bytes 196616 | tf_op jit(solution)/shard_map/ppermute | solution.py:384
  19.7 4.5 %collective-permute-start.1 = (bf16[8,4096]{1,0:T(8,128)(2,1)S(1)}, bf16[8,4096]{1,0:T(8,128)(2,1)S(1)}, u32[]{:S(2)}, u32[]{:S(2)}) collective-permute-start(bf16[8,4096]{1,0:T(8,128)(2,1)S(1)} %reshape.390), channel_id=1, source_target_pairs={{0,2},{2,0},{1,3},{3,1},{4,6},{6,4},{5,7},{7,5},{8,10},{10,8},{9,1... | collective-permute-start | bytes 196616 | tf_op jit(solution)/shard_map/ppermute | solution.py:378
  20.7 6.5 %collective-permute-start.2 = (bf16[8,4224]{1,0:T(8,128)(2,1)S(1)}, bf16[8,4224]{1,0:T(8,128)(2,1)S(1)}, u32[]{:S(2)}, u32[]{:S(2)}) collective-permute-start(bf16[8,4224]{1,0:T(8,128)(2,1)S(1)} %pad_maximum_fusion.11), channel_id=1, source_target_pairs={{0,16},{4,20},{8,24},{12,28},{16,0},{20,4},{24,8},{28,12},{1,17},{... | collective-permute-start | bytes 202760 | tf_op jit(solution)/shard_map/ppermute | solution.py:375
  27.8 5.1 %collective-permute-start.6 = (bf16[2,4,8320]{2,1,0:T(4,128)(2,1)S(1)}, bf16[2,4,8320]{2,1,0:T(4,128)(2,1)S(1)}, u32[]{:S(2)}, u32[]{:S(2)}) collective-permute-start(bf16[2,4,8320]{2,1,0:T(4,128)(2,1)S(1)} %get-tuple-element.17), channel_id=1, source_target_pairs={{0,4},{4,0},{8,12},{12,8},{16,20},{20,16},{24,28},{28,24},{1,5},{5... | collective-permute-start | bytes 399368 | tf_op jit(solution)/shard_map/ppermute | solution.py:264
  29.4 5.9 %collective-permute-start.4 = (bf16[2,4,8320]{2,1,0:T(4,128)(2,1)S(1)}, bf16[2,4,8320]{2,1,0:T(4,128)(2,1)S(1)}, u32[]{:S(2)}, u32[]{:S(2)}) collective-permute-start(bf16[2,4,8320]{2,1,0:T(4,128)(2,1)S(1)} %get-tuple-element.18), channel_id=1, source_target_pairs={{0,8},{4,12},{8,0},{12,4},{16,24},{20,28},{24,16},{28,20},{1,9},{5... | collective-permute-start | bytes 399368 | tf_op jit(solution)/shard_map/ppermute | solution.py:264
  33.0 7.1 %collective-permute-start.7 = (bf16[2,2,4,8320]{3,2,0,1:T(4,128)(2,1)S(1)}, bf16[2,2,4,8320]{3,2,0,1:T(4,128)(2,1)S(1)}, u32[]{:S(2)}, u32[]{:S(2)}) collective-permute-start(bf16[2,2,4,8320]{3,2,0,1:T(4,128)(2,1)S(1)} %get-tuple-element.16), channel_id=1, source_target_pairs={{0,8},{4,12},{8,0},{12,4},{16,24},{20,28},{24,16},{28,20},{1,9},{5... | collective-permute-start | bytes 798728 | tf_op jit(solution)/shard_map/ppermute | solution.py:264
  35.6 6.5 %collective-permute-start.5 = (bf16[2,2,4,8320]{3,2,0,1:T(4,128)(2,1)S(1)}, bf16[2,2,4,8320]{3,2,0,1:T(4,128)(2,1)S(1)}, u32[]{:S(2)}, u32[]{:S(2)}) collective-permute-start(bf16[2,2,4,8320]{3,2,0,1:T(4,128)(2,1)S(1)} %get-tuple-element.20), channel_id=1, source_target_pairs={{0,4},{4,0},{8,12},{12,8},{16,20},{20,16},{24,28},{28,24},{1,5},{5... | collective-permute-start | bytes 798728 | tf_op jit(solution)/shard_map/ppermute | solution.py:264

commit v20 on v19

--- a/solution.py
+++ b/solution.py
@@ -105,39 +105,47 @@
     lax.fori_loop(0, groups, one_group, 0)
 
 
-def dft_kernel_inline(rec_ref, oca_ref, osa_ref, ica_ref, isa_ref, ocb_ref, osb_ref, icb_ref, isb_ref,
-                      re_ref, im_ref):
+def dft_kernel_self(info_ref, rec_ref, re_ref, im_ref, cos_a_ref, nsin_a_ref, cos_b_ref, sin_b_ref):
     step = pl.program_id(0)
     lanes = 128
-    group = ica_ref.shape[0]
+    group = 8
     groups = rec_ref.shape[1] // (group * lanes)
-    norm_scale = 1.0 / math.sqrt(SEG_LEN)
 
     @pl.when(step == 0)
     def _():
         re_ref[...] = jnp.zeros_like(re_ref)
         im_ref[...] = jnp.zeros_like(im_ref)
-
-    icb = icb_ref[...]
-    isb = isb_ref[...]
-    cos_rows = []
-    sin_rows = []
-    for outer in range(ocb_ref.shape[0]):
-        ocb = ocb_ref[outer : outer + 1, :]
-        osb = osb_ref[outer : outer + 1, :]
-        cos_rows.append(ocb * icb - osb * isb)
-        sin_rows.append(osb * icb + ocb * isb)
-    cos_b = jnp.concatenate(cos_rows, axis=0) * norm_scale
-    sin_b = jnp.concatenate(sin_rows, axis=0) * norm_scale
-    ica = ica_ref[...]
-    isa = isa_ref[...]
+        wavenumber = info_ref[0:1, :]
+        first = info_ref[1:2, :]
+
+        def cos_sin(steps):
+            angle = (steps * wavenumber % SEG_LEN).astype(jnp.float32) * (TWO_PI / SEG_LEN)
+            return jnp.cos(angle), jnp.sin(angle)
+
+        width = wavenumber.shape[1]
+        eight = lax.broadcasted_iota(jnp.int32, (8, width), 0)
+        sixteen = lax.broadcasted_iota(jnp.int32, (16, width), 0)
+        outer_cos, outer_sin = cos_sin(first + lanes * 8 * eight)
+        inner_cos, inner_sin = cos_sin(lanes * eight)
+        fine_outer_cos, fine_outer_sin = cos_sin(16 * eight)
+        fine_inner_cos, fine_inner_sin = cos_sin(sixteen)
+        norm_scale = 1.0 / math.sqrt(SEG_LEN)
+        for outer in range(8):
+            oc = outer_cos[outer : outer + 1]
+            os_ = outer_sin[outer : outer + 1]
+            cos_a_ref[outer * 8 : outer * 8 + 8, :] = oc * inner_cos - os_ * inner_sin
+            nsin_a_ref[outer * 8 : outer * 8 + 8, :] = -(os_ * inner_cos + oc * inner_sin)
+            fc = fine_outer_cos[outer : outer + 1]
+            fs = fine_outer_sin[outer : outer + 1]
+            cos_b_ref[outer * 16 : outer * 16 + 16, :] = (fc * fine_inner_cos - fs * fine_inner_sin) * norm_scale
+            sin_b_ref[outer * 16 : outer * 16 + 16, :] = (fs * fine_inner_cos + fc * fine_inner_sin) * norm_scale
 
     def one_group(index, carry):
-        outer = step * groups + index
-        oca = oca_ref[outer]
-        osa = osa_ref[outer]
-        cos_a = oca * ica - osa * isa
-        nsin_a = -(osa * ica + oca * isa)
+        row = pl.multiple_of((step * groups + index) * group, group)
+        cos_a = cos_a_ref[pl.ds(row, group), :]
+        nsin_a = nsin_a_ref[pl.ds(row, group), :]
+        cos_b = cos_b_ref[...]
+        sin_b = sin_b_ref[...]
         for pair in range(group // 2):
             cos_parts = []
             sin_parts = []
@@ -184,26 +192,30 @@
     bins = band_index.shape[0]
     full = lambda step: (0, 0)
     if coarse_count == 64 and chunk == 2048:
-        outer_cos, outer_sin = cos_sin(first_sample + lanes * 8 * jnp.arange(8, dtype=jnp.int32))
-        inner_cos, inner_sin = cos_sin(lanes * jnp.arange(8, dtype=jnp.int32))
-        fine_outer_cos, fine_outer_sin = cos_sin(16 * jnp.arange(lanes // 16, dtype=jnp.int32))
-        fine_inner_cos, fine_inner_sin = cos_sin(jnp.arange(16, dtype=jnp.int32))
-        outer_cos = jnp.broadcast_to(outer_cos[:, None, :], (8, 8, bins))
-        outer_sin = jnp.broadcast_to(outer_sin[:, None, :], (8, 8, bins))
-        small = [inner_cos, inner_sin, fine_outer_cos, fine_outer_sin, fine_inner_cos, fine_inner_sin]
+        info = jnp.concatenate(
+            [
+                wavenumber[None, :].astype(jnp.int32),
+                jnp.broadcast_to(jnp.asarray(first_sample, jnp.int32), (7, bins)),
+            ],
+            axis=0,
+        )
         return pl.pallas_call(
-            dft_kernel_inline,
+            dft_kernel_self,
             grid=(count // chunk,),
-            in_specs=[pl.BlockSpec((rows, chunk), lambda step: (0, step))]
-            + [pl.BlockSpec((8, 8, bins), lambda step: (0, 0, 0))] * 2
-            + [pl.BlockSpec(table.shape, full) for table in small],
+            in_specs=[pl.BlockSpec((8, bins), full), pl.BlockSpec((rows, chunk), lambda step: (0, step))],
             out_specs=[pl.BlockSpec((rows, bins), full), pl.BlockSpec((rows, bins), full)],
             out_shape=[
                 jax.ShapeDtypeStruct((rows, bins), jnp.float32),
                 jax.ShapeDtypeStruct((rows, bins), jnp.float32),
             ],
+            scratch_shapes=[
+                pltpu.VMEM((64, bins), jnp.float32),
+                pltpu.VMEM((64, bins), jnp.float32),
+                pltpu.VMEM((128, bins), jnp.float32),
+                pltpu.VMEM((128, bins), jnp.float32),
+            ],
             compiler_params=pltpu.CompilerParams(dimension_semantics=("arbitrary",)),
-        )(records, outer_cos, outer_sin, *small)
+        )(info, records)
     coarse_outer = coarse_count // 8 if coarse_count % 8 == 0 else 1
     coarse_inner = coarse_count // coarse_outer
     cos_a, sin_a = combined(

time: 48.2 us -> 45.7 us (0.948)
  other arithmetic: 5.27 us -> 3.79 us
  local copies, waits for them, and re-layouts: 7.48 us -> 6.81 us
    sin x2 -> x0, other arithmetic: 1.48 us -> none  [cos_sin(): return (jnp.cos(angle), jnp.sin(angle))]
    broadcast_in_dim x2 -> x0, local copies, waits for them, and re-layouts: 1.25 us -> none  [the longest x1 0.63 us: dft_fused(): outer_cos = jnp.broadcast_to(outer_cos[:, None, :], (8, 8, bins))]
    concatenate x0 -> x1, local copies, waits for them, and re-layouts: none -> 0.58 us  [dft_fused(): jnp.concatenate([wavenumber[None, :].astype(jnp.int32), jnp.broadcast_to(...]
  transfers between devices with their start and end apart: 8 -> 8, of which waited for: 6 -> 6; matrix products, arithmetic and copies ran while one was open for 8% -> 9% of each run, Pallas kernels for 0% -> 0%
where the time goes in v20:
time: 45.7 us; the launch traced here: 45.5 us
  waiting for transfers between devices  16.1 us (35%)
  starting transfers between devices  8.57 us (19%)
  local copies, waits for them, and re-layouts  6.81 us (15%)
  Pallas kernels  6.5 us (14%)
  other arithmetic  3.79 us (8%)
  matrix products  3.25 us (7%)
  between operations  0.52 us (1%)
    ppermute x4, waiting for transfers between devices, gather_blocks(): arrived = lax.ppermute(part, 'blk', pairs)  10.6 us
    pallas_call x1, Pallas kernels, dft_fused(): pl.pallas_call(dft_kernel_self, grid=(count // chunk,), in_specs=[pl.Bloc...  6.5 us
    ppermute x1, starting transfers between devices, per_device(): from_diagonal = lax.ppermute(other_flat, ('blk', 'seg'), diagonal)  4.73 us
    ppermute x1, waiting for transfers between devices, per_device(): from_seg = lax.ppermute(other_flat, 'seg', [(0, 1), (1, 0)])  3.34 us
    ppermute x4, starting transfers between devices, gather_blocks(): arrived = lax.ppermute(part, 'blk', pairs)  2.61 us
    ppermute x1, waiting for transfers between devices, per_device(): lax.ppermute(keep_flat, 'blk', [(source, source ^ first) for source in ra...  2.18 us
    select_n x1, other arithmetic, per_device(): sent = jnp.where(freq_rank == 0, blocks[1], blocks[0])  1.27 us
    dot_general x1, matrix products, per_device(): jnp.einsum('bpq,bjq->bpj', lhs, routed, preferred_element_type=jnp.float32)  1.19 us
  transfers between devices with their start and end apart: 8, of which 6 were waited for; matrix products, arithmetic and copies ran while one was open for 9% of the time, Pallas kernels for 0%

profile of v20, /device:TPU:0, one launch (start us, length us, event | category | flops | bytes accessed | tf_op | source)
XLA Modules:
  0.0 45.5 jit_solution(17990963171138452130)
XLA Ops:
  0.0 0.6 %concatenate.58.info_ref = s32[8,256]{1,0:T(8,128)} pad(s32[1,256]{1,0:T(1,128)S(1)} %fusion.48, s32[]{:T(128)S(6)} %mul.175), padding=0_7x0_0 | pad | bytes 9220 | tf_op jit(solution)/shard_map/concatenate | solution.py:195
  0.6 6.5 %shard_map.46 = (f32[256,256]{1,0:T(8,128)}, f32[256,256]{1,0:T(8,128)}) custom-call(s32[8,256]{1,0:T(8,128)} %concatenate.58.info_ref, bf16[256,8192]{1,0:T(8,128)(2,1)} %bitcast.128), custom_call_target="tpu_custom_call" | custom-call | tf_op jit(solution)/shard_map/pallas_call | solution.py:202
  7.1 1.3 %broadcast_select_fusion = (f32[128,2,256]{0,2,1:T(8,128)S(1)}, f32[128,2,256]{0,2,1:T(8,128)S(1)}) fusion(pred[]{:T(512)S(6)} %eq.58, f32[256,1,256]{0,2,1:T(8,128)} %bitcast.150, f32[256,1,256]{0,2,1:T(8,128)} %bitcast.149), kind=kLoop, calls=%fused_computation.77 | loop fusion | flops 327680 | bytes 1048577 | tf_op jit(solution)/shard_map/jit(_where)/select_n | solution.py:310
  8.4 0.1 copy.101
  8.6 0.1 copy.102
  8.7 0.5 %collective-permute-start = (f32[144,2,256]{0,2,1:T(8,128)S(1)}, f32[144,2,256]{0,2,1:T(8,128)S(1)}, u32[]{:S(2)}, u32[]{:S(2)}) collective-permute-start(f32[144,2,256]{0,2,1:T(8,128)S(1)} %pad_maximum_fusion.2), channel_id=1, source_target_pairs={{0,1},{1,0},{2,3},{3,2},{4,5},{5,4},{6,7},{7,6},{8,9},{9,8},{10,11... | collective-permute-start | bytes 884744 | tf_op jit(solution)/shard_map/ppermute | solution.py:24
  9.3 0.5 %convolution_bitcast_fusion = f32[128]{0:T(128)S(1)} fusion(s32[128]{0:T(128)S(1)} %fusion.54, f32[128]{0:T(128)S(1)} %copy-done), kind=kOutput, calls=%fused_computation.4 | convolution fusion | flops 442368 | bytes 1536 | tf_op jit(solution)/shard_map/dot_general | solution.py:67
  9.8 0.5 %convolution_bitcast_fusion.1 = f32[128]{0:T(128)S(1)} fusion(s32[128]{0:T(128)S(1)} %fusion.54, f32[128]{0:T(128)S(1)} %copy-done), kind=kOutput, calls=%fused_computation.5 | convolution fusion | flops 425984 | bytes 1536 | tf_op jit(solution)/shard_map/dot_general | solution.py:66
  10.3 0.2 copy.103
  10.6 0.1 copy.117
  10.7 0.1 convert_element_type.37
  10.8 0.1 copy.104
  11.0 0.1 copy.105
  11.3 0.1 copy.108
  11.5 0.1 fusion.14
  11.6 0.1 copy.110
  11.8 0.1 stack.71
  11.9 0.1 stack.70
  12.1 0.2 copy.114
  12.3 0.3 reshape.394
  12.5 4.7 %collective-permute-start.3 = (bf16[8,4096]{1,0:T(8,128)(2,1)S(1)}, bf16[8,4096]{1,0:T(8,128)(2,1)S(1)}, u32[]{:S(2)}, u32[]{:S(2)}) collective-permute-start(bf16[8,4096]{1,0:T(8,128)(2,1)S(1)} %reshape.394), channel_id=1, source_target_pairs={{0,18},{2,16},{4,22},{6,20},{8,26},{10,24},{12,30},{14,28},{16,2},... | collective-permute-start | bytes 196616 | tf_op jit(solution)/shard_map/ppermute | solution.py:396
  17.3 0.5 %collective-permute-start.1 = (bf16[8,4096]{1,0:T(8,128)(2,1)S(1)}, bf16[8,4096]{1,0:T(8,128)(2,1)S(1)}, u32[]{:S(2)}, u32[]{:S(2)}) collective-permute-start(bf16[8,4096]{1,0:T(8,128)(2,1)S(1)} %reshape.394), channel_id=1, source_target_pairs={{0,2},{2,0},{1,3},{3,1},{4,6},{6,4},{5,7},{7,5},{8,10},{10,8},{9,1... | collective-permute-start | bytes 196616 | tf_op jit(solution)/shard_map/ppermute | solution.py:390
  17.8 0.2 copy.118
  18.0 0.3 reshape.398
  18.3 0.2 collective-permute-start.2
  18.5 3.3 %collective-permute-done.1 = bf16[8,4096]{1,0:T(8,128)(2,1)S(1)} collective-permute-done((bf16[8,4096]{1,0:T(8,128)(2,1)S(1)}, bf16[8,4096]{1,0:T(8,128)(2,1)S(1)}, u32[]{:S(2)}, u32[]{:S(2)}) %collective-permute-start.1) | collective-permute-done | bytes 65568 | tf_op jit(solution)/shard_map/ppermute | solution.py:390
  21.8 0.2 reshape.395
  22.0 0.1 copy.115
  22.2 0.1 copy.116
  22.3 0.1 copy.155
  22.5 0.2 reshape.400
  22.6 2.2 %collective-permute-done.2 = bf16[8,4224]{1,0:T(8,128)(2,1)S(1)} collective-permute-done((bf16[8,4224]{1,0:T(8,128)(2,1)S(1)}, bf16[8,4224]{1,0:T(8,128)(2,1)S(1)}, u32[]{:S(2)}, u32[]{:S(2)}) %collective-permute-start.2) | collective-permute-done | bytes 67616 | tf_op jit(solution)/shard_map/ppermute | solution.py:387
  24.8 0.2 reshape.399
  25.0 0.1 maximum_bitcast_fusion.2
  25.1 0.1 copy.154
  25.3 0.1 pad_maximum_fusion.8
  25.4 1.6 %collective-permute-start.6 = (bf16[2,4,8320]{2,1,0:T(4,128)(2,1)S(1)}, bf16[2,4,8320]{2,1,0:T(4,128)(2,1)S(1)}, u32[]{:S(2)}, u32[]{:S(2)}) collective-permute-start(bf16[2,4,8320]{2,1,0:T(4,128)(2,1)S(1)} %get-tuple-element.17), channel_id=1, source_target_pairs={{0,4},{4,0},{8,12},{12,8},{16,20},{20,16},{24,28},{28,24},{1,5},{5... | collective-permute-start | bytes 399368 | tf_op jit(solution)/shard_map/ppermute | solution.py:276
  27.0 0.3 collective-permute-start.4
  27.3 3.1 %collective-permute-done.6 = bf16[2,4,8320]{2,1,0:T(4,128)(2,1)S(1)} collective-permute-done((bf16[2,4,8320]{2,1,0:T(4,128)(2,1)S(1)}, bf16[2,4,8320]{2,1,0:T(4,128)(2,1)S(1)}, u32[]{:S(2)}, u32[]{:S(2)}) %collective-permute-start.6) | collective-permute-done | bytes 133152 | tf_op jit(solution)/shard_map/ppermute | solution.py:276
  30.4 0.2 fusion.62
  30.6 0.7 %collective-permute-start.7 = (bf16[2,2,4,8320]{3,2,0,1:T(4,128)(2,1)S(1)}, bf16[2,2,4,8320]{3,2,0,1:T(4,128)(2,1)S(1)}, u32[]{:S(2)}, u32[]{:S(2)}) collective-permute-start(bf16[2,2,4,8320]{3,2,0,1:T(4,128)(2,1)S(1)} %get-tuple-element.16), channel_id=1, source_target_pairs={{0,8},{4,12},{8,0},{12,4},{16,24},{20,28},{24,16},{28,20},{1,9},{5... | collective-permute-start | bytes 798728 | tf_op jit(solution)/shard_map/ppermute | solution.py:276
  31.3 1.6 %collective-permute-done.4 = bf16[2,4,8320]{2,1,0:T(4,128)(2,1)S(1)} collective-permute-done((bf16[2,4,8320]{2,1,0:T(4,128)(2,1)S(1)}, bf16[2,4,8320]{2,1,0:T(4,128)(2,1)S(1)}, u32[]{:S(2)}, u32[]{:S(2)}) %collective-permute-start.4) | collective-permute-done | bytes 133152 | tf_op jit(solution)/shard_map/ppermute | solution.py:276
  32.9 0.2 fusion.63
  33.2 4.5 %collective-permute-done.7 = bf16[2,2,4,8320]{3,2,0,1:T(4,128)(2,1)S(1)} collective-permute-done((bf16[2,2,4,8320]{3,2,0,1:T(4,128)(2,1)S(1)}, bf16[2,2,4,8320]{3,2,0,1:T(4,128)(2,1)S(1)}, u32[]{:S(2)}, u32[]{:S(2)}) %collective-permute-start.7) | collective-permute-done | bytes 266272 | tf_op jit(solution)/shard_map/ppermute | solution.py:276
  37.7 0.4 pad_maximum_fusion.1
  38.1 0.2 copy.120
  38.3 1.4 %collective-permute-done.5 = bf16[2,2,4,8320]{3,2,0,1:T(4,128)(2,1)S(1)} collective-permute-done((bf16[2,2,4,8320]{3,2,0,1:T(4,128)(2,1)S(1)}, bf16[2,2,4,8320]{3,2,0,1:T(4,128)(2,1)S(1)}, u32[]{:S(2)}, u32[]{:S(2)}) %collective-permute-start.5) | collective-permute-done | bytes 266272 | tf_op jit(solution)/shard_map/ppermute | solution.py:276
  39.6 0.4 pad_maximum_fusion
  40.0 0.2 copy.119
  40.2 0.2 copy.133
  40.5 0.1 copy.122
  40.5 0.1 multiply_reduce_fusion
  40.7 0.1 copy.138
  40.8 0.1 add_select_fusion.1
  40.8 0.1 copy.124
  41.0 0.1 eq.62
  41.1 0.1 copy.125
  41.2 0.1 eq.65
  41.4 1.0 %bitcast_convert_fusion = bf16[64,128,128]{1,2,0:T(8,128)(2,1)S(1)} fusion(s32[128]{0:T(128)S(1)} %eq.65, s32[128]{0:T(128)S(1)} %eq.62, bf16[8,4,8320]{2,1,0:T(4,128)(2,1)S(1)} %bitcast.132, bf16[8,4,8320]{2,1,0:T(4,128)(2,1)S(1)} %bitcast.130), kind=kOutput, calls=%fused_computation | convolution fusion | flops 139493376 | bytes 3163136 | tf_op jit(solution)/shard_map/rsc,scbq->brq/dot_general | solution.py:472
  42.5 0.3 copy.127
  42.9 0.1 pad_maximum_fusion.3
  43.0 0.3 copy.128
  43.3 1.2 %convolution_multiply_fusion = f32[64,32,128]{2,1,0:T(8,128)S(1)} fusion(bf16[64,128,128]{1,2,0:T(8,128)(2,1)S(1)} %bitcast_convert_fusion, bf16[64,16,128]{2,1,0:T(8,128)(2,1)S(1)} %copy.128, bf16[64,16,128]{2,1,0:T(8,128)(2,1)S(1)} %dynamic-slice_bitcast_fusion), kind=kOutput, calls=%fused_computation.1 | convolution fusion | flops 68419584 | bytes 3670016 | tf_op jit(solution)/shard_map/bpq,bjq->bpj/dot_general | solution.py:480
  44.5 1.1 %copy.153 = f32[64,2,16,128]{3,2,0,1:T(8,128)} copy(f32[64,2,16,128]{3,2,1,0:T(8,128)S(1)} %bitcast.127) | data formatting | bytes 2097152 | tf_op jit(solution)/shard_map/div | solution.py:483
  (46 shorter events, 1.0 us)
Async XLA Ops:
  0.0 9.3 %copy-start = (f32[128]{0:T(128)S(1)}, f32[128]{0:T(128)}, u32[]{:S(2)}) copy-start(f32[128]{0:T(128)} %param.5) | copy-start | bytes 1540
  7.1 3.4 %copy-start.1 = (s32[1,8,2]{1,2,0:T(2,128)S(1)}, s32[1,8,2]{1,2,0:T(2,128)}, u32[]{:S(2)}) copy-start(s32[1,8,2]{1,2,0:T(2,128)} %param.7) | copy-start | bytes 196
  7.1 3.4 %copy-start.2 = (s32[1,8,2]{1,2,0:T(2,128)S(1)}, s32[1,8,2]{1,2,0:T(2,128)}, u32[]{:S(2)}) copy-start(s32[1,8,2]{1,2,0:T(2,128)} %param.6) | copy-start | bytes 196
  8.7 2.3 %collective-permute-start = (f32[144,2,256]{0,2,1:T(8,128)S(1)}, f32[144,2,256]{0,2,1:T(8,128)S(1)}, u32[]{:S(2)}, u32[]{:S(2)}) collective-permute-start(f32[144,2,256]{0,2,1:T(8,128)S(1)} %pad_maximum_fusion.2), channel_id=1, source_target_pairs={{0,1},{1,0},{2,3},{3,2},{4,5},{5,4},{6,7},{7,6},{8,9},{9,8},{10,11... | collective-permute-start | bytes 884744 | tf_op jit(solution)/shard_map/ppermute | solution.py:24
  12.5 9.9 %collective-permute-start.3 = (bf16[8,4096]{1,0:T(8,128)(2,1)S(1)}, bf16[8,4096]{1,0:T(8,128)(2,1)S(1)}, u32[]{:S(2)}, u32[]{:S(2)}) collective-permute-start(bf16[8,4096]{1,0:T(8,128)(2,1)S(1)} %reshape.394), channel_id=1, source_target_pairs={{0,18},{2,16},{4,22},{6,20},{8,26},{10,24},{12,30},{14,28},{16,2},... | collective-permute-start | bytes 196616 | tf_op jit(solution)/shard_map/ppermute | solution.py:396
  17.3 4.5 %collective-permute-start.1 = (bf16[8,4096]{1,0:T(8,128)(2,1)S(1)}, bf16[8,4096]{1,0:T(8,128)(2,1)S(1)}, u32[]{:S(2)}, u32[]{:S(2)}) collective-permute-start(bf16[8,4096]{1,0:T(8,128)(2,1)S(1)} %reshape.394), channel_id=1, source_target_pairs={{0,2},{2,0},{1,3},{3,1},{4,6},{6,4},{5,7},{7,5},{8,10},{10,8},{9,1... | collective-permute-start | bytes 196616 | tf_op jit(solution)/shard_map/ppermute | solution.py:390
  18.3 6.5 %collective-permute-start.2 = (bf16[8,4224]{1,0:T(8,128)(2,1)S(1)}, bf16[8,4224]{1,0:T(8,128)(2,1)S(1)}, u32[]{:S(2)}, u32[]{:S(2)}) collective-permute-start(bf16[8,4224]{1,0:T(8,128)(2,1)S(1)} %pad_maximum_fusion.11), channel_id=1, source_target_pairs={{0,16},{4,20},{8,24},{12,28},{16,0},{20,4},{24,8},{28,12},{1,17},{... | collective-permute-start | bytes 202760 | tf_op jit(solution)/shard_map/ppermute | solution.py:387
  25.4 5.1 %collective-permute-start.6 = (bf16[2,4,8320]{2,1,0:T(4,128)(2,1)S(1)}, bf16[2,4,8320]{2,1,0:T(4,128)(2,1)S(1)}, u32[]{:S(2)}, u32[]{:S(2)}) collective-permute-start(bf16[2,4,8320]{2,1,0:T(4,128)(2,1)S(1)} %get-tuple-element.17), channel_id=1, source_target_pairs={{0,4},{4,0},{8,12},{12,8},{16,20},{20,16},{24,28},{28,24},{1,5},{5... | collective-permute-start | bytes 399368 | tf_op jit(solution)/shard_map/ppermute | solution.py:276
  27.0 5.9 %collective-permute-start.4 = (bf16[2,4,8320]{2,1,0:T(4,128)(2,1)S(1)}, bf16[2,4,8320]{2,1,0:T(4,128)(2,1)S(1)}, u32[]{:S(2)}, u32[]{:S(2)}) collective-permute-start(bf16[2,4,8320]{2,1,0:T(4,128)(2,1)S(1)} %get-tuple-element.18), channel_id=1, source_target_pairs={{0,8},{4,12},{8,0},{12,4},{16,24},{20,28},{24,16},{28,20},{1,9},{5... | collective-permute-start | bytes 399368 | tf_op jit(solution)/shard_map/ppermute | solution.py:276
  30.6 7.1 %collective-permute-start.7 = (bf16[2,2,4,8320]{3,2,0,1:T(4,128)(2,1)S(1)}, bf16[2,2,4,8320]{3,2,0,1:T(4,128)(2,1)S(1)}, u32[]{:S(2)}, u32[]{:S(2)}) collective-permute-start(bf16[2,2,4,8320]{3,2,0,1:T(4,128)(2,1)S(1)} %get-tuple-element.16), channel_id=1, source_target_pairs={{0,8},{4,12},{8,0},{12,4},{16,24},{20,28},{24,16},{28,20},{1,9},{5... | collective-permute-start | bytes 798728 | tf_op jit(solution)/shard_map/ppermute | solution.py:276
  33.2 6.5 %collective-permute-start.5 = (bf16[2,2,4,8320]{3,2,0,1:T(4,128)(2,1)S(1)}, bf16[2,2,4,8320]{3,2,0,1:T(4,128)(2,1)S(1)}, u32[]{:S(2)}, u32[]{:S(2)}) collective-permute-start(bf16[2,2,4,8320]{3,2,0,1:T(4,128)(2,1)S(1)} %get-tuple-element.20), channel_id=1, source_target_pairs={{0,4},{4,0},{8,12},{12,8},{16,20},{20,16},{24,28},{28,24},{1,5},{5... | collective-permute-start | bytes 798728 | tf_op jit(solution)/shard_map/ppermute | solution.py:276

commit v21 on v20

--- a/solution.py
+++ b/solution.py
@@ -105,7 +105,7 @@
     lax.fori_loop(0, groups, one_group, 0)
 
 
-def dft_kernel_self(info_ref, rec_ref, re_ref, im_ref, cos_a_ref, nsin_a_ref, cos_b_ref, sin_b_ref):
+def dft_kernel_self(info_ref, rec_ref, re_ref, im_ref, cos_a_ref, nsin_a_ref, cos_b_ref, sin_b_ref, layout=None):
     step = pl.program_id(0)
     lanes = 128
     group = 8
@@ -115,8 +115,17 @@
     def _():
         re_ref[...] = jnp.zeros_like(re_ref)
         im_ref[...] = jnp.zeros_like(im_ref)
-        wavenumber = info_ref[0:1, :]
-        first = info_ref[1:2, :]
+        if layout is None:
+            wavenumber = info_ref[0:1, :]
+            first = info_ref[1:2, :]
+        else:
+            device_bins, block_bins, freq_count, half_len = layout
+            row_ids = lax.broadcasted_iota(jnp.int32, (1, re_ref.shape[1]), 1)
+            owner_core = row_ids // device_bins
+            local_row = row_ids % device_bins
+            band = (local_row // block_bins * freq_count + owner_core) * block_bins + local_row % block_bins
+            wavenumber = BAND_LO + band
+            first = lax.axis_index("freq") * half_len
 
         def cos_sin(steps):
             angle = (steps * wavenumber % SEG_LEN).astype(jnp.float32) * (TWO_PI / SEG_LEN)
@@ -166,7 +175,7 @@
     lax.fori_loop(0, groups, one_group, 0)
 
 
-def dft_fused(records, band_index, first_sample):
+def dft_fused(records, band_index, first_sample, layout=None):
     lanes = 128
     chunk = 2048
     count = records.shape[1]
@@ -199,10 +208,20 @@
             ],
             axis=0,
         )
+        if layout is not None:
+            def kernel(rec_ref, re_ref, im_ref, *scratch):
+                dft_kernel_self(None, rec_ref, re_ref, im_ref, *scratch, layout=layout)
+
+            operands = (records,)
+            leading = []
+        else:
+            kernel = dft_kernel_self
+            operands = (info, records)
+            leading = [pl.BlockSpec((8, bins), full)]
         return pl.pallas_call(
-            dft_kernel_self,
+            kernel,
             grid=(count // chunk,),
-            in_specs=[pl.BlockSpec((8, bins), full), pl.BlockSpec((rows, chunk), lambda step: (0, step))],
+            in_specs=leading + [pl.BlockSpec((rows, chunk), lambda step: (0, step))],
             out_specs=[pl.BlockSpec((rows, bins), full), pl.BlockSpec((rows, bins), full)],
             out_shape=[
                 jax.ShapeDtypeStruct((rows, bins), jnp.float32),
@@ -215,7 +234,7 @@
                 pltpu.VMEM((128, bins), jnp.float32),
             ],
             compiler_params=pltpu.CompilerParams(dimension_semantics=("arbitrary",)),
-        )(info, records)
+        )(*operands)
     coarse_outer = coarse_count // 8 if coarse_count % 8 == 0 else 1
     coarse_inner = coarse_count // coarse_outer
     cos_a, sin_a = combined(
@@ -300,7 +319,9 @@
         ) * block_bins + local_row % block_bins
 
     band_rows = band_of(jnp.arange(device_bins * freq_count, dtype=jnp.int32))
-    real_t, imag_t = dft_fused(records, band_rows, freq_rank * half_len)
+    real_t, imag_t = dft_fused(
+        records, band_rows, freq_rank * half_len, (device_bins, block_bins, freq_count, half_len)
+    )
     real_all = real_t.T
     imag_all = imag_t.T
     blocks = jnp.stack([real_all, imag_all], axis=1)

time: 45.7 us -> 45.2 us (0.989)
  local copies, waits for them, and re-layouts: 6.81 us -> 6.23 us
    concatenate x1 -> x0, local copies, waits for them, and re-layouts: 0.58 us -> none  [dft_fused(): jnp.concatenate([wavenumber[None, :].astype(jnp.int32), jnp.broadcast_to(...]
where the time goes in v21:
time: 45.2 us; the launch traced here: 45 us
  waiting for transfers between devices  16.1 us (36%)
  starting transfers between devices  8.58 us (19%)
  Pallas kernels  6.54 us (14%)
  local copies, waits for them, and re-layouts  6.23 us (14%)
  other arithmetic  3.77 us (8%)
  matrix products  3.25 us (7%)
  between operations  0.51 us (1%)
    ppermute x4, waiting for transfers between devices, gather_blocks(): arrived = lax.ppermute(part, 'blk', pairs)  10.6 us
    pallas_call x1, Pallas kernels, dft_fused(): pl.pallas_call(kernel, grid=(count // chunk,), in_specs=leading + [pl.Blo...  6.54 us
    ppermute x1, starting transfers between devices, per_device(): from_diagonal = lax.ppermute(other_flat, ('blk', 'seg'), diagonal)  4.73 us
    ppermute x1, waiting for transfers between devices, per_device(): from_seg = lax.ppermute(other_flat, 'seg', [(0, 1), (1, 0)])  3.35 us
    ppermute x4, starting transfers between devices, gather_blocks(): arrived = lax.ppermute(part, 'blk', pairs)  2.62 us
    ppermute x1, waiting for transfers between devices, per_device(): lax.ppermute(keep_flat, 'blk', [(source, source ^ first) for source in ra...  2.17 us
    select_n x1, other arithmetic, per_device(): sent = jnp.where(freq_rank == 0, blocks[1], blocks[0])  1.27 us
    dot_general x1, matrix products, per_device(): jnp.einsum('bpq,bjq->bpj', lhs, routed, preferred_element_type=jnp.float32)  1.19 us
  transfers between devices with their start and end apart: 8, of which 6 were waited for; matrix products, arithmetic and copies ran while one was open for 9% of the time, Pallas kernels for 0%

profile of v21, /device:TPU:0, one launch (start us, length us, event | category | flops | bytes accessed | tf_op | source)
XLA Modules:
  0.0 45.0 jit_solution(16968808038213188591)
XLA Ops:
  0.0 6.5 %shard_map.46 = (f32[256,256]{1,0:T(8,128)}, f32[256,256]{1,0:T(8,128)}) custom-call(bf16[256,8192]{1,0:T(8,128)(2,1)} %bitcast.128), custom_call_target="tpu_custom_call" | custom-call | tf_op jit(solution)/shard_map/pallas_call | solution.py:221
  6.5 1.3 %broadcast_select_fusion = (f32[128,2,256]{0,2,1:T(8,128)S(1)}, f32[128,2,256]{0,2,1:T(8,128)S(1)}) fusion(pred[]{:T(512)S(6)} %eq.55, f32[256,1,256]{0,2,1:T(8,128)} %bitcast.150, f32[256,1,256]{0,2,1:T(8,128)} %bitcast.149), kind=kLoop, calls=%fused_computation.77 | loop fusion | flops 327680 | bytes 1048577 | tf_op jit(solution)/shard_map/jit(_where)/select_n | solution.py:331
  7.8 0.1 copy.101
  8.0 0.1 copy.102
  8.2 0.5 %collective-permute-start = (f32[144,2,256]{0,2,1:T(8,128)S(1)}, f32[144,2,256]{0,2,1:T(8,128)S(1)}, u32[]{:S(2)}, u32[]{:S(2)}) collective-permute-start(f32[144,2,256]{0,2,1:T(8,128)S(1)} %pad_maximum_fusion.2), channel_id=1, source_target_pairs={{0,1},{1,0},{2,3},{3,2},{4,5},{5,4},{6,7},{7,6},{8,9},{9,8},{10,11... | collective-permute-start | bytes 884744 | tf_op jit(solution)/shard_map/ppermute | solution.py:24
  8.7 0.5 %convolution_bitcast_fusion = f32[128]{0:T(128)S(1)} fusion(s32[128]{0:T(128)S(1)} %fusion.50, f32[128]{0:T(128)S(1)} %copy-done), kind=kOutput, calls=%fused_computation.4 | convolution fusion | flops 442368 | bytes 1536 | tf_op jit(solution)/shard_map/dot_general | solution.py:67
  9.2 0.5 %convolution_bitcast_fusion.1 = f32[128]{0:T(128)S(1)} fusion(s32[128]{0:T(128)S(1)} %fusion.50, f32[128]{0:T(128)S(1)} %copy-done), kind=kOutput, calls=%fused_computation.5 | convolution fusion | flops 425984 | bytes 1536 | tf_op jit(solution)/shard_map/dot_general | solution.py:66
  9.7 0.2 copy.103
  10.0 0.1 copy.117
  10.1 0.1 convert_element_type.37
  10.2 0.1 copy.104
  10.4 0.1 add_convert_fusion.1
  10.5 0.1 copy.105
  10.8 0.1 copy.108
  10.9 0.1 fusion.14
  11.0 0.1 copy.110
  11.2 0.1 stack.71
  11.3 0.1 stack.70
  11.5 0.2 copy.114
  11.7 0.3 reshape.266
  12.0 4.7 %collective-permute-start.3 = (bf16[8,4096]{1,0:T(8,128)(2,1)S(1)}, bf16[8,4096]{1,0:T(8,128)(2,1)S(1)}, u32[]{:S(2)}, u32[]{:S(2)}) collective-permute-start(bf16[8,4096]{1,0:T(8,128)(2,1)S(1)} %reshape.266), channel_id=1, source_target_pairs={{0,18},{2,16},{4,22},{6,20},{8,26},{10,24},{12,30},{14,28},{16,2},... | collective-permute-start | bytes 196616 | tf_op jit(solution)/shard_map/ppermute | solution.py:417
  16.7 0.5 %collective-permute-start.1 = (bf16[8,4096]{1,0:T(8,128)(2,1)S(1)}, bf16[8,4096]{1,0:T(8,128)(2,1)S(1)}, u32[]{:S(2)}, u32[]{:S(2)}) collective-permute-start(bf16[8,4096]{1,0:T(8,128)(2,1)S(1)} %reshape.266), channel_id=1, source_target_pairs={{0,2},{2,0},{1,3},{3,1},{4,6},{6,4},{5,7},{7,5},{8,10},{10,8},{9,1... | collective-permute-start | bytes 196616 | tf_op jit(solution)/shard_map/ppermute | solution.py:411
  17.2 0.2 copy.118
  17.4 0.3 reshape.270
  17.7 0.2 collective-permute-start.2
  17.9 3.4 %collective-permute-done.1 = bf16[8,4096]{1,0:T(8,128)(2,1)S(1)} collective-permute-done((bf16[8,4096]{1,0:T(8,128)(2,1)S(1)}, bf16[8,4096]{1,0:T(8,128)(2,1)S(1)}, u32[]{:S(2)}, u32[]{:S(2)}) %collective-permute-start.1) | collective-permute-done | bytes 65568 | tf_op jit(solution)/shard_map/ppermute | solution.py:411
  21.2 0.2 reshape.267
  21.4 0.1 copy.115
  21.6 0.1 copy.116
  21.8 0.1 copy.155
  21.9 0.2 reshape.272
  22.1 2.2 %collective-permute-done.2 = bf16[8,4224]{1,0:T(8,128)(2,1)S(1)} collective-permute-done((bf16[8,4224]{1,0:T(8,128)(2,1)S(1)}, bf16[8,4224]{1,0:T(8,128)(2,1)S(1)}, u32[]{:S(2)}, u32[]{:S(2)}) %collective-permute-start.2) | collective-permute-done | bytes 67616 | tf_op jit(solution)/shard_map/ppermute | solution.py:408
  24.3 0.2 reshape.271
  24.4 0.1 maximum_bitcast_fusion.2
  24.6 0.1 copy.154
  24.7 0.1 pad_maximum_fusion.8
  24.8 1.6 %collective-permute-start.6 = (bf16[2,4,8320]{2,1,0:T(4,128)(2,1)S(1)}, bf16[2,4,8320]{2,1,0:T(4,128)(2,1)S(1)}, u32[]{:S(2)}, u32[]{:S(2)}) collective-permute-start(bf16[2,4,8320]{2,1,0:T(4,128)(2,1)S(1)} %get-tuple-element.17), channel_id=1, source_target_pairs={{0,4},{4,0},{8,12},{12,8},{16,20},{20,16},{24,28},{28,24},{1,5},{5... | collective-permute-start | bytes 399368 | tf_op jit(solution)/shard_map/ppermute | solution.py:295
  26.4 0.3 collective-permute-start.4
  26.7 3.1 %collective-permute-done.6 = bf16[2,4,8320]{2,1,0:T(4,128)(2,1)S(1)} collective-permute-done((bf16[2,4,8320]{2,1,0:T(4,128)(2,1)S(1)}, bf16[2,4,8320]{2,1,0:T(4,128)(2,1)S(1)}, u32[]{:S(2)}, u32[]{:S(2)}) %collective-permute-start.6) | collective-permute-done | bytes 133152 | tf_op jit(solution)/shard_map/ppermute | solution.py:295
  29.8 0.2 fusion.58
  30.1 0.7 %collective-permute-start.7 = (bf16[2,2,4,8320]{3,2,0,1:T(4,128)(2,1)S(1)}, bf16[2,2,4,8320]{3,2,0,1:T(4,128)(2,1)S(1)}, u32[]{:S(2)}, u32[]{:S(2)}) collective-permute-start(bf16[2,2,4,8320]{3,2,0,1:T(4,128)(2,1)S(1)} %get-tuple-element.16), channel_id=1, source_target_pairs={{0,8},{4,12},{8,0},{12,4},{16,24},{20,28},{24,16},{28,20},{1,9},{5... | collective-permute-start | bytes 798728 | tf_op jit(solution)/shard_map/ppermute | solution.py:295
  30.7 1.7 %collective-permute-done.4 = bf16[2,4,8320]{2,1,0:T(4,128)(2,1)S(1)} collective-permute-done((bf16[2,4,8320]{2,1,0:T(4,128)(2,1)S(1)}, bf16[2,4,8320]{2,1,0:T(4,128)(2,1)S(1)}, u32[]{:S(2)}, u32[]{:S(2)}) %collective-permute-start.4) | collective-permute-done | bytes 133152 | tf_op jit(solution)/shard_map/ppermute | solution.py:295
  32.4 0.2 fusion.59
  32.7 4.5 %collective-permute-done.7 = bf16[2,2,4,8320]{3,2,0,1:T(4,128)(2,1)S(1)} collective-permute-done((bf16[2,2,4,8320]{3,2,0,1:T(4,128)(2,1)S(1)}, bf16[2,2,4,8320]{3,2,0,1:T(4,128)(2,1)S(1)}, u32[]{:S(2)}, u32[]{:S(2)}) %collective-permute-start.7) | collective-permute-done | bytes 266272 | tf_op jit(solution)/shard_map/ppermute | solution.py:295
  37.1 0.4 pad_maximum_fusion.1
  37.5 0.2 copy.120
  37.7 1.4 %collective-permute-done.5 = bf16[2,2,4,8320]{3,2,0,1:T(4,128)(2,1)S(1)} collective-permute-done((bf16[2,2,4,8320]{3,2,0,1:T(4,128)(2,1)S(1)}, bf16[2,2,4,8320]{3,2,0,1:T(4,128)(2,1)S(1)}, u32[]{:S(2)}, u32[]{:S(2)}) %collective-permute-start.5) | collective-permute-done | bytes 266272 | tf_op jit(solution)/shard_map/ppermute | solution.py:295
  39.1 0.4 pad_maximum_fusion
  39.5 0.2 copy.119
  39.7 0.2 copy.133
  39.9 0.1 copy.122
  40.0 0.1 multiply_reduce_fusion
  40.1 0.1 copy.138
  40.2 0.1 add_select_fusion.1
  40.3 0.1 copy.124
  40.4 0.1 eq.59
  40.5 0.1 copy.125
  40.7 0.1 eq.62
  40.8 1.0 %bitcast_convert_fusion = bf16[64,128,128]{1,2,0:T(8,128)(2,1)S(1)} fusion(s32[128]{0:T(128)S(1)} %eq.62, s32[128]{0:T(128)S(1)} %eq.59, bf16[8,4,8320]{2,1,0:T(4,128)(2,1)S(1)} %bitcast.132, bf16[8,4,8320]{2,1,0:T(4,128)(2,1)S(1)} %bitcast.130), kind=kOutput, calls=%fused_computation | convolution fusion | flops 139493376 | bytes 3163136 | tf_op jit(solution)/shard_map/rsc,scbq->brq/dot_general | solution.py:493
  41.9 0.3 copy.127
  42.3 0.1 pad_maximum_fusion.3
  42.5 0.3 copy.128
  42.7 1.2 %convolution_multiply_fusion = f32[64,32,128]{2,1,0:T(8,128)S(1)} fusion(bf16[64,128,128]{1,2,0:T(8,128)(2,1)S(1)} %bitcast_convert_fusion, bf16[64,16,128]{2,1,0:T(8,128)(2,1)S(1)} %copy.128, bf16[64,16,128]{2,1,0:T(8,128)(2,1)S(1)} %dynamic-slice_bitcast_fusion), kind=kOutput, calls=%fused_computation.1 | convolution fusion | flops 68419584 | bytes 3670016 | tf_op jit(solution)/shard_map/bpq,bjq->bpj/dot_general | solution.py:501
  43.9 1.1 %copy.153 = f32[64,2,16,128]{3,2,0,1:T(8,128)} copy(f32[64,2,16,128]{3,2,1,0:T(8,128)S(1)} %bitcast.127) | data formatting | bytes 2097152 | tf_op jit(solution)/shard_map/div | solution.py:504
  (44 shorter events, 0.9 us)
Async XLA Ops:
  0.0 8.7 %copy-start = (f32[128]{0:T(128)S(1)}, f32[128]{0:T(128)}, u32[]{:S(2)}) copy-start(f32[128]{0:T(128)} %param.5) | copy-start | bytes 1540
  6.5 3.4 %copy-start.1 = (s32[1,8,2]{1,2,0:T(2,128)S(1)}, s32[1,8,2]{1,2,0:T(2,128)}, u32[]{:S(2)}) copy-start(s32[1,8,2]{1,2,0:T(2,128)} %param.7) | copy-start | bytes 196
  6.5 3.4 %copy-start.2 = (s32[1,8,2]{1,2,0:T(2,128)S(1)}, s32[1,8,2]{1,2,0:T(2,128)}, u32[]{:S(2)}) copy-start(s32[1,8,2]{1,2,0:T(2,128)} %param.6) | copy-start | bytes 196
  8.2 2.3 %collective-permute-start = (f32[144,2,256]{0,2,1:T(8,128)S(1)}, f32[144,2,256]{0,2,1:T(8,128)S(1)}, u32[]{:S(2)}, u32[]{:S(2)}) collective-permute-start(f32[144,2,256]{0,2,1:T(8,128)S(1)} %pad_maximum_fusion.2), channel_id=1, source_target_pairs={{0,1},{1,0},{2,3},{3,2},{4,5},{5,4},{6,7},{7,6},{8,9},{9,8},{10,11... | collective-permute-start | bytes 884744 | tf_op jit(solution)/shard_map/ppermute | solution.py:24
  12.0 9.9 %collective-permute-start.3 = (bf16[8,4096]{1,0:T(8,128)(2,1)S(1)}, bf16[8,4096]{1,0:T(8,128)(2,1)S(1)}, u32[]{:S(2)}, u32[]{:S(2)}) collective-permute-start(bf16[8,4096]{1,0:T(8,128)(2,1)S(1)} %reshape.266), channel_id=1, source_target_pairs={{0,18},{2,16},{4,22},{6,20},{8,26},{10,24},{12,30},{14,28},{16,2},... | collective-permute-start | bytes 196616 | tf_op jit(solution)/shard_map/ppermute | solution.py:417
  16.7 4.5 %collective-permute-start.1 = (bf16[8,4096]{1,0:T(8,128)(2,1)S(1)}, bf16[8,4096]{1,0:T(8,128)(2,1)S(1)}, u32[]{:S(2)}, u32[]{:S(2)}) collective-permute-start(bf16[8,4096]{1,0:T(8,128)(2,1)S(1)} %reshape.266), channel_id=1, source_target_pairs={{0,2},{2,0},{1,3},{3,1},{4,6},{6,4},{5,7},{7,5},{8,10},{10,8},{9,1... | collective-permute-start | bytes 196616 | tf_op jit(solution)/shard_map/ppermute | solution.py:411
  17.7 6.5 %collective-permute-start.2 = (bf16[8,4224]{1,0:T(8,128)(2,1)S(1)}, bf16[8,4224]{1,0:T(8,128)(2,1)S(1)}, u32[]{:S(2)}, u32[]{:S(2)}) collective-permute-start(bf16[8,4224]{1,0:T(8,128)(2,1)S(1)} %pad_maximum_fusion.11), channel_id=1, source_target_pairs={{0,16},{4,20},{8,24},{12,28},{16,0},{20,4},{24,8},{28,12},{1,17},{... | collective-permute-start | bytes 202760 | tf_op jit(solution)/shard_map/ppermute | solution.py:408
  24.8 5.1 %collective-permute-start.6 = (bf16[2,4,8320]{2,1,0:T(4,128)(2,1)S(1)}, bf16[2,4,8320]{2,1,0:T(4,128)(2,1)S(1)}, u32[]{:S(2)}, u32[]{:S(2)}) collective-permute-start(bf16[2,4,8320]{2,1,0:T(4,128)(2,1)S(1)} %get-tuple-element.17), channel_id=1, source_target_pairs={{0,4},{4,0},{8,12},{12,8},{16,20},{20,16},{24,28},{28,24},{1,5},{5... | collective-permute-start | bytes 399368 | tf_op jit(solution)/shard_map/ppermute | solution.py:295
  26.4 5.9 %collective-permute-start.4 = (bf16[2,4,8320]{2,1,0:T(4,128)(2,1)S(1)}, bf16[2,4,8320]{2,1,0:T(4,128)(2,1)S(1)}, u32[]{:S(2)}, u32[]{:S(2)}) collective-permute-start(bf16[2,4,8320]{2,1,0:T(4,128)(2,1)S(1)} %get-tuple-element.18), channel_id=1, source_target_pairs={{0,8},{4,12},{8,0},{12,4},{16,24},{20,28},{24,16},{28,20},{1,9},{5... | collective-permute-start | bytes 399368 | tf_op jit(solution)/shard_map/ppermute | solution.py:295
  30.1 7.1 %collective-permute-start.7 = (bf16[2,2,4,8320]{3,2,0,1:T(4,128)(2,1)S(1)}, bf16[2,2,4,8320]{3,2,0,1:T(4,128)(2,1)S(1)}, u32[]{:S(2)}, u32[]{:S(2)}) collective-permute-start(bf16[2,2,4,8320]{3,2,0,1:T(4,128)(2,1)S(1)} %get-tuple-element.16), channel_id=1, source_target_pairs={{0,8},{4,12},{8,0},{12,4},{16,24},{20,28},{24,16},{28,20},{1,9},{5... | collective-permute-start | bytes 798728 | tf_op jit(solution)/shard_map/ppermute | solution.py:295
  32.6 6.5 %collective-permute-start.5 = (bf16[2,2,4,8320]{3,2,0,1:T(4,128)(2,1)S(1)}, bf16[2,2,4,8320]{3,2,0,1:T(4,128)(2,1)S(1)}, u32[]{:S(2)}, u32[]{:S(2)}) collective-permute-start(bf16[2,2,4,8320]{3,2,0,1:T(4,128)(2,1)S(1)} %get-tuple-element.20), channel_id=1, source_target_pairs={{0,4},{4,0},{8,12},{12,8},{16,20},{20,16},{24,28},{28,24},{1,5},{5... | collective-permute-start | bytes 798728 | tf_op jit(solution)/shard_map/ppermute | solution.py:295

commit v22 on v21

--- a/solution.py
+++ b/solution.py
@@ -324,32 +324,30 @@
     )
     real_all = real_t.T
     imag_all = imag_t.T
-    blocks = jnp.stack([real_all, imag_all], axis=1)
-    blocks = blocks.reshape(freq_count, device_bins, 2, records.shape[0])
     if freq_count == 2:
-        kept = jnp.where(freq_rank == 0, blocks[0], blocks[1])
-        sent = jnp.where(freq_rank == 0, blocks[1], blocks[0])
-        kept_blocks = kept.reshape(seg_count, block_bins, 2, -1)
-        sent_blocks = sent.reshape(seg_count, block_bins, 2, -1)
+        blocks = jnp.stack([real_all, imag_all], axis=0)
+        blocks = blocks.reshape(2, freq_count, device_bins, records.shape[0])
+        kept = jnp.where(freq_rank == 0, blocks[:, 0], blocks[:, 1])
+        sent = jnp.where(freq_rank == 0, blocks[:, 1], blocks[:, 0])
+        kept_blocks = kept.reshape(2, seg_count, block_bins, -1)
+        sent_blocks = sent.reshape(2, seg_count, block_bins, -1)
         own_edges = jnp.concatenate(
-            [kept_blocks[:, :HW], kept_blocks[:, block_bins - HW :]], axis=1
-        ).reshape(seg_count * 2 * HW, 2, -1)
-        message = jnp.concatenate([sent, own_edges], axis=0)
+            [kept_blocks[:, :, :HW], kept_blocks[:, :, block_bins - HW :]], axis=2
+        ).reshape(2, seg_count * 2 * HW, -1)
+        message = jnp.concatenate([sent, own_edges], axis=1)
         arrived = swapped(message, "freq", 0)
-        spectra = kept + arrived[:device_bins]
+        spectra_pair = kept + arrived[:, :device_bins]
         their_edges = jnp.concatenate(
-            [sent_blocks[:, :HW], sent_blocks[:, block_bins - HW :]], axis=1
-        ).reshape(seg_count * 2 * HW, 2, -1)
-        edge_spectra = (their_edges + arrived[device_bins:]).reshape(seg_count, 2, HW, 2, -1)
+            [sent_blocks[:, :, :HW], sent_blocks[:, :, block_bins - HW :]], axis=2
+        ).reshape(2, seg_count * 2 * HW, -1)
+        edge_spectra = (their_edges + arrived[:, device_bins:]).reshape(2, seg_count, 2, HW, -1)
         partner = jnp.transpose(
-            jnp.sqrt(
-                edge_spectra[..., 0, :] * edge_spectra[..., 0, :]
-                + edge_spectra[..., 1, :] * edge_spectra[..., 1, :]
-                + 1e-06
-            ),
+            jnp.sqrt(edge_spectra[0] * edge_spectra[0] + edge_spectra[1] * edge_spectra[1] + 1e-06),
             (1, 0, 2, 3),
         )
+        spectra = jnp.stack([spectra_pair[0], spectra_pair[1]], axis=1)
     else:
+        blocks = jnp.stack([real_all, imag_all], axis=1)
         spectra = lax.psum_scatter(
             blocks.reshape(device_bins * freq_count, 2, records.shape[0]),
             "freq",
@@ -358,6 +356,9 @@
         )
     real_part = spectra[:, 0]
     imag_part = spectra[:, 1]
+    if freq_count == 2:
+        real_part = spectra_pair[0]
+        imag_part = spectra_pair[1]
     amplitude = jnp.sqrt(real_part * real_part + imag_part * imag_part + 1e-06)
     amp_blocks = amplitude.reshape(seg_count, block_bins, -1)
     if freq_count != 2:

time: 45.2 us -> 45.8 us (1.013)
  local copies, waits for them, and re-layouts: 6.23 us -> 8.16 us
  other arithmetic: 3.77 us -> 2.61 us
    another operation x4 -> x2, local copies, waits for them, and re-layouts: 0.26 us -> 2.18 us  [per_device(): blocks = jnp.stack([real_all, imag_all], axis=0)]
    select_n x1, other arithmetic: 1.27 us -> 0.04 us  [per_device(): sent = jnp.where(freq_rank == 0, blocks[:, 1], blocks[:, 0])]
  transfers between devices with their start and end apart: 8 -> 8, of which waited for: 6 -> 6; matrix products, arithmetic and copies ran while one was open for 9% -> 8% of each run, Pallas kernels for 0% -> 0%
where the time goes in v22:
time: 45.8 us; the launch traced here: 45.6 us
  waiting for transfers between devices  16.2 us (35%)
  starting transfers between devices  8.33 us (18%)
  local copies, waits for them, and re-layouts  8.16 us (18%)
  Pallas kernels  6.56 us (14%)
  matrix products  3.25 us (7%)
  other arithmetic  2.61 us (6%)
  between operations  0.47 us (1%)
    ppermute x4, waiting for transfers between devices, gather_blocks(): arrived = lax.ppermute(part, 'blk', pairs)  10.5 us
    pallas_call x1, Pallas kernels, dft_fused(): pl.pallas_call(kernel, grid=(count // chunk,), in_specs=leading + [pl.Blo...  6.56 us
    ppermute x1, starting transfers between devices, per_device(): from_diagonal = lax.ppermute(other_flat, ('blk', 'seg'), diagonal)  4.6 us
    ppermute x1, waiting for transfers between devices, per_device(): from_seg = lax.ppermute(other_flat, 'seg', [(0, 1), (1, 0)])  3.33 us
    ppermute x4, starting transfers between devices, gather_blocks(): arrived = lax.ppermute(part, 'blk', pairs)  2.51 us
    ppermute x1, waiting for transfers between devices, per_device(): lax.ppermute(keep_flat, 'blk', [(source, source ^ first) for source in ra...  2.32 us
    another operation x2, local copies, waits for them, and re-layouts, per_device(): blocks = jnp.stack([real_all, imag_all], axis=0)  2.18 us
    dot_general x1, matrix products, per_device(): jnp.einsum('bpq,bjq->bpj', lhs, routed, preferred_element_type=jnp.float32)  1.19 us
  transfers between devices with their start and end apart: 8, of which 6 were waited for; matrix products, arithmetic and copies ran while one was open for 8% of the time, Pallas kernels for 0%

profile of v22, /device:TPU:0, one launch (start us, length us, event | category | flops | bytes accessed | tf_op | source)
XLA Modules:
  0.0 45.6 jit_solution(2701813280691258586)
XLA Ops:
  0.0 6.6 %shard_map.46 = (f32[256,256]{1,0:T(8,128)}, f32[256,256]{1,0:T(8,128)}) custom-call(bf16[256,8192]{1,0:T(8,128)(2,1)} %bitcast.128), custom_call_target="tpu_custom_call" | custom-call | tf_op jit(solution)/shard_map/pallas_call | solution.py:221
  6.6 1.1 %copy.129 = f32[256,256]{1,0:T(8,128)S(1)} copy(f32[256,256]{0,1:T(8,128)} %bitcast.152) | data formatting | bytes 524288 | tf_op jit(solution)/shard_map/stack | solution.py:328
  7.7 1.1 %copy.130 = f32[256,256]{1,0:T(8,128)S(1)} copy(f32[256,256]{0,1:T(8,128)} %bitcast.151) | data formatting | bytes 524288 | tf_op jit(solution)/shard_map/stack | solution.py:328
  8.9 0.5 %collective-permute-start = (f32[2,144,256]{2,1,0:T(8,128)S(1)}, f32[2,144,256]{2,1,0:T(8,128)S(1)}, u32[]{:S(2)}, u32[]{:S(2)}) collective-permute-start(f32[2,144,256]{2,1,0:T(8,128)S(1)} %pad_maximum_fusion.3), channel_id=1, source_target_pairs={{0,1},{1,0},{2,3},{3,2},{4,5},{5,4},{6,7},{7,6},{8,9},{9,8},{10,11... | collective-permute-start | bytes 884744 | tf_op jit(solution)/shard_map/ppermute | solution.py:24
  9.4 0.5 %convolution_bitcast_fusion = f32[128]{0:T(128)S(1)} fusion(s32[128]{0:T(128)S(1)} %fusion.56, f32[128]{0:T(128)S(1)} %copy-done), kind=kOutput, calls=%fused_computation.4 | convolution fusion | flops 442368 | bytes 1536 | tf_op jit(solution)/shard_map/dot_general | solution.py:67
  9.9 0.5 %convolution_bitcast_fusion.1 = f32[128]{0:T(128)S(1)} fusion(s32[128]{0:T(128)S(1)} %fusion.56, f32[128]{0:T(128)S(1)} %copy-done), kind=kOutput, calls=%fused_computation.5 | convolution fusion | flops 425984 | bytes 1536 | tf_op jit(solution)/shard_map/dot_general | solution.py:66
  10.5 0.1 mul.192
  10.6 0.1 mul.195
  10.8 0.1 copy.113
  10.9 0.1 convert_element_type.37
  11.2 0.1 copy.106
  11.3 0.1 fusion.14
  11.4 0.1 copy.103
  11.6 0.2 squeeze.37
  11.8 0.1 copy.99
  11.9 0.2 squeeze.16
  12.1 0.1 add_convert_fusion
  12.2 0.2 copy.110
  12.4 0.3 reshape.371
  12.7 4.6 %collective-permute-start.3 = (bf16[8,4096]{1,0:T(8,128)(2,1)S(1)}, bf16[8,4096]{1,0:T(8,128)(2,1)S(1)}, u32[]{:S(2)}, u32[]{:S(2)}) collective-permute-start(bf16[8,4096]{1,0:T(8,128)(2,1)S(1)} %reshape.371), channel_id=1, source_target_pairs={{0,18},{2,16},{4,22},{6,20},{8,26},{10,24},{12,30},{14,28},{16,2},... | collective-permute-start | bytes 196616 | tf_op jit(solution)/shard_map/ppermute | solution.py:418
  17.3 0.5 %collective-permute-start.1 = (bf16[8,4096]{1,0:T(8,128)(2,1)S(1)}, bf16[8,4096]{1,0:T(8,128)(2,1)S(1)}, u32[]{:S(2)}, u32[]{:S(2)}) collective-permute-start(bf16[8,4096]{1,0:T(8,128)(2,1)S(1)} %reshape.371), channel_id=1, source_target_pairs={{0,2},{2,0},{1,3},{3,1},{4,6},{6,4},{5,7},{7,5},{8,10},{10,8},{9,1... | collective-permute-start | bytes 196616 | tf_op jit(solution)/shard_map/ppermute | solution.py:412
  17.8 0.2 copy.114
  18.0 0.3 reshape.375
  18.3 0.2 collective-permute-start.2
  18.5 3.3 %collective-permute-done.1 = bf16[8,4096]{1,0:T(8,128)(2,1)S(1)} collective-permute-done((bf16[8,4096]{1,0:T(8,128)(2,1)S(1)}, bf16[8,4096]{1,0:T(8,128)(2,1)S(1)}, u32[]{:S(2)}, u32[]{:S(2)}) %collective-permute-start.1) | collective-permute-done | bytes 65568 | tf_op jit(solution)/shard_map/ppermute | solution.py:412
  21.8 0.2 reshape.372
  22.0 0.1 copy.111
  22.2 0.1 copy.112
  22.4 0.1 copy.158
  22.5 0.2 reshape.377
  22.7 2.3 %collective-permute-done.2 = bf16[8,4224]{1,0:T(8,128)(2,1)S(1)} collective-permute-done((bf16[8,4224]{1,0:T(8,128)(2,1)S(1)}, bf16[8,4224]{1,0:T(8,128)(2,1)S(1)}, u32[]{:S(2)}, u32[]{:S(2)}) %collective-permute-start.2) | collective-permute-done | bytes 67616 | tf_op jit(solution)/shard_map/ppermute | solution.py:409
  25.0 0.2 reshape.376
  25.2 0.1 maximum_bitcast_fusion.2
  25.3 0.1 copy.157
  25.4 0.1 pad_maximum_fusion.8
  25.5 1.6 %collective-permute-start.6 = (bf16[2,4,8320]{2,1,0:T(4,128)(2,1)S(1)}, bf16[2,4,8320]{2,1,0:T(4,128)(2,1)S(1)}, u32[]{:S(2)}, u32[]{:S(2)}) collective-permute-start(bf16[2,4,8320]{2,1,0:T(4,128)(2,1)S(1)} %get-tuple-element.17), channel_id=1, source_target_pairs={{0,4},{4,0},{8,12},{12,8},{16,20},{20,16},{24,28},{28,24},{1,5},{5... | collective-permute-start | bytes 399368 | tf_op jit(solution)/shard_map/ppermute | solution.py:295
  27.2 0.2 collective-permute-start.4
  27.4 3.2 %collective-permute-done.6 = bf16[2,4,8320]{2,1,0:T(4,128)(2,1)S(1)} collective-permute-done((bf16[2,4,8320]{2,1,0:T(4,128)(2,1)S(1)}, bf16[2,4,8320]{2,1,0:T(4,128)(2,1)S(1)}, u32[]{:S(2)}, u32[]{:S(2)}) %collective-permute-start.6) | collective-permute-done | bytes 133152 | tf_op jit(solution)/shard_map/ppermute | solution.py:295
  30.6 0.2 fusion.64
  30.8 0.7 %collective-permute-start.7 = (bf16[2,2,4,8320]{3,2,0,1:T(4,128)(2,1)S(1)}, bf16[2,2,4,8320]{3,2,0,1:T(4,128)(2,1)S(1)}, u32[]{:S(2)}, u32[]{:S(2)}) collective-permute-start(bf16[2,2,4,8320]{3,2,0,1:T(4,128)(2,1)S(1)} %get-tuple-element.16), channel_id=1, source_target_pairs={{0,8},{4,12},{8,0},{12,4},{16,24},{20,28},{24,16},{28,20},{1,9},{5... | collective-permute-start | bytes 798728 | tf_op jit(solution)/shard_map/ppermute | solution.py:295
  31.5 1.5 %collective-permute-done.4 = bf16[2,4,8320]{2,1,0:T(4,128)(2,1)S(1)} collective-permute-done((bf16[2,4,8320]{2,1,0:T(4,128)(2,1)S(1)}, bf16[2,4,8320]{2,1,0:T(4,128)(2,1)S(1)}, u32[]{:S(2)}, u32[]{:S(2)}) %collective-permute-start.4) | collective-permute-done | bytes 133152 | tf_op jit(solution)/shard_map/ppermute | solution.py:295
  33.0 0.2 fusion.65
  33.2 0.1 collective-permute-start.5
  33.3 4.6 %collective-permute-done.7 = bf16[2,2,4,8320]{3,2,0,1:T(4,128)(2,1)S(1)} collective-permute-done((bf16[2,2,4,8320]{3,2,0,1:T(4,128)(2,1)S(1)}, bf16[2,2,4,8320]{3,2,0,1:T(4,128)(2,1)S(1)}, u32[]{:S(2)}, u32[]{:S(2)}) %collective-permute-start.7) | collective-permute-done | bytes 266272 | tf_op jit(solution)/shard_map/ppermute | solution.py:295
  37.9 0.4 pad_maximum_fusion.1
  38.3 0.2 copy.116
  38.5 1.2 %collective-permute-done.5 = bf16[2,2,4,8320]{3,2,0,1:T(4,128)(2,1)S(1)} collective-permute-done((bf16[2,2,4,8320]{3,2,0,1:T(4,128)(2,1)S(1)}, bf16[2,2,4,8320]{3,2,0,1:T(4,128)(2,1)S(1)}, u32[]{:S(2)}, u32[]{:S(2)}) %collective-permute-start.5) | collective-permute-done | bytes 266272 | tf_op jit(solution)/shard_map/ppermute | solution.py:295
  39.7 0.4 pad_maximum_fusion
  40.0 0.2 copy.115
  40.3 0.2 copy.131
  40.5 0.1 copy.118
  40.6 0.1 multiply_reduce_fusion
  40.7 0.1 copy.135
  40.8 0.1 add_select_fusion.1
  40.9 0.1 copy.120
  41.0 0.1 eq.59
  41.1 0.1 copy.121
  41.3 0.1 eq.62
  41.4 1.0 %bitcast_convert_fusion = bf16[64,128,128]{1,2,0:T(8,128)(2,1)S(1)} fusion(s32[128]{0:T(128)S(1)} %eq.62, s32[128]{0:T(128)S(1)} %eq.59, bf16[8,4,8320]{2,1,0:T(4,128)(2,1)S(1)} %bitcast.132, bf16[8,4,8320]{2,1,0:T(4,128)(2,1)S(1)} %bitcast.130), kind=kOutput, calls=%fused_computation | convolution fusion | flops 139493376 | bytes 3163136 | tf_op jit(solution)/shard_map/rsc,scbq->brq/dot_general | solution.py:494
  42.5 0.3 copy.123
  42.9 0.1 pad_maximum_fusion.2
  43.0 0.3 copy.124
  43.3 1.2 %convolution_multiply_fusion = f32[64,32,128]{2,1,0:T(8,128)S(1)} fusion(bf16[64,128,128]{1,2,0:T(8,128)(2,1)S(1)} %bitcast_convert_fusion, bf16[64,16,128]{2,1,0:T(8,128)(2,1)S(1)} %copy.124, bf16[64,16,128]{2,1,0:T(8,128)(2,1)S(1)} %dynamic-slice_bitcast_fusion), kind=kOutput, calls=%fused_computation.1 | convolution fusion | flops 68419584 | bytes 3670016 | tf_op jit(solution)/shard_map/bpq,bjq->bpj/dot_general | solution.py:502
  44.5 1.1 %copy.156 = f32[64,2,16,128]{3,2,0,1:T(8,128)} copy(f32[64,2,16,128]{3,2,1,0:T(8,128)S(1)} %bitcast.127) | data formatting | bytes 2097152 | tf_op jit(solution)/shard_map/div | solution.py:505
  (42 shorter events, 0.8 us)
Async XLA Ops:
  0.0 9.4 %copy-start = (f32[128]{0:T(128)S(1)}, f32[128]{0:T(128)}, u32[]{:S(2)}) copy-start(f32[128]{0:T(128)} %param.5) | copy-start | bytes 1540
  6.6 4.1 %copy-start.1 = (s32[1,8,2]{1,2,0:T(2,128)S(1)}, s32[1,8,2]{1,2,0:T(2,128)}, u32[]{:S(2)}) copy-start(s32[1,8,2]{1,2,0:T(2,128)} %param.7) | copy-start | bytes 196
  6.6 4.1 %copy-start.2 = (s32[1,8,2]{1,2,0:T(2,128)S(1)}, s32[1,8,2]{1,2,0:T(2,128)}, u32[]{:S(2)}) copy-start(s32[1,8,2]{1,2,0:T(2,128)} %param.6) | copy-start | bytes 196
  8.9 2.1 %collective-permute-start = (f32[2,144,256]{2,1,0:T(8,128)S(1)}, f32[2,144,256]{2,1,0:T(8,128)S(1)}, u32[]{:S(2)}, u32[]{:S(2)}) collective-permute-start(f32[2,144,256]{2,1,0:T(8,128)S(1)} %pad_maximum_fusion.3), channel_id=1, source_target_pairs={{0,1},{1,0},{2,3},{3,2},{4,5},{5,4},{6,7},{7,6},{8,9},{9,8},{10,11... | collective-permute-start | bytes 884744 | tf_op jit(solution)/shard_map/ppermute | solution.py:24
  12.7 9.8 %collective-permute-start.3 = (bf16[8,4096]{1,0:T(8,128)(2,1)S(1)}, bf16[8,4096]{1,0:T(8,128)(2,1)S(1)}, u32[]{:S(2)}, u32[]{:S(2)}) collective-permute-start(bf16[8,4096]{1,0:T(8,128)(2,1)S(1)} %reshape.371), channel_id=1, source_target_pairs={{0,18},{2,16},{4,22},{6,20},{8,26},{10,24},{12,30},{14,28},{16,2},... | collective-permute-start | bytes 196616 | tf_op jit(solution)/shard_map/ppermute | solution.py:418
  17.3 4.5 %collective-permute-start.1 = (bf16[8,4096]{1,0:T(8,128)(2,1)S(1)}, bf16[8,4096]{1,0:T(8,128)(2,1)S(1)}, u32[]{:S(2)}, u32[]{:S(2)}) collective-permute-start(bf16[8,4096]{1,0:T(8,128)(2,1)S(1)} %reshape.371), channel_id=1, source_target_pairs={{0,2},{2,0},{1,3},{3,1},{4,6},{6,4},{5,7},{7,5},{8,10},{10,8},{9,1... | collective-permute-start | bytes 196616 | tf_op jit(solution)/shard_map/ppermute | solution.py:412
  18.3 6.7 %collective-permute-start.2 = (bf16[8,4224]{1,0:T(8,128)(2,1)S(1)}, bf16[8,4224]{1,0:T(8,128)(2,1)S(1)}, u32[]{:S(2)}, u32[]{:S(2)}) collective-permute-start(bf16[8,4224]{1,0:T(8,128)(2,1)S(1)} %pad_maximum_fusion.11), channel_id=1, source_target_pairs={{0,16},{4,20},{8,24},{12,28},{16,0},{20,4},{24,8},{28,12},{1,17},{... | collective-permute-start | bytes 202760 | tf_op jit(solution)/shard_map/ppermute | solution.py:409
  25.5 5.1 %collective-permute-start.6 = (bf16[2,4,8320]{2,1,0:T(4,128)(2,1)S(1)}, bf16[2,4,8320]{2,1,0:T(4,128)(2,1)S(1)}, u32[]{:S(2)}, u32[]{:S(2)}) collective-permute-start(bf16[2,4,8320]{2,1,0:T(4,128)(2,1)S(1)} %get-tuple-element.17), channel_id=1, source_target_pairs={{0,4},{4,0},{8,12},{12,8},{16,20},{20,16},{24,28},{28,24},{1,5},{5... | collective-permute-start | bytes 399368 | tf_op jit(solution)/shard_map/ppermute | solution.py:295
  27.2 5.8 %collective-permute-start.4 = (bf16[2,4,8320]{2,1,0:T(4,128)(2,1)S(1)}, bf16[2,4,8320]{2,1,0:T(4,128)(2,1)S(1)}, u32[]{:S(2)}, u32[]{:S(2)}) collective-permute-start(bf16[2,4,8320]{2,1,0:T(4,128)(2,1)S(1)} %get-tuple-element.18), channel_id=1, source_target_pairs={{0,8},{4,12},{8,0},{12,4},{16,24},{20,28},{24,16},{28,20},{1,9},{5... | collective-permute-start | bytes 399368 | tf_op jit(solution)/shard_map/ppermute | solution.py:295
  30.8 7.1 %collective-permute-start.7 = (bf16[2,2,4,8320]{3,2,0,1:T(4,128)(2,1)S(1)}, bf16[2,2,4,8320]{3,2,0,1:T(4,128)(2,1)S(1)}, u32[]{:S(2)}, u32[]{:S(2)}) collective-permute-start(bf16[2,2,4,8320]{3,2,0,1:T(4,128)(2,1)S(1)} %get-tuple-element.16), channel_id=1, source_target_pairs={{0,8},{4,12},{8,0},{12,4},{16,24},{20,28},{24,16},{28,20},{1,9},{5... | collective-permute-start | bytes 798728 | tf_op jit(solution)/shard_map/ppermute | solution.py:295
  33.2 6.5 %collective-permute-start.5 = (bf16[2,2,4,8320]{3,2,0,1:T(4,128)(2,1)S(1)}, bf16[2,2,4,8320]{3,2,0,1:T(4,128)(2,1)S(1)}, u32[]{:S(2)}, u32[]{:S(2)}) collective-permute-start(bf16[2,2,4,8320]{3,2,0,1:T(4,128)(2,1)S(1)} %get-tuple-element.20), channel_id=1, source_target_pairs={{0,4},{4,0},{8,12},{12,8},{16,20},{20,16},{24,28},{28,24},{1,5},{5... | collective-permute-start | bytes 798728 | tf_op jit(solution)/shard_map/ppermute | solution.py:295

commit v23 on v22

--- a/solution.py
+++ b/solution.py
@@ -120,7 +120,7 @@
             first = info_ref[1:2, :]
         else:
             device_bins, block_bins, freq_count, half_len = layout
-            row_ids = lax.broadcasted_iota(jnp.int32, (1, re_ref.shape[1]), 1)
+            row_ids = lax.broadcasted_iota(jnp.int32, (1, re_ref.shape[0]), 1)
             owner_core = row_ids // device_bins
             local_row = row_ids % device_bins
             band = (local_row // block_bins * freq_count + owner_core) * block_bins + local_row % block_bins
@@ -168,8 +168,8 @@
             sin_tile = jnp.concatenate(sin_parts, axis=0).astype(jnp.bfloat16)
             first = pl.multiple_of((index * group + 2 * pair) * lanes, 2 * lanes)
             rec = rec_ref[:, pl.ds(first, 2 * lanes)]
-            re_ref[...] += jnp.dot(rec, cos_tile, preferred_element_type=jnp.float32)
-            im_ref[...] += jnp.dot(rec, sin_tile, preferred_element_type=jnp.float32)
+            re_ref[...] += lax.dot_general(cos_tile, rec, (((0,), (1,)), ((), ())), preferred_element_type=jnp.float32)
+            im_ref[...] += lax.dot_general(sin_tile, rec, (((0,), (1,)), ((), ())), preferred_element_type=jnp.float32)
         return carry
 
     lax.fori_loop(0, groups, one_group, 0)
@@ -222,10 +222,10 @@
             kernel,
             grid=(count // chunk,),
             in_specs=leading + [pl.BlockSpec((rows, chunk), lambda step: (0, step))],
-            out_specs=[pl.BlockSpec((rows, bins), full), pl.BlockSpec((rows, bins), full)],
+            out_specs=[pl.BlockSpec((bins, rows), full), pl.BlockSpec((bins, rows), full)],
             out_shape=[
-                jax.ShapeDtypeStruct((rows, bins), jnp.float32),
-                jax.ShapeDtypeStruct((rows, bins), jnp.float32),
+                jax.ShapeDtypeStruct((bins, rows), jnp.float32),
+                jax.ShapeDtypeStruct((bins, rows), jnp.float32),
             ],
             scratch_shapes=[
                 pltpu.VMEM((64, bins), jnp.float32),
@@ -322,8 +322,8 @@
     real_t, imag_t = dft_fused(
         records, band_rows, freq_rank * half_len, (device_bins, block_bins, freq_count, half_len)
     )
-    real_all = real_t.T
-    imag_all = imag_t.T
+    real_all = real_t
+    imag_all = imag_t
     if freq_count == 2:
         blocks = jnp.stack([real_all, imag_all], axis=0)
         blocks = blocks.reshape(2, freq_count, device_bins, records.shape[0])

time: 45.8 us -> 44.9 us (0.980)
  local copies, waits for them, and re-layouts: 8.16 us -> 5.98 us
  other arithmetic: 2.61 us -> 3.84 us
    another operation x2 -> x0, local copies, waits for them, and re-layouts: 2.18 us -> none  [per_device(): blocks = jnp.stack([real_all, imag_all], axis=0)]
    select_n x1, other arithmetic: 0.04 us -> 1.27 us  [per_device(): sent = jnp.where(freq_rank == 0, blocks[:, 1], blocks[:, 0])]
  transfers between devices with their start and end apart: 8 -> 8, of which waited for: 6 -> 6; matrix products, arithmetic and copies ran while one was open for 8% -> 9% of each run, Pallas kernels for 0% -> 0%
where the time goes in v23:
time: 44.9 us; the launch traced here: 44.7 us
  waiting for transfers between devices  16.1 us (36%)
  starting transfers between devices  8.35 us (19%)
  Pallas kernels  6.68 us (15%)
  local copies, waits for them, and re-layouts  5.98 us (13%)
  other arithmetic  3.84 us (9%)
  matrix products  3.25 us (7%)
    ppermute x4, waiting for transfers between devices, gather_blocks(): arrived = lax.ppermute(part, 'blk', pairs)  10.5 us
    pallas_call x1, Pallas kernels, dft_fused(): pl.pallas_call(kernel, grid=(count // chunk,), in_specs=leading + [pl.Blo...  6.68 us
    ppermute x1, starting transfers between devices, per_device(): from_diagonal = lax.ppermute(other_flat, ('blk', 'seg'), diagonal)  4.61 us
    ppermute x1, waiting for transfers between devices, per_device(): from_seg = lax.ppermute(other_flat, 'seg', [(0, 1), (1, 0)])  3.35 us
    ppermute x4, starting transfers between devices, gather_blocks(): arrived = lax.ppermute(part, 'blk', pairs)  2.52 us
    ppermute x1, waiting for transfers between devices, per_device(): lax.ppermute(keep_flat, 'blk', [(source, source ^ first) for source in ra...  2.31 us
    select_n x1, other arithmetic, per_device(): sent = jnp.where(freq_rank == 0, blocks[:, 1], blocks[:, 0])  1.27 us
    dot_general x1, matrix products, per_device(): jnp.einsum('bpq,bjq->bpj', lhs, routed, preferred_element_type=jnp.float32)  1.19 us
  transfers between devices with their start and end apart: 8, of which 6 were waited for; matrix products, arithmetic and copies ran while one was open for 9% of the time, Pallas kernels for 0%

profile of v23, /device:TPU:0, one launch (start us, length us, event | category | flops | bytes accessed | tf_op | source)
XLA Modules:
  0.0 44.7 jit_solution(1595889894118784971)
XLA Ops:
  0.0 6.7 %shard_map.46 = (f32[256,256]{1,0:T(8,128)}, f32[256,256]{1,0:T(8,128)}) custom-call(bf16[256,8192]{1,0:T(8,128)(2,1)} %bitcast.130), custom_call_target="tpu_custom_call" | custom-call | tf_op jit(solution)/shard_map/pallas_call | solution.py:221
  6.7 1.3 %broadcast_select_fusion = (f32[2,1,128,256]{3,2,0,1:T(8,128)S(1)}, f32[2,1,128,256]{3,2,0,1:T(8,128)S(1)}) fusion(pred[]{:T(512)S(6)} %eq.55, f32[1,2,128,256]{3,2,0,1:T(8,128)} %bitcast.152, f32[1,2,128,256]{3,2,0,1:T(8,128)} %bitcast.151), kind=kLoop, calls=%fused_computation.83 | loop fusion | flops 327680 | bytes 1048577 | tf_op jit(solution)/shard_map/jit(_where)/select_n | solution.py:331
  8.0 0.5 %collective-permute-start = (f32[2,144,256]{2,1,0:T(8,128)S(1)}, f32[2,144,256]{2,1,0:T(8,128)S(1)}, u32[]{:S(2)}, u32[]{:S(2)}) collective-permute-start(f32[2,144,256]{2,1,0:T(8,128)S(1)} %pad_maximum_fusion.3), channel_id=1, source_target_pairs={{0,1},{1,0},{2,3},{3,2},{4,5},{5,4},{6,7},{7,6},{8,9},{9,8},{10,11... | collective-permute-start | bytes 884744 | tf_op jit(solution)/shard_map/ppermute | solution.py:24
  8.6 0.5 %convolution_bitcast_fusion = f32[128]{0:T(128)S(1)} fusion(s32[128]{0:T(128)S(1)} %fusion.56, f32[128]{0:T(128)S(1)} %copy-done), kind=kOutput, calls=%fused_computation.4 | convolution fusion | flops 442368 | bytes 1536 | tf_op jit(solution)/shard_map/dot_general | solution.py:67
  9.1 0.5 %convolution_bitcast_fusion.1 = f32[128]{0:T(128)S(1)} fusion(s32[128]{0:T(128)S(1)} %fusion.56, f32[128]{0:T(128)S(1)} %copy-done), kind=kOutput, calls=%fused_computation.5 | convolution fusion | flops 425984 | bytes 1536 | tf_op jit(solution)/shard_map/dot_general | solution.py:66
  9.6 0.1 add_convert_fusion.1
  9.7 0.1 mul.192
  9.8 0.1 mul.195
  9.9 0.1 copy.107
  10.0 0.1 convert_element_type.37
  10.3 0.1 copy.100
  10.4 0.1 fusion.14
  10.6 0.1 copy.97
  10.7 0.2 squeeze.37
  10.9 0.1 copy.93
  11.0 0.2 squeeze.16
  11.2 0.1 add_convert_fusion
  11.4 0.2 copy.104
  11.6 0.3 reshape.371
  11.8 4.6 %collective-permute-start.3 = (bf16[8,4096]{1,0:T(8,128)(2,1)S(1)}, bf16[8,4096]{1,0:T(8,128)(2,1)S(1)}, u32[]{:S(2)}, u32[]{:S(2)}) collective-permute-start(bf16[8,4096]{1,0:T(8,128)(2,1)S(1)} %reshape.371), channel_id=1, source_target_pairs={{0,18},{2,16},{4,22},{6,20},{8,26},{10,24},{12,30},{14,28},{16,2},... | collective-permute-start | bytes 196616 | tf_op jit(solution)/shard_map/ppermute | solution.py:418
  16.5 0.5 %collective-permute-start.1 = (bf16[8,4096]{1,0:T(8,128)(2,1)S(1)}, bf16[8,4096]{1,0:T(8,128)(2,1)S(1)}, u32[]{:S(2)}, u32[]{:S(2)}) collective-permute-start(bf16[8,4096]{1,0:T(8,128)(2,1)S(1)} %reshape.371), channel_id=1, source_target_pairs={{0,2},{2,0},{1,3},{3,1},{4,6},{6,4},{5,7},{7,5},{8,10},{10,8},{9,1... | collective-permute-start | bytes 196616 | tf_op jit(solution)/shard_map/ppermute | solution.py:412
  17.0 0.2 copy.108
  17.2 0.3 reshape.375
  17.5 0.2 collective-permute-start.2
  17.7 3.3 %collective-permute-done.1 = bf16[8,4096]{1,0:T(8,128)(2,1)S(1)} collective-permute-done((bf16[8,4096]{1,0:T(8,128)(2,1)S(1)}, bf16[8,4096]{1,0:T(8,128)(2,1)S(1)}, u32[]{:S(2)}, u32[]{:S(2)}) %collective-permute-start.1) | collective-permute-done | bytes 65568 | tf_op jit(solution)/shard_map/ppermute | solution.py:412
  21.0 0.2 reshape.372
  21.2 0.1 copy.105
  21.4 0.1 copy.106
  21.5 0.1 copy.150
  21.7 0.2 reshape.377
  21.8 2.3 %collective-permute-done.2 = bf16[8,4224]{1,0:T(8,128)(2,1)S(1)} collective-permute-done((bf16[8,4224]{1,0:T(8,128)(2,1)S(1)}, bf16[8,4224]{1,0:T(8,128)(2,1)S(1)}, u32[]{:S(2)}, u32[]{:S(2)}) %collective-permute-start.2) | collective-permute-done | bytes 67616 | tf_op jit(solution)/shard_map/ppermute | solution.py:409
  24.2 0.2 reshape.376
  24.3 0.1 maximum_bitcast_fusion.2
  24.5 0.1 copy.149
  24.6 0.1 pad_maximum_fusion.8
  24.7 1.6 %collective-permute-start.6 = (bf16[2,4,8320]{2,1,0:T(4,128)(2,1)S(1)}, bf16[2,4,8320]{2,1,0:T(4,128)(2,1)S(1)}, u32[]{:S(2)}, u32[]{:S(2)}) collective-permute-start(bf16[2,4,8320]{2,1,0:T(4,128)(2,1)S(1)} %get-tuple-element.17), channel_id=1, source_target_pairs={{0,4},{4,0},{8,12},{12,8},{16,20},{20,16},{24,28},{28,24},{1,5},{5... | collective-permute-start | bytes 399368 | tf_op jit(solution)/shard_map/ppermute | solution.py:295
  26.3 0.2 collective-permute-start.4
  26.5 3.2 %collective-permute-done.6 = bf16[2,4,8320]{2,1,0:T(4,128)(2,1)S(1)} collective-permute-done((bf16[2,4,8320]{2,1,0:T(4,128)(2,1)S(1)}, bf16[2,4,8320]{2,1,0:T(4,128)(2,1)S(1)}, u32[]{:S(2)}, u32[]{:S(2)}) %collective-permute-start.6) | collective-permute-done | bytes 133152 | tf_op jit(solution)/shard_map/ppermute | solution.py:295
  29.7 0.2 fusion.64
  30.0 0.7 %collective-permute-start.7 = (bf16[2,2,4,8320]{3,2,0,1:T(4,128)(2,1)S(1)}, bf16[2,2,4,8320]{3,2,0,1:T(4,128)(2,1)S(1)}, u32[]{:S(2)}, u32[]{:S(2)}) collective-permute-start(bf16[2,2,4,8320]{3,2,0,1:T(4,128)(2,1)S(1)} %get-tuple-element.16), channel_id=1, source_target_pairs={{0,8},{4,12},{8,0},{12,4},{16,24},{20,28},{24,16},{28,20},{1,9},{5... | collective-permute-start | bytes 798728 | tf_op jit(solution)/shard_map/ppermute | solution.py:295
  30.6 1.5 %collective-permute-done.4 = bf16[2,4,8320]{2,1,0:T(4,128)(2,1)S(1)} collective-permute-done((bf16[2,4,8320]{2,1,0:T(4,128)(2,1)S(1)}, bf16[2,4,8320]{2,1,0:T(4,128)(2,1)S(1)}, u32[]{:S(2)}, u32[]{:S(2)}) %collective-permute-start.4) | collective-permute-done | bytes 133152 | tf_op jit(solution)/shard_map/ppermute | solution.py:295
  32.1 0.2 fusion.65
  32.3 0.1 collective-permute-start.5
  32.4 4.6 %collective-permute-done.7 = bf16[2,2,4,8320]{3,2,0,1:T(4,128)(2,1)S(1)} collective-permute-done((bf16[2,2,4,8320]{3,2,0,1:T(4,128)(2,1)S(1)}, bf16[2,2,4,8320]{3,2,0,1:T(4,128)(2,1)S(1)}, u32[]{:S(2)}, u32[]{:S(2)}) %collective-permute-start.7) | collective-permute-done | bytes 266272 | tf_op jit(solution)/shard_map/ppermute | solution.py:295
  37.0 0.4 pad_maximum_fusion.1
  37.4 0.2 copy.110
  37.6 1.2 %collective-permute-done.5 = bf16[2,2,4,8320]{3,2,0,1:T(4,128)(2,1)S(1)} collective-permute-done((bf16[2,2,4,8320]{3,2,0,1:T(4,128)(2,1)S(1)}, bf16[2,2,4,8320]{3,2,0,1:T(4,128)(2,1)S(1)}, u32[]{:S(2)}, u32[]{:S(2)}) %collective-permute-start.5) | collective-permute-done | bytes 266272 | tf_op jit(solution)/shard_map/ppermute | solution.py:295
  38.8 0.4 pad_maximum_fusion
  39.2 0.2 copy.109
  39.4 0.2 copy.123
  39.6 0.1 copy.112
  39.7 0.1 multiply_reduce_fusion
  39.8 0.1 copy.127
  39.9 0.1 add_select_fusion.1
  40.0 0.1 copy.114
  40.1 0.1 eq.59
  40.3 0.1 copy.115
  40.4 0.1 eq.62
  40.5 1.0 %bitcast_convert_fusion = bf16[64,128,128]{1,2,0:T(8,128)(2,1)S(1)} fusion(s32[128]{0:T(128)S(1)} %eq.62, s32[128]{0:T(128)S(1)} %eq.59, bf16[8,4,8320]{2,1,0:T(4,128)(2,1)S(1)} %bitcast.134, bf16[8,4,8320]{2,1,0:T(4,128)(2,1)S(1)} %bitcast.132), kind=kOutput, calls=%fused_computation | convolution fusion | flops 139493376 | bytes 3163136 | tf_op jit(solution)/shard_map/rsc,scbq->brq/dot_general | solution.py:494
  41.6 0.3 copy.117
  42.0 0.1 pad_maximum_fusion.2
  42.2 0.3 copy.118
  42.5 1.2 %convolution_multiply_fusion = f32[64,32,128]{2,1,0:T(8,128)S(1)} fusion(bf16[64,128,128]{1,2,0:T(8,128)(2,1)S(1)} %bitcast_convert_fusion, bf16[64,16,128]{2,1,0:T(8,128)(2,1)S(1)} %copy.118, bf16[64,16,128]{2,1,0:T(8,128)(2,1)S(1)} %dynamic-slice_bitcast_fusion), kind=kOutput, calls=%fused_computation.1 | convolution fusion | flops 68419584 | bytes 3670016 | tf_op jit(solution)/shard_map/bpq,bjq->bpj/dot_general | solution.py:502
  43.6 1.1 %copy.148 = f32[64,2,16,128]{3,2,0,1:T(8,128)} copy(f32[64,2,16,128]{3,2,1,0:T(8,128)S(1)} %bitcast.129) | data formatting | bytes 2097152 | tf_op jit(solution)/shard_map/div | solution.py:505
  (40 shorter events, 0.7 us)
Async XLA Ops:
  0.0 8.6 %copy-start = (f32[128]{0:T(128)S(1)}, f32[128]{0:T(128)}, u32[]{:S(2)}) copy-start(f32[128]{0:T(128)} %param.5) | copy-start | bytes 1540
  6.7 3.2 %copy-start.1 = (s32[1,8,2]{1,2,0:T(2,128)S(1)}, s32[1,8,2]{1,2,0:T(2,128)}, u32[]{:S(2)}) copy-start(s32[1,8,2]{1,2,0:T(2,128)} %param.7) | copy-start | bytes 196
  6.7 3.2 %copy-start.2 = (s32[1,8,2]{1,2,0:T(2,128)S(1)}, s32[1,8,2]{1,2,0:T(2,128)}, u32[]{:S(2)}) copy-start(s32[1,8,2]{1,2,0:T(2,128)} %param.6) | copy-start | bytes 196
  8.0 2.1 %collective-permute-start = (f32[2,144,256]{2,1,0:T(8,128)S(1)}, f32[2,144,256]{2,1,0:T(8,128)S(1)}, u32[]{:S(2)}, u32[]{:S(2)}) collective-permute-start(f32[2,144,256]{2,1,0:T(8,128)S(1)} %pad_maximum_fusion.3), channel_id=1, source_target_pairs={{0,1},{1,0},{2,3},{3,2},{4,5},{5,4},{6,7},{7,6},{8,9},{9,8},{10,11... | collective-permute-start | bytes 884744 | tf_op jit(solution)/shard_map/ppermute | solution.py:24
  11.8 9.8 %collective-permute-start.3 = (bf16[8,4096]{1,0:T(8,128)(2,1)S(1)}, bf16[8,4096]{1,0:T(8,128)(2,1)S(1)}, u32[]{:S(2)}, u32[]{:S(2)}) collective-permute-start(bf16[8,4096]{1,0:T(8,128)(2,1)S(1)} %reshape.371), channel_id=1, source_target_pairs={{0,18},{2,16},{4,22},{6,20},{8,26},{10,24},{12,30},{14,28},{16,2},... | collective-permute-start | bytes 196616 | tf_op jit(solution)/shard_map/ppermute | solution.py:418
  16.5 4.5 %collective-permute-start.1 = (bf16[8,4096]{1,0:T(8,128)(2,1)S(1)}, bf16[8,4096]{1,0:T(8,128)(2,1)S(1)}, u32[]{:S(2)}, u32[]{:S(2)}) collective-permute-start(bf16[8,4096]{1,0:T(8,128)(2,1)S(1)} %reshape.371), channel_id=1, source_target_pairs={{0,2},{2,0},{1,3},{3,1},{4,6},{6,4},{5,7},{7,5},{8,10},{10,8},{9,1... | collective-permute-start | bytes 196616 | tf_op jit(solution)/shard_map/ppermute | solution.py:412
  17.5 6.7 %collective-permute-start.2 = (bf16[8,4224]{1,0:T(8,128)(2,1)S(1)}, bf16[8,4224]{1,0:T(8,128)(2,1)S(1)}, u32[]{:S(2)}, u32[]{:S(2)}) collective-permute-start(bf16[8,4224]{1,0:T(8,128)(2,1)S(1)} %pad_maximum_fusion.11), channel_id=1, source_target_pairs={{0,16},{4,20},{8,24},{12,28},{16,0},{20,4},{24,8},{28,12},{1,17},{... | collective-permute-start | bytes 202760 | tf_op jit(solution)/shard_map/ppermute | solution.py:409
  24.7 5.1 %collective-permute-start.6 = (bf16[2,4,8320]{2,1,0:T(4,128)(2,1)S(1)}, bf16[2,4,8320]{2,1,0:T(4,128)(2,1)S(1)}, u32[]{:S(2)}, u32[]{:S(2)}) collective-permute-start(bf16[2,4,8320]{2,1,0:T(4,128)(2,1)S(1)} %get-tuple-element.17), channel_id=1, source_target_pairs={{0,4},{4,0},{8,12},{12,8},{16,20},{20,16},{24,28},{28,24},{1,5},{5... | collective-permute-start | bytes 399368 | tf_op jit(solution)/shard_map/ppermute | solution.py:295
  26.3 5.8 %collective-permute-start.4 = (bf16[2,4,8320]{2,1,0:T(4,128)(2,1)S(1)}, bf16[2,4,8320]{2,1,0:T(4,128)(2,1)S(1)}, u32[]{:S(2)}, u32[]{:S(2)}) collective-permute-start(bf16[2,4,8320]{2,1,0:T(4,128)(2,1)S(1)} %get-tuple-element.18), channel_id=1, source_target_pairs={{0,8},{4,12},{8,0},{12,4},{16,24},{20,28},{24,16},{28,20},{1,9},{5... | collective-permute-start | bytes 399368 | tf_op jit(solution)/shard_map/ppermute | solution.py:295
  30.0 7.1 %collective-permute-start.7 = (bf16[2,2,4,8320]{3,2,0,1:T(4,128)(2,1)S(1)}, bf16[2,2,4,8320]{3,2,0,1:T(4,128)(2,1)S(1)}, u32[]{:S(2)}, u32[]{:S(2)}) collective-permute-start(bf16[2,2,4,8320]{3,2,0,1:T(4,128)(2,1)S(1)} %get-tuple-element.16), channel_id=1, source_target_pairs={{0,8},{4,12},{8,0},{12,4},{16,24},{20,28},{24,16},{28,20},{1,9},{5... | collective-permute-start | bytes 798728 | tf_op jit(solution)/shard_map/ppermute | solution.py:295
  32.3 6.5 %collective-permute-start.5 = (bf16[2,2,4,8320]{3,2,0,1:T(4,128)(2,1)S(1)}, bf16[2,2,4,8320]{3,2,0,1:T(4,128)(2,1)S(1)}, u32[]{:S(2)}, u32[]{:S(2)}) collective-permute-start(bf16[2,2,4,8320]{3,2,0,1:T(4,128)(2,1)S(1)} %get-tuple-element.20), channel_id=1, source_target_pairs={{0,4},{4,0},{8,12},{12,8},{16,20},{20,16},{24,28},{28,24},{1,5},{5... | collective-permute-start | bytes 798728 | tf_op jit(solution)/shard_map/ppermute | solution.py:295

commit v24 on v23

--- a/solution.py
+++ b/solution.py
@@ -122,6 +122,8 @@
             device_bins, block_bins, freq_count, half_len = layout
             row_ids = lax.broadcasted_iota(jnp.int32, (1, re_ref.shape[0]), 1)
             owner_core = row_ids // device_bins
+            if freq_count == 2:
+                owner_core = (owner_core + lax.axis_index("freq")) % freq_count
             local_row = row_ids % device_bins
             band = (local_row // block_bins * freq_count + owner_core) * block_bins + local_row % block_bins
             wavenumber = BAND_LO + band
@@ -250,7 +252,7 @@
     rows = records.shape[0]
     bins = band_index.shape[0]
     full = lambda step: (0, 0)
-    return pl.pallas_call(
+    outputs = pl.pallas_call(
         dft_kernel,
         grid=(count // chunk,),
         in_specs=[
@@ -267,6 +269,7 @@
         ],
         compiler_params=pltpu.CompilerParams(dimension_semantics=("arbitrary",)),
     )(records, cos_a, nsin_a, cos_b, sin_b)
+    return [part.T for part in outputs]
 
 
 def gather_blocks(carried, count, rank, held=None):
@@ -327,8 +330,8 @@
     if freq_count == 2:
         blocks = jnp.stack([real_all, imag_all], axis=0)
         blocks = blocks.reshape(2, freq_count, device_bins, records.shape[0])
-        kept = jnp.where(freq_rank == 0, blocks[:, 0], blocks[:, 1])
-        sent = jnp.where(freq_rank == 0, blocks[:, 1], blocks[:, 0])
+        kept = blocks[:, 0]
+        sent = blocks[:, 1]
         kept_blocks = kept.reshape(2, seg_count, block_bins, -1)
         sent_blocks = sent.reshape(2, seg_count, block_bins, -1)
         own_edges = jnp.concatenate(

time: 44.9 us -> 44.8 us (level)
    select_n x1 -> x0, other arithmetic: 1.27 us -> none  [per_device(): sent = jnp.where(freq_rank == 0, blocks[:, 1], blocks[:, 0])]
    another operation x1 -> x2, other arithmetic: 0.11 us -> 1.26 us  [the longest x1 1.15 us: per_device(): blocks = jnp.stack([real_all, imag_all], axis=0)]
where the time goes in v24:
time: 44.8 us; the launch traced here: 44.6 us
  waiting for transfers between devices  16.2 us (36%)
  starting transfers between devices  8.36 us (19%)
  Pallas kernels  6.68 us (15%)
  local copies, waits for them, and re-layouts  5.98 us (13%)
  other arithmetic  3.72 us (8%)
  matrix products  3.25 us (7%)
    ppermute x4, waiting for transfers between devices, gather_blocks(): arrived = lax.ppermute(part, 'blk', pairs)  10.5 us
    pallas_call x1, Pallas kernels, dft_fused(): pl.pallas_call(kernel, grid=(count // chunk,), in_specs=leading + [pl.Blo...  6.68 us
    ppermute x1, starting transfers between devices, per_device(): from_diagonal = lax.ppermute(other_flat, ('blk', 'seg'), diagonal)  4.61 us
    ppermute x1, waiting for transfers between devices, per_device(): from_seg = lax.ppermute(other_flat, 'seg', [(0, 1), (1, 0)])  3.33 us
    ppermute x4, starting transfers between devices, gather_blocks(): arrived = lax.ppermute(part, 'blk', pairs)  2.52 us
    ppermute x1, waiting for transfers between devices, per_device(): lax.ppermute(keep_flat, 'blk', [(source, source ^ first) for source in ra...  2.31 us
    dot_general x1, matrix products, per_device(): jnp.einsum('bpq,bjq->bpj', lhs, routed, preferred_element_type=jnp.float32)  1.19 us
    another operation x4, other arithmetic, gather_blocks(): part = jnp.stack([part, arrived], axis=axis)  1.18 us
  transfers between devices with their start and end apart: 8, of which 6 were waited for; matrix products, arithmetic and copies ran while one was open for 9% of the time, Pallas kernels for 0%

profile of v24, /device:TPU:0, one launch (start us, length us, event | category | flops | bytes accessed | tf_op | source)
XLA Modules:
  0.0 44.6 jit_solution(6477738182353562168)
XLA Ops:
  0.0 6.7 %shard_map.46 = (f32[256,256]{1,0:T(8,128)}, f32[256,256]{1,0:T(8,128)}) custom-call(bf16[256,8192]{1,0:T(8,128)(2,1)} %bitcast.130), custom_call_target="tpu_custom_call" | custom-call | tf_op jit(solution)/shard_map/pallas_call | solution.py:223
  6.7 1.2 %pad_maximum_fusion.6 = (f32[2,1,128,256]{3,2,0,1:T(8,128)S(1)}, f32[2,1,128,256]{3,2,0,1:T(8,128)S(1)}) fusion(f32[1,2,128,256]{3,2,0,1:T(8,128)} %bitcast.152, f32[1,2,128,256]{3,2,0,1:T(8,128)} %bitcast.151), kind=kLoop, calls=%fused_computation.39 | loop fusion | flops 131072 | bytes 1048576 | tf_op jit(solution)/shard_map/stack | solution.py:331
  7.9 0.5 %collective-permute-start = (f32[2,144,256]{2,1,0:T(8,128)S(1)}, f32[2,144,256]{2,1,0:T(8,128)S(1)}, u32[]{:S(2)}, u32[]{:S(2)}) collective-permute-start(f32[2,144,256]{2,1,0:T(8,128)S(1)} %pad_maximum_fusion.3), channel_id=1, source_target_pairs={{0,1},{1,0},{2,3},{3,2},{4,5},{5,4},{6,7},{7,6},{8,9},{9,8},{10,11... | collective-permute-start | bytes 884744 | tf_op jit(solution)/shard_map/ppermute | solution.py:24
  8.5 0.5 %convolution_bitcast_fusion = f32[128]{0:T(128)S(1)} fusion(s32[128]{0:T(128)S(1)} %fusion.56, f32[128]{0:T(128)S(1)} %copy-done), kind=kOutput, calls=%fused_computation.4 | convolution fusion | flops 442368 | bytes 1536 | tf_op jit(solution)/shard_map/dot_general | solution.py:67
  9.0 0.5 %convolution_bitcast_fusion.1 = f32[128]{0:T(128)S(1)} fusion(s32[128]{0:T(128)S(1)} %fusion.56, f32[128]{0:T(128)S(1)} %copy-done), kind=kOutput, calls=%fused_computation.5 | convolution fusion | flops 425984 | bytes 1536 | tf_op jit(solution)/shard_map/dot_general | solution.py:66
  9.5 0.1 add_convert_fusion.1
  9.6 0.1 mul.192
  9.6 0.1 mul.195
  9.8 0.1 copy.104
  9.9 0.1 convert_element_type.37
  10.2 0.1 copy.97
  10.3 0.1 fusion.14
  10.5 0.1 copy.94
  10.6 0.2 squeeze.41
  10.8 0.1 copy.90
  10.9 0.2 squeeze.38
  11.1 0.1 add_convert_fusion
  11.3 0.2 copy.101
  11.5 0.3 reshape.357
  11.7 4.6 %collective-permute-start.3 = (bf16[8,4096]{1,0:T(8,128)(2,1)S(1)}, bf16[8,4096]{1,0:T(8,128)(2,1)S(1)}, u32[]{:S(2)}, u32[]{:S(2)}) collective-permute-start(bf16[8,4096]{1,0:T(8,128)(2,1)S(1)} %reshape.357), channel_id=1, source_target_pairs={{0,18},{2,16},{4,22},{6,20},{8,26},{10,24},{12,30},{14,28},{16,2},... | collective-permute-start | bytes 196616 | tf_op jit(solution)/shard_map/ppermute | solution.py:421
  16.4 0.5 %collective-permute-start.1 = (bf16[8,4096]{1,0:T(8,128)(2,1)S(1)}, bf16[8,4096]{1,0:T(8,128)(2,1)S(1)}, u32[]{:S(2)}, u32[]{:S(2)}) collective-permute-start(bf16[8,4096]{1,0:T(8,128)(2,1)S(1)} %reshape.357), channel_id=1, source_target_pairs={{0,2},{2,0},{1,3},{3,1},{4,6},{6,4},{5,7},{7,5},{8,10},{10,8},{9,1... | collective-permute-start | bytes 196616 | tf_op jit(solution)/shard_map/ppermute | solution.py:415
  16.9 0.2 copy.105
  17.1 0.3 reshape.361
  17.4 0.2 collective-permute-start.2
  17.6 3.3 %collective-permute-done.1 = bf16[8,4096]{1,0:T(8,128)(2,1)S(1)} collective-permute-done((bf16[8,4096]{1,0:T(8,128)(2,1)S(1)}, bf16[8,4096]{1,0:T(8,128)(2,1)S(1)}, u32[]{:S(2)}, u32[]{:S(2)}) %collective-permute-start.1) | collective-permute-done | bytes 65568 | tf_op jit(solution)/shard_map/ppermute | solution.py:415
  20.9 0.2 reshape.358
  21.1 0.1 copy.102
  21.3 0.1 copy.103
  21.4 0.1 copy.147
  21.5 0.2 reshape.363
  21.7 2.3 %collective-permute-done.2 = bf16[8,4224]{1,0:T(8,128)(2,1)S(1)} collective-permute-done((bf16[8,4224]{1,0:T(8,128)(2,1)S(1)}, bf16[8,4224]{1,0:T(8,128)(2,1)S(1)}, u32[]{:S(2)}, u32[]{:S(2)}) %collective-permute-start.2) | collective-permute-done | bytes 67616 | tf_op jit(solution)/shard_map/ppermute | solution.py:412
  24.0 0.2 reshape.362
  24.2 0.1 maximum_bitcast_fusion.2
  24.3 0.1 copy.146
  24.5 0.1 pad_maximum_fusion.8
  24.6 1.6 %collective-permute-start.6 = (bf16[2,4,8320]{2,1,0:T(4,128)(2,1)S(1)}, bf16[2,4,8320]{2,1,0:T(4,128)(2,1)S(1)}, u32[]{:S(2)}, u32[]{:S(2)}) collective-permute-start(bf16[2,4,8320]{2,1,0:T(4,128)(2,1)S(1)} %get-tuple-element.17), channel_id=1, source_target_pairs={{0,4},{4,0},{8,12},{12,8},{16,20},{20,16},{24,28},{28,24},{1,5},{5... | collective-permute-start | bytes 399368 | tf_op jit(solution)/shard_map/ppermute | solution.py:298
  26.2 0.2 collective-permute-start.4
  26.4 3.2 %collective-permute-done.6 = bf16[2,4,8320]{2,1,0:T(4,128)(2,1)S(1)} collective-permute-done((bf16[2,4,8320]{2,1,0:T(4,128)(2,1)S(1)}, bf16[2,4,8320]{2,1,0:T(4,128)(2,1)S(1)}, u32[]{:S(2)}, u32[]{:S(2)}) %collective-permute-start.6) | collective-permute-done | bytes 133152 | tf_op jit(solution)/shard_map/ppermute | solution.py:298
  29.6 0.2 fusion.64
  29.8 0.7 %collective-permute-start.7 = (bf16[2,2,4,8320]{3,2,0,1:T(4,128)(2,1)S(1)}, bf16[2,2,4,8320]{3,2,0,1:T(4,128)(2,1)S(1)}, u32[]{:S(2)}, u32[]{:S(2)}) collective-permute-start(bf16[2,2,4,8320]{3,2,0,1:T(4,128)(2,1)S(1)} %get-tuple-element.16), channel_id=1, source_target_pairs={{0,8},{4,12},{8,0},{12,4},{16,24},{20,28},{24,16},{28,20},{1,9},{5... | collective-permute-start | bytes 798728 | tf_op jit(solution)/shard_map/ppermute | solution.py:298
  30.5 1.5 %collective-permute-done.4 = bf16[2,4,8320]{2,1,0:T(4,128)(2,1)S(1)} collective-permute-done((bf16[2,4,8320]{2,1,0:T(4,128)(2,1)S(1)}, bf16[2,4,8320]{2,1,0:T(4,128)(2,1)S(1)}, u32[]{:S(2)}, u32[]{:S(2)}) %collective-permute-start.4) | collective-permute-done | bytes 133152 | tf_op jit(solution)/shard_map/ppermute | solution.py:298
  32.0 0.2 fusion.65
  32.2 0.1 collective-permute-start.5
  32.3 4.6 %collective-permute-done.7 = bf16[2,2,4,8320]{3,2,0,1:T(4,128)(2,1)S(1)} collective-permute-done((bf16[2,2,4,8320]{3,2,0,1:T(4,128)(2,1)S(1)}, bf16[2,2,4,8320]{3,2,0,1:T(4,128)(2,1)S(1)}, u32[]{:S(2)}, u32[]{:S(2)}) %collective-permute-start.7) | collective-permute-done | bytes 266272 | tf_op jit(solution)/shard_map/ppermute | solution.py:298
  36.9 0.4 pad_maximum_fusion.1
  37.3 0.2 copy.107
  37.5 1.2 %collective-permute-done.5 = bf16[2,2,4,8320]{3,2,0,1:T(4,128)(2,1)S(1)} collective-permute-done((bf16[2,2,4,8320]{3,2,0,1:T(4,128)(2,1)S(1)}, bf16[2,2,4,8320]{3,2,0,1:T(4,128)(2,1)S(1)}, u32[]{:S(2)}, u32[]{:S(2)}) %collective-permute-start.5) | collective-permute-done | bytes 266272 | tf_op jit(solution)/shard_map/ppermute | solution.py:298
  38.7 0.4 pad_maximum_fusion
  39.1 0.2 copy.106
  39.3 0.2 copy.120
  39.5 0.1 copy.109
  39.6 0.1 multiply_reduce_fusion
  39.7 0.1 copy.124
  39.8 0.1 add_select_fusion.1
  39.9 0.1 copy.111
  40.0 0.1 eq.57
  40.1 0.1 copy.112
  40.3 0.1 eq.60
  40.4 1.0 %bitcast_convert_fusion = bf16[64,128,128]{1,2,0:T(8,128)(2,1)S(1)} fusion(s32[128]{0:T(128)S(1)} %eq.60, s32[128]{0:T(128)S(1)} %eq.57, bf16[8,4,8320]{2,1,0:T(4,128)(2,1)S(1)} %bitcast.134, bf16[8,4,8320]{2,1,0:T(4,128)(2,1)S(1)} %bitcast.132), kind=kOutput, calls=%fused_computation | convolution fusion | flops 139493376 | bytes 3163136 | tf_op jit(solution)/shard_map/rsc,scbq->brq/dot_general | solution.py:497
  41.5 0.3 copy.114
  41.9 0.1 pad_maximum_fusion.2
  42.1 0.3 copy.115
  42.3 1.2 %convolution_multiply_fusion = f32[64,32,128]{2,1,0:T(8,128)S(1)} fusion(bf16[64,128,128]{1,2,0:T(8,128)(2,1)S(1)} %bitcast_convert_fusion, bf16[64,16,128]{2,1,0:T(8,128)(2,1)S(1)} %copy.115, bf16[64,16,128]{2,1,0:T(8,128)(2,1)S(1)} %dynamic-slice_bitcast_fusion), kind=kOutput, calls=%fused_computation.1 | convolution fusion | flops 68419584 | bytes 3670016 | tf_op jit(solution)/shard_map/bpq,bjq->bpj/dot_general | solution.py:505
  43.5 1.1 %copy.145 = f32[64,2,16,128]{3,2,0,1:T(8,128)} copy(f32[64,2,16,128]{3,2,1,0:T(8,128)S(1)} %bitcast.129) | data formatting | bytes 2097152 | tf_op jit(solution)/shard_map/div | solution.py:508
  (40 shorter events, 0.7 us)
Async XLA Ops:
  0.0 8.5 %copy-start = (f32[128]{0:T(128)S(1)}, f32[128]{0:T(128)}, u32[]{:S(2)}) copy-start(f32[128]{0:T(128)} %param.5) | copy-start | bytes 1540
  6.7 3.0 %copy-start.1 = (s32[1,8,2]{1,2,0:T(2,128)S(1)}, s32[1,8,2]{1,2,0:T(2,128)}, u32[]{:S(2)}) copy-start(s32[1,8,2]{1,2,0:T(2,128)} %param.7) | copy-start | bytes 196
  6.7 3.0 %copy-start.2 = (s32[1,8,2]{1,2,0:T(2,128)S(1)}, s32[1,8,2]{1,2,0:T(2,128)}, u32[]{:S(2)}) copy-start(s32[1,8,2]{1,2,0:T(2,128)} %param.6) | copy-start | bytes 196
  7.9 2.1 %collective-permute-start = (f32[2,144,256]{2,1,0:T(8,128)S(1)}, f32[2,144,256]{2,1,0:T(8,128)S(1)}, u32[]{:S(2)}, u32[]{:S(2)}) collective-permute-start(f32[2,144,256]{2,1,0:T(8,128)S(1)} %pad_maximum_fusion.3), channel_id=1, source_target_pairs={{0,1},{1,0},{2,3},{3,2},{4,5},{5,4},{6,7},{7,6},{8,9},{9,8},{10,11... | collective-permute-start | bytes 884744 | tf_op jit(solution)/shard_map/ppermute | solution.py:24
  11.7 9.8 %collective-permute-start.3 = (bf16[8,4096]{1,0:T(8,128)(2,1)S(1)}, bf16[8,4096]{1,0:T(8,128)(2,1)S(1)}, u32[]{:S(2)}, u32[]{:S(2)}) collective-permute-start(bf16[8,4096]{1,0:T(8,128)(2,1)S(1)} %reshape.357), channel_id=1, source_target_pairs={{0,18},{2,16},{4,22},{6,20},{8,26},{10,24},{12,30},{14,28},{16,2},... | collective-permute-start | bytes 196616 | tf_op jit(solution)/shard_map/ppermute | solution.py:421
  16.4 4.5 %collective-permute-start.1 = (bf16[8,4096]{1,0:T(8,128)(2,1)S(1)}, bf16[8,4096]{1,0:T(8,128)(2,1)S(1)}, u32[]{:S(2)}, u32[]{:S(2)}) collective-permute-start(bf16[8,4096]{1,0:T(8,128)(2,1)S(1)} %reshape.357), channel_id=1, source_target_pairs={{0,2},{2,0},{1,3},{3,1},{4,6},{6,4},{5,7},{7,5},{8,10},{10,8},{9,1... | collective-permute-start | bytes 196616 | tf_op jit(solution)/shard_map/ppermute | solution.py:415
  17.4 6.7 %collective-permute-start.2 = (bf16[8,4224]{1,0:T(8,128)(2,1)S(1)}, bf16[8,4224]{1,0:T(8,128)(2,1)S(1)}, u32[]{:S(2)}, u32[]{:S(2)}) collective-permute-start(bf16[8,4224]{1,0:T(8,128)(2,1)S(1)} %pad_maximum_fusion.11), channel_id=1, source_target_pairs={{0,16},{4,20},{8,24},{12,28},{16,0},{20,4},{24,8},{28,12},{1,17},{... | collective-permute-start | bytes 202760 | tf_op jit(solution)/shard_map/ppermute | solution.py:412
  24.6 5.1 %collective-permute-start.6 = (bf16[2,4,8320]{2,1,0:T(4,128)(2,1)S(1)}, bf16[2,4,8320]{2,1,0:T(4,128)(2,1)S(1)}, u32[]{:S(2)}, u32[]{:S(2)}) collective-permute-start(bf16[2,4,8320]{2,1,0:T(4,128)(2,1)S(1)} %get-tuple-element.17), channel_id=1, source_target_pairs={{0,4},{4,0},{8,12},{12,8},{16,20},{20,16},{24,28},{28,24},{1,5},{5... | collective-permute-start | bytes 399368 | tf_op jit(solution)/shard_map/ppermute | solution.py:298
  26.2 5.8 %collective-permute-start.4 = (bf16[2,4,8320]{2,1,0:T(4,128)(2,1)S(1)}, bf16[2,4,8320]{2,1,0:T(4,128)(2,1)S(1)}, u32[]{:S(2)}, u32[]{:S(2)}) collective-permute-start(bf16[2,4,8320]{2,1,0:T(4,128)(2,1)S(1)} %get-tuple-element.18), channel_id=1, source_target_pairs={{0,8},{4,12},{8,0},{12,4},{16,24},{20,28},{24,16},{28,20},{1,9},{5... | collective-permute-start | bytes 399368 | tf_op jit(solution)/shard_map/ppermute | solution.py:298
  29.8 7.1 %collective-permute-start.7 = (bf16[2,2,4,8320]{3,2,0,1:T(4,128)(2,1)S(1)}, bf16[2,2,4,8320]{3,2,0,1:T(4,128)(2,1)S(1)}, u32[]{:S(2)}, u32[]{:S(2)}) collective-permute-start(bf16[2,2,4,8320]{3,2,0,1:T(4,128)(2,1)S(1)} %get-tuple-element.16), channel_id=1, source_target_pairs={{0,8},{4,12},{8,0},{12,4},{16,24},{20,28},{24,16},{28,20},{1,9},{5... | collective-permute-start | bytes 798728 | tf_op jit(solution)/shard_map/ppermute | solution.py:298
  32.2 6.5 %collective-permute-start.5 = (bf16[2,2,4,8320]{3,2,0,1:T(4,128)(2,1)S(1)}, bf16[2,2,4,8320]{3,2,0,1:T(4,128)(2,1)S(1)}, u32[]{:S(2)}, u32[]{:S(2)}) collective-permute-start(bf16[2,2,4,8320]{3,2,0,1:T(4,128)(2,1)S(1)} %get-tuple-element.20), channel_id=1, source_target_pairs={{0,4},{4,0},{8,12},{12,8},{16,20},{20,16},{24,28},{28,24},{1,5},{5... | collective-permute-start | bytes 798728 | tf_op jit(solution)/shard_map/ppermute | solution.py:298

commit v25 on v24

--- a/solution.py
+++ b/solution.py
@@ -337,13 +337,16 @@
         own_edges = jnp.concatenate(
             [kept_blocks[:, :, :HW], kept_blocks[:, :, block_bins - HW :]], axis=2
         ).reshape(2, seg_count * 2 * HW, -1)
-        message = jnp.concatenate([sent, own_edges], axis=1)
-        arrived = swapped(message, "freq", 0)
-        spectra_pair = kept + arrived[:, :device_bins]
+        arrived_all = swapped(blocks, "freq", 0)
+        spectra_pair = kept + arrived_all[:, 1]
+        partner_own = arrived_all[:, 0].reshape(2, seg_count, block_bins, -1)
+        partner_edges = jnp.concatenate(
+            [partner_own[:, :, :HW], partner_own[:, :, block_bins - HW :]], axis=2
+        ).reshape(2, seg_count * 2 * HW, -1)
         their_edges = jnp.concatenate(
             [sent_blocks[:, :, :HW], sent_blocks[:, :, block_bins - HW :]], axis=2
         ).reshape(2, seg_count * 2 * HW, -1)
-        edge_spectra = (their_edges + arrived[:, device_bins:]).reshape(2, seg_count, 2, HW, -1)
+        edge_spectra = (their_edges + partner_edges).reshape(2, seg_count, 2, HW, -1)
         partner = jnp.transpose(
             jnp.sqrt(edge_spectra[0] * edge_spectra[0] + edge_spectra[1] * edge_spectra[1] + 1e-06),
             (1, 0, 2, 3),

time: 44.8 us -> 45.2 us (level)
  waiting for transfers between devices: 16.2 us -> 12.9 us
  starting transfers between devices: 8.36 us -> 11 us
  other arithmetic: 3.72 us -> 4.75 us
    ppermute x4, starting transfers between devices: 2.52 us -> 4.9 us  [gather_blocks(): arrived = lax.ppermute(part, 'blk', pairs)]
    ppermute x4, waiting for transfers between devices: 10.5 us -> 8.22 us  [gather_blocks(): arrived = lax.ppermute(part, 'blk', pairs)]
    slice x0 -> x1, other arithmetic: none -> 1.17 us  [per_device(): partner_own = arrived_all[:, 0].reshape(2, seg_count, block_bins, -1)]
    ppermute x1, waiting for transfers between devices: 2.31 us -> 1.32 us  [per_device(): lax.ppermute(keep_flat, 'blk', [(source, source ^ first) for source in ra...]
where the time goes in v25:
time: 45.2 us; the launch traced here: 45 us
  waiting for transfers between devices  12.9 us (29%)
  starting transfers between devices  11 us (24%)
  Pallas kernels  6.7 us (15%)
  local copies, waits for them, and re-layouts  5.99 us (13%)
  other arithmetic  4.75 us (11%)
  matrix products  3.25 us (7%)
    ppermute x4, waiting for transfers between devices, gather_blocks(): arrived = lax.ppermute(part, 'blk', pairs)  8.22 us
    pallas_call x1, Pallas kernels, dft_fused(): pl.pallas_call(kernel, grid=(count // chunk,), in_specs=leading + [pl.Blo...  6.7 us
    ppermute x1, starting transfers between devices, per_device(): from_diagonal = lax.ppermute(other_flat, ('blk', 'seg'), diagonal)  4.9 us
    ppermute x4, starting transfers between devices, gather_blocks(): arrived = lax.ppermute(part, 'blk', pairs)  4.9 us
    ppermute x1, waiting for transfers between devices, per_device(): from_seg = lax.ppermute(other_flat, 'seg', [(0, 1), (1, 0)])  3.32 us
    ppermute x1, waiting for transfers between devices, per_device(): lax.ppermute(keep_flat, 'blk', [(source, source ^ first) for source in ra...  1.32 us
    dot_general x1, matrix products, per_device(): jnp.einsum('bpq,bjq->bpj', lhs, routed, preferred_element_type=jnp.float32)  1.19 us
    another operation x4, other arithmetic, gather_blocks(): part = jnp.stack([part, arrived], axis=axis)  1.18 us
  transfers between devices with their start and end apart: 8, of which 6 were waited for; matrix products, arithmetic and copies ran while one was open for 9% of the time, Pallas kernels for 0%

profile of v25, /device:TPU:0, one launch (start us, length us, event | category | flops | bytes accessed | tf_op | source)
XLA Modules:
  0.0 45.0 jit_solution(5841419444553669687)
XLA Ops:
  0.0 6.7 %shard_map.46 = (f32[256,256]{1,0:T(8,128)}, f32[256,256]{1,0:T(8,128)}) custom-call(bf16[256,8192]{1,0:T(8,128)(2,1)} %bitcast.123), custom_call_target="tpu_custom_call" | custom-call | tf_op jit(solution)/shard_map/pallas_call | solution.py:223
  6.7 1.1 %pad_maximum_fusion = f32[2,2,128,256]{3,2,0,1:T(8,128)S(1)} fusion(f32[1,2,128,256]{3,2,0,1:T(8,128)} %bitcast.132, f32[1,2,128,256]{3,2,0,1:T(8,128)} %bitcast.130), kind=kLoop, calls=%fused_computation.15 | loop fusion | flops 131072 | bytes 1048576 | tf_op jit(solution)/shard_map/stack | solution.py:331
  7.8 0.5 %collective-permute-start = (f32[2,2,128,256]{3,2,0,1:T(8,128)S(1)}, f32[2,2,128,256]{3,2,0,1:T(8,128)S(1)}, u32[]{:S(2)}, u32[]{:S(2)}) collective-permute-start(f32[2,2,128,256]{3,2,0,1:T(8,128)S(1)} %pad_maximum_fusion), channel_id=1, source_target_pairs={{0,1},{1,0},{2,3},{3,2},{4,5},{5,4},{6,7},{7,6},{8,9},{9,8},{10,11... | collective-permute-start | bytes 1572872 | tf_op jit(solution)/shard_map/ppermute | solution.py:24
  8.3 0.5 %convolution_bitcast_fusion = f32[128]{0:T(128)S(1)} fusion(s32[128]{0:T(128)S(1)} %fusion.58, f32[128]{0:T(128)S(1)} %copy-done), kind=kOutput, calls=%fused_computation.4 | convolution fusion | flops 442368 | bytes 1536 | tf_op jit(solution)/shard_map/dot_general | solution.py:67
  8.8 0.5 %convolution_bitcast_fusion.1 = f32[128]{0:T(128)S(1)} fusion(s32[128]{0:T(128)S(1)} %fusion.58, f32[128]{0:T(128)S(1)} %copy-done), kind=kOutput, calls=%fused_computation.5 | convolution fusion | flops 425984 | bytes 1536 | tf_op jit(solution)/shard_map/dot_general | solution.py:66
  9.3 0.1 mul.196
  9.4 0.1 mul.199
  9.6 0.1 copy.104
  9.7 0.1 convert_element_type.37
  9.9 1.2 %fusion.69 = (f32[2,1,128,256]{3,2,0,1:T(8,128)S(1)}, f32[2,1,128,256]{3,2,0,1:T(8,128)S(1)}, f32[2,1,128,256]{3,2,0,1:T(8,128)S(1)}) fusion(f32[2,2,128,256]{3,2,0,1:T(8,128)S(1)} %collective-permute-done, f32[1,2,128,256]{3,2,0,1:T(8,128)} %bitcast.133, f32[1,2,128,256]{3,2,0,1:T(8,128)} %bitcast.131), kind=kLoop, calls=%fused_computation.156 | loop fusion | flops 196608 | bytes 1835008 | tf_op jit(solution)/shard_map/slice | solution.py:342
  11.3 0.1 copy.97
  11.4 0.1 fusion.16
  11.5 0.1 copy.94
  11.6 0.2 squeeze.35
  11.8 0.1 copy.89
  11.9 0.2 squeeze.32
  12.1 0.1 add_convert_fusion
  12.3 0.2 copy.101
  12.5 0.3 reshape.369
  12.8 4.9 %collective-permute-start.3 = (bf16[8,4096]{1,0:T(8,128)(2,1)S(1)}, bf16[8,4096]{1,0:T(8,128)(2,1)S(1)}, u32[]{:S(2)}, u32[]{:S(2)}) collective-permute-start(bf16[8,4096]{1,0:T(8,128)(2,1)S(1)} %reshape.369), channel_id=1, source_target_pairs={{0,18},{2,16},{4,22},{6,20},{8,26},{10,24},{12,30},{14,28},{16,2},... | collective-permute-start | bytes 196616 | tf_op jit(solution)/shard_map/ppermute | solution.py:424
  17.7 0.5 %collective-permute-start.1 = (bf16[8,4096]{1,0:T(8,128)(2,1)S(1)}, bf16[8,4096]{1,0:T(8,128)(2,1)S(1)}, u32[]{:S(2)}, u32[]{:S(2)}) collective-permute-start(bf16[8,4096]{1,0:T(8,128)(2,1)S(1)} %reshape.369), channel_id=1, source_target_pairs={{0,2},{2,0},{1,3},{3,1},{4,6},{6,4},{5,7},{7,5},{8,10},{10,8},{9,1... | collective-permute-start | bytes 196616 | tf_op jit(solution)/shard_map/ppermute | solution.py:418
  18.2 0.2 copy.105
  18.4 0.3 reshape.373
  18.7 0.2 collective-permute-start.2
  18.9 3.3 %collective-permute-done.1 = bf16[8,4096]{1,0:T(8,128)(2,1)S(1)} collective-permute-done((bf16[8,4096]{1,0:T(8,128)(2,1)S(1)}, bf16[8,4096]{1,0:T(8,128)(2,1)S(1)}, u32[]{:S(2)}, u32[]{:S(2)}) %collective-permute-start.1) | collective-permute-done | bytes 65568 | tf_op jit(solution)/shard_map/ppermute | solution.py:418
  22.2 0.2 reshape.370
  22.4 0.1 copy.102
  22.6 0.1 copy.103
  22.7 0.1 copy.145
  22.9 0.2 reshape.375
  23.0 1.3 %collective-permute-done.2 = bf16[8,4224]{1,0:T(8,128)(2,1)S(1)} collective-permute-done((bf16[8,4224]{1,0:T(8,128)(2,1)S(1)}, bf16[8,4224]{1,0:T(8,128)(2,1)S(1)}, u32[]{:S(2)}, u32[]{:S(2)}) %collective-permute-start.2) | collective-permute-done | bytes 67616 | tf_op jit(solution)/shard_map/ppermute | solution.py:415
  24.4 0.2 reshape.374
  24.5 0.1 maximum_bitcast_fusion.2
  24.7 0.1 copy.144
  24.8 0.1 pad_maximum_fusion.7
  24.9 1.6 %collective-permute-start.6 = (bf16[2,4,8320]{2,1,0:T(4,128)(2,1)S(1)}, bf16[2,4,8320]{2,1,0:T(4,128)(2,1)S(1)}, u32[]{:S(2)}, u32[]{:S(2)}) collective-permute-start(bf16[2,4,8320]{2,1,0:T(4,128)(2,1)S(1)} %get-tuple-element.18), channel_id=1, source_target_pairs={{0,4},{4,0},{8,12},{12,8},{16,20},{20,16},{24,28},{28,24},{1,5},{5... | collective-permute-start | bytes 399368 | tf_op jit(solution)/shard_map/ppermute | solution.py:298
  26.6 1.3 %collective-permute-start.4 = (bf16[2,4,8320]{2,1,0:T(4,128)(2,1)S(1)}, bf16[2,4,8320]{2,1,0:T(4,128)(2,1)S(1)}, u32[]{:S(2)}, u32[]{:S(2)}) collective-permute-start(bf16[2,4,8320]{2,1,0:T(4,128)(2,1)S(1)} %get-tuple-element.19), channel_id=1, source_target_pairs={{0,8},{4,12},{8,0},{12,4},{16,24},{20,28},{24,16},{28,20},{1,9},{5... | collective-permute-start | bytes 399368 | tf_op jit(solution)/shard_map/ppermute | solution.py:298
  27.8 2.1 %collective-permute-done.6 = bf16[2,4,8320]{2,1,0:T(4,128)(2,1)S(1)} collective-permute-done((bf16[2,4,8320]{2,1,0:T(4,128)(2,1)S(1)}, bf16[2,4,8320]{2,1,0:T(4,128)(2,1)S(1)}, u32[]{:S(2)}, u32[]{:S(2)}) %collective-permute-start.6) | collective-permute-done | bytes 133152 | tf_op jit(solution)/shard_map/ppermute | solution.py:298
  29.9 0.2 fusion.66
  30.2 1.3 %collective-permute-start.7 = (bf16[2,2,4,8320]{3,2,0,1:T(4,128)(2,1)S(1)}, bf16[2,2,4,8320]{3,2,0,1:T(4,128)(2,1)S(1)}, u32[]{:S(2)}, u32[]{:S(2)}) collective-permute-start(bf16[2,2,4,8320]{3,2,0,1:T(4,128)(2,1)S(1)} %get-tuple-element.17), channel_id=1, source_target_pairs={{0,8},{4,12},{8,0},{12,4},{16,24},{20,28},{24,16},{28,20},{1,9},{5... | collective-permute-start | bytes 798728 | tf_op jit(solution)/shard_map/ppermute | solution.py:298
  31.5 0.9 %collective-permute-done.4 = bf16[2,4,8320]{2,1,0:T(4,128)(2,1)S(1)} collective-permute-done((bf16[2,4,8320]{2,1,0:T(4,128)(2,1)S(1)}, bf16[2,4,8320]{2,1,0:T(4,128)(2,1)S(1)}, u32[]{:S(2)}, u32[]{:S(2)}) %collective-permute-start.4) | collective-permute-done | bytes 133152 | tf_op jit(solution)/shard_map/ppermute | solution.py:298
  32.4 0.2 fusion.67
  32.6 0.7 %collective-permute-start.5 = (bf16[2,2,4,8320]{3,2,0,1:T(4,128)(2,1)S(1)}, bf16[2,2,4,8320]{3,2,0,1:T(4,128)(2,1)S(1)}, u32[]{:S(2)}, u32[]{:S(2)}) collective-permute-start(bf16[2,2,4,8320]{3,2,0,1:T(4,128)(2,1)S(1)} %get-tuple-element.21), channel_id=1, source_target_pairs={{0,4},{4,0},{8,12},{12,8},{16,20},{20,16},{24,28},{28,24},{1,5},{5... | collective-permute-start | bytes 798728 | tf_op jit(solution)/shard_map/ppermute | solution.py:298
  33.3 3.9 %collective-permute-done.7 = bf16[2,2,4,8320]{3,2,0,1:T(4,128)(2,1)S(1)} collective-permute-done((bf16[2,2,4,8320]{3,2,0,1:T(4,128)(2,1)S(1)}, bf16[2,2,4,8320]{3,2,0,1:T(4,128)(2,1)S(1)}, u32[]{:S(2)}, u32[]{:S(2)}) %collective-permute-start.7) | collective-permute-done | bytes 266272 | tf_op jit(solution)/shard_map/ppermute | solution.py:298
  37.2 0.4 pad_maximum_fusion.2
  37.6 0.2 copy.107
  37.8 1.3 %collective-permute-done.5 = bf16[2,2,4,8320]{3,2,0,1:T(4,128)(2,1)S(1)} collective-permute-done((bf16[2,2,4,8320]{3,2,0,1:T(4,128)(2,1)S(1)}, bf16[2,2,4,8320]{3,2,0,1:T(4,128)(2,1)S(1)}, u32[]{:S(2)}, u32[]{:S(2)}) %collective-permute-start.5) | collective-permute-done | bytes 266272 | tf_op jit(solution)/shard_map/ppermute | solution.py:298
  39.1 0.4 pad_maximum_fusion.1
  39.5 0.2 copy.106
  39.7 0.2 copy.120
  39.9 0.1 copy.109
  40.0 0.1 multiply_reduce_fusion
  40.1 0.1 copy.122
  40.2 0.1 add_select_fusion.1
  40.3 0.1 copy.111
  40.4 0.1 eq.57
  40.6 0.1 copy.112
  40.7 0.1 eq.60
  40.8 1.0 %bitcast_convert_fusion = bf16[64,128,128]{1,2,0:T(8,128)(2,1)S(1)} fusion(s32[128]{0:T(128)S(1)} %eq.60, s32[128]{0:T(128)S(1)} %eq.57, bf16[8,4,8320]{2,1,0:T(4,128)(2,1)S(1)} %bitcast.127, bf16[8,4,8320]{2,1,0:T(4,128)(2,1)S(1)} %bitcast.125), kind=kOutput, calls=%fused_computation | convolution fusion | flops 139493376 | bytes 3163136 | tf_op jit(solution)/shard_map/rsc,scbq->brq/dot_general | solution.py:500
  41.9 0.3 copy.114
  42.4 0.1 pad_maximum_fusion.3
  42.5 0.3 copy.115
  42.8 1.2 %convolution_multiply_fusion = f32[64,32,128]{2,1,0:T(8,128)S(1)} fusion(bf16[64,128,128]{1,2,0:T(8,128)(2,1)S(1)} %bitcast_convert_fusion, bf16[64,16,128]{2,1,0:T(8,128)(2,1)S(1)} %copy.115, bf16[64,16,128]{2,1,0:T(8,128)(2,1)S(1)} %dynamic-slice_bitcast_fusion), kind=kOutput, calls=%fused_computation.1 | convolution fusion | flops 68419584 | bytes 3670016 | tf_op jit(solution)/shard_map/bpq,bjq->bpj/dot_general | solution.py:508
  44.0 1.1 %copy.143 = f32[64,2,16,128]{3,2,0,1:T(8,128)} copy(f32[64,2,16,128]{3,2,1,0:T(8,128)S(1)} %bitcast.122) | data formatting | bytes 2097152 | tf_op jit(solution)/shard_map/div | solution.py:511
  (39 shorter events, 0.7 us)
Async XLA Ops:
  0.0 8.3 %copy-start = (f32[128]{0:T(128)S(1)}, f32[128]{0:T(128)}, u32[]{:S(2)}) copy-start(f32[128]{0:T(128)} %param.5) | copy-start | bytes 1540
  0.0 9.5 %copy-start.1 = (s32[1,8,2]{1,2,0:T(2,128)S(1)}, s32[1,8,2]{1,2,0:T(2,128)}, u32[]{:S(2)}) copy-start(s32[1,8,2]{1,2,0:T(2,128)} %param.7) | copy-start | bytes 196
  0.0 9.5 %copy-start.2 = (s32[1,8,2]{1,2,0:T(2,128)S(1)}, s32[1,8,2]{1,2,0:T(2,128)}, u32[]{:S(2)}) copy-start(s32[1,8,2]{1,2,0:T(2,128)} %param.6) | copy-start | bytes 196
  7.8 2.1 %collective-permute-start = (f32[2,2,128,256]{3,2,0,1:T(8,128)S(1)}, f32[2,2,128,256]{3,2,0,1:T(8,128)S(1)}, u32[]{:S(2)}, u32[]{:S(2)}) collective-permute-start(f32[2,2,128,256]{3,2,0,1:T(8,128)S(1)} %pad_maximum_fusion), channel_id=1, source_target_pairs={{0,1},{1,0},{2,3},{3,2},{4,5},{5,4},{6,7},{7,6},{8,9},{9,8},{10,11... | collective-permute-start | bytes 1572872 | tf_op jit(solution)/shard_map/ppermute | solution.py:24
  12.8 10.1 %collective-permute-start.3 = (bf16[8,4096]{1,0:T(8,128)(2,1)S(1)}, bf16[8,4096]{1,0:T(8,128)(2,1)S(1)}, u32[]{:S(2)}, u32[]{:S(2)}) collective-permute-start(bf16[8,4096]{1,0:T(8,128)(2,1)S(1)} %reshape.369), channel_id=1, source_target_pairs={{0,18},{2,16},{4,22},{6,20},{8,26},{10,24},{12,30},{14,28},{16,2},... | collective-permute-start | bytes 196616 | tf_op jit(solution)/shard_map/ppermute | solution.py:424
  17.7 4.5 %collective-permute-start.1 = (bf16[8,4096]{1,0:T(8,128)(2,1)S(1)}, bf16[8,4096]{1,0:T(8,128)(2,1)S(1)}, u32[]{:S(2)}, u32[]{:S(2)}) collective-permute-start(bf16[8,4096]{1,0:T(8,128)(2,1)S(1)} %reshape.369), channel_id=1, source_target_pairs={{0,2},{2,0},{1,3},{3,1},{4,6},{6,4},{5,7},{7,5},{8,10},{10,8},{9,1... | collective-permute-start | bytes 196616 | tf_op jit(solution)/shard_map/ppermute | solution.py:418
  18.7 5.7 %collective-permute-start.2 = (bf16[8,4224]{1,0:T(8,128)(2,1)S(1)}, bf16[8,4224]{1,0:T(8,128)(2,1)S(1)}, u32[]{:S(2)}, u32[]{:S(2)}) collective-permute-start(bf16[8,4224]{1,0:T(8,128)(2,1)S(1)} %pad_maximum_fusion.10), channel_id=1, source_target_pairs={{0,16},{4,20},{8,24},{12,28},{16,0},{20,4},{24,8},{28,12},{1,17},{... | collective-permute-start | bytes 202760 | tf_op jit(solution)/shard_map/ppermute | solution.py:415
  24.9 5.1 %collective-permute-start.6 = (bf16[2,4,8320]{2,1,0:T(4,128)(2,1)S(1)}, bf16[2,4,8320]{2,1,0:T(4,128)(2,1)S(1)}, u32[]{:S(2)}, u32[]{:S(2)}) collective-permute-start(bf16[2,4,8320]{2,1,0:T(4,128)(2,1)S(1)} %get-tuple-element.18), channel_id=1, source_target_pairs={{0,4},{4,0},{8,12},{12,8},{16,20},{20,16},{24,28},{28,24},{1,5},{5... | collective-permute-start | bytes 399368 | tf_op jit(solution)/shard_map/ppermute | solution.py:298
  26.6 5.9 %collective-permute-start.4 = (bf16[2,4,8320]{2,1,0:T(4,128)(2,1)S(1)}, bf16[2,4,8320]{2,1,0:T(4,128)(2,1)S(1)}, u32[]{:S(2)}, u32[]{:S(2)}) collective-permute-start(bf16[2,4,8320]{2,1,0:T(4,128)(2,1)S(1)} %get-tuple-element.19), channel_id=1, source_target_pairs={{0,8},{4,12},{8,0},{12,4},{16,24},{20,28},{24,16},{28,20},{1,9},{5... | collective-permute-start | bytes 399368 | tf_op jit(solution)/shard_map/ppermute | solution.py:298
  30.2 7.1 %collective-permute-start.7 = (bf16[2,2,4,8320]{3,2,0,1:T(4,128)(2,1)S(1)}, bf16[2,2,4,8320]{3,2,0,1:T(4,128)(2,1)S(1)}, u32[]{:S(2)}, u32[]{:S(2)}) collective-permute-start(bf16[2,2,4,8320]{3,2,0,1:T(4,128)(2,1)S(1)} %get-tuple-element.17), channel_id=1, source_target_pairs={{0,8},{4,12},{8,0},{12,4},{16,24},{20,28},{24,16},{28,20},{1,9},{5... | collective-permute-start | bytes 798728 | tf_op jit(solution)/shard_map/ppermute | solution.py:298
  32.6 6.5 %collective-permute-start.5 = (bf16[2,2,4,8320]{3,2,0,1:T(4,128)(2,1)S(1)}, bf16[2,2,4,8320]{3,2,0,1:T(4,128)(2,1)S(1)}, u32[]{:S(2)}, u32[]{:S(2)}) collective-permute-start(bf16[2,2,4,8320]{3,2,0,1:T(4,128)(2,1)S(1)} %get-tuple-element.21), channel_id=1, source_target_pairs={{0,4},{4,0},{8,12},{12,8},{16,20},{20,16},{24,28},{28,24},{1,5},{5... | collective-permute-start | bytes 798728 | tf_op jit(solution)/shard_map/ppermute | solution.py:298
